TPU v7x, 256 devices: a whole 4x4x8 slice. The times are simulated.
256 devices in a mesh: cast: 64 (over z, x, core), width: 4 (over y).
Axes of the slice: x: 4, y: 4, z: 8, core: 2. Of those that a mesh axis runs over, the one named last changes fastest.
Arguments:
- stored_caloric_content: float32 [64, 512, 512], P(None, 'cast', 'width'), may hold values from -6 to 6
- zones: int32 [2, 512, 512], P(None, 'cast', 'width'), may hold values from 0 to 9
- spray_coef: float32 [10], replicated, may hold values from 0.2 to 5
Outputs:
- new_enthalpy: float32 [64, 512, 512], P(None, 'cast', 'width')
All inputs are finite; a program needn't handle non-finite values.
Results may differ from a plain program's by a relative error of at most 0.0018.
Values sent between devices are 32-bit elements; how exact they have to be, the bound alone decides.
No kernel may reach another device: no remote copies, remote signals or barrier semaphores. Data moves between devices by JAX's collectives and lax.ppermute only.
A program may use at most 64 MiB of HBM per device.

v0:
```python
import jax
import jax.numpy as jnp
from jax import lax
from jax.sharding import Mesh
from jax.sharding import PartitionSpec as P

CAST = ("cast_0", "cast_1", "cast_2")


solidification_release = 0.4
quench_medium_hotness = -2.0


def in_blocks(value, dim, size):
    before, after = (value.shape[:dim], value.shape[dim + 1 :])
    return jnp.moveaxis(value.reshape(*before, size, -1, *after), dim, 0)


def in_order(tiles, dim):
    dims = list(tiles.shape[1:])
    dims[dim] *= tiles.shape[0]
    return jnp.moveaxis(tiles, 0, dim).reshape(dims)


def exchange_in_order(tiles, axes, sequence):
    inside = tiles.shape[1:]
    out = tiles.reshape(*(lax.axis_size(a) for a in axes), *inside)
    for k in sequence:
        out = lax.all_to_all(out, axes[k], k, k, tiled=True)
    return out.reshape(-1, *inside)


def exchange_by_chip(value, groups, sequence, split_dim, concat_dim):
    size = lax.axis_size(groups[0]) * lax.axis_size(groups[1])
    tiles = in_blocks(value, split_dim, size)
    return in_order(exchange_in_order(tiles, groups, sequence), concat_dim)


def from_everyone(value, axis):
    size = lax.axis_size(axis)
    return lax.all_to_all(
        jnp.broadcast_to(value[None], (size, *value.shape)), axis, 0, 0, tiled=True
    )


def combined_pairwise(pieces, combine):
    while len(jax.tree.leaves(pieces)[0]) > 1:
        pieces = jax.vmap(combine)(
            *(jax.tree.map(lambda part: part[side::2], pieces) for side in (0, 1))
        )
    return jax.tree.map(lambda part: part[0], pieces)


def entering(value, axis, combine, identity, reverse):
    size, place = (lax.axis_size(axis), lax.axis_index(axis))
    passed = jnp.arange(size) > place if reverse else jnp.arange(size) < place

    def kept(part, zero, own):
        part = jnp.where(
            passed.reshape(-1, *(1 for _ in own.shape)), part, jnp.asarray(zero, own.dtype)
        )
        return part[::-1] if reverse else part

    pieces = jax.tree.map(lambda part: from_everyone(part, axis), value)
    return combined_pairwise(jax.tree.map(kept, pieces, identity, value), combine)


def extended(value, sides, width):
    edges = {}
    for axis, dim in sides:
        size, length = (lax.axis_size(axis), value.shape[dim])
        up = [(i, (i + 1) % size) for i in range(size - 1)]
        last = lax.slice_in_dim(value, length - width, length, axis=dim)
        first = lax.slice_in_dim(value, 0, width, axis=dim)
        edges[dim] = (
            lax.ppermute(last, axis, up),
            lax.ppermute(first, axis, [(b, a) for a, b in up]),
        )
    done = []
    for _, dim in sides:
        low, high = edges[dim]
        around = [(width, width) if d in done else (0, 0) for d in range(value.ndim)]
        value = jnp.concatenate([jnp.pad(low, around), value, jnp.pad(high, around)], axis=dim)
        done.append(dim)
    return value


def medium_parameters(caloric_content_mesh):
    phase_change_threshold = jnp.tanh(caloric_content_mesh)
    hotness_mesh = caloric_content_mesh - solidification_release * phase_change_threshold
    transport_modulus = 1.5 - 0.5 * jnp.tanh(hotness_mesh)
    caloric_content_incline = (
        1.0
        - solidification_release
        + solidification_release * phase_change_threshold * phase_change_threshold
    )
    return (hotness_mesh, transport_modulus, caloric_content_incline)


def displaced_entries_list(caloric_content_mesh):
    before = jnp.concatenate([caloric_content_mesh[:1], caloric_content_mesh[:-1]], 0)
    after = jnp.concatenate([caloric_content_mesh[1:], caloric_content_mesh[-1:]], 0)
    return (before, after)


def sweep(step, carry, seqs, reverse):
    count_rows = seqs[0].shape[0]
    block_size = 8 if count_rows % 8 == 0 else 1
    blocks = tuple(
        (piece.reshape((count_rows // block_size, block_size) + piece.shape[1:]) for piece in seqs)
    )

    def outer(state, block):
        results = [None] * block_size
        order = range(block_size - 1, -1, -1) if reverse else range(block_size)
        for position in order:
            state, produced = step(state, tuple((member[position] for member in block)))
            results[position] = produced
        return (state, jax.tree.map(lambda *values: jnp.stack(values), *results))

    state, stacked = lax.scan(outer, carry, blocks, reverse=reverse)
    stacked = jax.tree.map(lambda value: value.reshape((count_rows,) + value.shape[2:]), stacked)
    return (state, stacked)


def compose_step(matrix, row_vals):
    lower_row, middle_row, upper_row, source_row = row_vals
    top_row, centre_row, bottom_row = matrix
    new_top = upper_row * bottom_row
    new_centre = source_row * bottom_row - lower_row * centre_row
    new_bottom = middle_row * bottom_row - lower_row * top_row
    scale = jnp.max(jnp.abs(jnp.stack([new_top, new_centre, new_bottom])), axis=(0, 1))
    return ((new_top / scale, new_centre / scale, new_bottom / scale), None)


def compose_lines(lower, middle, upper, source):
    lines = lower.shape[1]
    zeros_line = jnp.zeros((lines,), jnp.float32)
    ones_line = jnp.ones((lines,), jnp.float32)
    start = (
        jnp.stack([ones_line, zeros_line, zeros_line]),
        jnp.stack([zeros_line, ones_line, zeros_line]),
        jnp.stack([zeros_line, zeros_line, ones_line]),
    )
    final, _ = sweep(compose_step, start, (lower, middle, upper, source), False)
    return jnp.stack(final)


def eliminate(state, row_vals):
    cprime, dprime = state
    lower_row, middle_row, upper_row, source_row = row_vals
    pivot = middle_row - lower_row * cprime
    new_c = upper_row / pivot
    new_d = (source_row - lower_row * dprime) / pivot
    return ((new_c, new_d), (new_c, new_d))


def collapse(state, row_vals):
    alpha_next, beta_next = state
    cprime, dprime = row_vals
    alpha_val = dprime - cprime * alpha_next
    beta_val = -cprime * beta_next
    return ((alpha_val, beta_val), (alpha_val, beta_val))


def substitute(after_val, row_vals):
    cprime, dprime = row_vals
    value = dprime - cprime * after_val
    return (value, value)


def pass_device(state, row_vals):
    matrix = row_vals[0]
    cprime, dprime = state
    top_val = matrix[0, 0] * cprime + matrix[0, 1] * dprime + matrix[0, 2]
    centre_val = matrix[1, 0] * cprime + matrix[1, 1] * dprime + matrix[1, 2]
    bottom_val = matrix[2, 0] * cprime + matrix[2, 1] * dprime + matrix[2, 2]
    return ((top_val / bottom_val, centre_val / bottom_val), (cprime, dprime))


def climb(after_val, row_vals):
    alpha_val, beta_val = row_vals
    return (alpha_val + beta_val * after_val, after_val)


def chain_matrices(earlier, later):
    product = jnp.sum(later[:, :, None, :] * earlier[None, :, :, :], axis=1)
    scale = jnp.max(jnp.abs(product), axis=(0, 1))
    return product / scale[None, None]


def chain_maps(earlier, later):
    return (later[0] + later[1] * earlier[0], later[1] * earlier[1])


def identity_matrix(lines):
    return jnp.eye(3, dtype=jnp.float32)[:, :, None] * jnp.ones((1, 1, lines), jnp.float32)


def states_from(prefix):
    column = prefix[:, 2, :]
    return (column[0] / column[2], column[1] / column[2])


def forward_states(received):
    groups = received.shape[1]
    count_lines = received.shape[2]
    moved = jnp.moveaxis(received.reshape(3, 3, groups, count_lines), 2, 0)
    zeros_line = jnp.zeros((count_lines,), jnp.float32)
    _, (cprimes, dprimes) = sweep(pass_device, (zeros_line, zeros_line), (moved,), False)
    states = jnp.stack([cprimes, dprimes])
    return lax.all_to_all(states, CAST, split_axis=1, concat_axis=1, tiled=True)


def backward_values(received):
    count_lines = received.shape[2]
    zeros_line = jnp.zeros((count_lines,), jnp.float32)
    _, values = sweep(climb, zeros_line, (received[0], received[1]), True)
    return lax.all_to_all(values[None], CAST, split_axis=1, concat_axis=1, tiled=True)


def cast_forward(matrix):
    lines = matrix.shape[2]
    groups = lax.axis_size(CAST)
    packed = matrix.reshape(9, groups, lines // groups)
    result = forward_states(lax.all_to_all(packed, CAST, split_axis=1, concat_axis=1, tiled=True))
    result = result.reshape(2, lines)
    incoming = (result[0], result[1])
    return incoming


def cast_backward(alpha_first, beta_first):
    lines = alpha_first.shape[0]
    groups = lax.axis_size(CAST)
    packed = jnp.stack([alpha_first, beta_first]).reshape(2, groups, lines // groups)
    result = backward_values(
        exchange_by_chip(packed, (("cast_0", "cast_1"), "cast_2"), (1, 0), 1, 1)
    )
    following = result.reshape(lines)
    return following


def width_forward(matrix):
    lines = matrix.shape[2]
    prefix = entering(matrix, "width", chain_matrices, identity_matrix(lines), False)
    incoming = states_from(prefix)
    return incoming


def width_backward(alpha_first, beta_first):
    lines = alpha_first.shape[0]
    zeros_line = jnp.zeros((lines,), jnp.float32)
    ones_line = jnp.ones((lines,), jnp.float32)
    total = entering((alpha_first, beta_first), "width", chain_maps, (zeros_line, ones_line), True)
    following = total[0]
    return following


def distributed_solve(lower, middle, upper, source, forward_link, backward_link):
    lines = lower.shape[1]
    matrix = compose_lines(lower, middle, upper, source)
    incoming = forward_link(matrix)
    _, (cprimes, dprimes) = sweep(eliminate, incoming, (lower, middle, upper, source), False)
    zeros_line = jnp.zeros((lines,), jnp.float32)
    ones_line = jnp.ones((lines,), jnp.float32)
    _, (alphas, betas) = sweep(collapse, (zeros_line, ones_line), (cprimes, dprimes), True)
    following = backward_link(alphas[0], betas[0])
    return alphas + betas * following[None]


def local_solve(lower, middle, upper, source):
    zeros_line = jnp.zeros((lower.shape[1],), jnp.float32)
    _, (cprimes, dprimes) = sweep(
        eliminate, (zeros_line, zeros_line), (lower, middle, upper, source), False
    )
    _, values = sweep(substitute, zeros_line, (cprimes, dprimes), True)
    return values


def shards(stored_caloric_content, zones, spray_coef):
    depth_cells, rows_cast, rows_width = stored_caloric_content.shape
    widened_mesh = extended(stored_caloric_content, ((CAST, 1), ("width", 2)), 1)
    hotness_widened, widened_transport_modulus, widened_incline = medium_parameters(widened_mesh)
    hotness_mesh = hotness_widened[:, 1:-1, 1:-1]
    transport_modulus = widened_transport_modulus[:, 1:-1, 1:-1]
    caloric_content_incline = widened_incline[:, 1:-1, 1:-1]
    cast_low = (lax.axis_index(CAST) > 0).astype(jnp.float32)
    cast_high = (lax.axis_index(CAST) < lax.axis_size(CAST) - 1).astype(jnp.float32)
    width_low = (lax.axis_index("width") > 0).astype(jnp.float32)
    width_high = (lax.axis_index("width") < lax.axis_size("width") - 1).astype(jnp.float32)
    edge_cast = jnp.ones((rows_cast + 1,), jnp.float32).at[0].set(cast_low).at[-1].set(cast_high)
    edge_width = (
        jnp.ones((rows_width + 1,), jnp.float32).at[0].set(width_low).at[-1].set(width_high)
    )
    gain_cast = rows_cast * rows_cast * 4.0
    cast_faces = (
        gain_cast
        * 0.5
        * (widened_transport_modulus[:, 1:, 1:-1] + widened_transport_modulus[:, :-1, 1:-1])
        * edge_cast[None, :, None]
    )
    pour_sweep_sub_band = cast_faces[:, :-1]
    casting_upper = cast_faces[:, 1:]
    gain_width = rows_width * rows_width / 4.0
    width_faces = (
        gain_width
        * 0.5
        * (widened_transport_modulus[:, 1:-1, 1:] + widened_transport_modulus[:, 1:-1, :-1])
        * edge_width[None, None, :]
    )
    spanwise_sub_band = width_faces[:, :, :-1]
    width_upper = width_faces[:, :, 1:]
    gain_thick = depth_cells * depth_cells / 4.0
    thick_mid = gain_thick * 0.5 * (transport_modulus[1:] + transport_modulus[:-1])
    zero_face = jnp.zeros((1, rows_cast, rows_width), jnp.float32)
    transverse_sub_band = jnp.concatenate([zero_face, thick_mid], 0)
    transverse_super_band = jnp.concatenate([thick_mid, zero_face], 0)
    zone_ids = jnp.arange(spray_coef.shape[0], dtype=jnp.int32)
    onehot = (zones[None] == zone_ids[:, None, None, None]).astype(jnp.float32)
    surface = jnp.sum(spray_coef[:, None, None, None] * onehot, axis=0) * (
        depth_cells * depth_cells / 8.0
    )
    inner_zero = jnp.zeros((depth_cells - 2, rows_cast, rows_width), jnp.float32)
    exchange_rim_relation = jnp.concatenate([surface[0:1], inner_zero, surface[1:2]], 0)
    hotness_earlier_step, hotness_later_step = displaced_entries_list(hotness_mesh)
    casting_flux = casting_upper * (
        hotness_widened[:, 2:, 1:-1] - hotness_mesh
    ) - pour_sweep_sub_band * (hotness_mesh - hotness_widened[:, :-2, 1:-1])
    width_flux = width_upper * (hotness_widened[:, 1:-1, 2:] - hotness_mesh) - spanwise_sub_band * (
        hotness_mesh - hotness_widened[:, 1:-1, :-2]
    )
    transverse_stream = transverse_super_band * (
        hotness_later_step - hotness_mesh
    ) - transverse_sub_band * (hotness_mesh - hotness_earlier_step)
    known_side_increment = (
        exchange_rim_relation * (quench_medium_hotness - hotness_mesh)
        + casting_flux
        + width_flux
        + transverse_stream
    )

    def cast_lines(caloric_content_mesh):
        return caloric_content_mesh.transpose(1, 0, 2).reshape(rows_cast, -1)

    lower = -pour_sweep_sub_band * widened_incline[:, :-2, 1:-1]
    upper = -casting_upper * widened_incline[:, 2:, 1:-1]
    middle = 1.0 + caloric_content_incline * (pour_sweep_sub_band + casting_upper)
    solved = distributed_solve(
        cast_lines(lower),
        cast_lines(middle),
        cast_lines(upper),
        cast_lines(known_side_increment),
        cast_forward,
        cast_backward,
    )
    step_cast = solved.reshape(rows_cast, depth_cells, rows_width).transpose(1, 0, 2)

    def width_lines(caloric_content_mesh):
        return caloric_content_mesh.transpose(2, 0, 1).reshape(rows_width, -1)

    lower = -spanwise_sub_band * widened_incline[:, 1:-1, :-2]
    upper = -width_upper * widened_incline[:, 1:-1, 2:]
    middle = 1.0 + caloric_content_incline * (spanwise_sub_band + width_upper)
    solved = distributed_solve(
        width_lines(lower),
        width_lines(middle),
        width_lines(upper),
        width_lines(step_cast),
        width_forward,
        width_backward,
    )
    step_width = solved.reshape(rows_width, depth_cells, rows_cast).transpose(1, 2, 0)
    slope_before, slope_after = displaced_entries_list(caloric_content_incline)
    lower = -transverse_sub_band * slope_before
    upper = -transverse_super_band * slope_after
    middle = 1.0 + caloric_content_incline * (
        transverse_sub_band + transverse_super_band + exchange_rim_relation
    )
    solved = local_solve(
        lower.reshape(depth_cells, -1),
        middle.reshape(depth_cells, -1),
        upper.reshape(depth_cells, -1),
        step_width.reshape(depth_cells, -1),
    )
    step_thick = solved.reshape(depth_cells, rows_cast, rows_width)
    return stored_caloric_content + step_thick


def solution(mesh):
    split = Mesh(
        mesh.devices.reshape(8, 4, 2, mesh.shape["width"]), ("cast_0", "cast_1", "cast_2", "width")
    )
    in_specs = (P(None, CAST, "width"), P(None, CAST, "width"), P())
    out_specs = P(None, CAST, "width")
    return jax.shard_map(
        shards, mesh=split, in_specs=in_specs, out_specs=out_specs, check_vma=False
    )
```

profile of v0, /device:TPU:1, one launch (start us, length us, event | category | flops | bytes accessed | tf_op | source)
XLA Modules:
  0.0 232.8 jit_solution(7734884264257626669)
XLA Ops:
  1.1 4.0 %collective-permute-start = (f32[64,8,1]{2,0,1:T(8,128)S(1)}, f32[64,8,1]{2,0,1:T(8,128)S(1)}, u32[]{:S(2)}, u32[]{:S(2)}) collective-permute-start(f32[64,8,1]{2,0,1:T(8,128)S(1)} %get-tuple-element.1287), channel_id=1, source_target_pairs={{0,1},{1,2},{2,3},{4,5},{5,6},{6,7},{8,9},{9,10},{10,11},{12,13},{... | collective-permute-start | bytes 6152 | tf_op jit(solution)/shard_map/ppermute | solution.py:76
  6.5 4.0 %collective-permute-start.1 = (f32[64,1,128]{2,0,1:T(8,128)S(1)}, f32[64,1,128]{2,0,1:T(8,128)S(1)}, u32[]{:S(2)}, u32[]{:S(2)}) collective-permute-start(f32[64,1,128]{2,0,1:T(8,128)S(1)} %get-tuple-element.1289), channel_id=1, source_target_pairs={{0,4},{4,8},{8,12},{12,16},{16,20},{20,24},{24,28},{28,32},{32,36}... | collective-permute-start | bytes 98312 | tf_op jit(solution)/shard_map/ppermute | solution.py:76
  22.0 13.6 %all-to-all-start = ((f32[9,64,128]{2,0,1:T(8,128)}), f32[9,64,128]{2,0,1:T(8,128)S(1)}, u32[]{:S(2)}, u32[]{:S(2)}) async-start(f32[9,64,128]{2,0,1:T(8,128)} %copy.218), calls=%async_computation | async-start | bytes 1048576 | tf_op jit(solution)/shard_map/all_to_all | solution.py:226
  35.7 17.7 %all-to-all-done = f32[9,64,128]{2,0,1:T(8,128)S(1)} async-done(((f32[9,64,128]{2,0,1:T(8,128)}), f32[9,64,128]{2,0,1:T(8,128)S(1)}, u32[]{:S(2)}, u32[]{:S(2)}) %all-to-all-start) | async-done | bytes 294944 | tf_op jit(solution)/shard_map/all_to_all | solution.py:226
  54.2 13.4 %while.145 = (s32[]{:T(128)}, f32[128]{0:T(128)S(1)}, f32[128]{0:T(128)S(1)}, f32[8,8,128]{2,1,0:T(8,128)S(1)}, f32[8,8,128]{2,1,0:T(8,128)S(1)}, /*index=5*/f32...) while((s32[]{:T(128)}, f32[128]{0:T(128)S(1)}, ...), condition=%wide.region_10.11_spmd.clone, body=%wide.region_9.10_spmd.clone.sunk | while | flops 14602 | bytes 243983 | solution.py:121
  68.3 5.7 %all-to-all-start.1 = ((f32[2,64,128]{2,0,1:T(2,128)}), f32[2,64,128]{2,0,1:T(2,128)S(1)}, u32[]{:S(2)}, u32[]{:S(2)}) async-start(f32[2,64,128]{2,0,1:T(2,128)} %pad_maximum_fusion.2), calls=%async_computation.1 | async-start | bytes 131072 | tf_op jit(solution)/shard_map/all_to_all | solution.py:212
  75.1 4.4 %copy.215 = f32[128,64,8]{2,1,0:T(8,128)} copy(f32[128,64,8]{0,1,2:T(8,128)S(1)} %get-tuple-element.1238) | data formatting | bytes 524288 | tf_op jit(solution)/shard_map/transpose | solution.py:359
  79.5 4.0 %reshape_reshape.21 = f32[16,8,512]{2,1,0:T(8,128)S(1)} reshape(f32[128,64,8]{2,1,0:T(8,128)} %copy.215) | data formatting | bytes 524288 | tf_op jit(solution)/shard_map/reshape;reshape | solution.py:110
  83.5 4.4 %copy.216 = f32[128,64,8]{2,1,0:T(8,128)} copy(f32[128,64,8]{0,1,2:T(8,128)S(1)} %get-tuple-element.1239) | data formatting | bytes 524288 | tf_op jit(solution)/shard_map/transpose | solution.py:359
  87.9 4.0 %reshape_reshape.44 = f32[16,8,512]{2,1,0:T(8,128)S(1)} reshape(f32[128,64,8]{2,1,0:T(8,128)} %copy.216) | data formatting | bytes 524288 | tf_op jit(solution)/shard_map/reshape;reshape | solution.py:110
  91.9 4.4 %copy.217 = f32[128,64,8]{2,1,0:T(8,128)} copy(f32[128,64,8]{0,1,2:T(8,128)S(1)} %get-tuple-element.1240) | data formatting | bytes 524288 | tf_op jit(solution)/shard_map/transpose | solution.py:359
  96.3 4.0 %reshape_reshape.45 = f32[16,8,512]{2,1,0:T(8,128)S(1)} reshape(f32[128,64,8]{2,1,0:T(8,128)} %copy.217) | data formatting | bytes 524288 | tf_op jit(solution)/shard_map/reshape;reshape | solution.py:110
  100.7 4.1 %all_to_all.48 = f32[32,2,2,1,128]{4,0,2,3,1:T(8,128)S(1)} all-to-all(f32[32,2,2,1,128]{4,0,2,3,1:T(8,128)S(1)} %copy.223), channel_id=1, replica_groups=mesh['cast_0'=8,'cast_1'=4,'cast_2'=2,'width'=4] {'cast_2'}, dimensions={1} | all-to-all | bytes 131072 | tf_op jit(solution)/shard_map/all_to_all | solution.py:29
  105.5 9.3 %all-to-all-start.3 = ((f32[32,2,2,1,128]{4,1,2,3,0:T(2,128)}), f32[32,2,2,1,128]{4,1,2,3,0:T(2,128)}, u32[]{:S(2)}, u32[]{:S(2)}) async-start(f32[32,2,2,1,128]{4,1,2,3,0:T(2,128)} %copy.224), calls=%async_computation.3 | async-start | bytes 131072 | tf_op jit(solution)/shard_map/all_to_all | solution.py:29
  116.4 7.2 %all-to-all-done.3 = f32[32,2,2,1,128]{4,1,2,3,0:T(2,128)} async-done(((f32[32,2,2,1,128]{4,1,2,3,0:T(2,128)}), f32[32,2,2,1,128]{4,1,2,3,0:T(2,128)}, u32[]{:S(2)}, u32[]{:S(2)}) %all-to-all-start.3) | async-done | bytes 65568 | tf_op jit(solution)/shard_map/all_to_all | solution.py:29
  125.1 13.3 %while.146 = (s32[]{:T(128)}, f32[128]{0:T(128)}, f32[8,8,128]{2,1,0:T(8,128)}, f32[8,8,128]{2,1,0:T(8,128)S(1)}, f32[8,8,128]{2,1,0:T(8,128)S(1)}, /*index=5*/s32[]{:T(128)}, s32[]{:T(128)}, s32[]{:T(128)}) while((s32[]{:T(128)}, f32[128]{0:T(128)}, f32[8,8,128]{2,1,0:T(8,128)}, f32[8,8,128]{2,1,0:T(8,128)S(1)}, ...), condition=%wide.region_12.13_spmd.clone, body=%wide.region_11.12_spmd.clone.sunk | while | flops 2180 | bytes 46195 | solution.py:121
  138.4 5.8 %all-to-all-start.4 = ((f32[1,64,128]{2,0,1:T(1,128)}), f32[1,64,128]{2,0,1:T(1,128)S(1)}, u32[]{:S(2)}, u32[]{:S(2)}) async-start(f32[1,64,128]{2,0,1:T(1,128)} %bitcast.191), calls=%async_computation.4 | async-start | bytes 65536 | tf_op jit(solution)/shard_map/all_to_all | solution.py:219
  145.0 8.7 %all-to-all-done.4 = f32[1,64,128]{2,0,1:T(1,128)S(1)} async-done(((f32[1,64,128]{2,0,1:T(1,128)}), f32[1,64,128]{2,0,1:T(1,128)S(1)}, u32[]{:S(2)}, u32[]{:S(2)}) %all-to-all-start.4) | async-done | bytes 32800 | tf_op jit(solution)/shard_map/all_to_all | solution.py:219
  153.8 4.4 %copy.226 = f32[128,64,8]{2,1,0:T(8,128)} copy(f32[128,64,8]{0,1,2:T(8,128)S(1)} %add_bitcast_fusion.1) | data formatting | bytes 524288 | tf_op jit(solution)/shard_map/transpose;transpose | solution.py:359
  158.2 4.0 %reshape_reshape.46 = f32[16,8,512]{2,1,0:T(8,128)S(1)} reshape(f32[128,64,8]{2,1,0:T(8,128)} %copy.226) | data formatting | bytes 524288 | tf_op jit(solution)/shard_map/reshape;reshape | solution.py:110
  162.2 9.8 %while.143 = (s32[]{:T(128)}, f32[3,512]{1,0:T(4,128)S(1)}, f32[3,512]{1,0:T(4,128)S(1)}, f32[3,512]{1,0:T(4,128)S(1)}, f32[16,8,512]{2,1,0:T(8,128)S(1)}, /*ind...) while((s32[]{:T(128)}, f32[3,512]{1,0:T(4,128)S(1)}, ...), condition=%wide.region_22.23_spmd, body=%wide.region_13.22_spmd.sunk | while | flops 296969 | bytes 766257 | solution.py:121
  172.7 5.2 %all-to-all-start.5 = ((f32[4,3,3,512]{3,2,1,0:T(4,128)}), f32[4,3,3,512]{3,2,1,0:T(4,128)S(1)}, u32[]{:S(2)}, u32[]{:S(2)}) async-start(f32[4,3,3,512]{3,2,1,0:T(4,128)} %broadcast_in_dim.199), calls=%async_computation.5 | async-start | bytes 196608 | tf_op jit(solution)/shard_map/all_to_all | solution.py:41
  178.0 4.6 %all-to-all-done.5 = f32[4,3,3,512]{3,2,1,0:T(4,128)S(1)} async-done(((f32[4,3,3,512]{3,2,1,0:T(4,128)}), f32[4,3,3,512]{3,2,1,0:T(4,128)S(1)}, u32[]{:S(2)}, u32[]{:S(2)}) %all-to-all-start.5) | async-done | bytes 73760 | tf_op jit(solution)/shard_map/all_to_all | solution.py:41
  183.2 7.1 %while.144 = (s32[]{:T(128)}, f32[512]{0:T(512)S(1)}, f32[512]{0:T(512)S(1)}, f32[16,8,512]{2,1,0:T(8,128)S(1)}, f32[16,8,512]{2,1,0:T(8,128)S(1)}, /*index=5*/f...) while((s32[]{:T(128)}, f32[512]{0:T(512)S(1)}, ...), condition=%wide.region_28.29_spmd, body=%wide.region_27.28_spmd.sunk | while | flops 25609 | bytes 371069 | solution.py:121
  190.3 4.3 %while.147 = (s32[]{:T(128)}, f32[512]{0:T(512)S(1)}, f32[512]{0:T(512)S(1)}, f32[16,8,512]{2,1,0:T(8,128)S(1)}, f32[16,8,512]{2,1,0:T(8,128)S(1)}, /*index=5*/f...) while((s32[]{:T(128)}, f32[512]{0:T(512)S(1)}, ...), condition=%wide.region_30.31_spmd.clone, body=%wide.region_29.30_spmd.clone.sunk | while | flops 17419 | bytes 266571 | solution.py:121
  195.3 3.2 %all-to-all-start.6 = ((f32[4,1,512]{2,1,0:T(1,128)}), f32[4,1,512]{2,1,0:T(1,128)S(1)}, u32[]{:S(2)}, u32[]{:S(2)}) async-start(f32[4,1,512]{2,1,0:T(1,128)} %broadcast_in_dim.202), calls=%async_computation.6 | async-start | bytes 16384 | tf_op jit(solution)/shard_map/all_to_all | solution.py:41
  198.7 3.9 %all-to-all-done.6 = f32[4,1,512]{2,1,0:T(1,128)S(1)} async-done(((f32[4,1,512]{2,1,0:T(1,128)}), f32[4,1,512]{2,1,0:T(1,128)S(1)}, u32[]{:S(2)}, u32[]{:S(2)}) %all-to-all-start.6) | async-done | bytes 8224 | tf_op jit(solution)/shard_map/all_to_all | solution.py:41
  207.3 3.7 %reshape.18270 = f32[128,64,8]{2,1,0:T(8,128)} reshape(f32[16,8,512]{2,1,0:T(8,128)S(1)} %get-tuple-element.654) | data formatting | bytes 524288 | tf_op jit(solution)/shard_map/reshape | solution.py:122
  211.1 3.6 %reshape.18271 = f32[128,64,8]{2,1,0:T(8,128)} reshape(f32[16,8,512]{2,1,0:T(8,128)S(1)} %get-tuple-element.655) | data formatting | bytes 524288 | tf_op jit(solution)/shard_map/reshape | solution.py:122
  215.6 6.9 %add_bitcast_fusion = f32[64,8,128]{1,0,2:T(8,128)} fusion(f32[128,64,8]{2,1,0:T(8,128)} %reshape.18270, f32[128,64,8]{2,1,0:T(8,128)} %reshape.18271, f32[64,8]{1,0:T(8,128)S(1)} %mul.5273), kind=kLoop, calls=%fused_computation.489 | loop fusion | flops 131072 | bytes 788480 | tf_op jit(solution)/shard_map/transpose | solution.py:372
  222.5 3.7 %copy.229 = f32[64,8,128]{2,1,0:T(8,128)S(1)} copy(f32[64,8,128]{1,0,2:T(8,128)} %add_bitcast_fusion) | data formatting | bytes 524288 | tf_op jit(solution)/shard_map/transpose | solution.py:372
  226.3 4.0 %while.148 = (s32[]{:T(128)}, f32[1024]{0:T(1024)S(1)}, f32[1024]{0:T(1024)S(1)}, f32[8,8,1024]{2,1,0:T(8,128)S(1)}, f32[8,8,1024]{2,1,0:T(8,128)S(1)}, /*index=...) while((s32[]{:T(128)}, f32[1024]{0:T(1024)S(1)}, ...), condition=%wide.region_32.33_spmd.clone, body=%wide.region_31.32_spmd.clone.sunk | while | flops 53258 | bytes 741767 | solution.py:121
  (1036 shorter events, 78.9 us)
Async XLA Ops:
  1.1 12.3 %collective-permute-start = (f32[64,8,1]{2,0,1:T(8,128)S(1)}, f32[64,8,1]{2,0,1:T(8,128)S(1)}, u32[]{:S(2)}, u32[]{:S(2)}) collective-permute-start(f32[64,8,1]{2,0,1:T(8,128)S(1)} %get-tuple-element.1287), channel_id=1, source_target_pairs={{0,1},{1,2},{2,3},{4,5},{5,6},{6,7},{8,9},{9,10},{10,11},{12,13},{... | collective-permute-start | bytes 6152 | tf_op jit(solution)/shard_map/ppermute | solution.py:76
  5.2 8.8 %collective-permute-start.3 = (f32[64,8,1]{2,0,1:T(8,128)S(1)}, f32[64,8,1]{2,0,1:T(8,128)S(1)}, u32[]{:S(2)}, u32[]{:S(2)}) collective-permute-start(f32[64,8,1]{2,0,1:T(8,128)S(1)} %get-tuple-element.1288), channel_id=1, source_target_pairs={{1,0},{2,1},{3,2},{5,4},{6,5},{7,6},{9,8},{10,9},{11,10},{13,12},{... | collective-permute-start | bytes 6152 | tf_op jit(solution)/shard_map/ppermute | solution.py:77
  6.5 7.5 %collective-permute-start.1 = (f32[64,1,128]{2,0,1:T(8,128)S(1)}, f32[64,1,128]{2,0,1:T(8,128)S(1)}, u32[]{:S(2)}, u32[]{:S(2)}) collective-permute-start(f32[64,1,128]{2,0,1:T(8,128)S(1)} %get-tuple-element.1289), channel_id=1, source_target_pairs={{0,4},{4,8},{8,12},{12,16},{16,20},{20,24},{24,28},{28,32},{32,36}... | collective-permute-start | bytes 98312 | tf_op jit(solution)/shard_map/ppermute | solution.py:76
  10.5 5.2 %collective-permute-start.2 = (f32[64,1,128]{2,0,1:T(8,128)S(1)}, f32[64,1,128]{2,0,1:T(8,128)S(1)}, u32[]{:S(2)}, u32[]{:S(2)}) collective-permute-start(f32[64,1,128]{2,0,1:T(8,128)S(1)} %get-tuple-element.1290), channel_id=1, source_target_pairs={{4,0},{8,4},{12,8},{16,12},{20,16},{24,20},{28,24},{32,28},{36,32}... | collective-permute-start | bytes 98312 | tf_op jit(solution)/shard_map/ppermute | solution.py:77
  13.4 4.0 %copy-start.10 = (f32[64]{0:T(128)}, f32[64]{0:T(128)S(1)}, u32[]{:S(2)}) copy-start(f32[64]{0:T(128)S(1)} %pad.88.clone) | copy-start | bytes 772
  17.0 1.0 copy-start.1
  17.0 1.0 copy-start.2
  17.0 1.0 copy-start.6
  22.0 31.3 %all-to-all-start = ((f32[9,64,128]{2,0,1:T(8,128)}), f32[9,64,128]{2,0,1:T(8,128)S(1)}, u32[]{:S(2)}, u32[]{:S(2)}) async-start(f32[9,64,128]{2,0,1:T(8,128)} %copy.218), calls=%async_computation | async-start | bytes 1048576 | tf_op jit(solution)/shard_map/all_to_all | solution.py:226
  68.3 32.0 %all-to-all-start.1 = ((f32[2,64,128]{2,0,1:T(2,128)}), f32[2,64,128]{2,0,1:T(2,128)S(1)}, u32[]{:S(2)}, u32[]{:S(2)}) async-start(f32[2,64,128]{2,0,1:T(2,128)} %pad_maximum_fusion.2), calls=%async_computation.1 | async-start | bytes 131072 | tf_op jit(solution)/shard_map/all_to_all | solution.py:212
  100.5 14.5 %copy-start.8 = (f32[1,64,128]{2,1,0:T(8,128)}, f32[1,64,128]{2,1,0:T(8,128)S(1)}, u32[]{:S(2)}) copy-start(f32[1,64,128]{2,1,0:T(8,128)S(1)} %get-tuple-element.1001) | copy-start | bytes 98308
  105.5 18.2 %all-to-all-start.3 = ((f32[32,2,2,1,128]{4,1,2,3,0:T(2,128)}), f32[32,2,2,1,128]{4,1,2,3,0:T(2,128)}, u32[]{:S(2)}, u32[]{:S(2)}) async-start(f32[32,2,2,1,128]{4,1,2,3,0:T(2,128)} %copy.224), calls=%async_computation.3 | async-start | bytes 131072 | tf_op jit(solution)/shard_map/all_to_all | solution.py:29
  115.8 0.6 copy-start.7
  138.4 15.3 %all-to-all-start.4 = ((f32[1,64,128]{2,0,1:T(1,128)}), f32[1,64,128]{2,0,1:T(1,128)S(1)}, u32[]{:S(2)}, u32[]{:S(2)}) async-start(f32[1,64,128]{2,0,1:T(1,128)} %bitcast.191), calls=%async_computation.4 | async-start | bytes 65536 | tf_op jit(solution)/shard_map/all_to_all | solution.py:219
  153.7 8.5 %copy-start = (f32[3,512]{1,0:T(4,128)S(1)}, f32[3,512]{1,0:T(4,128)}, u32[]{:S(2)}) copy-start(f32[3,512]{1,0:T(4,128)} %constant.688.clone.1) | copy-start | bytes 18436
  153.8 8.5 %copy-start.3 = (f32[3,512]{1,0:T(4,128)S(1)}, f32[3,512]{1,0:T(4,128)}, u32[]{:S(2)}) copy-start(f32[3,512]{1,0:T(4,128)} %constant.686.clone.1) | copy-start | bytes 18436
  153.8 8.5 %copy-start.4 = (f32[3,512]{1,0:T(4,128)S(1)}, f32[3,512]{1,0:T(4,128)}, u32[]{:S(2)}) copy-start(f32[3,512]{1,0:T(4,128)} %constant.687.clone.1) | copy-start | bytes 18436
  162.2 20.3 %copy-start.9 = (f32[3,3]{1,0:T(4,128)S(1)}, f32[3,3]{1,0:T(4,128)}, u32[]{:S(2)}) copy-start(f32[3,3]{1,0:T(4,128)} %fusion.216) | copy-start | bytes 112
  162.2 20.3 %copy-start.12 = (pred[4]{0:T(512)(128)(4,1)S(1)}, pred[4]{0:T(512)(128)(4,1)}, u32[]{:S(2)}) copy-start(pred[4]{0:T(512)(128)(4,1)} %iota_compare_fusion.5) | copy-start | bytes 16
  172.7 9.9 %all-to-all-start.5 = ((f32[4,3,3,512]{3,2,1,0:T(4,128)}), f32[4,3,3,512]{3,2,1,0:T(4,128)S(1)}, u32[]{:S(2)}, u32[]{:S(2)}) async-start(f32[4,3,3,512]{3,2,1,0:T(4,128)} %broadcast_in_dim.199), calls=%async_computation.5 | async-start | bytes 196608 | tf_op jit(solution)/shard_map/all_to_all | solution.py:41
  182.9 23.6 %copy-start.11 = (f32[64]{0:T(128)S(1)}, f32[64]{0:T(128)}, u32[]{:S(2)}) copy-start(f32[64]{0:T(128)} %copy-done.10) | copy-start | bytes 772
  195.3 7.4 %all-to-all-start.6 = ((f32[4,1,512]{2,1,0:T(1,128)}), f32[4,1,512]{2,1,0:T(1,128)S(1)}, u32[]{:S(2)}, u32[]{:S(2)}) async-start(f32[4,1,512]{2,1,0:T(1,128)} %broadcast_in_dim.202), calls=%async_computation.6 | async-start | bytes 16384 | tf_op jit(solution)/shard_map/all_to_all | solution.py:41
  203.3 11.4 %all-to-all-start.7 = ((f32[4,1,512]{2,1,0:T(1,128)}), f32[4,1,512]{2,1,0:T(1,128)S(1)}, u32[]{:S(2)}, u32[]{:S(2)}) async-start(f32[4,1,512]{2,1,0:T(1,128)} %broadcast_in_dim.204), calls=%async_computation.7 | async-start | bytes 16384 | tf_op jit(solution)/shard_map/all_to_all | solution.py:41
  226.3 5.8 %copy-start.5 = (f32[64,8,128]{2,1,0:T(8,128)S(1)}, f32[64,8,128]{2,1,0:T(8,128)}, u32[]{:S(2)}) copy-start(f32[64,8,128]{2,1,0:T(8,128)} %param.25) | copy-start | bytes 786436
where the time goes:
time: 237 us; the launch traced here: 233 us
  local copies, waits for them, and re-layouts  83 us (35%)
  starting transfers between devices  57.4 us (24%)
  waiting for transfers between devices  44.4 us (19%)
  other arithmetic  37.1 us (16%)
  loops' own time  5.84 us (2%)
  blocking collectives  4.07 us (2%)
    all_to_all x1, waiting for transfers between devices, cast_forward(): lax.all_to_all(packed, CAST, split_axis=1, concat_axis=1, tiled=True)  17.7 us
    slice x176, local copies, waits for them, and re-layouts, outer(): state, produced = step(state, tuple((member[position] for member in block)))  17.1 us
    another operation x9, local copies, waits for them, and re-layouts, sweep(): piece.reshape((count_rows // block_size, block_size) + piece.shape[1:])  16.1 us
    all_to_all x1, starting transfers between devices, cast_forward(): lax.all_to_all(packed, CAST, split_axis=1, concat_axis=1, tiled=True)  13.6 us
    transpose x3, local copies, waits for them, and re-layouts, width_lines(): return caloric_content_mesh.transpose(2, 0, 1).reshape(rows_width, -1)  13.3 us
    all_to_all x3, starting transfers between devices, from_everyone(): lax.all_to_all(jnp.broadcast_to(value[None], (size, *value.shape)), axis,...  11.7 us
    all_to_all x1, starting transfers between devices, exchange_in_order(): out = lax.all_to_all(out, axes[k], k, k, tiled=True)  9.35 us
    all_to_all x1, waiting for transfers between devices, backward_values(): lax.all_to_all(values[None], CAST, split_axis=1, concat_axis=1, tiled=True)  8.67 us
  transfers between devices with their start and end apart: 11, of which 7 were waited for; matrix products, arithmetic and copies ran while one was open for 16% of the time, Pallas kernels for 0%

commit v1 on v0

v1 whole, which is shorter than its diff:
```python
import functools

import jax
import jax.numpy as jnp
from jax import lax
from jax.experimental import pallas as pl
from jax.experimental.pallas import tpu as pltpu
from jax.sharding import PartitionSpec as P

F32 = jnp.float32
solidification_release = 0.4
quench_medium_hotness = -2.0


def _spike_kernel(with_vw, unroll, a_ref, b_ref, c_ref, d_ref, *refs):
    if with_vw:
        y_ref, v_ref, w_ref, cp_ref = refs
    else:
        y_ref, cp_ref = refs
    n = a_ref.shape[0]
    zero = jnp.zeros(a_ref.shape[1:], F32)
    one = jnp.ones(a_ref.shape[1:], F32)

    def fwd(i, carry):
        cprev, dprev, vprev = carry
        a = a_ref[i]
        r = 1.0 / (b_ref[i] - a * cprev)
        cn = c_ref[i] * r
        dn = (d_ref[i] - a * dprev) * r
        cp_ref[i] = cn
        y_ref[i] = dn
        if with_vw:
            vprev = -(a * vprev) * r
            v_ref[i] = vprev
        return cn, dn, vprev

    cl, dl, vl = lax.fori_loop(0, n, fwd, (zero, zero, one), unroll=unroll)
    if with_vw:
        w_ref[n - 1] = -cl

    def bwd(j, carry):
        i = n - 2 - j
        yn, vn, wn = carry
        cp = cp_ref[i]
        yn = y_ref[i] - cp * yn
        y_ref[i] = yn
        if with_vw:
            vn = v_ref[i] - cp * vn
            wn = -cp * wn
            v_ref[i] = vn
            w_ref[i] = wn
        return yn, vn, wn

    lax.fori_loop(0, n - 1, bwd, (dl, vl, -cl), unroll=unroll)


def spike(a, b, c, d, with_vw, unroll):
    nout = 3 if with_vw else 1
    out = pl.pallas_call(
        functools.partial(_spike_kernel, with_vw, unroll),
        out_shape=[jax.ShapeDtypeStruct(a.shape, F32)] * nout,
        scratch_shapes=[pltpu.VMEM(a.shape, F32)],
    )(a, b, c, d)
    return out


def _reduced_kernel(s_ref, lr_ref, st_ref):
    nb = s_ref.shape[1]
    zero = jnp.zeros((1,) + s_ref.shape[2:], F32)
    pp, qq = zero, zero
    for p in range(nb):
        y0, v0, w0, yn, vn, wn = (s_ref[k, p : p + 1] for k in range(6))
        rd = 1.0 / (1.0 - v0 * qq)
        fa = (y0 + v0 * pp) * rd
        fb = w0 * rd
        st_ref[0, p : p + 1] = fa
        st_ref[1, p : p + 1] = fb
        st_ref[2, p : p + 1] = pp
        st_ref[3, p : p + 1] = qq
        pp, qq = yn + vn * (pp + qq * fa), wn + vn * qq * fb
    f_next = zero
    for p in range(nb - 1, -1, -1):
        f = st_ref[0, p : p + 1] + st_ref[1, p : p + 1] * f_next
        lr_ref[0, p : p + 1] = st_ref[2, p : p + 1] + st_ref[3, p : p + 1] * f
        lr_ref[1, p : p + 1] = f_next
        f_next = f


def reduced(s):
    return pl.pallas_call(
        _reduced_kernel,
        out_shape=jax.ShapeDtypeStruct((2,) + s.shape[1:], F32),
        scratch_shapes=[pltpu.VMEM((4,) + s.shape[1:], F32)],
    )(s)


def medium_parameters(x):
    t = jnp.tanh(x)
    hot = x - solidification_release * t
    cond = 1.5 - 0.5 * jnp.tanh(hot)
    slope = (1.0 - solidification_release) + solidification_release * t * t
    return hot, cond, slope


def summary(y, v, w):
    return jnp.stack([y[0], v[0], w[0], y[-1], v[-1], w[-1]])


def shards(h, zones, spray_coef):
    nt, ncl, nwl = h.shape
    nc, nw = lax.axis_size("cast"), lax.axis_size("width")
    ci, wi = lax.axis_index("cast"), lax.axis_index("width")
    up_c = [(i, i + 1) for i in range(nc - 1)]
    up_w = [(i, i + 1) for i in range(nw - 1)]
    h_cl = lax.ppermute(h[:, -1:, :], "cast", up_c)
    h_ch = lax.ppermute(h[:, :1, :], "cast", [(b, a) for a, b in up_c])
    h_wl = lax.ppermute(h[:, :, -1:], "width", up_w)
    h_wh = lax.ppermute(h[:, :, :1], "width", [(b, a) for a, b in up_w])

    T, k, s = medium_parameters(h)
    T_cl, k_cl, s_cl = medium_parameters(h_cl)
    T_ch, k_ch, s_ch = medium_parameters(h_ch)
    T_wl, k_wl, s_wl = medium_parameters(h_wl)
    T_wh, k_wh, s_wh = medium_parameters(h_wh)

    cast_low = (ci > 0).astype(F32)
    cast_high = (ci < nc - 1).astype(F32)
    width_low = (wi > 0).astype(F32)
    width_high = (wi < nw - 1).astype(F32)

    kc = jnp.concatenate([k_cl, k, k_ch], 1)
    Tc = jnp.concatenate([T_cl, T, T_ch], 1)
    sc = jnp.concatenate([s_cl, s, s_ch], 1)
    edge_c = jnp.ones((ncl + 1,), F32).at[0].set(cast_low).at[-1].set(cast_high)
    fc = (ncl * ncl * 4.0) * 0.5 * (kc[:, 1:] + kc[:, :-1]) * edge_c[None, :, None]
    gcl, gch = fc[:, :-1], fc[:, 1:]
    kw = jnp.concatenate([k_wl, k, k_wh], 2)
    Tw = jnp.concatenate([T_wl, T, T_wh], 2)
    sw = jnp.concatenate([s_wl, s, s_wh], 2)
    edge_w = jnp.ones((nwl + 1,), F32).at[0].set(width_low).at[-1].set(width_high)
    fw = (nwl * nwl / 4.0) * 0.5 * (kw[:, :, 1:] + kw[:, :, :-1]) * edge_w[None, None, :]
    gwl, gwh = fw[:, :, :-1], fw[:, :, 1:]
    mid = (nt * nt / 4.0) * 0.5 * (k[1:] + k[:-1])
    zf = jnp.zeros((1, ncl, nwl), F32)
    gtl = jnp.concatenate([zf, mid], 0)
    gth = jnp.concatenate([mid, zf], 0)

    surf = jnp.zeros(zones.shape, F32)
    for z in range(spray_coef.shape[0]):
        surf = jnp.where(zones == z, spray_coef[z], surf)
    surf = surf * (nt * nt / 8.0)
    rim = jnp.concatenate([surf[0:1], jnp.zeros((nt - 2, ncl, nwl), F32), surf[1:2]], 0)

    T_prev = jnp.concatenate([T[:1], T[:-1]], 0)
    T_next = jnp.concatenate([T[1:], T[-1:]], 0)
    explicit = rim * (quench_medium_hotness - T)
    explicit = explicit + (gch * (Tc[:, 2:] - T) - gcl * (T - Tc[:, :-2]))
    explicit = explicit + (gwh * (Tw[:, :, 2:] - T) - gwl * (T - Tw[:, :, :-2]))
    explicit = explicit + (gth * (T_next - T) - gtl * (T - T_prev))

    def ctw(x):
        return jnp.transpose(x, (1, 0, 2))

    lo = -gcl * sc[:, :-2]
    hi = -gch * sc[:, 2:]
    md = 1.0 + s * (gcl + gch)
    y, v, w = spike(ctw(lo), ctw(md), ctw(hi), ctw(explicit), True, True)
    summ = summary(y, v, w).reshape(6, nc, -1)
    recv = lax.all_to_all(summ, "cast", 1, 1, tiled=True)
    lr = reduced(recv)
    back = lax.all_to_all(lr, "cast", 1, 1, tiled=True).reshape(2, nt, nwl)
    step_cast = y + v * back[0][None] + w * back[1][None]

    lines = nt * ncl

    def wl(x):
        return jnp.transpose(x, (2, 0, 1)).reshape(nwl, lines // 128, 128)

    lo = -gwl * sw[:, :, :-2]
    hi = -gwh * sw[:, :, 2:]
    md = 1.0 + s * (gwl + gwh)
    rhs = jnp.transpose(step_cast, (2, 1, 0)).reshape(nwl, lines // 128, 128)
    y, v, w = spike(wl(lo), wl(md), wl(hi), rhs, True, 8)
    summ = summary(y, v, w)
    gath = lax.all_gather(summ, "width", axis=1)
    lr = reduced(gath)
    mine = lax.dynamic_index_in_dim(lr, wi, axis=1, keepdims=False)
    step_width = y + v * mine[0][None] + w * mine[1][None]
    step_width = step_width.reshape(nwl, nt, ncl).transpose(1, 2, 0)

    s_prev = jnp.concatenate([s[:1], s[:-1]], 0)
    s_next = jnp.concatenate([s[1:], s[-1:]], 0)
    lo = -gtl * s_prev
    hi = -gth * s_next
    md = 1.0 + s * (gtl + gth + rim)
    (step_thick,) = spike(lo, md, hi, step_width, False, 8)
    return h + step_thick


def solution(mesh):
    spec = P(None, "cast", "width")
    return jax.shard_map(
        shards, mesh=mesh, in_specs=(spec, spec, P()), out_specs=spec, check_vma=False
    )
```

time: 237 us -> 111 us (0.47)
  local copies, waits for them, and re-layouts: 83 us -> 24.3 us
  starting transfers between devices: 57.4 us -> 30 us
  other arithmetic: 37.1 us -> 12.4 us
  waiting for transfers between devices: 44.4 us -> 19.7 us
  Pallas kernels: 0 us -> 12.5 us
  loops' own time: 5.84 us -> 0 us
  blocking collectives: 4.07 us -> 9.48 us
    all_to_all x7 -> x2, starting transfers between devices: 46.2 us -> 17.6 us  [the longest x1 12.8 us: shards(): recv = lax.all_to_all(summ, 'cast', 1, 1, tiled=True)]
    another operation x133 -> x5, local copies, waits for them, and re-layouts: 26.9 us -> 2.27 us  [the longest x4 2.26 us: summary(): return jnp.stack([y[0], v[0], w[0], y[-1], v[-1], w[-1]])]
    all_to_all x7 -> x2, waiting for transfers between devices: 42.1 us -> 19.7 us  [the longest x1 13 us: shards(): recv = lax.all_to_all(summ, 'cast', 1, 1, tiled=True)]
    slice x196 -> x9, local copies, waits for them, and re-layouts: 18.3 us -> 3.05 us  [the longest x1 1.16 us: shards(): h_wh = lax.ppermute(h[:, :, :1], 'width', [(b, a) for a, b in up_w])]
    transpose x4 -> x5, local copies, waits for them, and re-layouts: 17 us -> 3.16 us  [the longest x4 3 us: ctw(): return jnp.transpose(x, (1, 0, 2))]
    pallas_call x0 -> x5, Pallas kernels: none -> 12.5 us  [the longest x3 8.64 us: spike(): pl.pallas_call(functools.partial(_spike_kernel, with_vw, unroll), out_sha...]
    all_gather x0 -> x1, blocking collectives: none -> 9.48 us  [shards(): gath = lax.all_gather(summ, 'width', axis=1)]
    transpose x3 -> x2, other arithmetic: 7.75 us -> 0.51 us  [the longest x1 0.45 us: ctw(): return jnp.transpose(x, (1, 0, 2))]
  transfers between devices with their start and end apart: 11 -> 6, of which waited for: 7 -> 2; matrix products, arithmetic and copies ran while one was open for 16% -> 12% of each run, Pallas kernels for 0% -> 0%
where the time goes in v1:
time: 111 us; the launch traced here: 109 us
  starting transfers between devices  30 us (27%)
  local copies, waits for them, and re-layouts  24.3 us (22%)
  waiting for transfers between devices  19.7 us (18%)
  Pallas kernels  12.5 us (11%)
  other arithmetic  12.4 us (11%)
  blocking collectives  9.48 us (9%)
    all_to_all x1, waiting for transfers between devices, shards(): recv = lax.all_to_all(summ, 'cast', 1, 1, tiled=True)  13 us
    all_to_all x1, starting transfers between devices, shards(): recv = lax.all_to_all(summ, 'cast', 1, 1, tiled=True)  12.8 us
    all_gather x1, blocking collectives, shards(): gath = lax.all_gather(summ, 'width', axis=1)  9.48 us
    pallas_call x3, Pallas kernels, spike(): pl.pallas_call(functools.partial(_spike_kernel, with_vw, unroll), out_sha...  8.64 us
    unnamed x26, local copies, waits for them, and re-layouts  7.9 us
    all_to_all x1, waiting for transfers between devices, shards(): back = lax.all_to_all(lr, 'cast', 1, 1, tiled=True).reshape(2, nt, nwl)  6.63 us
    mul x1, other arithmetic, shards(): surf = surf * (nt * nt / 8.0)  6.17 us
    ppermute x1, starting transfers between devices, shards(): h_ch = lax.ppermute(h[:, :1, :], 'cast', [(b, a) for a, b in up_c])  5.11 us
  transfers between devices with their start and end apart: 6, of which 2 were waited for; matrix products, arithmetic and copies ran while one was open for 12% of the time, Pallas kernels for 0%

profile of v1, /device:TPU:1, one launch (start us, length us, event | category | flops | bytes accessed | tf_op | source)
XLA Modules:
  0.0 108.7 jit_solution(9465097632229502524)
XLA Ops:
  0.0 1.1 fusion.37
  1.1 5.1 %collective-permute-start.2 = (f32[64,1,128]{2,1,0:T(1,128)S(1)}, f32[64,1,128]{2,1,0:T(1,128)S(1)}, u32[]{:S(2)}, u32[]{:S(2)}) collective-permute-start(f32[64,1,128]{2,1,0:T(1,128)S(1)} %get-tuple-element.85), channel_id=1, source_target_pairs={{4,0},{8,4},{12,8},{16,12},{20,16},{24,20},{28,24},{32,28},{36,32}... | collective-permute-start | bytes 98312 | tf_op jit(solution)/shard_map/ppermute | solution.py:116
  6.2 2.1 %collective-permute-start.3 = (f32[64,1,128]{2,1,0:T(1,128)S(1)}, f32[64,1,128]{2,1,0:T(1,128)S(1)}, u32[]{:S(2)}, u32[]{:S(2)}) collective-permute-start(f32[64,1,128]{2,1,0:T(1,128)S(1)} %get-tuple-element.86), channel_id=1, source_target_pairs={{0,4},{4,8},{8,12},{12,16},{16,20},{20,24},{24,28},{28,32},{32,36}... | collective-permute-start | bytes 98312 | tf_op jit(solution)/shard_map/ppermute | solution.py:115
  8.3 1.2 %fusion.38 = (f32[64,8,1]{2,1,0:T(8,128)S(1)}, f32[64,8,1]{2,1,0:T(8,128)S(1)}) fusion(f32[64,8,128]{2,1,0:T(8,128)} %param.11), kind=kLoop, calls=%fused_computation.94 | loop fusion | bytes 8192 | tf_op jit(solution)/shard_map/slice | solution.py:118
  9.4 1.3 %collective-permute-start = (f32[64,8,1]{2,1,0:T(8,128)S(1)}, f32[64,8,1]{2,1,0:T(8,128)S(1)}, u32[]{:S(2)}, u32[]{:S(2)}) collective-permute-start(f32[64,8,1]{2,1,0:T(8,128)S(1)} %get-tuple-element.87), channel_id=1, source_target_pairs={{1,0},{2,1},{3,2},{5,4},{6,5},{7,6},{9,8},{10,9},{11,10},{13,12},{... | collective-permute-start | bytes 6152 | tf_op jit(solution)/shard_map/ppermute | solution.py:118
  10.7 4.0 %collective-permute-start.1 = (f32[64,8,1]{2,1,0:T(8,128)S(1)}, f32[64,8,1]{2,1,0:T(8,128)S(1)}, u32[]{:S(2)}, u32[]{:S(2)}) collective-permute-start(f32[64,8,1]{2,1,0:T(8,128)S(1)} %get-tuple-element.88), channel_id=1, source_target_pairs={{0,1},{1,2},{2,3},{4,5},{5,6},{6,7},{8,9},{9,10},{10,11},{12,13},{... | collective-permute-start | bytes 6152 | tf_op jit(solution)/shard_map/ppermute | solution.py:117
  16.9 6.2 %select_multiply_fusion = f32[2,8,128]{2,1,0:T(8,128)S(1)} fusion(s32[2,8,128]{2,1,0:T(8,128)S(1)} %copy-done.6, f32[]{:T(128)} %bitcast.9, f32[]{:T(128)} %bitcast.8, f32[]{:T(128)} %bitcast.7, f32[]{:T(128)} %bitcast.6, f32[]{:T(128)} %bitcast.5, f32[]{:T(128)} %bitcast.4, f32[]{:T(128)} %bitcast.3, f32[]{:T(128)} %bitcast.2, f32[]{:T(128)} %bitcast.1, ...), kind=kLoop, calls=%fused_computation.82 | loop fusion | flops 43008 | bytes 16424 | tf_op jit(solution)/shard_map/mul | solution.py:151
  23.3 0.8 fusion.28
  28.8 2.2 %shard_map.37 = (f32[8,64,128]{2,1,0:T(8,128)}, f32[8,64,128]{2,1,0:T(8,128)}, f32[8,64,128]{2,1,0:T(8,128)}) custom-call(f32[8,64,128]{2,1,0:T(8,128)} %copy.42.a_ref, f32[8,64,128]{2,1,0:T(8,128)} %copy.43.b_ref, f32[8,64,128]{2,1,0:T(8,128)} %copy.44.c_ref, f32[8,64,128]{2,1,0:T(8,128)} %copy.45.d_ref), custom_call_target="tpu_custom_call" | custom-call | tf_op jit(solution)/shard_map/pallas_call | solution.py:59
  31.0 0.8 slice_dynamic-update-slice_fusion.5
  31.8 0.8 slice_dynamic-update-slice_fusion.4
  32.6 0.8 slice_dynamic-update-slice_fusion.3
  34.1 0.8 slice_dynamic-update-slice_fusion
  34.9 0.8 copy.46
  35.7 12.8 %all-to-all-start = ((f32[6,64,128]{2,0,1:T(8,128)}), f32[6,64,128]{2,0,1:T(8,128)S(1)}, u32[]{:S(2)}, u32[]{:S(2)}) async-start(f32[6,64,128]{2,0,1:T(8,128)} %copy.46), calls=%async_computation | async-start | bytes 524288 | tf_op jit(solution)/shard_map/all_to_all | solution.py:169
  48.5 13.0 %all-to-all-done = f32[6,64,128]{2,0,1:T(8,128)S(1)} async-done(((f32[6,64,128]{2,0,1:T(8,128)}), f32[6,64,128]{2,0,1:T(8,128)S(1)}, u32[]{:S(2)}, u32[]{:S(2)}) %all-to-all-start) | async-done | bytes 196640 | tf_op jit(solution)/shard_map/all_to_all | solution.py:169
  62.3 2.4 %shard_map.38 = f32[2,64,128]{2,1,0:T(8,128)} custom-call(f32[6,64,128]{2,1,0:T(8,128)} %copy.47.s_ref), custom_call_target="tpu_custom_call" | custom-call | tf_op jit(solution)/shard_map/pallas_call | solution.py:90
  64.7 1.5 %copy.48 = f32[2,64,128]{2,0,1:T(2,128)} copy(f32[2,64,128]{2,1,0:T(8,128)} %shard_map.38) | data formatting | bytes 131072 | tf_op jit(solution)/shard_map/pallas_call | solution.py:90
  66.2 4.8 %all-to-all-start.1 = ((f32[2,64,128]{2,0,1:T(2,128)}), f32[2,64,128]{2,0,1:T(2,128)S(1)}, u32[]{:S(2)}, u32[]{:S(2)}) async-start(f32[2,64,128]{2,0,1:T(2,128)} %copy.48), calls=%async_computation.1 | async-start | bytes 131072 | tf_op jit(solution)/shard_map/all_to_all | solution.py:171
  71.0 0.9 maximum_multiply_fusion.1
  71.9 0.8 copy.50.a_ref
  72.7 0.9 copy.51.b_ref
  73.6 0.8 copy.52.c_ref
  74.4 6.6 %all-to-all-done.1 = f32[2,64,128]{2,0,1:T(2,128)S(1)} async-done(((f32[2,64,128]{2,0,1:T(2,128)}), f32[2,64,128]{2,0,1:T(2,128)S(1)}, u32[]{:S(2)}, u32[]{:S(2)}) %all-to-all-start.1) | async-done | bytes 65568 | tf_op jit(solution)/shard_map/all_to_all | solution.py:171
  81.4 0.8 copy.53.d_ref
  82.2 3.8 %shard_map.39 = (f32[128,4,128]{2,1,0:T(4,128)}, f32[128,4,128]{2,1,0:T(4,128)}, f32[128,4,128]{2,1,0:T(4,128)}) custom-call(f32[128,4,128]{2,1,0:T(4,128)} %copy.50.a_ref, f32[128,4,128]{2,1,0:T(4,128)} %copy.51.b_ref, f32[128,4,128]{2,1,0:T(4,128)} %copy.52.c_ref, f32[128,4,128]{2,1,0:T(4,128)} %copy.53.d_ref), custom_call_target="tpu_custom_call" | custom-call | tf_op jit(solution)/shard_map/pallas_call | solution.py:59
  90.1 9.5 %all-gather = f32[6,16,128]{2,0,1:T(8,128)S(1)} all-gather(f32[6,4,128]{2,0,1:T(8,128)S(1)} %copy.54), channel_id=2, replica_groups=mesh['cast'=64,'width'=4] {'width'}, dimensions={1}, use_global_device_ids=true | all-gather | bytes 61440 | tf_op jit(solution)/shard_map/all_gather | solution.py:185
  100.2 1.5 %shard_map.40 = f32[2,4,4,128]{3,2,1,0:T(4,128)} custom-call(f32[6,4,4,128]{3,2,1,0:T(4,128)} %bitcast.60), custom_call_target="tpu_custom_call" | custom-call | tf_op jit(solution)/shard_map/pallas_call | solution.py:90
  102.4 1.1 multiply_add_fusion
  103.4 0.8 copy.56
  104.3 2.7 %shard_map.41 = f32[64,8,128]{2,1,0:T(8,128)} custom-call(f32[64,8,128]{2,1,0:T(8,128)} %get-tuple-element.96.a_ref, f32[64,8,128]{2,1,0:T(8,128)} %get-tuple-element.93.b_ref, f32[64,8,128]{2,1,0:T(8,128)} %get-tuple-element.95.c_ref, f32[64,8,128]{2,1,0:T(8,128)} %bitcast.51), custom_call_target="tpu_custom_call" | custom-call | tf_op jit(solution)/shard_map/pallas_call | solution.py:59
  107.0 1.7 %add.112 = f32[64,8,128]{2,1,0:T(8,128)} add(f32[64,8,128]{2,1,0:T(8,128)S(1)} %copy-done, f32[64,8,128]{2,1,0:T(8,128)} %shard_map.41) | non-fusion elementwise | flops 65536 | bytes 786432 | tf_op jit(solution)/shard_map/add | solution.py:197
  (63 shorter events, 14.1 us)
Async XLA Ops:
  1.1 23.5 %collective-permute-start.2 = (f32[64,1,128]{2,1,0:T(1,128)S(1)}, f32[64,1,128]{2,1,0:T(1,128)S(1)}, u32[]{:S(2)}, u32[]{:S(2)}) collective-permute-start(f32[64,1,128]{2,1,0:T(1,128)S(1)} %get-tuple-element.85), channel_id=1, source_target_pairs={{4,0},{8,4},{12,8},{16,12},{20,16},{24,20},{28,24},{32,28},{36,32}... | collective-permute-start | bytes 98312 | tf_op jit(solution)/shard_map/ppermute | solution.py:116
  6.2 8.5 %copy-start = (f32[64,8,128]{2,1,0:T(8,128)S(1)}, f32[64,8,128]{2,1,0:T(8,128)}, u32[]{:S(2)}) copy-start(f32[64,8,128]{2,1,0:T(8,128)} %param.11) | copy-start | bytes 786436
  6.2 18.3 %collective-permute-start.3 = (f32[64,1,128]{2,1,0:T(1,128)S(1)}, f32[64,1,128]{2,1,0:T(1,128)S(1)}, u32[]{:S(2)}, u32[]{:S(2)}) collective-permute-start(f32[64,1,128]{2,1,0:T(1,128)S(1)} %get-tuple-element.86), channel_id=1, source_target_pairs={{0,4},{4,8},{8,12},{12,16},{16,20},{20,24},{24,28},{28,32},{32,36}... | collective-permute-start | bytes 98312 | tf_op jit(solution)/shard_map/ppermute | solution.py:115
  9.4 14.7 %collective-permute-start = (f32[64,8,1]{2,1,0:T(8,128)S(1)}, f32[64,8,1]{2,1,0:T(8,128)S(1)}, u32[]{:S(2)}, u32[]{:S(2)}) collective-permute-start(f32[64,8,1]{2,1,0:T(8,128)S(1)} %get-tuple-element.87), channel_id=1, source_target_pairs={{1,0},{2,1},{3,2},{5,4},{6,5},{7,6},{9,8},{10,9},{11,10},{13,12},{... | collective-permute-start | bytes 6152 | tf_op jit(solution)/shard_map/ppermute | solution.py:118
  10.7 13.5 %collective-permute-start.1 = (f32[64,8,1]{2,1,0:T(8,128)S(1)}, f32[64,8,1]{2,1,0:T(8,128)S(1)}, u32[]{:S(2)}, u32[]{:S(2)}) collective-permute-start(f32[64,8,1]{2,1,0:T(8,128)S(1)} %get-tuple-element.88), channel_id=1, source_target_pairs={{0,1},{1,2},{2,3},{4,5},{5,6},{6,7},{8,9},{9,10},{10,11},{12,13},{... | collective-permute-start | bytes 6152 | tf_op jit(solution)/shard_map/ppermute | solution.py:117
  14.8 0.7 copy-start.5
  16.2 0.7 copy-start.6
  31.0 3.1 %copy-start.2 = (f32[8,64,128]{2,1,0:T(8,128)S(1)}, f32[8,64,128]{2,1,0:T(8,128)}, u32[]{:S(2)}) copy-start(f32[8,64,128]{2,1,0:T(8,128)} %get-tuple-element.60) | copy-start | bytes 786436
  35.7 25.9 %all-to-all-start = ((f32[6,64,128]{2,0,1:T(8,128)}), f32[6,64,128]{2,0,1:T(8,128)S(1)}, u32[]{:S(2)}, u32[]{:S(2)}) async-start(f32[6,64,128]{2,0,1:T(8,128)} %copy.46), calls=%async_computation | async-start | bytes 524288 | tf_op jit(solution)/shard_map/all_to_all | solution.py:169
  66.2 14.9 %all-to-all-start.1 = ((f32[2,64,128]{2,0,1:T(2,128)}), f32[2,64,128]{2,0,1:T(2,128)S(1)}, u32[]{:S(2)}, u32[]{:S(2)}) async-start(f32[2,64,128]{2,0,1:T(2,128)} %copy.48), calls=%async_computation.1 | async-start | bytes 131072 | tf_op jit(solution)/shard_map/all_to_all | solution.py:171
  73.6 7.5 %copy-start.1 = (f32[8,64,128]{2,1,0:T(8,128)S(1)}, f32[8,64,128]{2,1,0:T(8,128)}, u32[]{:S(2)}) copy-start(f32[8,64,128]{2,1,0:T(8,128)} %get-tuple-element.59) | copy-start | bytes 786436
  73.6 7.6 %copy-start.3 = (f32[8,64,128]{2,1,0:T(8,128)S(1)}, f32[8,64,128]{2,1,0:T(8,128)}, u32[]{:S(2)}) copy-start(f32[8,64,128]{2,1,0:T(8,128)} %get-tuple-element.61) | copy-start | bytes 786436
  86.0 16.4 %copy-start.4 = (f32[128,4,128]{2,1,0:T(4,128)S(1)}, f32[128,4,128]{2,1,0:T(4,128)}, u32[]{:S(2)}) copy-start(f32[128,4,128]{2,1,0:T(4,128)} %get-tuple-element.62) | copy-start | bytes 786436

commit v2 on v1

v2 whole, which is shorter than its diff:
```python
import functools

import jax
import jax.numpy as jnp
from jax import lax
from jax.experimental import pallas as pl
from jax.experimental.pallas import tpu as pltpu
from jax.sharding import PartitionSpec as P

F32 = jnp.float32
solidification_release = 0.4
quench_medium_hotness = -2.0
SMEM_SPEC = pl.BlockSpec(memory_space=pltpu.SMEM)


def _sweep(n, ld, st, a_ref, b_ref, c_ref, d_ref, y_ref, v_ref, w_ref, cp_ref, unroll, shape):
    with_vw = v_ref is not None
    zero = jnp.zeros(shape, F32)
    one = jnp.ones(shape, F32)

    def fwd(i, carry):
        cprev, dprev, vprev = carry
        a = ld(a_ref, i)
        r = 1.0 / (ld(b_ref, i) - a * cprev)
        cn = ld(c_ref, i) * r
        dn = (ld(d_ref, i) - a * dprev) * r
        st(cp_ref, i, cn)
        st(y_ref, i, dn)
        if with_vw:
            vprev = -(a * vprev) * r
            st(v_ref, i, vprev)
        return cn, dn, vprev

    if unroll is True:
        carry = (zero, zero, one)
        for i in range(n):
            carry = fwd(i, carry)
    else:
        carry = lax.fori_loop(0, n, fwd, (zero, zero, one), unroll=unroll)
    cl, dl, vl = carry
    if with_vw:
        st(w_ref, n - 1, -cl)

    def bwd(j, carry):
        i = n - 2 - j
        yn, vn, wn = carry
        cp = ld(cp_ref, i)
        yn = ld(y_ref, i) - cp * yn
        st(y_ref, i, yn)
        if with_vw:
            vn = ld(v_ref, i) - cp * vn
            wn = -cp * wn
            st(v_ref, i, vn)
            st(w_ref, i, wn)
        return yn, vn, wn

    carry = (dl, vl, -cl)
    if unroll is True:
        for j in range(n - 1):
            carry = bwd(j, carry)
    else:
        lax.fori_loop(0, n - 1, bwd, carry, unroll=unroll)


def _put_summary(sm_ref, ld, n, y_ref, v_ref, w_ref):
    for k, (ref, i) in enumerate(
        [(y_ref, 0), (v_ref, 0), (w_ref, 0), (y_ref, n - 1), (v_ref, n - 1), (w_ref, n - 1)]
    ):
        sm_ref[k] = ld(ref, i)


def _cast_kernel(n, a_ref, b_ref, c_ref, d_ref, y_ref, v_ref, w_ref, sm_ref, cp_ref):
    m = a_ref.shape[0] // n

    def ld(ref, i):
        return ref[pl.ds(i, m, stride=n), :]

    def st(ref, i, val):
        ref[pl.ds(i, m, stride=n), :] = val

    shape = (m, a_ref.shape[1])
    _sweep(n, ld, st, a_ref, b_ref, c_ref, d_ref, y_ref, v_ref, w_ref, cp_ref, True, shape)
    _put_summary(sm_ref, ld, n, y_ref, v_ref, w_ref)


def _lead_ld(ref, i):
    return ref[i]


def _lead_st(ref, i, val):
    ref[i] = val


def _width_kernel(a_ref, b_ref, c_ref, d_ref, y_ref, v_ref, w_ref, sm_ref, cp_ref):
    n = a_ref.shape[0]
    shape = a_ref.shape[1:]
    _sweep(n, _lead_ld, _lead_st, a_ref, b_ref, c_ref, d_ref, y_ref, v_ref, w_ref, cp_ref, 8, shape)
    _put_summary(sm_ref, _lead_ld, n, y_ref, v_ref, w_ref)


def _thick_kernel(a_ref, b_ref, c_ref, d_ref, h_ref, o_ref, y_ref, cp_ref):
    n = a_ref.shape[0]
    shape = a_ref.shape[1:]
    _sweep(n, _lead_ld, _lead_st, a_ref, b_ref, c_ref, d_ref, y_ref, None, None, cp_ref, 8, shape)
    o_ref[...] = h_ref[...] + y_ref[...]


def cast_solve(a, b, c, d, n):
    shp = jax.ShapeDtypeStruct(a.shape, F32)
    m = a.shape[0] // n
    return pl.pallas_call(
        functools.partial(_cast_kernel, n),
        out_shape=[shp, shp, shp, jax.ShapeDtypeStruct((6, m, a.shape[1]), F32)],
        scratch_shapes=[pltpu.VMEM(a.shape, F32)],
    )(a, b, c, d)


def width_solve(a, b, c, d):
    shp = jax.ShapeDtypeStruct(a.shape, F32)
    return pl.pallas_call(
        _width_kernel,
        out_shape=[shp, shp, shp, jax.ShapeDtypeStruct((6,) + a.shape[1:], F32)],
        scratch_shapes=[pltpu.VMEM(a.shape, F32)],
    )(a, b, c, d)


def thick_solve(a, b, c, d, h):
    return pl.pallas_call(
        _thick_kernel,
        out_shape=jax.ShapeDtypeStruct(a.shape, F32),
        scratch_shapes=[pltpu.VMEM(a.shape, F32), pltpu.VMEM(a.shape, F32)],
    )(a, b, c, d, h)


def _reduce_blocks(nb, blk, emit, zero):
    pp, qq = zero, zero
    saved = []
    for p in range(nb):
        y0, v0, w0, yn, vn, wn = blk(p)
        rd = 1.0 / (1.0 - v0 * qq)
        fa = (y0 + v0 * pp) * rd
        fb = w0 * rd
        saved.append((fa, fb, pp, qq))
        pp, qq = yn + vn * (pp + qq * fa), wn + vn * qq * fb
    f_next = zero
    for p in range(nb - 1, -1, -1):
        fa, fb, pp, qq = saved[p]
        f = fa + fb * f_next
        emit(p, pp + qq * f, f_next)
        f_next = f


def _cast_reduced_kernel(s_ref, lr_ref):
    nb = s_ref.shape[1]

    def blk(p):
        return tuple(s_ref[k, p : p + 1] for k in range(6))

    def emit(p, left, right):
        lr_ref[0, p : p + 1] = left
        lr_ref[1, p : p + 1] = right

    _reduce_blocks(nb, blk, emit, jnp.zeros((1, s_ref.shape[2]), F32))


def _width_reduced_kernel(me_ref, r_ref, lr_ref):
    nb = r_ref.shape[0]
    me = me_ref[0]

    def blk(p):
        k = (me - p + nb) % nb
        return tuple(r_ref[k, q] for q in range(6))

    def emit(p, left, right):
        @pl.when(me == p)
        def _():
            lr_ref[0] = left
            lr_ref[1] = right

    _reduce_blocks(nb, blk, emit, jnp.zeros(r_ref.shape[2:], F32))


def _surface_kernel(scale, z_ref, sp_ref, o_ref):
    z = z_ref[...]
    acc = jnp.zeros(z.shape, F32)
    for q in range(sp_ref.shape[0]):
        acc = jnp.where(z == q, sp_ref[q], acc)
    o_ref[...] = acc * scale


def medium_parameters(x):
    t = jnp.tanh(x)
    hot = x - solidification_release * t
    cond = 1.5 - 0.5 * jnp.tanh(hot)
    slope = (1.0 - solidification_release) + solidification_release * t * t
    return hot, cond, slope


def shards(h, zones, spray_coef):
    nt, ncl, nwl = h.shape
    nc, nw = lax.axis_size("cast"), lax.axis_size("width")
    ci, wi = lax.axis_index("cast"), lax.axis_index("width")
    up_c = [(i, i + 1) for i in range(nc - 1)]
    up_w = [(i, i + 1) for i in range(nw - 1)]
    h_cl = lax.ppermute(h[:, -1, :], "cast", up_c)[:, None, :]
    h_ch = lax.ppermute(h[:, 0, :], "cast", [(b, a) for a, b in up_c])[:, None, :]
    h_wl = lax.ppermute(h[:, :, -1], "width", up_w)[:, :, None]
    h_wh = lax.ppermute(h[:, :, 0], "width", [(b, a) for a, b in up_w])[:, :, None]

    surf = pl.pallas_call(
        functools.partial(_surface_kernel, nt * nt / 8.0),
        out_shape=jax.ShapeDtypeStruct((2 * ncl, nwl), F32),
        in_specs=[pl.BlockSpec(memory_space=pltpu.VMEM), SMEM_SPEC],
    )(zones.reshape(2 * ncl, nwl), spray_coef).reshape(2, ncl, nwl)

    T, k, s = medium_parameters(h)
    T_cl, k_cl, s_cl = medium_parameters(h_cl)
    T_ch, k_ch, s_ch = medium_parameters(h_ch)
    T_wl, k_wl, s_wl = medium_parameters(h_wl)
    T_wh, k_wh, s_wh = medium_parameters(h_wh)

    cast_low = (ci > 0).astype(F32)
    cast_high = (ci < nc - 1).astype(F32)
    width_low = (wi > 0).astype(F32)
    width_high = (wi < nw - 1).astype(F32)

    kc = jnp.concatenate([k_cl, k, k_ch], 1)
    Tc = jnp.concatenate([T_cl, T, T_ch], 1)
    sc = jnp.concatenate([s_cl, s, s_ch], 1)
    edge_c = jnp.ones((ncl + 1,), F32).at[0].set(cast_low).at[-1].set(cast_high)
    fc = (ncl * ncl * 4.0) * 0.5 * (kc[:, 1:] + kc[:, :-1]) * edge_c[None, :, None]
    gcl, gch = fc[:, :-1], fc[:, 1:]
    kw = jnp.concatenate([k_wl, k, k_wh], 2)
    Tw = jnp.concatenate([T_wl, T, T_wh], 2)
    sw = jnp.concatenate([s_wl, s, s_wh], 2)
    edge_w = jnp.ones((nwl + 1,), F32).at[0].set(width_low).at[-1].set(width_high)
    fw = (nwl * nwl / 4.0) * 0.5 * (kw[:, :, 1:] + kw[:, :, :-1]) * edge_w[None, None, :]
    gwl, gwh = fw[:, :, :-1], fw[:, :, 1:]
    mid = (nt * nt / 4.0) * 0.5 * (k[1:] + k[:-1])
    zf = jnp.zeros((1, ncl, nwl), F32)
    gtl = jnp.concatenate([zf, mid], 0)
    gth = jnp.concatenate([mid, zf], 0)
    rim = jnp.concatenate([surf[0:1], jnp.zeros((nt - 2, ncl, nwl), F32), surf[1:2]], 0)

    T_prev = jnp.concatenate([T[:1], T[:-1]], 0)
    T_next = jnp.concatenate([T[1:], T[-1:]], 0)
    explicit = rim * (quench_medium_hotness - T)
    explicit = explicit + (gch * (Tc[:, 2:] - T) - gcl * (T - Tc[:, :-2]))
    explicit = explicit + (gwh * (Tw[:, :, 2:] - T) - gwl * (T - Tw[:, :, :-2]))
    explicit = explicit + (gth * (T_next - T) - gtl * (T - T_prev))

    def flat(x):
        return x.reshape(nt * ncl, nwl)

    lo = -gcl * sc[:, :-2]
    hi = -gch * sc[:, 2:]
    md = 1.0 + s * (gcl + gch)
    y, v, w, summ = cast_solve(flat(lo), flat(md), flat(hi), flat(explicit), ncl)
    recv = lax.all_to_all(summ.reshape(6, nc, -1), "cast", 1, 1, tiled=True)
    lr = pl.pallas_call(
        _cast_reduced_kernel, out_shape=jax.ShapeDtypeStruct((2,) + recv.shape[1:], F32)
    )(recv)
    back = lax.all_to_all(lr, "cast", 1, 1, tiled=True).reshape(2, nt, 1, nwl)
    y, v, w = (x.reshape(nt, ncl, nwl) for x in (y, v, w))
    step_cast = y + v * back[0] + w * back[1]

    lines = nt * ncl

    def wl(x):
        return jnp.transpose(x, (2, 0, 1)).reshape(nwl, lines // 128, 128)

    lo = -gwl * sw[:, :, :-2]
    hi = -gwh * sw[:, :, 2:]
    md = 1.0 + s * (gwl + gwh)
    y, v, w, summ = width_solve(wl(lo), wl(md), wl(hi), wl(step_cast))
    got = [summ] + [
        lax.ppermute(summ, "width", [(i, (i + q) % nw) for i in range(nw)]) for q in range(1, nw)
    ]
    lr = pl.pallas_call(
        _width_reduced_kernel,
        out_shape=jax.ShapeDtypeStruct((2,) + summ.shape[1:], F32),
        in_specs=[SMEM_SPEC, pl.BlockSpec(memory_space=pltpu.VMEM)],
    )(wi.astype(jnp.int32).reshape(1), jnp.stack(got))
    step_width = y + v * lr[0][None] + w * lr[1][None]
    step_width = step_width.reshape(nwl, nt, ncl).transpose(1, 2, 0)

    s_prev = jnp.concatenate([s[:1], s[:-1]], 0)
    s_next = jnp.concatenate([s[1:], s[-1:]], 0)
    lo = -gtl * s_prev
    hi = -gth * s_next
    md = 1.0 + s * (gtl + gth + rim)
    return thick_solve(lo, md, hi, step_width, h)


def solution(mesh):
    spec = P(None, "cast", "width")
    return jax.shard_map(
        shards, mesh=mesh, in_specs=(spec, spec, P()), out_specs=spec, check_vma=False
    )
```

time: 111 us -> 89.6 us (0.81)
  local copies, waits for them, and re-layouts: 24.3 us -> 12.4 us
  blocking collectives: 9.48 us -> 0 us
  other arithmetic: 12.4 us -> 5.37 us
  starting transfers between devices: 30 us -> 34.9 us
  Pallas kernels: 12.5 us -> 14.5 us
  waiting for transfers between devices: 19.7 us -> 20.9 us
    all_gather x1 -> x0, blocking collectives: 9.48 us -> none  [shards(): gath = lax.all_gather(summ, 'width', axis=1)]
    unnamed x26 -> x20, local copies, waits for them, and re-layouts: 7.9 us -> 0.31 us
    mul x1 -> x0, other arithmetic: 6.17 us -> none  [shards(): surf = surf * (nt * nt / 8.0)]
    ppermute x4 -> x7, starting transfers between devices: 12.5 us -> 17.9 us  [the longest x1 5.01 us: shards(): lax.ppermute(h[:, 0, :], 'cast', [(b, a) for a, b in up_c])[:, None, :]]
    transpose x5 -> x0, local copies, waits for them, and re-layouts: 3.16 us -> none  [the longest x4 3 us: ctw(): return jnp.transpose(x, (1, 0, 2))]
    add x2, other arithmetic: 2.75 us -> 0.13 us  [the longest x1 0.08 us: shards(): step_cast = y + v * back[0] + w * back[1]]
    another operation x5 -> x0, local copies, waits for them, and re-layouts: 2.27 us -> none  [the longest x4 2.26 us: summary(): return jnp.stack([y[0], v[0], w[0], y[-1], v[-1], w[-1]])]
    pallas_call x5 -> x6, Pallas kernels: 12.5 us -> 14.5 us  [the longest x1 3.77 us: width_solve(): pl.pallas_call(_width_kernel, out_shape=[shp, shp, shp, jax.ShapeDtypeStr...]
  transfers between devices with their start and end apart: 6 -> 9, of which waited for: 2 -> 3; matrix products, arithmetic and copies ran while one was open for 12% -> 8% of each run, Pallas kernels for 0% -> 2%
where the time goes in v2:
time: 89.6 us; the launch traced here: 88.3 us
  starting transfers between devices  34.9 us (39%)
  waiting for transfers between devices  20.9 us (23%)
  Pallas kernels  14.5 us (16%)
  local copies, waits for them, and re-layouts  12.4 us (14%)
  other arithmetic  5.37 us (6%)
    all_to_all x1, waiting for transfers between devices, shards(): recv = lax.all_to_all(summ.reshape(6, nc, -1), 'cast', 1, 1, tiled=True)  13 us
    all_to_all x1, starting transfers between devices, shards(): recv = lax.all_to_all(summ.reshape(6, nc, -1), 'cast', 1, 1, tiled=True)  12.2 us
    all_to_all x1, waiting for transfers between devices, shards(): back = lax.all_to_all(lr, 'cast', 1, 1, tiled=True).reshape(2, nt, 1, nwl)  7.56 us
    ppermute x1, starting transfers between devices, shards(): lax.ppermute(h[:, 0, :], 'cast', [(b, a) for a, b in up_c])[:, None, :]  5.01 us
    ppermute x3, starting transfers between devices, shards(): lax.ppermute(summ, 'width', [(i, (i + q) % nw) for i in range(nw)])  4.99 us
    all_to_all x1, starting transfers between devices, shards(): back = lax.all_to_all(lr, 'cast', 1, 1, tiled=True).reshape(2, nt, 1, nwl)  4.77 us
    ppermute x1, starting transfers between devices, shards(): h_wl = lax.ppermute(h[:, :, -1], 'width', up_w)[:, :, None]  4.65 us
    pallas_call x1, Pallas kernels, width_solve(): pl.pallas_call(_width_kernel, out_shape=[shp, shp, shp, jax.ShapeDtypeStr...  3.77 us
  transfers between devices with their start and end apart: 9, of which 3 were waited for; matrix products, arithmetic and copies ran while one was open for 8% of the time, Pallas kernels for 2%

profile of v2, /device:TPU:1, one launch (start us, length us, event | category | flops | bytes accessed | tf_op | source)
XLA Modules:
  0.0 88.3 jit_solution(16630190574739107326)
XLA Ops:
  0.0 1.2 %fusion.44 = (f32[64,8,1]{2,1,0:T(8,128)S(1)}, f32[64,8,1]{2,1,0:T(8,128)S(1)}) fusion(f32[64,8,128]{2,1,0:T(8,128)} %h_ref.1), kind=kLoop, calls=%fused_computation.91 | loop fusion | bytes 8192 | tf_op jit(solution)/shard_map/slice | solution.py:208
  1.3 1.3 %collective-permute-start = (f32[64,8]{0,1:T(8,128)S(1)}, f32[64,8]{0,1:T(8,128)S(1)}, u32[]{:S(2)}, u32[]{:S(2)}) collective-permute-start(f32[64,8]{0,1:T(8,128)S(1)} %bitcast.124), channel_id=1, source_target_pairs={{1,0},{2,1},{3,2},{5,4},{6,5},{7,6},{9,8},{10,9},{11,10},{13,12},{... | collective-permute-start | bytes 6152 | tf_op jit(solution)/shard_map/ppermute | solution.py:208
  2.8 4.7 %collective-permute-start.1 = (f32[64,8]{0,1:T(8,128)S(1)}, f32[64,8]{0,1:T(8,128)S(1)}, u32[]{:S(2)}, u32[]{:S(2)}) collective-permute-start(f32[64,8]{0,1:T(8,128)S(1)} %bitcast.123), channel_id=1, source_target_pairs={{0,1},{1,2},{2,3},{4,5},{5,6},{6,7},{8,9},{9,10},{10,11},{12,13},{... | collective-permute-start | bytes 6152 | tf_op jit(solution)/shard_map/ppermute | solution.py:207
  7.5 5.0 %collective-permute-start.2 = (f32[64,128]{1,0:T(8,128)S(1)}, f32[64,128]{1,0:T(8,128)S(1)}, u32[]{:S(2)}, u32[]{:S(2)}) collective-permute-start(f32[64,128]{1,0:T(8,128)S(1)} %bitcast.115), channel_id=1, source_target_pairs={{4,0},{8,4},{12,8},{16,12},{20,16},{24,20},{28,24},{32,28},{36,32}... | collective-permute-start | bytes 98312 | tf_op jit(solution)/shard_map/ppermute | solution.py:206
  12.5 1.9 %collective-permute-start.3 = (f32[64,128]{1,0:T(8,128)S(1)}, f32[64,128]{1,0:T(8,128)S(1)}, u32[]{:S(2)}, u32[]{:S(2)}) collective-permute-start(f32[64,128]{1,0:T(8,128)S(1)} %bitcast.114), channel_id=1, source_target_pairs={{0,4},{4,8},{8,12},{12,16},{16,20},{20,24},{24,28},{28,32},{32,36}... | collective-permute-start | bytes 98312 | tf_op jit(solution)/shard_map/ppermute | solution.py:205
  14.6 1.4 %shard_map.37 = f32[16,128]{1,0:T(8,128)} custom-call(s32[16,128]{1,0:T(8,128)} %bitcast.122, f32[10]{0:T(128)} %sp_ref.1), custom_call_target="tpu_custom_call" | custom-call | tf_op jit(solution)/shard_map/pallas_call | solution.py:210
  16.0 0.7 slice_bitcast_fusion.1
  16.8 0.8 fusion.26
  19.2 1.3 %fusion.21 = (f32[64,8,128]{2,1,0:T(8,128)S(1)}, f32[64,8,128]{2,1,0:T(8,128)S(1)}, f32[64,8,128]{2,1,0:T(8,128)S(1)}, f32[512,128]{1,0:T(8,128)}, f32[512,128]{...) fusion(f32[64,8,1]{2,1,0:T(8,128)S(1)} %copy.162, f32[64,8,128]{2,1,0:T(8,128)S(1)} %get-tuple-element.92, ...), kind=kLoop, calls=%fused_computation.32 | loop fusion | flops 1441792 | bytes 3477504 | tf_op jit(solution)/shard_map/mul | solution.py:273
  20.6 1.2 %fusion.8.d_ref = f32[512,128]{1,0:T(8,128)} fusion(f32[64,8,128]{2,1,0:T(8,128)S(1)} %get-tuple-element.78, f32[64,8,1]{2,1,0:T(8,128)S(1)} %copy.171, f32[64,8,1]{2,1,0:T(8,128)S(1)} %copy.170, f32[64,1,128]{2,1,0:T(1,128)S(1)} %bitcast.107, f32[64,1,128]{2,1,0:T(1,128)S(1)} %bitcast.106, f32[1,8,128]{2,1,0:T(8,128)S(1)} %get-tuple-element.104, ...), kind=kLoop, calls=%fused_computation.13 | loop fusion | flops 1835008 | bytes 2433280 | tf_op jit(solution)/shard_map/reshape | solution.py:253
  21.7 2.7 %shard_map.38 = (f32[512,128]{1,0:T(8,128)}, f32[512,128]{1,0:T(8,128)}, f32[512,128]{1,0:T(8,128)}, f32[6,64,128]{2,1,0:T(8,128)}) custom-call(f32[512,128]{1,0:T(8,128)} %get-tuple-element.76.a_ref, f32[512,128]{1,0:T(8,128)} %get-tuple-element.75.b_ref, f32[512,128]{1,0:T(8,128)} %get-tuple-element.77.c_ref, f32[512,128]{1,0:T(8,128)} %fusion.8.d_ref), custom_call_target="tpu_custom_call" | custom-call | tf_op jit(solution)/shard_map/pallas_call | solution.py:111
  24.4 1.7 %copy.172 = f32[6,64,128]{2,0,1:T(8,128)} copy(f32[6,64,128]{2,1,0:T(8,128)} %get-tuple-element.63) | data formatting | bytes 393216 | tf_op jit(solution)/shard_map/pallas_call | solution.py:111
  26.1 12.2 %all-to-all-start = ((f32[6,64,128]{2,0,1:T(8,128)}), f32[6,64,128]{2,0,1:T(8,128)S(1)}, u32[]{:S(2)}, u32[]{:S(2)}) async-start(f32[6,64,128]{2,0,1:T(8,128)} %copy.172), calls=%async_computation | async-start | bytes 524288 | tf_op jit(solution)/shard_map/all_to_all | solution.py:259
  38.4 13.0 %all-to-all-done = f32[6,64,128]{2,0,1:T(8,128)S(1)} async-done(((f32[6,64,128]{2,0,1:T(8,128)}), f32[6,64,128]{2,0,1:T(8,128)S(1)}, u32[]{:S(2)}, u32[]{:S(2)}) %all-to-all-start) | async-done | bytes 196640 | tf_op jit(solution)/shard_map/all_to_all | solution.py:259
  51.5 0.7 copy.173.s_ref
  52.2 2.4 %shard_map.39 = f32[2,64,128]{2,1,0:T(8,128)} custom-call(f32[6,64,128]{2,1,0:T(8,128)} %copy.173.s_ref), custom_call_target="tpu_custom_call" | custom-call | tf_op jit(solution)/shard_map/pallas_call | solution.py:260
  54.6 1.5 %copy.174 = f32[2,64,128]{2,0,1:T(2,128)} copy(f32[2,64,128]{2,1,0:T(8,128)} %shard_map.39) | data formatting | bytes 131072 | tf_op jit(solution)/shard_map/pallas_call | solution.py:260
  56.1 4.8 %all-to-all-start.1 = ((f32[2,64,128]{2,0,1:T(2,128)}), f32[2,64,128]{2,0,1:T(2,128)S(1)}, u32[]{:S(2)}, u32[]{:S(2)}) async-start(f32[2,64,128]{2,0,1:T(2,128)} %copy.174), calls=%async_computation.1 | async-start | bytes 131072 | tf_op jit(solution)/shard_map/all_to_all | solution.py:263
  60.9 0.8 copy.175.a_ref
  61.7 0.8 copy.176.b_ref
  62.5 0.8 copy.177.c_ref
  63.4 7.6 %all-to-all-done.1 = f32[2,64,128]{2,0,1:T(2,128)S(1)} async-done(((f32[2,64,128]{2,0,1:T(2,128)}), f32[2,64,128]{2,0,1:T(2,128)S(1)}, u32[]{:S(2)}, u32[]{:S(2)}) %all-to-all-start.1) | async-done | bytes 65568 | tf_op jit(solution)/shard_map/all_to_all | solution.py:263
  71.1 0.8 copy.178.d_ref
  71.9 3.8 %shard_map.40 = (f32[128,4,128]{2,1,0:T(4,128)}, f32[128,4,128]{2,1,0:T(4,128)}, f32[128,4,128]{2,1,0:T(4,128)}, f32[6,4,128]{2,1,0:T(4,128)}) custom-call(f32[128,4,128]{2,1,0:T(4,128)} %copy.175.a_ref, f32[128,4,128]{2,1,0:T(4,128)} %copy.176.b_ref, f32[128,4,128]{2,1,0:T(4,128)} %copy.177.c_ref, f32[128,4,128]{2,1,0:T(4,128)} %copy.178.d_ref), custom_call_target="tpu_custom_call" | custom-call | tf_op jit(solution)/shard_map/pallas_call | solution.py:120
  75.7 1.3 %collective-permute-start.4 = (f32[6,4,128]{2,1,0:T(4,128)}, f32[6,4,128]{2,1,0:T(4,128)S(1)}, u32[]{:S(2)}, u32[]{:S(2)}) collective-permute-start(f32[6,4,128]{2,1,0:T(4,128)} %get-tuple-element.67), channel_id=1, source_target_pairs={{0,1},{1,2},{2,3},{3,0},{4,5},{5,6},{6,7},{7,4},{8,9},{9,10},{10,1... | collective-permute-start | bytes 36872 | tf_op jit(solution)/shard_map/ppermute | solution.py:277
  77.0 1.6 %collective-permute-start.5 = (f32[6,4,128]{2,1,0:T(4,128)}, f32[6,4,128]{2,1,0:T(4,128)S(1)}, u32[]{:S(2)}, u32[]{:S(2)}) collective-permute-start(f32[6,4,128]{2,1,0:T(4,128)} %get-tuple-element.67), channel_id=1, source_target_pairs={{0,2},{1,3},{2,0},{3,1},{4,6},{5,7},{6,4},{7,5},{8,10},{9,11},{10,... | collective-permute-start | bytes 36872 | tf_op jit(solution)/shard_map/ppermute | solution.py:277
  78.7 2.0 %collective-permute-start.6 = (f32[6,4,128]{2,1,0:T(4,128)}, f32[6,4,128]{2,1,0:T(4,128)S(1)}, u32[]{:S(2)}, u32[]{:S(2)}) collective-permute-start(f32[6,4,128]{2,1,0:T(4,128)} %get-tuple-element.67), channel_id=1, source_target_pairs={{0,3},{1,0},{2,1},{3,2},{4,7},{5,4},{6,5},{7,6},{8,11},{9,8},{10,9... | collective-permute-start | bytes 36872 | tf_op jit(solution)/shard_map/ppermute | solution.py:277
  80.7 0.8 maximum_multiply_fusion.1
  82.5 1.4 %shard_map.41 = f32[2,4,128]{2,1,0:T(4,128)} custom-call(s32[1]{0:T(128)} %bitcast.45.me_ref, f32[4,6,4,128]{3,2,1,0:T(4,128)} %pad_maximum_fusion.9.r_ref), custom_call_target="tpu_custom_call" | custom-call | tf_op jit(solution)/shard_map/pallas_call | solution.py:279
  83.9 0.7 slice_bitcast_fusion.3
  84.7 0.8 copy.179
  85.5 2.8 %shard_map.42 = f32[64,8,128]{2,1,0:T(8,128)} custom-call(f32[64,8,128]{2,1,0:T(8,128)} %get-tuple-element.94.a_ref, f32[64,8,128]{2,1,0:T(8,128)} %get-tuple-element.91.b_ref, f32[64,8,128]{2,1,0:T(8,128)} %get-tuple-element.93.c_ref, f32[64,8,128]{2,1,0:T(8,128)} %bitcast.98, f32[64,8,128]{2,1,0:T(8,128)} %h_ref.1), custom_call_target="tpu_custom_call" | custom-call | tf_op jit(solution)/shard_map/pallas_call | solution.py:128
  (58 shorter events, 3.2 us)
Async XLA Ops:
  1.2 6.3 %copy-start = (f32[64,8,128]{2,1,0:T(8,128)S(1)}, f32[64,8,128]{2,1,0:T(8,128)}, u32[]{:S(2)}) copy-start(f32[64,8,128]{2,1,0:T(8,128)} %h_ref.1) | copy-start | bytes 786436
  1.3 16.4 %collective-permute-start = (f32[64,8]{0,1:T(8,128)S(1)}, f32[64,8]{0,1:T(8,128)S(1)}, u32[]{:S(2)}, u32[]{:S(2)}) collective-permute-start(f32[64,8]{0,1:T(8,128)S(1)} %bitcast.124), channel_id=1, source_target_pairs={{1,0},{2,1},{3,2},{5,4},{6,5},{7,6},{9,8},{10,9},{11,10},{13,12},{... | collective-permute-start | bytes 6152 | tf_op jit(solution)/shard_map/ppermute | solution.py:208
  2.8 15.1 %collective-permute-start.1 = (f32[64,8]{0,1:T(8,128)S(1)}, f32[64,8]{0,1:T(8,128)S(1)}, u32[]{:S(2)}, u32[]{:S(2)}) collective-permute-start(f32[64,8]{0,1:T(8,128)S(1)} %bitcast.123), channel_id=1, source_target_pairs={{0,1},{1,2},{2,3},{4,5},{5,6},{6,7},{8,9},{9,10},{10,11},{12,13},{... | collective-permute-start | bytes 6152 | tf_op jit(solution)/shard_map/ppermute | solution.py:207
  7.5 11.5 %collective-permute-start.2 = (f32[64,128]{1,0:T(8,128)S(1)}, f32[64,128]{1,0:T(8,128)S(1)}, u32[]{:S(2)}, u32[]{:S(2)}) collective-permute-start(f32[64,128]{1,0:T(8,128)S(1)} %bitcast.115), channel_id=1, source_target_pairs={{4,0},{8,4},{12,8},{16,12},{20,16},{24,20},{28,24},{32,28},{36,32}... | collective-permute-start | bytes 98312 | tf_op jit(solution)/shard_map/ppermute | solution.py:206
  12.5 6.6 %collective-permute-start.3 = (f32[64,128]{1,0:T(8,128)S(1)}, f32[64,128]{1,0:T(8,128)S(1)}, u32[]{:S(2)}, u32[]{:S(2)}) collective-permute-start(f32[64,128]{1,0:T(8,128)S(1)} %bitcast.114), channel_id=1, source_target_pairs={{0,4},{4,8},{8,12},{12,16},{16,20},{20,24},{24,28},{28,32},{32,36}... | collective-permute-start | bytes 98312 | tf_op jit(solution)/shard_map/ppermute | solution.py:205
  26.1 25.3 %all-to-all-start = ((f32[6,64,128]{2,0,1:T(8,128)}), f32[6,64,128]{2,0,1:T(8,128)S(1)}, u32[]{:S(2)}, u32[]{:S(2)}) async-start(f32[6,64,128]{2,0,1:T(8,128)} %copy.172), calls=%async_computation | async-start | bytes 524288 | tf_op jit(solution)/shard_map/all_to_all | solution.py:259
  56.1 14.9 %all-to-all-start.1 = ((f32[2,64,128]{2,0,1:T(2,128)}), f32[2,64,128]{2,0,1:T(2,128)S(1)}, u32[]{:S(2)}, u32[]{:S(2)}) async-start(f32[2,64,128]{2,0,1:T(2,128)} %copy.174), calls=%async_computation.1 | async-start | bytes 131072 | tf_op jit(solution)/shard_map/all_to_all | solution.py:263
  61.7 9.3 %copy-start.3 = (f32[512,128]{1,0:T(8,128)S(1)}, f32[512,128]{1,0:T(8,128)}, u32[]{:S(2)}) copy-start(f32[512,128]{1,0:T(8,128)} %get-tuple-element.64) | copy-start | bytes 786436
  62.5 8.5 %copy-start.1 = (f32[512,128]{1,0:T(8,128)S(1)}, f32[512,128]{1,0:T(8,128)}, u32[]{:S(2)}) copy-start(f32[512,128]{1,0:T(8,128)} %get-tuple-element.61) | copy-start | bytes 786436
  62.5 8.5 %copy-start.2 = (f32[512,128]{1,0:T(8,128)S(1)}, f32[512,128]{1,0:T(8,128)}, u32[]{:S(2)}) copy-start(f32[512,128]{1,0:T(8,128)} %get-tuple-element.62) | copy-start | bytes 786436
  75.7 5.8 %collective-permute-start.4 = (f32[6,4,128]{2,1,0:T(4,128)}, f32[6,4,128]{2,1,0:T(4,128)S(1)}, u32[]{:S(2)}, u32[]{:S(2)}) collective-permute-start(f32[6,4,128]{2,1,0:T(4,128)} %get-tuple-element.67), channel_id=1, source_target_pairs={{0,1},{1,2},{2,3},{3,0},{4,5},{5,6},{6,7},{7,4},{8,9},{9,10},{10,1... | collective-permute-start | bytes 36872 | tf_op jit(solution)/shard_map/ppermute | solution.py:277
  77.0 4.5 %collective-permute-start.5 = (f32[6,4,128]{2,1,0:T(4,128)}, f32[6,4,128]{2,1,0:T(4,128)S(1)}, u32[]{:S(2)}, u32[]{:S(2)}) collective-permute-start(f32[6,4,128]{2,1,0:T(4,128)} %get-tuple-element.67), channel_id=1, source_target_pairs={{0,2},{1,3},{2,0},{3,1},{4,6},{5,7},{6,4},{7,5},{8,10},{9,11},{10,... | collective-permute-start | bytes 36872 | tf_op jit(solution)/shard_map/ppermute | solution.py:277
  78.7 3.2 %collective-permute-start.6 = (f32[6,4,128]{2,1,0:T(4,128)}, f32[6,4,128]{2,1,0:T(4,128)S(1)}, u32[]{:S(2)}, u32[]{:S(2)}) collective-permute-start(f32[6,4,128]{2,1,0:T(4,128)} %get-tuple-element.67), channel_id=1, source_target_pairs={{0,3},{1,0},{2,1},{3,2},{4,7},{5,4},{6,5},{7,6},{8,11},{9,8},{10,9... | collective-permute-start | bytes 36872 | tf_op jit(solution)/shard_map/ppermute | solution.py:277
  80.7 1.1 %copy-start.7 = (f32[6,4,128]{2,1,0:T(4,128)S(1)}, f32[6,4,128]{2,1,0:T(4,128)}, u32[]{:S(2)}) copy-start(f32[6,4,128]{2,1,0:T(4,128)} %get-tuple-element.67) | copy-start | bytes 36868
  80.7 3.9 %copy-start.4 = (f32[128,4,128]{2,1,0:T(4,128)S(1)}, f32[128,4,128]{2,1,0:T(4,128)}, u32[]{:S(2)}) copy-start(f32[128,4,128]{2,1,0:T(4,128)} %get-tuple-element.65) | copy-start | bytes 786436
  80.7 3.9 %copy-start.5 = (f32[128,4,128]{2,1,0:T(4,128)S(1)}, f32[128,4,128]{2,1,0:T(4,128)}, u32[]{:S(2)}) copy-start(f32[128,4,128]{2,1,0:T(4,128)} %get-tuple-element.66) | copy-start | bytes 786436
  80.7 3.9 %copy-start.6 = (f32[128,4,128]{2,1,0:T(4,128)S(1)}, f32[128,4,128]{2,1,0:T(4,128)}, u32[]{:S(2)}) copy-start(f32[128,4,128]{2,1,0:T(4,128)} %get-tuple-element.68) | copy-start | bytes 786436

commit v3 on v2

--- a/solution.py
+++ b/solution.py
@@ -13,60 +13,64 @@
 SMEM_SPEC = pl.BlockSpec(memory_space=pltpu.SMEM)
 
 
-def _sweep(n, ld, st, a_ref, b_ref, c_ref, d_ref, y_ref, v_ref, w_ref, cp_ref, unroll, shape):
+def _sweep(n, subs, ld, st, a_ref, b_ref, c_ref, d_ref, y_ref, v_ref, w_ref, cp_ref, unroll, shape):
     with_vw = v_ref is not None
     zero = jnp.zeros(shape, F32)
     one = jnp.ones(shape, F32)
 
-    def fwd(i, carry):
-        cprev, dprev, vprev = carry
-        a = ld(a_ref, i)
-        r = 1.0 / (ld(b_ref, i) - a * cprev)
-        cn = ld(c_ref, i) * r
-        dn = (ld(d_ref, i) - a * dprev) * r
-        st(cp_ref, i, cn)
-        st(y_ref, i, dn)
-        if with_vw:
-            vprev = -(a * vprev) * r
-            st(v_ref, i, vprev)
-        return cn, dn, vprev
-
+    def fwd(i, carries):
+        out = []
+        for s0, (cprev, dprev, vprev) in zip(subs, carries):
+            j = s0 + i
+            a = ld(a_ref, j)
+            r = 1.0 / (ld(b_ref, j) - a * cprev)
+            cn = ld(c_ref, j) * r
+            dn = (ld(d_ref, j) - a * dprev) * r
+            st(cp_ref, j, cn)
+            st(y_ref, j, dn)
+            if with_vw:
+                vprev = -(a * vprev) * r
+                st(v_ref, j, vprev)
+            out.append((cn, dn, vprev))
+        return tuple(out)
+
+    carries = tuple((zero, zero, one) for _ in subs)
     if unroll is True:
-        carry = (zero, zero, one)
         for i in range(n):
-            carry = fwd(i, carry)
+            carries = fwd(i, carries)
     else:
-        carry = lax.fori_loop(0, n, fwd, (zero, zero, one), unroll=unroll)
-    cl, dl, vl = carry
+        carries = lax.fori_loop(0, n, fwd, carries, unroll=unroll)
     if with_vw:
-        st(w_ref, n - 1, -cl)
-
-    def bwd(j, carry):
-        i = n - 2 - j
-        yn, vn, wn = carry
-        cp = ld(cp_ref, i)
-        yn = ld(y_ref, i) - cp * yn
-        st(y_ref, i, yn)
-        if with_vw:
-            vn = ld(v_ref, i) - cp * vn
-            wn = -cp * wn
-            st(v_ref, i, vn)
-            st(w_ref, i, wn)
-        return yn, vn, wn
-
-    carry = (dl, vl, -cl)
+        for s0, (cl, _, _) in zip(subs, carries):
+            st(w_ref, s0 + n - 1, -cl)
+
+    def bwd(jj, carries):
+        i = n - 2 - jj
+        out = []
+        for s0, (yn, vn, wn) in zip(subs, carries):
+            j = s0 + i
+            cp = ld(cp_ref, j)
+            yn = ld(y_ref, j) - cp * yn
+            st(y_ref, j, yn)
+            if with_vw:
+                vn = ld(v_ref, j) - cp * vn
+                wn = -cp * wn
+                st(v_ref, j, vn)
+                st(w_ref, j, wn)
+            out.append((yn, vn, wn))
+        return tuple(out)
+
+    carries = tuple((dl, vl, -cl) for cl, dl, vl in carries)
     if unroll is True:
-        for j in range(n - 1):
-            carry = bwd(j, carry)
+        for jj in range(n - 1):
+            carries = bwd(jj, carries)
     else:
-        lax.fori_loop(0, n - 1, bwd, carry, unroll=unroll)
-
-
-def _put_summary(sm_ref, ld, n, y_ref, v_ref, w_ref):
-    for k, (ref, i) in enumerate(
-        [(y_ref, 0), (v_ref, 0), (w_ref, 0), (y_ref, n - 1), (v_ref, n - 1), (w_ref, n - 1)]
-    ):
-        sm_ref[k] = ld(ref, i)
+        lax.fori_loop(0, n - 1, bwd, carries, unroll=unroll)
+
+
+def _summary_rows(ld, s0, n, y_ref, v_ref, w_ref):
+    return [ld(y_ref, s0), ld(v_ref, s0), ld(w_ref, s0),
+            ld(y_ref, s0 + n - 1), ld(v_ref, s0 + n - 1), ld(w_ref, s0 + n - 1)]
 
 
 def _cast_kernel(n, a_ref, b_ref, c_ref, d_ref, y_ref, v_ref, w_ref, sm_ref, cp_ref):
@@ -79,8 +83,11 @@
         ref[pl.ds(i, m, stride=n), :] = val
 
     shape = (m, a_ref.shape[1])
-    _sweep(n, ld, st, a_ref, b_ref, c_ref, d_ref, y_ref, v_ref, w_ref, cp_ref, True, shape)
-    _put_summary(sm_ref, ld, n, y_ref, v_ref, w_ref)
+    _sweep(n, [0], ld, st, a_ref, b_ref, c_ref, d_ref, y_ref, v_ref, w_ref, cp_ref, True, shape)
+    rows = _summary_rows(ld, 0, n, y_ref, v_ref, w_ref)
+    rows += [jnp.zeros(shape, F32)] * (8 - len(rows))
+    for k, val in enumerate(rows):
+        sm_ref[pl.ds(k, m, stride=8), :] = val
 
 
 def _lead_ld(ref, i):
@@ -91,17 +98,20 @@
     ref[i] = val
 
 
-def _width_kernel(a_ref, b_ref, c_ref, d_ref, y_ref, v_ref, w_ref, sm_ref, cp_ref):
-    n = a_ref.shape[0]
+def _width_kernel(nsub, a_ref, b_ref, c_ref, d_ref, y_ref, v_ref, w_ref, sm_ref, cp_ref):
+    n = a_ref.shape[0] // nsub
+    subs = [q * n for q in range(nsub)]
     shape = a_ref.shape[1:]
-    _sweep(n, _lead_ld, _lead_st, a_ref, b_ref, c_ref, d_ref, y_ref, v_ref, w_ref, cp_ref, 8, shape)
-    _put_summary(sm_ref, _lead_ld, n, y_ref, v_ref, w_ref)
+    _sweep(n, subs, _lead_ld, _lead_st, a_ref, b_ref, c_ref, d_ref, y_ref, v_ref, w_ref, cp_ref, 4, shape)
+    for q, s0 in enumerate(subs):
+        for k, val in enumerate(_summary_rows(_lead_ld, s0, n, y_ref, v_ref, w_ref)):
+            sm_ref[q, k] = val
 
 
 def _thick_kernel(a_ref, b_ref, c_ref, d_ref, h_ref, o_ref, y_ref, cp_ref):
     n = a_ref.shape[0]
     shape = a_ref.shape[1:]
-    _sweep(n, _lead_ld, _lead_st, a_ref, b_ref, c_ref, d_ref, y_ref, None, None, cp_ref, 8, shape)
+    _sweep(n, [0], _lead_ld, _lead_st, a_ref, b_ref, c_ref, d_ref, y_ref, None, None, cp_ref, 8, shape)
     o_ref[...] = h_ref[...] + y_ref[...]
 
 
@@ -110,16 +120,16 @@
     m = a.shape[0] // n
     return pl.pallas_call(
         functools.partial(_cast_kernel, n),
-        out_shape=[shp, shp, shp, jax.ShapeDtypeStruct((6, m, a.shape[1]), F32)],
+        out_shape=[shp, shp, shp, jax.ShapeDtypeStruct((m * 8, a.shape[1]), F32)],
         scratch_shapes=[pltpu.VMEM(a.shape, F32)],
     )(a, b, c, d)
 
 
-def width_solve(a, b, c, d):
+def width_solve(a, b, c, d, nsub):
     shp = jax.ShapeDtypeStruct(a.shape, F32)
     return pl.pallas_call(
-        _width_kernel,
-        out_shape=[shp, shp, shp, jax.ShapeDtypeStruct((6,) + a.shape[1:], F32)],
+        functools.partial(_width_kernel, nsub),
+        out_shape=[shp, shp, shp, jax.ShapeDtypeStruct((nsub, 6) + a.shape[1:], F32)],
         scratch_shapes=[pltpu.VMEM(a.shape, F32)],
     )(a, b, c, d)
 
@@ -151,33 +161,45 @@
 
 
 def _cast_reduced_kernel(s_ref, lr_ref):
-    nb = s_ref.shape[1]
+    nb = s_ref.shape[0]
+    lr_ref[...] = jnp.zeros(lr_ref.shape, F32)
 
     def blk(p):
-        return tuple(s_ref[k, p : p + 1] for k in range(6))
+        return tuple(s_ref[p, :, k, :] for k in range(6))
 
     def emit(p, left, right):
-        lr_ref[0, p : p + 1] = left
-        lr_ref[1, p : p + 1] = right
-
-    _reduce_blocks(nb, blk, emit, jnp.zeros((1, s_ref.shape[2]), F32))
-
-
-def _width_reduced_kernel(me_ref, r_ref, lr_ref):
-    nb = r_ref.shape[0]
+        lr_ref[p, :, 0, :] = left
+        lr_ref[p, :, 1, :] = right
+
+    _reduce_blocks(nb, blk, emit, jnp.zeros((s_ref.shape[1], s_ref.shape[3]), F32))
+
+
+def _width_reduced_kernel(me_ref, *refs):
+    *r_refs, lr_ref = refs
+    nw = len(r_refs)
+    nsub = r_refs[0].shape[0]
     me = me_ref[0]
 
-    def blk(p):
-        k = (me - p + nb) % nb
-        return tuple(r_ref[k, q] for q in range(6))
-
-    def emit(p, left, right):
-        @pl.when(me == p)
+    def blk(b):
+        dev, q = divmod(b, nsub)
+        kk = (me - dev + nw) % nw
+        vals = []
+        for k6 in range(6):
+            val = r_refs[0][q, k6]
+            for k in range(1, nw):
+                val = jnp.where(kk == k, r_refs[k][q, k6], val)
+            vals.append(val)
+        return tuple(vals)
+
+    def emit(b, left, right):
+        dev, q = divmod(b, nsub)
+
+        @pl.when(me == dev)
         def _():
-            lr_ref[0] = left
-            lr_ref[1] = right
-
-    _reduce_blocks(nb, blk, emit, jnp.zeros(r_ref.shape[2:], F32))
+            lr_ref[q, 0] = left
+            lr_ref[q, 1] = right
+
+    _reduce_blocks(nw * nsub, blk, emit, jnp.zeros(r_refs[0].shape[2:], F32))
 
 
 def _surface_kernel(scale, z_ref, sp_ref, o_ref):
@@ -256,15 +278,14 @@
     hi = -gch * sc[:, 2:]
     md = 1.0 + s * (gcl + gch)
     y, v, w, summ = cast_solve(flat(lo), flat(md), flat(hi), flat(explicit), ncl)
-    recv = lax.all_to_all(summ.reshape(6, nc, -1), "cast", 1, 1, tiled=True)
-    lr = pl.pallas_call(
-        _cast_reduced_kernel, out_shape=jax.ShapeDtypeStruct((2,) + recv.shape[1:], F32)
-    )(recv)
-    back = lax.all_to_all(lr, "cast", 1, 1, tiled=True).reshape(2, nt, 1, nwl)
+    recv = lax.all_to_all(summ.reshape(nc, nt // nc, 8, nwl), "cast", 0, 0, tiled=True)
+    lr = pl.pallas_call(_cast_reduced_kernel, out_shape=jax.ShapeDtypeStruct(recv.shape, F32))(recv)
+    back = lax.all_to_all(lr, "cast", 0, 0, tiled=True).reshape(nt, 8, nwl)
     y, v, w = (x.reshape(nt, ncl, nwl) for x in (y, v, w))
-    step_cast = y + v * back[0] + w * back[1]
+    step_cast = y + v * back[:, 0:1] + w * back[:, 1:2]
 
     lines = nt * ncl
+    nsub = 4
 
     def wl(x):
         return jnp.transpose(x, (2, 0, 1)).reshape(nwl, lines // 128, 128)
@@ -272,16 +293,18 @@
     lo = -gwl * sw[:, :, :-2]
     hi = -gwh * sw[:, :, 2:]
     md = 1.0 + s * (gwl + gwh)
-    y, v, w, summ = width_solve(wl(lo), wl(md), wl(hi), wl(step_cast))
+    y, v, w, summ = width_solve(wl(lo), wl(md), wl(hi), wl(step_cast), nsub)
     got = [summ] + [
         lax.ppermute(summ, "width", [(i, (i + q) % nw) for i in range(nw)]) for q in range(1, nw)
     ]
     lr = pl.pallas_call(
         _width_reduced_kernel,
-        out_shape=jax.ShapeDtypeStruct((2,) + summ.shape[1:], F32),
-        in_specs=[SMEM_SPEC, pl.BlockSpec(memory_space=pltpu.VMEM)],
-    )(wi.astype(jnp.int32).reshape(1), jnp.stack(got))
-    step_width = y + v * lr[0][None] + w * lr[1][None]
+        out_shape=jax.ShapeDtypeStruct((nsub, 2) + summ.shape[2:], F32),
+        in_specs=[SMEM_SPEC] + [pl.BlockSpec(memory_space=pltpu.VMEM)] * nw,
+    )(wi.astype(jnp.int32).reshape(1), *got)
+    sub = (nsub, nwl // nsub) + y.shape[1:]
+    y, v, w = (x.reshape(sub) for x in (y, v, w))
+    step_width = y + v * lr[:, 0:1] + w * lr[:, 1:2]
     step_width = step_width.reshape(nwl, nt, ncl).transpose(1, 2, 0)
 
     s_prev = jnp.concatenate([s[:1], s[:-1]], 0)

time: 89.6 us -> 92.1 us (1.028)
  blocking collectives: 0 us -> 25.4 us
  starting transfers between devices: 34.9 us -> 22.6 us
  waiting for transfers between devices: 20.9 us -> 10.5 us
    all_to_all x0 -> x1, blocking collectives: none -> 25.4 us  [shards(): lax.all_to_all(summ.reshape(nc, nt // nc, 8, nwl), 'cast', 0, 0, tiled=True)]
    all_to_all x2 -> x1, starting transfers between devices: 17 us -> 4.77 us  [shards(): back = lax.all_to_all(lr, 'cast', 0, 0, tiled=True).reshape(nt, 8, nwl)]
    all_to_all x2 -> x1, waiting for transfers between devices: 20.6 us -> 10.5 us  [shards(): back = lax.all_to_all(lr, 'cast', 0, 0, tiled=True).reshape(nt, 8, nwl)]
    pallas_call x2 -> x3, local copies, waits for them, and re-layouts: 3.27 us -> 0.38 us  [width_solve(): pl.pallas_call(functools.partial(_width_kernel, nsub), out_shape=[shp, sh...]
    mul x1 -> x7, local copies, waits for them, and re-layouts: 0.68 us -> 3.14 us  [shards(): step_width = y + v * lr[:, 0:1] + w * lr[:, 1:2]]
    unnamed x20 -> x22, local copies, waits for them, and re-layouts: 0.31 us -> 2.69 us
  transfers between devices with their start and end apart: 9 -> 8, of which waited for: 3 -> 1; matrix products, arithmetic and copies ran while one was open for 8% -> 8% of each run, Pallas kernels for 2% -> 2%
where the time goes in v3:
time: 92.1 us; the launch traced here: 91.3 us
  blocking collectives  25.4 us (28%)
  starting transfers between devices  22.6 us (25%)
  Pallas kernels  14.1 us (15%)
  local copies, waits for them, and re-layouts  12.7 us (14%)
  waiting for transfers between devices  10.5 us (11%)
  other arithmetic  5.46 us (6%)
    all_to_all x1, blocking collectives, shards(): lax.all_to_all(summ.reshape(nc, nt // nc, 8, nwl), 'cast', 0, 0, tiled=True)  25.4 us
    all_to_all x1, waiting for transfers between devices, shards(): back = lax.all_to_all(lr, 'cast', 0, 0, tiled=True).reshape(nt, 8, nwl)  10.5 us
    ppermute x1, starting transfers between devices, shards(): lax.ppermute(h[:, 0, :], 'cast', [(b, a) for a, b in up_c])[:, None, :]  5.01 us
    ppermute x3, starting transfers between devices, shards(): lax.ppermute(summ, 'width', [(i, (i + q) % nw) for i in range(nw)])  4.99 us
    all_to_all x1, starting transfers between devices, shards(): back = lax.all_to_all(lr, 'cast', 0, 0, tiled=True).reshape(nt, 8, nwl)  4.77 us
    ppermute x1, starting transfers between devices, shards(): h_wl = lax.ppermute(h[:, :, -1], 'width', up_w)[:, :, None]  4.65 us
    reshape x4, local copies, waits for them, and re-layouts, wl(): return jnp.transpose(x, (2, 0, 1)).reshape(nwl, lines // 128, 128)  3.35 us
    mul x7, local copies, waits for them, and re-layouts, shards(): step_width = y + v * lr[:, 0:1] + w * lr[:, 1:2]  3.14 us
  transfers between devices with their start and end apart: 8, of which 1 were waited for; matrix products, arithmetic and copies ran while one was open for 8% of the time, Pallas kernels for 2%

profile of v3, /device:TPU:1, one launch (start us, length us, event | category | flops | bytes accessed | tf_op | source)
XLA Modules:
  0.0 91.3 jit_solution(3176237216834528931)
XLA Ops:
  0.0 1.2 %fusion.45 = (f32[64,8,1]{2,1,0:T(8,128)S(1)}, f32[64,8,1]{2,1,0:T(8,128)S(1)}) fusion(f32[64,8,128]{2,1,0:T(8,128)} %h_ref.1), kind=kLoop, calls=%fused_computation.91 | loop fusion | bytes 8192 | tf_op jit(solution)/shard_map/slice | solution.py:230
  1.3 1.3 %collective-permute-start = (f32[64,8]{0,1:T(8,128)S(1)}, f32[64,8]{0,1:T(8,128)S(1)}, u32[]{:S(2)}, u32[]{:S(2)}) collective-permute-start(f32[64,8]{0,1:T(8,128)S(1)} %bitcast.116), channel_id=1, source_target_pairs={{1,0},{2,1},{3,2},{5,4},{6,5},{7,6},{9,8},{10,9},{11,10},{13,12},{... | collective-permute-start | bytes 6152 | tf_op jit(solution)/shard_map/ppermute | solution.py:230
  2.8 4.7 %collective-permute-start.1 = (f32[64,8]{0,1:T(8,128)S(1)}, f32[64,8]{0,1:T(8,128)S(1)}, u32[]{:S(2)}, u32[]{:S(2)}) collective-permute-start(f32[64,8]{0,1:T(8,128)S(1)} %bitcast.115), channel_id=1, source_target_pairs={{0,1},{1,2},{2,3},{4,5},{5,6},{6,7},{8,9},{9,10},{10,11},{12,13},{... | collective-permute-start | bytes 6152 | tf_op jit(solution)/shard_map/ppermute | solution.py:229
  7.5 5.0 %collective-permute-start.2 = (f32[64,128]{1,0:T(8,128)S(1)}, f32[64,128]{1,0:T(8,128)S(1)}, u32[]{:S(2)}, u32[]{:S(2)}) collective-permute-start(f32[64,128]{1,0:T(8,128)S(1)} %bitcast.113), channel_id=1, source_target_pairs={{4,0},{8,4},{12,8},{16,12},{20,16},{24,20},{28,24},{32,28},{36,32}... | collective-permute-start | bytes 98312 | tf_op jit(solution)/shard_map/ppermute | solution.py:228
  12.5 1.9 %collective-permute-start.3 = (f32[64,128]{1,0:T(8,128)S(1)}, f32[64,128]{1,0:T(8,128)S(1)}, u32[]{:S(2)}, u32[]{:S(2)}) collective-permute-start(f32[64,128]{1,0:T(8,128)S(1)} %bitcast.112), channel_id=1, source_target_pairs={{0,4},{4,8},{8,12},{12,16},{16,20},{20,24},{24,28},{28,32},{32,36}... | collective-permute-start | bytes 98312 | tf_op jit(solution)/shard_map/ppermute | solution.py:227
  14.6 1.4 %shard_map.37 = f32[16,128]{1,0:T(8,128)} custom-call(s32[16,128]{1,0:T(8,128)} %bitcast.114, f32[10]{0:T(128)} %sp_ref.1), custom_call_target="tpu_custom_call" | custom-call | tf_op jit(solution)/shard_map/pallas_call | solution.py:232
  16.0 0.7 slice_bitcast_fusion.3
  16.8 0.8 fusion.26
  19.2 1.3 %fusion.21 = (f32[64,8,128]{2,1,0:T(8,128)S(1)}, f32[64,8,128]{2,1,0:T(8,128)S(1)}, f32[64,8,128]{2,1,0:T(8,128)S(1)}, f32[512,128]{1,0:T(8,128)}, f32[512,128]{...) fusion(f32[64,8,1]{2,1,0:T(8,128)S(1)} %copy.166, f32[64,8,128]{2,1,0:T(8,128)S(1)} %get-tuple-element.94, ...), kind=kLoop, calls=%fused_computation.32 | loop fusion | flops 1441792 | bytes 3477504 | tf_op jit(solution)/shard_map/mul | solution.py:294
  20.6 1.1 %fusion.8.d_ref = f32[512,128]{1,0:T(8,128)} fusion(f32[64,8,128]{2,1,0:T(8,128)S(1)} %get-tuple-element.78, f32[64,8,1]{2,1,0:T(8,128)S(1)} %copy.175, f32[64,8,1]{2,1,0:T(8,128)S(1)} %copy.174, f32[64,1,128]{2,1,0:T(1,128)S(1)} %bitcast.105, f32[64,1,128]{2,1,0:T(1,128)S(1)} %bitcast.104, f32[1,8,128]{2,1,0:T(8,128)S(1)} %get-tuple-element.106, ...), kind=kLoop, calls=%fused_computation.13 | loop fusion | flops 1835008 | bytes 2433280 | tf_op jit(solution)/shard_map/reshape | solution.py:275
  21.7 2.8 %shard_map.38 = (f32[512,128]{1,0:T(8,128)}, f32[512,128]{1,0:T(8,128)}, f32[512,128]{1,0:T(8,128)}, f32[512,128]{1,0:T(8,128)}) custom-call(f32[512,128]{1,0:T(8,128)} %get-tuple-element.76.a_ref, f32[512,128]{1,0:T(8,128)} %get-tuple-element.75.b_ref, f32[512,128]{1,0:T(8,128)} %get-tuple-element.77.c_ref, f32[512,128]{1,0:T(8,128)} %fusion.8.d_ref), custom_call_target="tpu_custom_call" | custom-call | tf_op jit(solution)/shard_map/pallas_call | solution.py:121
  24.5 25.4 %all_to_all.10.s_ref = f32[64,1,8,128]{3,2,1,0:T(8,128)} all-to-all(f32[64,1,8,128]{3,2,1,0:T(8,128)} %bitcast.103), channel_id=1, replica_groups=mesh['cast'=64,'width'=4] {'cast'}, dimensions={0} | all-to-all | bytes 524288 | tf_op jit(solution)/shard_map/all_to_all | solution.py:281
  49.9 2.5 %shard_map.39 = f32[64,1,8,128]{3,2,1,0:T(8,128)} custom-call(f32[64,1,8,128]{3,2,1,0:T(8,128)} %all_to_all.10.s_ref), custom_call_target="tpu_custom_call" | custom-call | tf_op jit(solution)/shard_map/pallas_call | solution.py:282
  52.4 4.8 %all-to-all-start.1 = ((f32[64,1,8,128]{3,2,1,0:T(8,128)}), f32[64,1,8,128]{3,2,1,0:T(8,128)S(1)}, u32[]{:S(2)}, u32[]{:S(2)}) async-start(f32[64,1,8,128]{3,2,1,0:T(8,128)} %shard_map.39), calls=%async_computation.1 | async-start | bytes 524288 | tf_op jit(solution)/shard_map/all_to_all | solution.py:283
  57.2 0.8 copy.176.a_ref
  58.0 0.8 copy.177.b_ref
  58.9 0.8 copy.178.c_ref
  59.7 10.5 %all-to-all-done.1 = f32[64,1,8,128]{3,2,1,0:T(8,128)S(1)} async-done(((f32[64,1,8,128]{3,2,1,0:T(8,128)}), f32[64,1,8,128]{3,2,1,0:T(8,128)S(1)}, u32[]{:S(2)}, u32[]{:S(2)}) %all-to-all-start.1) | async-done | bytes 262176 | tf_op jit(solution)/shard_map/all_to_all | solution.py:283
  70.4 0.8 copy.179.d_ref
  71.2 3.0 %shard_map.40 = (f32[128,4,128]{2,1,0:T(4,128)}, f32[128,4,128]{2,1,0:T(4,128)}, f32[128,4,128]{2,1,0:T(4,128)}, f32[4,6,4,128]{3,2,1,0:T(4,128)}) custom-call(f32[128,4,128]{2,1,0:T(4,128)} %copy.176.a_ref, f32[128,4,128]{2,1,0:T(4,128)} %copy.177.b_ref, f32[128,4,128]{2,1,0:T(4,128)} %copy.178.c_ref, f32[128,4,128]{2,1,0:T(4,128)} %copy.179.d_ref), custom_call_target="tpu_custom_call" | custom-call | tf_op jit(solution)/shard_map/pallas_call | solution.py:130
  74.2 1.3 %collective-permute-start.4 = (f32[4,6,4,128]{3,2,1,0:T(4,128)}, f32[4,6,4,128]{3,2,1,0:T(4,128)S(1)}, u32[]{:S(2)}, u32[]{:S(2)}) collective-permute-start(f32[4,6,4,128]{3,2,1,0:T(4,128)} %get-tuple-element.67.refs_0_), channel_id=1, source_target_pairs={{0,1},{1,2},{2,3},{3,0},{4,5},{5,6},{6,7},{7,4},{8,9},{9,10},{10,1... | collective-permute-start | bytes 147464 | tf_op jit(solution)/shard_map/ppermute | solution.py:298
  75.5 1.6 %collective-permute-start.5 = (f32[4,6,4,128]{3,2,1,0:T(4,128)}, f32[4,6,4,128]{3,2,1,0:T(4,128)S(1)}, u32[]{:S(2)}, u32[]{:S(2)}) collective-permute-start(f32[4,6,4,128]{3,2,1,0:T(4,128)} %get-tuple-element.67.refs_0_), channel_id=1, source_target_pairs={{0,2},{1,3},{2,0},{3,1},{4,6},{5,7},{6,4},{7,5},{8,10},{9,11},{10,... | collective-permute-start | bytes 147464 | tf_op jit(solution)/shard_map/ppermute | solution.py:298
  77.1 2.1 %collective-permute-start.6 = (f32[4,6,4,128]{3,2,1,0:T(4,128)}, f32[4,6,4,128]{3,2,1,0:T(4,128)S(1)}, u32[]{:S(2)}, u32[]{:S(2)}) collective-permute-start(f32[4,6,4,128]{3,2,1,0:T(4,128)} %get-tuple-element.67.refs_0_), channel_id=1, source_target_pairs={{0,3},{1,0},{2,1},{3,2},{4,7},{5,4},{6,5},{7,6},{8,11},{9,8},{10,9... | collective-permute-start | bytes 147464 | tf_op jit(solution)/shard_map/ppermute | solution.py:298
  79.2 0.8 maximum_multiply_fusion.1
  80.3 0.8 copy-done.5
  81.3 0.8 copy-done.4
  82.9 1.7 %shard_map.41 = f32[4,2,4,128]{3,2,1,0:T(4,128)} custom-call(s32[1]{0:T(128)} %bitcast.49.me_ref, f32[4,6,4,128]{3,2,1,0:T(4,128)} %get-tuple-element.67.refs_0_, f32[4,6,4,128]{3,2,1,0:T(4,128)} %copy-done.7, f32[4,6,4,128]{3,2,1,0:T(4,128)} %copy-done.8, f32[4,6,4,128]{3,2,1,0:T(4,128)} %copy-done.9), custom_call_target="tpu_custom_call" | custom-call | tf_op jit(solution)/shard_map/pallas_call | solution.py:300
  84.6 0.7 slice_bitcast_fusion.1
  85.5 0.6 mul.254
  86.7 0.6 mul.258
  87.8 0.8 add_bitcast_fusion.d_ref
  88.6 2.8 %shard_map.42 = f32[64,8,128]{2,1,0:T(8,128)} custom-call(f32[64,8,128]{2,1,0:T(8,128)} %get-tuple-element.96.a_ref, f32[64,8,128]{2,1,0:T(8,128)} %get-tuple-element.93.b_ref, f32[64,8,128]{2,1,0:T(8,128)} %get-tuple-element.95.c_ref, f32[64,8,128]{2,1,0:T(8,128)} %add_bitcast_fusion.d_ref, f32[64,8,128]{2,1,0:T(8,128)} %h_ref.1), custom_call_target="tpu_custom_call" | custom-call | tf_op jit(solution)/shard_map/pallas_call | solution.py:138
  (63 shorter events, 4.6 us)
Async XLA Ops:
  1.2 6.3 %copy-start = (f32[64,8,128]{2,1,0:T(8,128)S(1)}, f32[64,8,128]{2,1,0:T(8,128)}, u32[]{:S(2)}) copy-start(f32[64,8,128]{2,1,0:T(8,128)} %h_ref.1) | copy-start | bytes 786436
  1.3 16.4 %collective-permute-start = (f32[64,8]{0,1:T(8,128)S(1)}, f32[64,8]{0,1:T(8,128)S(1)}, u32[]{:S(2)}, u32[]{:S(2)}) collective-permute-start(f32[64,8]{0,1:T(8,128)S(1)} %bitcast.116), channel_id=1, source_target_pairs={{1,0},{2,1},{3,2},{5,4},{6,5},{7,6},{9,8},{10,9},{11,10},{13,12},{... | collective-permute-start | bytes 6152 | tf_op jit(solution)/shard_map/ppermute | solution.py:230
  2.8 15.1 %collective-permute-start.1 = (f32[64,8]{0,1:T(8,128)S(1)}, f32[64,8]{0,1:T(8,128)S(1)}, u32[]{:S(2)}, u32[]{:S(2)}) collective-permute-start(f32[64,8]{0,1:T(8,128)S(1)} %bitcast.115), channel_id=1, source_target_pairs={{0,1},{1,2},{2,3},{4,5},{5,6},{6,7},{8,9},{9,10},{10,11},{12,13},{... | collective-permute-start | bytes 6152 | tf_op jit(solution)/shard_map/ppermute | solution.py:229
  7.5 11.5 %collective-permute-start.2 = (f32[64,128]{1,0:T(8,128)S(1)}, f32[64,128]{1,0:T(8,128)S(1)}, u32[]{:S(2)}, u32[]{:S(2)}) collective-permute-start(f32[64,128]{1,0:T(8,128)S(1)} %bitcast.113), channel_id=1, source_target_pairs={{4,0},{8,4},{12,8},{16,12},{20,16},{24,20},{28,24},{32,28},{36,32}... | collective-permute-start | bytes 98312 | tf_op jit(solution)/shard_map/ppermute | solution.py:228
  12.5 6.6 %collective-permute-start.3 = (f32[64,128]{1,0:T(8,128)S(1)}, f32[64,128]{1,0:T(8,128)S(1)}, u32[]{:S(2)}, u32[]{:S(2)}) collective-permute-start(f32[64,128]{1,0:T(8,128)S(1)} %bitcast.112), channel_id=1, source_target_pairs={{0,4},{4,8},{8,12},{12,16},{16,20},{20,24},{24,28},{28,32},{32,36}... | collective-permute-start | bytes 98312 | tf_op jit(solution)/shard_map/ppermute | solution.py:227
  52.4 17.9 %all-to-all-start.1 = ((f32[64,1,8,128]{3,2,1,0:T(8,128)}), f32[64,1,8,128]{3,2,1,0:T(8,128)S(1)}, u32[]{:S(2)}, u32[]{:S(2)}) async-start(f32[64,1,8,128]{3,2,1,0:T(8,128)} %shard_map.39), calls=%async_computation.1 | async-start | bytes 524288 | tf_op jit(solution)/shard_map/all_to_all | solution.py:283
  58.0 12.2 %copy-start.3 = (f32[512,128]{1,0:T(8,128)S(1)}, f32[512,128]{1,0:T(8,128)}, u32[]{:S(2)}) copy-start(f32[512,128]{1,0:T(8,128)} %get-tuple-element.64) | copy-start | bytes 786436
  58.9 11.4 %copy-start.1 = (f32[512,128]{1,0:T(8,128)S(1)}, f32[512,128]{1,0:T(8,128)}, u32[]{:S(2)}) copy-start(f32[512,128]{1,0:T(8,128)} %get-tuple-element.61) | copy-start | bytes 786436
  58.9 11.4 %copy-start.2 = (f32[512,128]{1,0:T(8,128)S(1)}, f32[512,128]{1,0:T(8,128)}, u32[]{:S(2)}) copy-start(f32[512,128]{1,0:T(8,128)} %get-tuple-element.62) | copy-start | bytes 786436
  74.2 8.0 %collective-permute-start.4 = (f32[4,6,4,128]{3,2,1,0:T(4,128)}, f32[4,6,4,128]{3,2,1,0:T(4,128)S(1)}, u32[]{:S(2)}, u32[]{:S(2)}) collective-permute-start(f32[4,6,4,128]{3,2,1,0:T(4,128)} %get-tuple-element.67.refs_0_), channel_id=1, source_target_pairs={{0,1},{1,2},{2,3},{3,0},{4,5},{5,6},{6,7},{7,4},{8,9},{9,10},{10,1... | collective-permute-start | bytes 147464 | tf_op jit(solution)/shard_map/ppermute | solution.py:298
  75.5 6.7 %collective-permute-start.5 = (f32[4,6,4,128]{3,2,1,0:T(4,128)}, f32[4,6,4,128]{3,2,1,0:T(4,128)S(1)}, u32[]{:S(2)}, u32[]{:S(2)}) collective-permute-start(f32[4,6,4,128]{3,2,1,0:T(4,128)} %get-tuple-element.67.refs_0_), channel_id=1, source_target_pairs={{0,2},{1,3},{2,0},{3,1},{4,6},{5,7},{6,4},{7,5},{8,10},{9,11},{10,... | collective-permute-start | bytes 147464 | tf_op jit(solution)/shard_map/ppermute | solution.py:298
  77.1 5.1 %collective-permute-start.6 = (f32[4,6,4,128]{3,2,1,0:T(4,128)}, f32[4,6,4,128]{3,2,1,0:T(4,128)S(1)}, u32[]{:S(2)}, u32[]{:S(2)}) collective-permute-start(f32[4,6,4,128]{3,2,1,0:T(4,128)} %get-tuple-element.67.refs_0_), channel_id=1, source_target_pairs={{0,3},{1,0},{2,1},{3,2},{4,7},{5,4},{6,5},{7,6},{8,11},{9,8},{10,9... | collective-permute-start | bytes 147464 | tf_op jit(solution)/shard_map/ppermute | solution.py:298
  79.2 1.0 %copy-start.6 = (f32[128,4,128]{2,1,0:T(4,128)S(1)}, f32[128,4,128]{2,1,0:T(4,128)}, u32[]{:S(2)}) copy-start(f32[128,4,128]{2,1,0:T(4,128)} %get-tuple-element.65) | copy-start | bytes 786436
  80.2 0.9 %copy-start.5 = (f32[128,4,128]{2,1,0:T(4,128)S(1)}, f32[128,4,128]{2,1,0:T(4,128)}, u32[]{:S(2)}) copy-start(f32[128,4,128]{2,1,0:T(4,128)} %get-tuple-element.66) | copy-start | bytes 786436
  81.1 0.9 %copy-start.4 = (f32[128,4,128]{2,1,0:T(4,128)S(1)}, f32[128,4,128]{2,1,0:T(4,128)}, u32[]{:S(2)}) copy-start(f32[128,4,128]{2,1,0:T(4,128)} %get-tuple-element.68) | copy-start | bytes 786436
  82.2 0.6 copy-start.7
  82.2 0.6 copy-start.8
  82.3 0.6 copy-start.9

commit v4 on v3

--- a/solution.py
+++ b/solution.py
@@ -98,7 +98,13 @@
     ref[i] = val
 
 
-def _width_kernel(nsub, a_ref, b_ref, c_ref, d_ref, y_ref, v_ref, w_ref, sm_ref, cp_ref):
+def _width_kernel(nsub, yc_ref, vc_ref, wc_ref, bk_ref, a_ref, b_ref, c_ref,
+                  y_ref, v_ref, w_ref, sm_ref, cp_ref, d_ref):
+    sc = yc_ref[...] + vc_ref[...] * bk_ref[:, 0:1, :] + wc_ref[...] * bk_ref[:, 1:2, :]
+    nt, ncl, nwl = sc.shape
+    sc = sc.reshape(nt * ncl, nwl)
+    for q in range(d_ref.shape[1]):
+        d_ref[:, q, :] = sc[q * 128 : (q + 1) * 128, :].T
     n = a_ref.shape[0] // nsub
     subs = [q * n for q in range(nsub)]
     shape = a_ref.shape[1:]
@@ -108,10 +114,18 @@
             sm_ref[q, k] = val
 
 
-def _thick_kernel(a_ref, b_ref, c_ref, d_ref, h_ref, o_ref, y_ref, cp_ref):
-    n = a_ref.shape[0]
+def _thick_kernel(nsub, yw_ref, vw_ref, ww_ref, lr_ref, a_ref, b_ref, c_ref, h_ref,
+                  o_ref, sw_ref, d_ref, y_ref, cp_ref):
+    m = yw_ref.shape[0] // nsub
+    for q in range(nsub):
+        sl = slice(q * m, (q + 1) * m)
+        sw_ref[sl] = yw_ref[sl] + vw_ref[sl] * lr_ref[q, 0] + ww_ref[sl] * lr_ref[q, 1]
+    nt, ncl, nwl = a_ref.shape
+    per_q = 128 // ncl
+    for q in range(sw_ref.shape[1]):
+        d_ref[q * per_q : (q + 1) * per_q] = sw_ref[:, q, :].T.reshape(per_q, ncl, nwl)
     shape = a_ref.shape[1:]
-    _sweep(n, [0], _lead_ld, _lead_st, a_ref, b_ref, c_ref, d_ref, y_ref, None, None, cp_ref, 8, shape)
+    _sweep(nt, [0], _lead_ld, _lead_st, a_ref, b_ref, c_ref, d_ref, y_ref, None, None, cp_ref, 8, shape)
     o_ref[...] = h_ref[...] + y_ref[...]
 
 
@@ -125,21 +139,21 @@
     )(a, b, c, d)
 
 
-def width_solve(a, b, c, d, nsub):
+def width_solve(yc, vc, wc, bk, a, b, c, nsub):
     shp = jax.ShapeDtypeStruct(a.shape, F32)
     return pl.pallas_call(
         functools.partial(_width_kernel, nsub),
         out_shape=[shp, shp, shp, jax.ShapeDtypeStruct((nsub, 6) + a.shape[1:], F32)],
-        scratch_shapes=[pltpu.VMEM(a.shape, F32)],
-    )(a, b, c, d)
-
-
-def thick_solve(a, b, c, d, h):
+        scratch_shapes=[pltpu.VMEM(a.shape, F32), pltpu.VMEM(a.shape, F32)],
+    )(yc, vc, wc, bk, a, b, c)
+
+
+def thick_solve(yw, vw, ww, lr, a, b, c, h, nsub):
     return pl.pallas_call(
-        _thick_kernel,
+        functools.partial(_thick_kernel, nsub),
         out_shape=jax.ShapeDtypeStruct(a.shape, F32),
-        scratch_shapes=[pltpu.VMEM(a.shape, F32), pltpu.VMEM(a.shape, F32)],
-    )(a, b, c, d, h)
+        scratch_shapes=[pltpu.VMEM(yw.shape, F32)] + [pltpu.VMEM(a.shape, F32)] * 3,
+    )(yw, vw, ww, lr, a, b, c, h)
 
 
 def _reduce_blocks(nb, blk, emit, zero):
@@ -162,14 +176,12 @@
 
 def _cast_reduced_kernel(s_ref, lr_ref):
     nb = s_ref.shape[0]
-    lr_ref[...] = jnp.zeros(lr_ref.shape, F32)
-
     def blk(p):
         return tuple(s_ref[p, :, k, :] for k in range(6))
 
     def emit(p, left, right):
-        lr_ref[p, :, 0, :] = left
-        lr_ref[p, :, 1, :] = right
+        lr_ref[p, :, 0:1, :] = left[:, None]
+        lr_ref[p, :, 1:2, :] = right[:, None]
 
     _reduce_blocks(nb, blk, emit, jnp.zeros((s_ref.shape[1], s_ref.shape[3]), F32))
 
@@ -279,10 +291,10 @@
     md = 1.0 + s * (gcl + gch)
     y, v, w, summ = cast_solve(flat(lo), flat(md), flat(hi), flat(explicit), ncl)
     recv = lax.all_to_all(summ.reshape(nc, nt // nc, 8, nwl), "cast", 0, 0, tiled=True)
-    lr = pl.pallas_call(_cast_reduced_kernel, out_shape=jax.ShapeDtypeStruct(recv.shape, F32))(recv)
-    back = lax.all_to_all(lr, "cast", 0, 0, tiled=True).reshape(nt, 8, nwl)
+    lr_shape = recv.shape[:2] + (2, nwl)
+    lr = pl.pallas_call(_cast_reduced_kernel, out_shape=jax.ShapeDtypeStruct(lr_shape, F32))(recv)
+    back = lax.all_to_all(lr, "cast", 0, 0, tiled=True).reshape(nt, 2, nwl)
     y, v, w = (x.reshape(nt, ncl, nwl) for x in (y, v, w))
-    step_cast = y + v * back[:, 0:1] + w * back[:, 1:2]
 
     lines = nt * ncl
     nsub = 4
@@ -293,7 +305,7 @@
     lo = -gwl * sw[:, :, :-2]
     hi = -gwh * sw[:, :, 2:]
     md = 1.0 + s * (gwl + gwh)
-    y, v, w, summ = width_solve(wl(lo), wl(md), wl(hi), wl(step_cast), nsub)
+    y, v, w, summ = width_solve(y, v, w, back, wl(lo), wl(md), wl(hi), nsub)
     got = [summ] + [
         lax.ppermute(summ, "width", [(i, (i + q) % nw) for i in range(nw)]) for q in range(1, nw)
     ]
@@ -302,17 +314,12 @@
         out_shape=jax.ShapeDtypeStruct((nsub, 2) + summ.shape[2:], F32),
         in_specs=[SMEM_SPEC] + [pl.BlockSpec(memory_space=pltpu.VMEM)] * nw,
     )(wi.astype(jnp.int32).reshape(1), *got)
-    sub = (nsub, nwl // nsub) + y.shape[1:]
-    y, v, w = (x.reshape(sub) for x in (y, v, w))
-    step_width = y + v * lr[:, 0:1] + w * lr[:, 1:2]
-    step_width = step_width.reshape(nwl, nt, ncl).transpose(1, 2, 0)
-
     s_prev = jnp.concatenate([s[:1], s[:-1]], 0)
     s_next = jnp.concatenate([s[1:], s[-1:]], 0)
     lo = -gtl * s_prev
     hi = -gth * s_next
     md = 1.0 + s * (gtl + gth + rim)
-    return thick_solve(lo, md, hi, step_width, h)
+    return thick_solve(y, v, w, lr, lo, md, hi, h, nsub)
 
 
 def solution(mesh):

time: 92.1 us -> 85 us (0.923)
  blocking collectives: 25.4 us -> 0 us
  starting transfers between devices: 22.6 us -> 34.9 us
  waiting for transfers between devices: 10.5 us -> 21.6 us
  local copies, waits for them, and re-layouts: 12.7 us -> 7.89 us
    all_to_all x1 -> x0, blocking collectives: 25.4 us -> none  [shards(): lax.all_to_all(summ.reshape(nc, nt // nc, 8, nwl), 'cast', 0, 0, tiled=True)]
    all_to_all x1 -> x2, starting transfers between devices: 4.77 us -> 17 us  [the longest x1 12.2 us: shards(): lax.all_to_all(summ.reshape(nc, nt // nc, 8, nwl), 'cast', 0, 0, tiled=True)]
    all_to_all x1 -> x2, waiting for transfers between devices: 10.5 us -> 20.5 us  [the longest x1 13 us: shards(): lax.all_to_all(summ.reshape(nc, nt // nc, 8, nwl), 'cast', 0, 0, tiled=True)]
    mul x7 -> x0, local copies, waits for them, and re-layouts: 3.14 us -> none  [shards(): step_width = y + v * lr[:, 0:1] + w * lr[:, 1:2]]
    mul x1 -> x0, other arithmetic: 1.29 us -> none  [shards(): hi = -gwh * sw[:, :, 2:]]
    reshape x1 -> x2, other arithmetic: 1.15 us -> 2.43 us  [flat(): return x.reshape(nt * ncl, nwl)]
    ppermute x3, waiting for transfers between devices: 0.01 us -> 1.05 us  [shards(): lax.ppermute(summ, 'width', [(i, (i + q) % nw) for i in range(nw)])]
    reshape x4 -> x3, local copies, waits for them, and re-layouts: 3.35 us -> 2.53 us  [wl(): return jnp.transpose(x, (2, 0, 1)).reshape(nwl, lines // 128, 128)]
  transfers between devices with their start and end apart: 8 -> 9, of which waited for: 1 -> 4; matrix products, arithmetic and copies ran while one was open for 8% -> 8% of each run, Pallas kernels for 2% -> 2%
where the time goes in v4:
time: 85 us; the launch traced here: 84.1 us
  starting transfers between devices  34.9 us (41%)
  waiting for transfers between devices  21.6 us (25%)
  Pallas kernels  14.9 us (18%)
  local copies, waits for them, and re-layouts  7.89 us (9%)
  other arithmetic  4.62 us (5%)
    all_to_all x1, waiting for transfers between devices, shards(): lax.all_to_all(summ.reshape(nc, nt // nc, 8, nwl), 'cast', 0, 0, tiled=True)  13 us
    all_to_all x1, starting transfers between devices, shards(): lax.all_to_all(summ.reshape(nc, nt // nc, 8, nwl), 'cast', 0, 0, tiled=True)  12.2 us
    all_to_all x1, waiting for transfers between devices, shards(): back = lax.all_to_all(lr, 'cast', 0, 0, tiled=True).reshape(nt, 2, nwl)  7.46 us
    ppermute x1, starting transfers between devices, shards(): lax.ppermute(h[:, 0, :], 'cast', [(b, a) for a, b in up_c])[:, None, :]  5.01 us
    ppermute x3, starting transfers between devices, shards(): lax.ppermute(summ, 'width', [(i, (i + q) % nw) for i in range(nw)])  4.99 us
    all_to_all x1, starting transfers between devices, shards(): back = lax.all_to_all(lr, 'cast', 0, 0, tiled=True).reshape(nt, 2, nwl)  4.77 us
    ppermute x1, starting transfers between devices, shards(): h_wl = lax.ppermute(h[:, :, -1], 'width', up_w)[:, :, None]  4.65 us
    pallas_call x1, Pallas kernels, width_solve(): pl.pallas_call(functools.partial(_width_kernel, nsub), out_shape=[shp, sh...  3.36 us
  transfers between devices with their start and end apart: 9, of which 4 were waited for; matrix products, arithmetic and copies ran while one was open for 8% of the time, Pallas kernels for 2%

profile of v4, /device:TPU:1, one launch (start us, length us, event | category | flops | bytes accessed | tf_op | source)
XLA Modules:
  0.0 84.1 jit_solution(15928102183588138203)
XLA Ops:
  0.0 1.2 %fusion.43 = (f32[64,8,1]{2,1,0:T(8,128)S(1)}, f32[64,8,1]{2,1,0:T(8,128)S(1)}) fusion(f32[64,8,128]{2,1,0:T(8,128)} %h_ref.1), kind=kLoop, calls=%fused_computation.84 | loop fusion | bytes 8192 | tf_op jit(solution)/shard_map/slice | solution.py:242
  1.3 1.3 %collective-permute-start.2 = (f32[64,8]{0,1:T(8,128)S(1)}, f32[64,8]{0,1:T(8,128)S(1)}, u32[]{:S(2)}, u32[]{:S(2)}) collective-permute-start(f32[64,8]{0,1:T(8,128)S(1)} %bitcast.86), channel_id=1, source_target_pairs={{1,0},{2,1},{3,2},{5,4},{6,5},{7,6},{9,8},{10,9},{11,10},{13,12},{... | collective-permute-start | bytes 6152 | tf_op jit(solution)/shard_map/ppermute | solution.py:242
  2.8 4.7 %collective-permute-start.3 = (f32[64,8]{0,1:T(8,128)S(1)}, f32[64,8]{0,1:T(8,128)S(1)}, u32[]{:S(2)}, u32[]{:S(2)}) collective-permute-start(f32[64,8]{0,1:T(8,128)S(1)} %bitcast.85), channel_id=1, source_target_pairs={{0,1},{1,2},{2,3},{4,5},{5,6},{6,7},{8,9},{9,10},{10,11},{12,13},{... | collective-permute-start | bytes 6152 | tf_op jit(solution)/shard_map/ppermute | solution.py:241
  7.5 5.0 %collective-permute-start = (f32[64,128]{1,0:T(8,128)S(1)}, f32[64,128]{1,0:T(8,128)S(1)}, u32[]{:S(2)}, u32[]{:S(2)}) collective-permute-start(f32[64,128]{1,0:T(8,128)S(1)} %bitcast.83), channel_id=1, source_target_pairs={{4,0},{8,4},{12,8},{16,12},{20,16},{24,20},{28,24},{32,28},{36,32}... | collective-permute-start | bytes 98312 | tf_op jit(solution)/shard_map/ppermute | solution.py:240
  12.5 1.9 %collective-permute-start.1 = (f32[64,128]{1,0:T(8,128)S(1)}, f32[64,128]{1,0:T(8,128)S(1)}, u32[]{:S(2)}, u32[]{:S(2)}) collective-permute-start(f32[64,128]{1,0:T(8,128)S(1)} %bitcast.82), channel_id=1, source_target_pairs={{0,4},{4,8},{8,12},{12,16},{16,20},{20,24},{24,28},{28,32},{32,36}... | collective-permute-start | bytes 98312 | tf_op jit(solution)/shard_map/ppermute | solution.py:239
  14.6 1.4 %shard_map.37 = f32[16,128]{1,0:T(8,128)} custom-call(s32[16,128]{1,0:T(8,128)} %bitcast.84, f32[10]{0:T(128)} %sp_ref.1), custom_call_target="tpu_custom_call" | custom-call | tf_op jit(solution)/shard_map/pallas_call | solution.py:244
  16.0 0.7 slice_bitcast_fusion.1
  16.8 0.8 fusion.26
  17.7 0.2 copy.154
  18.1 0.2 fusion.1
  19.2 1.3 %fusion.20 = (f32[512,128]{1,0:T(8,128)}, f32[512,128]{1,0:T(8,128)}, f32[512,128]{1,0:T(8,128)}, f32[64,8,128]{2,1,0:T(8,128)S(1)}, f32[64,8,128]{2,1,0:T(8,128...) fusion(f32[64,1,128]{2,1,0:T(1,128)S(1)} %bitcast.78, f32[64,8,128]{2,1,0:T(8,128)S(1)} %get-tuple-element.84, ...), kind=kLoop, calls=%fused_computation.31 | loop fusion | flops 1441792 | bytes 3477504 | tf_op jit(solution)/shard_map/reshape | solution.py:287
  20.5 1.2 %fusion.10.d_ref = f32[512,128]{1,0:T(8,128)} fusion(f32[64,8,128]{2,1,0:T(8,128)S(1)} %get-tuple-element.78, f32[64,8,1]{2,1,0:T(8,128)S(1)} %copy.158, f32[64,8,1]{2,1,0:T(8,128)S(1)} %copy.157, f32[64,1,128]{2,1,0:T(1,128)S(1)} %bitcast.77, f32[64,1,128]{2,1,0:T(1,128)S(1)} %bitcast.76, f32[1,8,128]{2,1,0:T(8,128)S(1)} %get-tuple-element.102, ...), kind=kLoop, calls=%fused_computation.17 | loop fusion | flops 1835008 | bytes 2433280 | tf_op jit(solution)/shard_map/reshape | solution.py:287
  21.7 2.7 %shard_map.38 = (f32[512,128]{1,0:T(8,128)}, f32[512,128]{1,0:T(8,128)}, f32[512,128]{1,0:T(8,128)}, f32[512,128]{1,0:T(8,128)}) custom-call(f32[512,128]{1,0:T(8,128)} %get-tuple-element.72.a_ref, f32[512,128]{1,0:T(8,128)} %get-tuple-element.74.b_ref, f32[512,128]{1,0:T(8,128)} %get-tuple-element.71.c_ref, f32[512,128]{1,0:T(8,128)} %fusion.10.d_ref), custom_call_target="tpu_custom_call" | custom-call | tf_op jit(solution)/shard_map/pallas_call | solution.py:135
  24.4 12.2 %all-to-all-start = ((f32[64,1,8,128]{3,2,1,0:T(8,128)}), f32[64,1,8,128]{3,2,1,0:T(8,128)S(1)}, u32[]{:S(2)}, u32[]{:S(2)}) async-start(f32[64,1,8,128]{3,2,1,0:T(8,128)} %bitcast.75), calls=%async_computation | async-start | bytes 524288 | tf_op jit(solution)/shard_map/all_to_all | solution.py:293
  36.7 13.0 %all-to-all-done.s_ref = f32[64,1,8,128]{3,2,1,0:T(8,128)S(1)} async-done(((f32[64,1,8,128]{3,2,1,0:T(8,128)}), f32[64,1,8,128]{3,2,1,0:T(8,128)S(1)}, u32[]{:S(2)}, u32[]{:S(2)}) %all-to-all-start) | async-done | bytes 262176 | tf_op jit(solution)/shard_map/all_to_all | solution.py:293
  49.8 0.7 copy-done.1
  50.5 2.4 %shard_map.39 = f32[64,1,2,128]{3,2,1,0:T(2,128)} custom-call(f32[64,1,8,128]{3,2,1,0:T(8,128)} %copy-done.1), custom_call_target="tpu_custom_call" | custom-call | tf_op jit(solution)/shard_map/pallas_call | solution.py:295
  52.9 4.8 %all-to-all-start.1 = ((f32[64,1,2,128]{3,2,1,0:T(2,128)}), f32[64,1,2,128]{3,2,1,0:T(2,128)S(1)}, u32[]{:S(2)}, u32[]{:S(2)}) async-start(f32[64,1,2,128]{3,2,1,0:T(2,128)} %shard_map.39), calls=%async_computation.1 | async-start | bytes 131072 | tf_op jit(solution)/shard_map/all_to_all | solution.py:296
  57.7 0.8 copy.161.a_ref
  58.5 0.8 %copy.162.b_ref = f32[128,4,128]{2,1,0:T(4,128)} copy(f32[128,4,128]{0,2,1:T(8,128)S(1)} %bitcast.69) | data formatting | bytes 524288 | tf_op jit(solution)/shard_map/reshape | solution.py:303
  59.3 0.8 %copy.163.c_ref = f32[128,4,128]{2,1,0:T(4,128)} copy(f32[128,4,128]{0,2,1:T(8,128)S(1)} %bitcast.68) | data formatting | bytes 524288 | tf_op jit(solution)/shard_map/reshape | solution.py:303
  60.2 7.5 %all-to-all-done.1 = f32[64,1,2,128]{3,2,1,0:T(2,128)S(1)} async-done(((f32[64,1,2,128]{3,2,1,0:T(2,128)}), f32[64,1,2,128]{3,2,1,0:T(2,128)S(1)}, u32[]{:S(2)}, u32[]{:S(2)}) %all-to-all-start.1) | async-done | bytes 65568 | tf_op jit(solution)/shard_map/all_to_all | solution.py:296
  67.7 0.6 copy-done.2
  68.3 3.4 %shard_map.40 = (f32[128,4,128]{2,1,0:T(4,128)}, f32[128,4,128]{2,1,0:T(4,128)}, f32[128,4,128]{2,1,0:T(4,128)}, f32[4,6,4,128]{3,2,1,0:T(4,128)}) custom-call(f32[64,8,128]{2,1,0:T(8,128)} %bitcast.71, f32[64,8,128]{2,1,0:T(8,128)} %bitcast.72, f32[64,8,128]{2,1,0:T(8,128)} %bitcast.73, f32[64,2,128]{2,1,0:T(2,128)} %bitcast.74, ...), custom_call_target="tpu_custom_call" | custom-call | tf_op jit(solution)/shard_map/pallas_call | solution.py:144
  71.6 1.3 %collective-permute-start.4 = (f32[4,6,4,128]{3,2,1,0:T(4,128)}, f32[4,6,4,128]{3,2,1,0:T(4,128)S(1)}, u32[]{:S(2)}, u32[]{:S(2)}) collective-permute-start(f32[4,6,4,128]{3,2,1,0:T(4,128)} %get-tuple-element.68.refs_0_), channel_id=1, source_target_pairs={{0,1},{1,2},{2,3},{3,0},{4,5},{5,6},{6,7},{7,4},{8,9},{9,10},{10,1... | collective-permute-start | bytes 147464 | tf_op jit(solution)/shard_map/ppermute | solution.py:310
  72.9 1.7 %collective-permute-start.5 = (f32[4,6,4,128]{3,2,1,0:T(4,128)}, f32[4,6,4,128]{3,2,1,0:T(4,128)S(1)}, u32[]{:S(2)}, u32[]{:S(2)}) collective-permute-start(f32[4,6,4,128]{3,2,1,0:T(4,128)} %get-tuple-element.68.refs_0_), channel_id=1, source_target_pairs={{0,2},{1,3},{2,0},{3,1},{4,6},{5,7},{6,4},{7,5},{8,10},{9,11},{10,... | collective-permute-start | bytes 147464 | tf_op jit(solution)/shard_map/ppermute | solution.py:310
  74.6 2.0 %collective-permute-start.6 = (f32[4,6,4,128]{3,2,1,0:T(4,128)}, f32[4,6,4,128]{3,2,1,0:T(4,128)S(1)}, u32[]{:S(2)}, u32[]{:S(2)}) collective-permute-start(f32[4,6,4,128]{3,2,1,0:T(4,128)} %get-tuple-element.68.refs_0_), channel_id=1, source_target_pairs={{0,3},{1,0},{2,1},{3,2},{4,7},{5,4},{6,5},{7,6},{8,11},{9,8},{10,9... | collective-permute-start | bytes 147464 | tf_op jit(solution)/shard_map/ppermute | solution.py:310
  76.6 0.9 %maximum_multiply_fusion.1 = (f32[64,8,128]{2,1,0:T(8,128)}, f32[64,8,128]{2,1,0:T(8,128)}) fusion(f32[1,8,128]{2,1,0:T(8,128)S(1)} %get-tuple-element.81, f32[63,8,128]{2,1,0:T(8,128)S(1)} %get-tuple-element.79, f32[63,8,128]{2,1,0:T(8,128)S(1)} %fusion.30, f32[63,8,128]{2,1,0:T(8,128)S(1)} %get-tuple-element.80, f32[1,8,128]{2,1,0:T(8,128)S(1)} %get-tuple-element.82), kind=kLoop, calls=%fused_computation.46 | loop fusion | flops 393216 | bytes 1306624 | tf_op jit(solution)/shard_map/mul | solution.py:320
  77.6 0.9 %collective-permute-done.6.refs_3_ = f32[4,6,4,128]{3,2,1,0:T(4,128)S(1)} collective-permute-done((f32[4,6,4,128]{3,2,1,0:T(4,128)}, f32[4,6,4,128]{3,2,1,0:T(4,128)S(1)}, u32[]{:S(2)}, u32[]{:S(2)}) %collective-permute-start.6) | collective-permute-done | bytes 49184 | tf_op jit(solution)/shard_map/ppermute | solution.py:310
  78.5 0.6 copy-done.5
  79.1 1.7 %shard_map.41.lr_ref = f32[4,2,4,128]{3,2,1,0:T(4,128)} custom-call(s32[1]{0:T(128)} %bitcast.43.me_ref, f32[4,6,4,128]{3,2,1,0:T(4,128)} %get-tuple-element.68.refs_0_, f32[4,6,4,128]{3,2,1,0:T(4,128)} %copy-done.3, f32[4,6,4,128]{3,2,1,0:T(4,128)} %copy-done.4, f32[4,6,4,128]{3,2,1,0:T(4,128)} %copy-done.5), custom_call_target="tpu_custom_call" | custom-call | tf_op jit(solution)/shard_map/pallas_call | solution.py:312
  80.9 3.3 %shard_map.42 = f32[64,8,128]{2,1,0:T(8,128)} custom-call(f32[128,4,128]{2,1,0:T(4,128)} %get-tuple-element.65.yw_ref, f32[128,4,128]{2,1,0:T(4,128)} %get-tuple-element.66.vw_ref, f32[128,4,128]{2,1,0:T(4,128)} %get-tuple-element.67.ww_ref, f32[4,2,4,128]{3,2,1,0:T(4,128)} %shard_map.41.lr_ref, f32[64,8,128]{2,1,0:T(8,128)} %get-tuple-element.94.a_ref, ...), custom_call_target="tpu_custom_call" | custom-call | tf_op jit(solution)/shard_map/pallas_call | solution.py:152
  (42 shorter events, 1.8 us)
Async XLA Ops:
  1.2 6.3 %copy-start = (f32[64,8,128]{2,1,0:T(8,128)S(1)}, f32[64,8,128]{2,1,0:T(8,128)}, u32[]{:S(2)}) copy-start(f32[64,8,128]{2,1,0:T(8,128)} %h_ref.1) | copy-start | bytes 786436
  1.3 16.4 %collective-permute-start.2 = (f32[64,8]{0,1:T(8,128)S(1)}, f32[64,8]{0,1:T(8,128)S(1)}, u32[]{:S(2)}, u32[]{:S(2)}) collective-permute-start(f32[64,8]{0,1:T(8,128)S(1)} %bitcast.86), channel_id=1, source_target_pairs={{1,0},{2,1},{3,2},{5,4},{6,5},{7,6},{9,8},{10,9},{11,10},{13,12},{... | collective-permute-start | bytes 6152 | tf_op jit(solution)/shard_map/ppermute | solution.py:242
  2.8 15.1 %collective-permute-start.3 = (f32[64,8]{0,1:T(8,128)S(1)}, f32[64,8]{0,1:T(8,128)S(1)}, u32[]{:S(2)}, u32[]{:S(2)}) collective-permute-start(f32[64,8]{0,1:T(8,128)S(1)} %bitcast.85), channel_id=1, source_target_pairs={{0,1},{1,2},{2,3},{4,5},{5,6},{6,7},{8,9},{9,10},{10,11},{12,13},{... | collective-permute-start | bytes 6152 | tf_op jit(solution)/shard_map/ppermute | solution.py:241
  7.5 11.5 %collective-permute-start = (f32[64,128]{1,0:T(8,128)S(1)}, f32[64,128]{1,0:T(8,128)S(1)}, u32[]{:S(2)}, u32[]{:S(2)}) collective-permute-start(f32[64,128]{1,0:T(8,128)S(1)} %bitcast.83), channel_id=1, source_target_pairs={{4,0},{8,4},{12,8},{16,12},{20,16},{24,20},{28,24},{32,28},{36,32}... | collective-permute-start | bytes 98312 | tf_op jit(solution)/shard_map/ppermute | solution.py:240
  12.5 6.6 %collective-permute-start.1 = (f32[64,128]{1,0:T(8,128)S(1)}, f32[64,128]{1,0:T(8,128)S(1)}, u32[]{:S(2)}, u32[]{:S(2)}) collective-permute-start(f32[64,128]{1,0:T(8,128)S(1)} %bitcast.82), channel_id=1, source_target_pairs={{0,4},{4,8},{8,12},{12,16},{16,20},{20,24},{24,28},{28,32},{32,36}... | collective-permute-start | bytes 98312 | tf_op jit(solution)/shard_map/ppermute | solution.py:239
  24.4 25.3 %all-to-all-start = ((f32[64,1,8,128]{3,2,1,0:T(8,128)}), f32[64,1,8,128]{3,2,1,0:T(8,128)S(1)}, u32[]{:S(2)}, u32[]{:S(2)}) async-start(f32[64,1,8,128]{3,2,1,0:T(8,128)} %bitcast.75), calls=%async_computation | async-start | bytes 524288 | tf_op jit(solution)/shard_map/all_to_all | solution.py:293
  49.7 0.7 copy-start.1
  52.9 14.8 %all-to-all-start.1 = ((f32[64,1,2,128]{3,2,1,0:T(2,128)}), f32[64,1,2,128]{3,2,1,0:T(2,128)S(1)}, u32[]{:S(2)}, u32[]{:S(2)}) async-start(f32[64,1,2,128]{3,2,1,0:T(2,128)} %shard_map.39), calls=%async_computation.1 | async-start | bytes 131072 | tf_op jit(solution)/shard_map/all_to_all | solution.py:296
  67.7 0.6 copy-start.2
  71.6 5.8 %collective-permute-start.4 = (f32[4,6,4,128]{3,2,1,0:T(4,128)}, f32[4,6,4,128]{3,2,1,0:T(4,128)S(1)}, u32[]{:S(2)}, u32[]{:S(2)}) collective-permute-start(f32[4,6,4,128]{3,2,1,0:T(4,128)} %get-tuple-element.68.refs_0_), channel_id=1, source_target_pairs={{0,1},{1,2},{2,3},{3,0},{4,5},{5,6},{6,7},{7,4},{8,9},{9,10},{10,1... | collective-permute-start | bytes 147464 | tf_op jit(solution)/shard_map/ppermute | solution.py:310
  72.9 4.7 %collective-permute-start.5 = (f32[4,6,4,128]{3,2,1,0:T(4,128)}, f32[4,6,4,128]{3,2,1,0:T(4,128)S(1)}, u32[]{:S(2)}, u32[]{:S(2)}) collective-permute-start(f32[4,6,4,128]{3,2,1,0:T(4,128)} %get-tuple-element.68.refs_0_), channel_id=1, source_target_pairs={{0,2},{1,3},{2,0},{3,1},{4,6},{5,7},{6,4},{7,5},{8,10},{9,11},{10,... | collective-permute-start | bytes 147464 | tf_op jit(solution)/shard_map/ppermute | solution.py:310
  74.6 3.9 %collective-permute-start.6 = (f32[4,6,4,128]{3,2,1,0:T(4,128)}, f32[4,6,4,128]{3,2,1,0:T(4,128)S(1)}, u32[]{:S(2)}, u32[]{:S(2)}) collective-permute-start(f32[4,6,4,128]{3,2,1,0:T(4,128)} %get-tuple-element.68.refs_0_), channel_id=1, source_target_pairs={{0,3},{1,0},{2,1},{3,2},{4,7},{5,4},{6,5},{7,6},{8,11},{9,8},{10,9... | collective-permute-start | bytes 147464 | tf_op jit(solution)/shard_map/ppermute | solution.py:310
  77.5 1.1 %copy-start.3 = (f32[4,6,4,128]{3,2,1,0:T(4,128)}, f32[4,6,4,128]{3,2,1,0:T(4,128)S(1)}, u32[]{:S(2)}) copy-start(f32[4,6,4,128]{3,2,1,0:T(4,128)S(1)} %collective-permute-done.4.refs_1_) | copy-start | bytes 147460
  77.6 0.9 %copy-start.4 = (f32[4,6,4,128]{3,2,1,0:T(4,128)}, f32[4,6,4,128]{3,2,1,0:T(4,128)S(1)}, u32[]{:S(2)}) copy-start(f32[4,6,4,128]{3,2,1,0:T(4,128)S(1)} %collective-permute-done.5.refs_2_) | copy-start | bytes 147460
  78.5 0.6 copy-start.5

commit v5 on v4

--- a/solution.py
+++ b/solution.py
@@ -114,8 +114,8 @@
             sm_ref[q, k] = val
 
 
-def _thick_kernel(nsub, yw_ref, vw_ref, ww_ref, lr_ref, a_ref, b_ref, c_ref, h_ref,
-                  o_ref, sw_ref, d_ref, y_ref, cp_ref):
+def _thick_kernel(nsub, tsub, yw_ref, vw_ref, ww_ref, lr_ref, a_ref, b_ref, c_ref, h_ref,
+                  o_ref, sw_ref, d_ref, y_ref, v_ref, w_ref, cp_ref):
     m = yw_ref.shape[0] // nsub
     for q in range(nsub):
         sl = slice(q * m, (q + 1) * m)
@@ -124,9 +124,21 @@
     per_q = 128 // ncl
     for q in range(sw_ref.shape[1]):
         d_ref[q * per_q : (q + 1) * per_q] = sw_ref[:, q, :].T.reshape(per_q, ncl, nwl)
+    n = nt // tsub
+    subs = [q * n for q in range(tsub)]
     shape = a_ref.shape[1:]
-    _sweep(nt, [0], _lead_ld, _lead_st, a_ref, b_ref, c_ref, d_ref, y_ref, None, None, cp_ref, 8, shape)
-    o_ref[...] = h_ref[...] + y_ref[...]
+    _sweep(n, subs, _lead_ld, _lead_st, a_ref, b_ref, c_ref, d_ref, y_ref, v_ref, w_ref, cp_ref, 4, shape)
+    sums = [tuple(_summary_rows(_lead_ld, s0, n, y_ref, v_ref, w_ref)) for s0 in subs]
+    lrs = [None] * tsub
+
+    def emit(p, left, right):
+        lrs[p] = (left, right)
+
+    _reduce_blocks(tsub, lambda p: sums[p], emit, jnp.zeros(shape, F32))
+    for q, s0 in enumerate(subs):
+        sl = slice(s0, s0 + n)
+        left, right = lrs[q]
+        o_ref[sl] = h_ref[sl] + (y_ref[sl] + v_ref[sl] * left + w_ref[sl] * right)
 
 
 def cast_solve(a, b, c, d, n):
@@ -148,11 +160,11 @@
     )(yc, vc, wc, bk, a, b, c)
 
 
-def thick_solve(yw, vw, ww, lr, a, b, c, h, nsub):
+def thick_solve(yw, vw, ww, lr, a, b, c, h, nsub, tsub):
     return pl.pallas_call(
-        functools.partial(_thick_kernel, nsub),
+        functools.partial(_thick_kernel, nsub, tsub),
         out_shape=jax.ShapeDtypeStruct(a.shape, F32),
-        scratch_shapes=[pltpu.VMEM(yw.shape, F32)] + [pltpu.VMEM(a.shape, F32)] * 3,
+        scratch_shapes=[pltpu.VMEM(yw.shape, F32)] + [pltpu.VMEM(a.shape, F32)] * 5,
     )(yw, vw, ww, lr, a, b, c, h)
 
 
@@ -319,7 +331,7 @@
     lo = -gtl * s_prev
     hi = -gth * s_next
     md = 1.0 + s * (gtl + gth + rim)
-    return thick_solve(y, v, w, lr, lo, md, hi, h, nsub)
+    return thick_solve(y, v, w, lr, lo, md, hi, h, nsub, 4)
 
 
 def solution(mesh):

time: 85 us -> 84.7 us (level)
  no operation moved by 1% of the time
where the time goes in v5:
time: 84.7 us; the launch traced here: 83.8 us
  starting transfers between devices  34.9 us (41%)
  waiting for transfers between devices  21.6 us (26%)
  Pallas kernels  14.6 us (17%)
  local copies, waits for them, and re-layouts  7.89 us (9%)
  other arithmetic  4.62 us (5%)
    all_to_all x1, waiting for transfers between devices, shards(): lax.all_to_all(summ.reshape(nc, nt // nc, 8, nwl), 'cast', 0, 0, tiled=True)  13 us
    all_to_all x1, starting transfers between devices, shards(): lax.all_to_all(summ.reshape(nc, nt // nc, 8, nwl), 'cast', 0, 0, tiled=True)  12.2 us
    all_to_all x1, waiting for transfers between devices, shards(): back = lax.all_to_all(lr, 'cast', 0, 0, tiled=True).reshape(nt, 2, nwl)  7.46 us
    ppermute x1, starting transfers between devices, shards(): lax.ppermute(h[:, 0, :], 'cast', [(b, a) for a, b in up_c])[:, None, :]  5.01 us
    ppermute x3, starting transfers between devices, shards(): lax.ppermute(summ, 'width', [(i, (i + q) % nw) for i in range(nw)])  4.99 us
    all_to_all x1, starting transfers between devices, shards(): back = lax.all_to_all(lr, 'cast', 0, 0, tiled=True).reshape(nt, 2, nwl)  4.77 us
    ppermute x1, starting transfers between devices, shards(): h_wl = lax.ppermute(h[:, :, -1], 'width', up_w)[:, :, None]  4.65 us
    pallas_call x1, Pallas kernels, width_solve(): pl.pallas_call(functools.partial(_width_kernel, nsub), out_shape=[shp, sh...  3.36 us
  transfers between devices with their start and end apart: 9, of which 4 were waited for; matrix products, arithmetic and copies ran while one was open for 8% of the time, Pallas kernels for 2%

profile of v5, /device:TPU:1, one launch (start us, length us, event | category | flops | bytes accessed | tf_op | source)
XLA Modules:
  0.0 83.8 jit_solution(2390935509319680220)
XLA Ops:
  0.0 1.2 %fusion.43 = (f32[64,8,1]{2,1,0:T(8,128)S(1)}, f32[64,8,1]{2,1,0:T(8,128)S(1)}) fusion(f32[64,8,128]{2,1,0:T(8,128)} %h_ref.1), kind=kLoop, calls=%fused_computation.84 | loop fusion | bytes 8192 | tf_op jit(solution)/shard_map/slice | solution.py:254
  1.3 1.3 %collective-permute-start.2 = (f32[64,8]{0,1:T(8,128)S(1)}, f32[64,8]{0,1:T(8,128)S(1)}, u32[]{:S(2)}, u32[]{:S(2)}) collective-permute-start(f32[64,8]{0,1:T(8,128)S(1)} %bitcast.86), channel_id=1, source_target_pairs={{1,0},{2,1},{3,2},{5,4},{6,5},{7,6},{9,8},{10,9},{11,10},{13,12},{... | collective-permute-start | bytes 6152 | tf_op jit(solution)/shard_map/ppermute | solution.py:254
  2.8 4.7 %collective-permute-start.3 = (f32[64,8]{0,1:T(8,128)S(1)}, f32[64,8]{0,1:T(8,128)S(1)}, u32[]{:S(2)}, u32[]{:S(2)}) collective-permute-start(f32[64,8]{0,1:T(8,128)S(1)} %bitcast.85), channel_id=1, source_target_pairs={{0,1},{1,2},{2,3},{4,5},{5,6},{6,7},{8,9},{9,10},{10,11},{12,13},{... | collective-permute-start | bytes 6152 | tf_op jit(solution)/shard_map/ppermute | solution.py:253
  7.5 5.0 %collective-permute-start = (f32[64,128]{1,0:T(8,128)S(1)}, f32[64,128]{1,0:T(8,128)S(1)}, u32[]{:S(2)}, u32[]{:S(2)}) collective-permute-start(f32[64,128]{1,0:T(8,128)S(1)} %bitcast.83), channel_id=1, source_target_pairs={{4,0},{8,4},{12,8},{16,12},{20,16},{24,20},{28,24},{32,28},{36,32}... | collective-permute-start | bytes 98312 | tf_op jit(solution)/shard_map/ppermute | solution.py:252
  12.5 1.9 %collective-permute-start.1 = (f32[64,128]{1,0:T(8,128)S(1)}, f32[64,128]{1,0:T(8,128)S(1)}, u32[]{:S(2)}, u32[]{:S(2)}) collective-permute-start(f32[64,128]{1,0:T(8,128)S(1)} %bitcast.82), channel_id=1, source_target_pairs={{0,4},{4,8},{8,12},{12,16},{16,20},{20,24},{24,28},{28,32},{32,36}... | collective-permute-start | bytes 98312 | tf_op jit(solution)/shard_map/ppermute | solution.py:251
  14.6 1.4 %shard_map.37 = f32[16,128]{1,0:T(8,128)} custom-call(s32[16,128]{1,0:T(8,128)} %bitcast.84, f32[10]{0:T(128)} %sp_ref.1), custom_call_target="tpu_custom_call" | custom-call | tf_op jit(solution)/shard_map/pallas_call | solution.py:256
  16.0 0.7 slice_bitcast_fusion.1
  16.8 0.8 fusion.26
  17.7 0.2 copy.154
  18.1 0.2 fusion.1
  19.2 1.3 %fusion.20 = (f32[512,128]{1,0:T(8,128)}, f32[512,128]{1,0:T(8,128)}, f32[512,128]{1,0:T(8,128)}, f32[64,8,128]{2,1,0:T(8,128)S(1)}, f32[64,8,128]{2,1,0:T(8,128...) fusion(f32[64,1,128]{2,1,0:T(1,128)S(1)} %bitcast.78, f32[64,8,128]{2,1,0:T(8,128)S(1)} %get-tuple-element.84, ...), kind=kLoop, calls=%fused_computation.31 | loop fusion | flops 1441792 | bytes 3477504 | tf_op jit(solution)/shard_map/reshape | solution.py:299
  20.5 1.2 %fusion.10.d_ref = f32[512,128]{1,0:T(8,128)} fusion(f32[64,8,128]{2,1,0:T(8,128)S(1)} %get-tuple-element.78, f32[64,8,1]{2,1,0:T(8,128)S(1)} %copy.158, f32[64,8,1]{2,1,0:T(8,128)S(1)} %copy.157, f32[64,1,128]{2,1,0:T(1,128)S(1)} %bitcast.77, f32[64,1,128]{2,1,0:T(1,128)S(1)} %bitcast.76, f32[1,8,128]{2,1,0:T(8,128)S(1)} %get-tuple-element.102, ...), kind=kLoop, calls=%fused_computation.17 | loop fusion | flops 1835008 | bytes 2433280 | tf_op jit(solution)/shard_map/reshape | solution.py:299
  21.7 2.7 %shard_map.38 = (f32[512,128]{1,0:T(8,128)}, f32[512,128]{1,0:T(8,128)}, f32[512,128]{1,0:T(8,128)}, f32[512,128]{1,0:T(8,128)}) custom-call(f32[512,128]{1,0:T(8,128)} %get-tuple-element.72.a_ref, f32[512,128]{1,0:T(8,128)} %get-tuple-element.74.b_ref, f32[512,128]{1,0:T(8,128)} %get-tuple-element.71.c_ref, f32[512,128]{1,0:T(8,128)} %fusion.10.d_ref), custom_call_target="tpu_custom_call" | custom-call | tf_op jit(solution)/shard_map/pallas_call | solution.py:147
  24.4 12.2 %all-to-all-start = ((f32[64,1,8,128]{3,2,1,0:T(8,128)}), f32[64,1,8,128]{3,2,1,0:T(8,128)S(1)}, u32[]{:S(2)}, u32[]{:S(2)}) async-start(f32[64,1,8,128]{3,2,1,0:T(8,128)} %bitcast.75), calls=%async_computation | async-start | bytes 524288 | tf_op jit(solution)/shard_map/all_to_all | solution.py:305
  36.7 13.0 %all-to-all-done.s_ref = f32[64,1,8,128]{3,2,1,0:T(8,128)S(1)} async-done(((f32[64,1,8,128]{3,2,1,0:T(8,128)}), f32[64,1,8,128]{3,2,1,0:T(8,128)S(1)}, u32[]{:S(2)}, u32[]{:S(2)}) %all-to-all-start) | async-done | bytes 262176 | tf_op jit(solution)/shard_map/all_to_all | solution.py:305
  49.8 0.7 copy-done.1
  50.5 2.4 %shard_map.39 = f32[64,1,2,128]{3,2,1,0:T(2,128)} custom-call(f32[64,1,8,128]{3,2,1,0:T(8,128)} %copy-done.1), custom_call_target="tpu_custom_call" | custom-call | tf_op jit(solution)/shard_map/pallas_call | solution.py:307
  52.9 4.8 %all-to-all-start.1 = ((f32[64,1,2,128]{3,2,1,0:T(2,128)}), f32[64,1,2,128]{3,2,1,0:T(2,128)S(1)}, u32[]{:S(2)}, u32[]{:S(2)}) async-start(f32[64,1,2,128]{3,2,1,0:T(2,128)} %shard_map.39), calls=%async_computation.1 | async-start | bytes 131072 | tf_op jit(solution)/shard_map/all_to_all | solution.py:308
  57.7 0.8 copy.161.a_ref
  58.5 0.8 %copy.162.b_ref = f32[128,4,128]{2,1,0:T(4,128)} copy(f32[128,4,128]{0,2,1:T(8,128)S(1)} %bitcast.69) | data formatting | bytes 524288 | tf_op jit(solution)/shard_map/reshape | solution.py:315
  59.3 0.8 %copy.163.c_ref = f32[128,4,128]{2,1,0:T(4,128)} copy(f32[128,4,128]{0,2,1:T(8,128)S(1)} %bitcast.68) | data formatting | bytes 524288 | tf_op jit(solution)/shard_map/reshape | solution.py:315
  60.2 7.5 %all-to-all-done.1 = f32[64,1,2,128]{3,2,1,0:T(2,128)S(1)} async-done(((f32[64,1,2,128]{3,2,1,0:T(2,128)}), f32[64,1,2,128]{3,2,1,0:T(2,128)S(1)}, u32[]{:S(2)}, u32[]{:S(2)}) %all-to-all-start.1) | async-done | bytes 65568 | tf_op jit(solution)/shard_map/all_to_all | solution.py:308
  67.7 0.6 copy-done.2
  68.3 3.4 %shard_map.40 = (f32[128,4,128]{2,1,0:T(4,128)}, f32[128,4,128]{2,1,0:T(4,128)}, f32[128,4,128]{2,1,0:T(4,128)}, f32[4,6,4,128]{3,2,1,0:T(4,128)}) custom-call(f32[64,8,128]{2,1,0:T(8,128)} %bitcast.71, f32[64,8,128]{2,1,0:T(8,128)} %bitcast.72, f32[64,8,128]{2,1,0:T(8,128)} %bitcast.73, f32[64,2,128]{2,1,0:T(2,128)} %bitcast.74, ...), custom_call_target="tpu_custom_call" | custom-call | tf_op jit(solution)/shard_map/pallas_call | solution.py:156
  71.6 1.3 %collective-permute-start.4 = (f32[4,6,4,128]{3,2,1,0:T(4,128)}, f32[4,6,4,128]{3,2,1,0:T(4,128)S(1)}, u32[]{:S(2)}, u32[]{:S(2)}) collective-permute-start(f32[4,6,4,128]{3,2,1,0:T(4,128)} %get-tuple-element.68.refs_0_), channel_id=1, source_target_pairs={{0,1},{1,2},{2,3},{3,0},{4,5},{5,6},{6,7},{7,4},{8,9},{9,10},{10,1... | collective-permute-start | bytes 147464 | tf_op jit(solution)/shard_map/ppermute | solution.py:322
  72.9 1.7 %collective-permute-start.5 = (f32[4,6,4,128]{3,2,1,0:T(4,128)}, f32[4,6,4,128]{3,2,1,0:T(4,128)S(1)}, u32[]{:S(2)}, u32[]{:S(2)}) collective-permute-start(f32[4,6,4,128]{3,2,1,0:T(4,128)} %get-tuple-element.68.refs_0_), channel_id=1, source_target_pairs={{0,2},{1,3},{2,0},{3,1},{4,6},{5,7},{6,4},{7,5},{8,10},{9,11},{10,... | collective-permute-start | bytes 147464 | tf_op jit(solution)/shard_map/ppermute | solution.py:322
  74.6 2.0 %collective-permute-start.6 = (f32[4,6,4,128]{3,2,1,0:T(4,128)}, f32[4,6,4,128]{3,2,1,0:T(4,128)S(1)}, u32[]{:S(2)}, u32[]{:S(2)}) collective-permute-start(f32[4,6,4,128]{3,2,1,0:T(4,128)} %get-tuple-element.68.refs_0_), channel_id=1, source_target_pairs={{0,3},{1,0},{2,1},{3,2},{4,7},{5,4},{6,5},{7,6},{8,11},{9,8},{10,9... | collective-permute-start | bytes 147464 | tf_op jit(solution)/shard_map/ppermute | solution.py:322
  76.6 0.9 %maximum_multiply_fusion.1 = (f32[64,8,128]{2,1,0:T(8,128)}, f32[64,8,128]{2,1,0:T(8,128)}) fusion(f32[1,8,128]{2,1,0:T(8,128)S(1)} %get-tuple-element.81, f32[63,8,128]{2,1,0:T(8,128)S(1)} %get-tuple-element.79, f32[63,8,128]{2,1,0:T(8,128)S(1)} %fusion.30, f32[63,8,128]{2,1,0:T(8,128)S(1)} %get-tuple-element.80, f32[1,8,128]{2,1,0:T(8,128)S(1)} %get-tuple-element.82), kind=kLoop, calls=%fused_computation.46 | loop fusion | flops 393216 | bytes 1306624 | tf_op jit(solution)/shard_map/mul | solution.py:332
  77.6 0.9 %collective-permute-done.6.refs_3_ = f32[4,6,4,128]{3,2,1,0:T(4,128)S(1)} collective-permute-done((f32[4,6,4,128]{3,2,1,0:T(4,128)}, f32[4,6,4,128]{3,2,1,0:T(4,128)S(1)}, u32[]{:S(2)}, u32[]{:S(2)}) %collective-permute-start.6) | collective-permute-done | bytes 49184 | tf_op jit(solution)/shard_map/ppermute | solution.py:322
  78.5 0.6 copy-done.5
  79.1 1.7 %shard_map.41.lr_ref = f32[4,2,4,128]{3,2,1,0:T(4,128)} custom-call(s32[1]{0:T(128)} %bitcast.43.me_ref, f32[4,6,4,128]{3,2,1,0:T(4,128)} %get-tuple-element.68.refs_0_, f32[4,6,4,128]{3,2,1,0:T(4,128)} %copy-done.3, f32[4,6,4,128]{3,2,1,0:T(4,128)} %copy-done.4, f32[4,6,4,128]{3,2,1,0:T(4,128)} %copy-done.5), custom_call_target="tpu_custom_call" | custom-call | tf_op jit(solution)/shard_map/pallas_call | solution.py:324
  80.9 3.0 %shard_map.42 = f32[64,8,128]{2,1,0:T(8,128)} custom-call(f32[128,4,128]{2,1,0:T(4,128)} %get-tuple-element.65.yw_ref, f32[128,4,128]{2,1,0:T(4,128)} %get-tuple-element.66.vw_ref, f32[128,4,128]{2,1,0:T(4,128)} %get-tuple-element.67.ww_ref, f32[4,2,4,128]{3,2,1,0:T(4,128)} %shard_map.41.lr_ref, f32[64,8,128]{2,1,0:T(8,128)} %get-tuple-element.94.a_ref, ...), custom_call_target="tpu_custom_call" | custom-call | tf_op jit(solution)/shard_map/pallas_call | solution.py:164
  (42 shorter events, 1.8 us)
Async XLA Ops:
  1.2 6.3 %copy-start = (f32[64,8,128]{2,1,0:T(8,128)S(1)}, f32[64,8,128]{2,1,0:T(8,128)}, u32[]{:S(2)}) copy-start(f32[64,8,128]{2,1,0:T(8,128)} %h_ref.1) | copy-start | bytes 786436
  1.3 16.4 %collective-permute-start.2 = (f32[64,8]{0,1:T(8,128)S(1)}, f32[64,8]{0,1:T(8,128)S(1)}, u32[]{:S(2)}, u32[]{:S(2)}) collective-permute-start(f32[64,8]{0,1:T(8,128)S(1)} %bitcast.86), channel_id=1, source_target_pairs={{1,0},{2,1},{3,2},{5,4},{6,5},{7,6},{9,8},{10,9},{11,10},{13,12},{... | collective-permute-start | bytes 6152 | tf_op jit(solution)/shard_map/ppermute | solution.py:254
  2.8 15.1 %collective-permute-start.3 = (f32[64,8]{0,1:T(8,128)S(1)}, f32[64,8]{0,1:T(8,128)S(1)}, u32[]{:S(2)}, u32[]{:S(2)}) collective-permute-start(f32[64,8]{0,1:T(8,128)S(1)} %bitcast.85), channel_id=1, source_target_pairs={{0,1},{1,2},{2,3},{4,5},{5,6},{6,7},{8,9},{9,10},{10,11},{12,13},{... | collective-permute-start | bytes 6152 | tf_op jit(solution)/shard_map/ppermute | solution.py:253
  7.5 11.5 %collective-permute-start = (f32[64,128]{1,0:T(8,128)S(1)}, f32[64,128]{1,0:T(8,128)S(1)}, u32[]{:S(2)}, u32[]{:S(2)}) collective-permute-start(f32[64,128]{1,0:T(8,128)S(1)} %bitcast.83), channel_id=1, source_target_pairs={{4,0},{8,4},{12,8},{16,12},{20,16},{24,20},{28,24},{32,28},{36,32}... | collective-permute-start | bytes 98312 | tf_op jit(solution)/shard_map/ppermute | solution.py:252
  12.5 6.6 %collective-permute-start.1 = (f32[64,128]{1,0:T(8,128)S(1)}, f32[64,128]{1,0:T(8,128)S(1)}, u32[]{:S(2)}, u32[]{:S(2)}) collective-permute-start(f32[64,128]{1,0:T(8,128)S(1)} %bitcast.82), channel_id=1, source_target_pairs={{0,4},{4,8},{8,12},{12,16},{16,20},{20,24},{24,28},{28,32},{32,36}... | collective-permute-start | bytes 98312 | tf_op jit(solution)/shard_map/ppermute | solution.py:251
  24.4 25.3 %all-to-all-start = ((f32[64,1,8,128]{3,2,1,0:T(8,128)}), f32[64,1,8,128]{3,2,1,0:T(8,128)S(1)}, u32[]{:S(2)}, u32[]{:S(2)}) async-start(f32[64,1,8,128]{3,2,1,0:T(8,128)} %bitcast.75), calls=%async_computation | async-start | bytes 524288 | tf_op jit(solution)/shard_map/all_to_all | solution.py:305
  49.7 0.7 copy-start.1
  52.9 14.8 %all-to-all-start.1 = ((f32[64,1,2,128]{3,2,1,0:T(2,128)}), f32[64,1,2,128]{3,2,1,0:T(2,128)S(1)}, u32[]{:S(2)}, u32[]{:S(2)}) async-start(f32[64,1,2,128]{3,2,1,0:T(2,128)} %shard_map.39), calls=%async_computation.1 | async-start | bytes 131072 | tf_op jit(solution)/shard_map/all_to_all | solution.py:308
  67.7 0.6 copy-start.2
  71.6 5.8 %collective-permute-start.4 = (f32[4,6,4,128]{3,2,1,0:T(4,128)}, f32[4,6,4,128]{3,2,1,0:T(4,128)S(1)}, u32[]{:S(2)}, u32[]{:S(2)}) collective-permute-start(f32[4,6,4,128]{3,2,1,0:T(4,128)} %get-tuple-element.68.refs_0_), channel_id=1, source_target_pairs={{0,1},{1,2},{2,3},{3,0},{4,5},{5,6},{6,7},{7,4},{8,9},{9,10},{10,1... | collective-permute-start | bytes 147464 | tf_op jit(solution)/shard_map/ppermute | solution.py:322
  72.9 4.7 %collective-permute-start.5 = (f32[4,6,4,128]{3,2,1,0:T(4,128)}, f32[4,6,4,128]{3,2,1,0:T(4,128)S(1)}, u32[]{:S(2)}, u32[]{:S(2)}) collective-permute-start(f32[4,6,4,128]{3,2,1,0:T(4,128)} %get-tuple-element.68.refs_0_), channel_id=1, source_target_pairs={{0,2},{1,3},{2,0},{3,1},{4,6},{5,7},{6,4},{7,5},{8,10},{9,11},{10,... | collective-permute-start | bytes 147464 | tf_op jit(solution)/shard_map/ppermute | solution.py:322
  74.6 3.9 %collective-permute-start.6 = (f32[4,6,4,128]{3,2,1,0:T(4,128)}, f32[4,6,4,128]{3,2,1,0:T(4,128)S(1)}, u32[]{:S(2)}, u32[]{:S(2)}) collective-permute-start(f32[4,6,4,128]{3,2,1,0:T(4,128)} %get-tuple-element.68.refs_0_), channel_id=1, source_target_pairs={{0,3},{1,0},{2,1},{3,2},{4,7},{5,4},{6,5},{7,6},{8,11},{9,8},{10,9... | collective-permute-start | bytes 147464 | tf_op jit(solution)/shard_map/ppermute | solution.py:322
  77.5 1.1 %copy-start.3 = (f32[4,6,4,128]{3,2,1,0:T(4,128)}, f32[4,6,4,128]{3,2,1,0:T(4,128)S(1)}, u32[]{:S(2)}) copy-start(f32[4,6,4,128]{3,2,1,0:T(4,128)S(1)} %collective-permute-done.4.refs_1_) | copy-start | bytes 147460
  77.6 0.9 %copy-start.4 = (f32[4,6,4,128]{3,2,1,0:T(4,128)}, f32[4,6,4,128]{3,2,1,0:T(4,128)S(1)}, u32[]{:S(2)}) copy-start(f32[4,6,4,128]{3,2,1,0:T(4,128)S(1)} %collective-permute-done.5.refs_2_) | copy-start | bytes 147460
  78.5 0.6 copy-start.5

commit v6 on v5

--- a/solution.py
+++ b/solution.py
@@ -96,6 +96,113 @@
 
 def _lead_st(ref, i, val):
     ref[i] = val
+
+
+def _prep_kernel(n, h_ref, hcl_ref, hch_ref, hwl_ref, hwh_ref, z_ref, sp_ref, fl_ref,
+                 y_ref, v_ref, w_ref, sm_ref, wa_ref, wb_ref, wc_ref, ta_ref, tb_ref, tc_ref,
+                 tp_ref, kp_ref, sp2_ref, a_ref, b_ref, c_ref, d_ref, cp_ref):
+    rows, nwl = h_ref.shape
+    nt = rows // n
+    hot, cond, slope = medium_parameters(h_ref[...])
+    zpad = jnp.zeros((n, nwl), F32)
+    for ref, val in ((tp_ref, hot), (kp_ref, cond), (sp2_ref, slope)):
+        ref[0:n] = zpad
+        ref[n : n + rows] = val
+        ref[n + rows : 2 * n + rows] = zpad
+
+    def row(ref, off):
+        return ref[pl.ds(off, nt, stride=n), :]
+
+    lane = lax.broadcasted_iota(jnp.int32, (nt, nwl), 1)
+    tix = lax.broadcasted_iota(jnp.int32, (nt, nwl), 0)
+    cast_lo = medium_parameters(hcl_ref[...])
+    cast_hi = medium_parameters(hch_ref[...])
+    g_c = n * n * 4.0 * 0.5
+    g_w = nwl * nwl / 4.0 * 0.5
+    g_t = nt * nt / 4.0 * 0.5
+    edge_wl = jnp.where(lane == 0, fl_ref[2], 1.0)
+    edge_wh = jnp.where(lane == nwl - 1, fl_ref[3], 1.0)
+    nz = sp_ref.shape[0]
+
+    def surf_row(zr):
+        acc = jnp.zeros(zr.shape, F32)
+        for q in range(nz):
+            acc = jnp.where(zr == q, sp_ref[q], acc)
+        return acc * (nt * nt / 8.0)
+
+    for c in range(n):
+        T0, k0, s0 = (row(r, n + c) for r in (tp_ref, kp_ref, sp2_ref))
+        if c == 0:
+            Tm, km, sm = cast_lo
+        else:
+            Tm, km, sm = (row(r, n + c - 1) for r in (tp_ref, kp_ref, sp2_ref))
+        if c == n - 1:
+            Tq, kq, sq = cast_hi
+        else:
+            Tq, kq, sq = (row(r, n + c + 1) for r in (tp_ref, kp_ref, sp2_ref))
+        Ttm, ktm, stm = (row(r, c) for r in (tp_ref, kp_ref, sp2_ref))
+        Ttp, ktp, stp = (row(r, 2 * n + c) for r in (tp_ref, kp_ref, sp2_ref))
+        wlo = medium_parameters(hwl_ref[c])
+        whi = medium_parameters(hwh_ref[c])
+        Twm, kwm, swm = (jnp.where(lane == 0, b, pltpu.roll(f, 1, 1)) for f, b in zip((T0, k0, s0), wlo))
+        Twp, kwp, swp = (
+            jnp.where(lane == nwl - 1, b, pltpu.roll(f, nwl - 1, 1)) for f, b in zip((T0, k0, s0), whi)
+        )
+        gcl = g_c * (k0 + km)
+        if c == 0:
+            gcl = gcl * fl_ref[0]
+        gch = g_c * (kq + k0)
+        if c == n - 1:
+            gch = gch * fl_ref[1]
+        gwl = g_w * (k0 + kwm) * edge_wl
+        gwh = g_w * (kwp + k0) * edge_wh
+        gtl = jnp.where(tix == 0, 0.0, g_t * (k0 + ktm))
+        gth = jnp.where(tix == nt - 1, 0.0, g_t * (ktp + k0))
+        s_lo = surf_row(z_ref[c : c + 1, :])
+        s_hi = surf_row(z_ref[n + c : n + c + 1, :])
+        rim = jnp.where(tix == 0, s_lo, jnp.where(tix == nt - 1, s_hi, 0.0))
+        ex = rim * (quench_medium_hotness - T0)
+        ex = ex + (gch * (Tq - T0) - gcl * (T0 - Tm))
+        ex = ex + (gwh * (Twp - T0) - gwl * (T0 - Twm))
+        ex = ex + (gth * (Ttp - T0) - gtl * (T0 - Ttm))
+        sel = pl.ds(c, nt, stride=n)
+        a_ref[sel, :] = -gcl * sm
+        c_ref[sel, :] = -gch * sq
+        b_ref[sel, :] = 1.0 + s0 * (gcl + gch)
+        d_ref[sel, :] = ex
+        wa_ref[sel, :] = -gwl * swm
+        wc_ref[sel, :] = -gwh * swp
+        wb_ref[sel, :] = 1.0 + s0 * (gwl + gwh)
+        ta_ref[sel, :] = -gtl * stm
+        tc_ref[sel, :] = -gth * stp
+        tb_ref[sel, :] = 1.0 + s0 * (gtl + gth + rim)
+
+    def ld(ref, i):
+        return ref[pl.ds(i, nt, stride=n), :]
+
+    def st(ref, i, val):
+        ref[pl.ds(i, nt, stride=n), :] = val
+
+    shape = (nt, nwl)
+    _sweep(n, [0], ld, st, a_ref, b_ref, c_ref, d_ref, y_ref, v_ref, w_ref, cp_ref, True, shape)
+    rws = _summary_rows(ld, 0, n, y_ref, v_ref, w_ref)
+    rws += [jnp.zeros(shape, F32)] * (8 - len(rws))
+    for k, val in enumerate(rws):
+        sm_ref[pl.ds(k, nt, stride=8), :] = val
+
+
+def prep_solve(h2, hcl, hch, hwl, hwh, z2, spray, flags, n):
+    rows, nwl = h2.shape
+    nt = rows // n
+    shp = jax.ShapeDtypeStruct(h2.shape, F32)
+    vm = pl.BlockSpec(memory_space=pltpu.VMEM)
+    pad = pltpu.VMEM((rows + 2 * n, nwl), F32)
+    return pl.pallas_call(
+        functools.partial(_prep_kernel, n),
+        out_shape=[shp] * 3 + [jax.ShapeDtypeStruct((nt * 8, nwl), F32)] + [shp] * 6,
+        in_specs=[vm] * 6 + [SMEM_SPEC, SMEM_SPEC],
+        scratch_shapes=[pad, pad, pad] + [pltpu.VMEM(h2.shape, F32)] * 5,
+    )(h2, hcl, hch, hwl, hwh, z2, spray, flags)
 
 
 def _width_kernel(nsub, yc_ref, vc_ref, wc_ref, bk_ref, a_ref, b_ref, c_ref,
@@ -248,60 +355,23 @@
     ci, wi = lax.axis_index("cast"), lax.axis_index("width")
     up_c = [(i, i + 1) for i in range(nc - 1)]
     up_w = [(i, i + 1) for i in range(nw - 1)]
-    h_cl = lax.ppermute(h[:, -1, :], "cast", up_c)[:, None, :]
-    h_ch = lax.ppermute(h[:, 0, :], "cast", [(b, a) for a, b in up_c])[:, None, :]
+    h_cl = lax.ppermute(h[:, -1, :], "cast", up_c)
+    h_ch = lax.ppermute(h[:, 0, :], "cast", [(b, a) for a, b in up_c])
     h_wl = lax.ppermute(h[:, :, -1], "width", up_w)[:, :, None]
     h_wh = lax.ppermute(h[:, :, 0], "width", [(b, a) for a, b in up_w])[:, :, None]
-
-    surf = pl.pallas_call(
-        functools.partial(_surface_kernel, nt * nt / 8.0),
-        out_shape=jax.ShapeDtypeStruct((2 * ncl, nwl), F32),
-        in_specs=[pl.BlockSpec(memory_space=pltpu.VMEM), SMEM_SPEC],
-    )(zones.reshape(2 * ncl, nwl), spray_coef).reshape(2, ncl, nwl)
-
-    T, k, s = medium_parameters(h)
-    T_cl, k_cl, s_cl = medium_parameters(h_cl)
-    T_ch, k_ch, s_ch = medium_parameters(h_ch)
-    T_wl, k_wl, s_wl = medium_parameters(h_wl)
-    T_wh, k_wh, s_wh = medium_parameters(h_wh)
 
     cast_low = (ci > 0).astype(F32)
     cast_high = (ci < nc - 1).astype(F32)
     width_low = (wi > 0).astype(F32)
     width_high = (wi < nw - 1).astype(F32)
-
-    kc = jnp.concatenate([k_cl, k, k_ch], 1)
-    Tc = jnp.concatenate([T_cl, T, T_ch], 1)
-    sc = jnp.concatenate([s_cl, s, s_ch], 1)
-    edge_c = jnp.ones((ncl + 1,), F32).at[0].set(cast_low).at[-1].set(cast_high)
-    fc = (ncl * ncl * 4.0) * 0.5 * (kc[:, 1:] + kc[:, :-1]) * edge_c[None, :, None]
-    gcl, gch = fc[:, :-1], fc[:, 1:]
-    kw = jnp.concatenate([k_wl, k, k_wh], 2)
-    Tw = jnp.concatenate([T_wl, T, T_wh], 2)
-    sw = jnp.concatenate([s_wl, s, s_wh], 2)
-    edge_w = jnp.ones((nwl + 1,), F32).at[0].set(width_low).at[-1].set(width_high)
-    fw = (nwl * nwl / 4.0) * 0.5 * (kw[:, :, 1:] + kw[:, :, :-1]) * edge_w[None, None, :]
-    gwl, gwh = fw[:, :, :-1], fw[:, :, 1:]
-    mid = (nt * nt / 4.0) * 0.5 * (k[1:] + k[:-1])
-    zf = jnp.zeros((1, ncl, nwl), F32)
-    gtl = jnp.concatenate([zf, mid], 0)
-    gth = jnp.concatenate([mid, zf], 0)
-    rim = jnp.concatenate([surf[0:1], jnp.zeros((nt - 2, ncl, nwl), F32), surf[1:2]], 0)
-
-    T_prev = jnp.concatenate([T[:1], T[:-1]], 0)
-    T_next = jnp.concatenate([T[1:], T[-1:]], 0)
-    explicit = rim * (quench_medium_hotness - T)
-    explicit = explicit + (gch * (Tc[:, 2:] - T) - gcl * (T - Tc[:, :-2]))
-    explicit = explicit + (gwh * (Tw[:, :, 2:] - T) - gwl * (T - Tw[:, :, :-2]))
-    explicit = explicit + (gth * (T_next - T) - gtl * (T - T_prev))
-
-    def flat(x):
-        return x.reshape(nt * ncl, nwl)
-
-    lo = -gcl * sc[:, :-2]
-    hi = -gch * sc[:, 2:]
-    md = 1.0 + s * (gcl + gch)
-    y, v, w, summ = cast_solve(flat(lo), flat(md), flat(hi), flat(explicit), ncl)
+    flags = jnp.stack([cast_low, cast_high, width_low, width_high])
+    outs = prep_solve(
+        h.reshape(nt * ncl, nwl), h_cl, h_ch,
+        jnp.transpose(h_wl, (1, 0, 2)), jnp.transpose(h_wh, (1, 0, 2)),
+        zones.reshape(2 * ncl, nwl), spray_coef, flags, ncl,
+    )
+    y, v, w, summ = outs[:4]
+    wlo, wmd, whi, tlo, tmd, thi = (x.reshape(nt, ncl, nwl) for x in outs[4:])
     recv = lax.all_to_all(summ.reshape(nc, nt // nc, 8, nwl), "cast", 0, 0, tiled=True)
     lr_shape = recv.shape[:2] + (2, nwl)
     lr = pl.pallas_call(_cast_reduced_kernel, out_shape=jax.ShapeDtypeStruct(lr_shape, F32))(recv)
@@ -314,10 +384,7 @@
     def wl(x):
         return jnp.transpose(x, (2, 0, 1)).reshape(nwl, lines // 128, 128)
 
-    lo = -gwl * sw[:, :, :-2]
-    hi = -gwh * sw[:, :, 2:]
-    md = 1.0 + s * (gwl + gwh)
-    y, v, w, summ = width_solve(y, v, w, back, wl(lo), wl(md), wl(hi), nsub)
+    y, v, w, summ = width_solve(y, v, w, back, wl(wlo), wl(wmd), wl(whi), nsub)
     got = [summ] + [
         lax.ppermute(summ, "width", [(i, (i + q) % nw) for i in range(nw)]) for q in range(1, nw)
     ]
@@ -326,12 +393,7 @@
         out_shape=jax.ShapeDtypeStruct((nsub, 2) + summ.shape[2:], F32),
         in_specs=[SMEM_SPEC] + [pl.BlockSpec(memory_space=pltpu.VMEM)] * nw,
     )(wi.astype(jnp.int32).reshape(1), *got)
-    s_prev = jnp.concatenate([s[:1], s[:-1]], 0)
-    s_next = jnp.concatenate([s[1:], s[-1:]], 0)
-    lo = -gtl * s_prev
-    hi = -gth * s_next
-    md = 1.0 + s * (gtl + gth + rim)
-    return thick_solve(y, v, w, lr, lo, md, hi, h, nsub, 4)
+    return thick_solve(y, v, w, lr, tlo, tmd, thi, h, nsub, 4)
 
 
 def solution(mesh):

time: 84.7 us -> 86.1 us (1.017)
  blocking collectives: 0 us -> 27.6 us
  starting transfers between devices: 34.9 us -> 19.2 us
  waiting for transfers between devices: 21.6 us -> 13.8 us
  other arithmetic: 4.62 us -> 0.64 us
  local copies, waits for them, and re-layouts: 7.89 us -> 8.82 us
    all_to_all x0 -> x1, blocking collectives: none -> 27.6 us  [shards(): lax.all_to_all(summ.reshape(nc, nt // nc, 8, nwl), 'cast', 0, 0, tiled=True)]
    all_to_all x1 -> x0, waiting for transfers between devices: 13 us -> none  [shards(): lax.all_to_all(summ.reshape(nc, nt // nc, 8, nwl), 'cast', 0, 0, tiled=True)]
    all_to_all x1 -> x0, starting transfers between devices: 12.2 us -> none  [shards(): lax.all_to_all(summ.reshape(nc, nt // nc, 8, nwl), 'cast', 0, 0, tiled=True)]
    ppermute x3, waiting for transfers between devices: 1.05 us -> 4.1 us  [shards(): lax.ppermute(summ, 'width', [(i, (i + q) % nw) for i in range(nw)])]
    reshape x2 -> x0, other arithmetic: 2.43 us -> none  [flat(): return x.reshape(nt * ncl, nwl)]
    ppermute x1, waiting for transfers between devices: 0.01 us -> 2.4 us  [shards(): lax.ppermute(h[:, :, 0], 'width', [(b, a) for a, b in up_w])[:, :, None]]
    broadcast_in_dim x1 -> x2, local copies, waits for them, and re-layouts: 0.01 us -> 1.73 us  [the longest x1 0.87 us: shards(): lax.ppermute(h[:, :, 0], 'width', [(b, a) for a, b in up_w])[:, :, None]]
    ppermute x3, starting transfers between devices: 4.99 us -> 3.49 us  [shards(): lax.ppermute(summ, 'width', [(i, (i + q) % nw) for i in range(nw)])]
  transfers between devices with their start and end apart: 9 -> 8, of which waited for: 4 -> 4; matrix products, arithmetic and copies ran while one was open for 8% -> 7% of each run, Pallas kernels for 2% -> 0%
where the time goes in v6:
time: 86.1 us; the launch traced here: 85.5 us
  blocking collectives  27.6 us (32%)
  starting transfers between devices  19.2 us (22%)
  Pallas kernels  15.3 us (18%)
  waiting for transfers between devices  13.8 us (16%)
  local copies, waits for them, and re-layouts  8.82 us (10%)
    all_to_all x1, blocking collectives, shards(): lax.all_to_all(summ.reshape(nc, nt // nc, 8, nwl), 'cast', 0, 0, tiled=True)  27.6 us
    all_to_all x1, waiting for transfers between devices, shards(): back = lax.all_to_all(lr, 'cast', 0, 0, tiled=True).reshape(nt, 2, nwl)  7.33 us
    pallas_call x1, Pallas kernels, prep_solve(): pl.pallas_call(functools.partial(_prep_kernel, n), out_shape=[shp] * 3 +...  4.85 us
    all_to_all x1, starting transfers between devices, shards(): back = lax.all_to_all(lr, 'cast', 0, 0, tiled=True).reshape(nt, 2, nwl)  4.77 us
    ppermute x1, starting transfers between devices, shards(): h_cl = lax.ppermute(h[:, -1, :], 'cast', up_c)  4.5 us
    ppermute x3, waiting for transfers between devices, shards(): lax.ppermute(summ, 'width', [(i, (i + q) % nw) for i in range(nw)])  4.1 us
    ppermute x3, starting transfers between devices, shards(): lax.ppermute(summ, 'width', [(i, (i + q) % nw) for i in range(nw)])  3.49 us
    pallas_call x1, Pallas kernels, width_solve(): pl.pallas_call(functools.partial(_width_kernel, nsub), out_shape=[shp, sh...  3.34 us
  transfers between devices with their start and end apart: 8, of which 4 were waited for; matrix products, arithmetic and copies ran while one was open for 7% of the time, Pallas kernels for 0%

profile of v6, /device:TPU:1, one launch (start us, length us, event | category | flops | bytes accessed | tf_op | source)
XLA Modules:
  0.0 85.5 jit_solution(11942184203374588815)
XLA Ops:
  0.0 1.1 %fusion.1 = (f32[64,1,128]{2,1,0:T(1,128)S(1)}, f32[64,1,128]{2,1,0:T(1,128)S(1)}) fusion(f32[64,8,128]{2,1,0:T(8,128)} %h_ref.1), kind=kLoop, calls=%fused_computation.2 | loop fusion | bytes 131072 | tf_op jit(solution)/shard_map/slice | solution.py:359
  1.1 4.5 %collective-permute-start = (f32[64,128]{1,0:T(8,128)S(1)}, f32[64,128]{1,0:T(8,128)S(1)}, u32[]{:S(2)}, u32[]{:S(2)}) collective-permute-start(f32[64,128]{1,0:T(8,128)S(1)} %bitcast.57), channel_id=1, source_target_pairs={{0,4},{4,8},{8,12},{12,16},{16,20},{20,24},{24,28},{28,32},{32,36}... | collective-permute-start | bytes 98312 | tf_op jit(solution)/shard_map/ppermute | solution.py:358
  5.6 1.9 %collective-permute-start.1 = (f32[64,128]{1,0:T(8,128)S(1)}, f32[64,128]{1,0:T(8,128)S(1)}, u32[]{:S(2)}, u32[]{:S(2)}) collective-permute-start(f32[64,128]{1,0:T(8,128)S(1)} %bitcast.56), channel_id=1, source_target_pairs={{4,0},{8,4},{12,8},{16,12},{20,16},{24,20},{28,24},{32,28},{36,32}... | collective-permute-start | bytes 98312 | tf_op jit(solution)/shard_map/ppermute | solution.py:359
  7.5 1.2 %fusion = (f32[64,8,1]{2,1,0:T(8,128)S(1)}, f32[64,8,1]{2,1,0:T(8,128)S(1)}) fusion(f32[64,8,128]{2,1,0:T(8,128)} %h_ref.1), kind=kLoop, calls=%fused_computation.1 | loop fusion | bytes 8192 | tf_op jit(solution)/shard_map/slice | solution.py:361
  8.7 0.1 copy.33
  8.8 3.2 %collective-permute-start.2 = (f32[64,8]{0,1:T(8,128)S(1)}, f32[64,8]{0,1:T(8,128)S(1)}, u32[]{:S(2)}, u32[]{:S(2)}) collective-permute-start(f32[64,8]{0,1:T(8,128)S(1)} %bitcast.59), channel_id=1, source_target_pairs={{0,1},{1,2},{2,3},{4,5},{5,6},{6,7},{8,9},{9,10},{10,11},{12,13},{... | collective-permute-start | bytes 6152 | tf_op jit(solution)/shard_map/ppermute | solution.py:360
  12.0 0.1 copy.34
  12.2 1.3 %collective-permute-start.3 = (f32[64,8]{0,1:T(8,128)S(1)}, f32[64,8]{0,1:T(8,128)S(1)}, u32[]{:S(2)}, u32[]{:S(2)}) collective-permute-start(f32[64,8]{0,1:T(8,128)S(1)} %bitcast.61), channel_id=1, source_target_pairs={{1,0},{2,1},{3,2},{5,4},{6,5},{7,6},{9,8},{10,9},{11,10},{13,12},{... | collective-permute-start | bytes 6152 | tf_op jit(solution)/shard_map/ppermute | solution.py:361
  13.5 0.6 add_convert_fusion.fl_ref
  14.1 2.4 %collective-permute-done.3 = f32[64,8]{0,1:T(8,128)S(1)} collective-permute-done((f32[64,8]{0,1:T(8,128)S(1)}, f32[64,8]{0,1:T(8,128)S(1)}, u32[]{:S(2)}, u32[]{:S(2)}) %collective-permute-start.3) | collective-permute-done | bytes 2080 | tf_op jit(solution)/shard_map/ppermute | solution.py:361
  16.5 0.9 %copy.27 = f32[64,8,1]{2,0,1:T(8,128)} copy(f32[64,8,1]{0,1,2:T(8,128)S(1)} %bitcast.62) | data formatting | bytes 4096 | tf_op jit(solution)/shard_map/broadcast_in_dim | solution.py:361
  17.4 0.9 %copy.25 = f32[64,8,1]{2,0,1:T(8,128)} copy(f32[64,8,1]{0,1,2:T(8,128)S(1)} %bitcast.60) | data formatting | bytes 4096 | tf_op jit(solution)/shard_map/broadcast_in_dim | solution.py:360
  18.3 0.6 copy-done.7
  18.9 4.8 %shard_map.37 = (f32[512,128]{1,0:T(8,128)}, f32[512,128]{1,0:T(8,128)}, f32[512,128]{1,0:T(8,128)}, f32[512,128]{1,0:T(8,128)}, f32[512,128]{1,0:T(8,128)}, /*i...) custom-call(f32[512,128]{1,0:T(8,128)} %bitcast.42, ...), custom_call_target="tpu_custom_call" | custom-call | tf_op jit(solution)/shard_map/pallas_call | solution.py:200
  23.7 27.6 %all_to_all.10.s_ref = f32[64,1,8,128]{3,2,1,0:T(8,128)} all-to-all(f32[64,1,8,128]{3,2,1,0:T(8,128)} %bitcast.52), channel_id=1, replica_groups=mesh['cast'=64,'width'=4] {'cast'}, dimensions={0} | all-to-all | bytes 524288 | tf_op jit(solution)/shard_map/all_to_all | solution.py:375
  51.3 2.4 %shard_map.38 = f32[64,1,2,128]{3,2,1,0:T(2,128)} custom-call(f32[64,1,8,128]{3,2,1,0:T(8,128)} %all_to_all.10.s_ref), custom_call_target="tpu_custom_call" | custom-call | tf_op jit(solution)/shard_map/pallas_call | solution.py:377
  53.8 4.8 %all-to-all-start.1 = ((f32[64,1,2,128]{3,2,1,0:T(2,128)}), f32[64,1,2,128]{3,2,1,0:T(2,128)S(1)}, u32[]{:S(2)}, u32[]{:S(2)}) async-start(f32[64,1,2,128]{3,2,1,0:T(2,128)} %shard_map.38), calls=%async_computation.1 | async-start | bytes 131072 | tf_op jit(solution)/shard_map/all_to_all | solution.py:378
  58.6 0.8 copy.28.a_ref
  59.5 0.8 copy.29.b_ref
  60.4 0.1 copy-done.1
  60.5 0.8 copy.30.c_ref
  61.3 7.3 %all-to-all-done.1 = f32[64,1,2,128]{3,2,1,0:T(2,128)S(1)} async-done(((f32[64,1,2,128]{3,2,1,0:T(2,128)}), f32[64,1,2,128]{3,2,1,0:T(2,128)S(1)}, u32[]{:S(2)}, u32[]{:S(2)}) %all-to-all-start.1) | async-done | bytes 65568 | tf_op jit(solution)/shard_map/all_to_all | solution.py:378
  68.7 0.6 copy-done
  69.3 3.3 %shard_map.39 = (f32[128,4,128]{2,1,0:T(4,128)}, f32[128,4,128]{2,1,0:T(4,128)}, f32[128,4,128]{2,1,0:T(4,128)}, f32[4,6,4,128]{3,2,1,0:T(4,128)}) custom-call(f32[64,8,128]{2,1,0:T(8,128)} %bitcast.45, f32[64,8,128]{2,1,0:T(8,128)} %bitcast.46, f32[64,8,128]{2,1,0:T(8,128)} %bitcast.47, f32[64,2,128]{2,1,0:T(2,128)} %bitcast.48, ...), custom_call_target="tpu_custom_call" | custom-call | tf_op jit(solution)/shard_map/pallas_call | solution.py:263
  72.6 0.9 %collective-permute-start.6 = (f32[4,6,4,128]{3,2,1,0:T(4,128)}, f32[4,6,4,128]{3,2,1,0:T(4,128)S(1)}, u32[]{:S(2)}, u32[]{:S(2)}) collective-permute-start(f32[4,6,4,128]{3,2,1,0:T(4,128)} %get-tuple-element.29.refs_0_), channel_id=1, source_target_pairs={{0,3},{1,0},{2,1},{3,2},{4,7},{5,4},{6,5},{7,6},{8,11},{9,8},{10,9... | collective-permute-start | bytes 147464 | tf_op jit(solution)/shard_map/ppermute | solution.py:389
  73.5 2.2 %collective-permute-start.5 = (f32[4,6,4,128]{3,2,1,0:T(4,128)}, f32[4,6,4,128]{3,2,1,0:T(4,128)S(1)}, u32[]{:S(2)}, u32[]{:S(2)}) collective-permute-start(f32[4,6,4,128]{3,2,1,0:T(4,128)} %get-tuple-element.29.refs_0_), channel_id=1, source_target_pairs={{0,2},{1,3},{2,0},{3,1},{4,6},{5,7},{6,4},{7,5},{8,10},{9,11},{10,... | collective-permute-start | bytes 147464 | tf_op jit(solution)/shard_map/ppermute | solution.py:389
  75.7 0.4 collective-permute-start.4
  76.1 2.1 %collective-permute-done.5.refs_2_ = f32[4,6,4,128]{3,2,1,0:T(4,128)S(1)} collective-permute-done((f32[4,6,4,128]{3,2,1,0:T(4,128)}, f32[4,6,4,128]{3,2,1,0:T(4,128)S(1)}, u32[]{:S(2)}, u32[]{:S(2)}) %collective-permute-start.5) | collective-permute-done | bytes 49184 | tf_op jit(solution)/shard_map/ppermute | solution.py:389
  78.2 2.0 %collective-permute-done.4.refs_1_ = f32[4,6,4,128]{3,2,1,0:T(4,128)S(1)} collective-permute-done((f32[4,6,4,128]{3,2,1,0:T(4,128)}, f32[4,6,4,128]{3,2,1,0:T(4,128)S(1)}, u32[]{:S(2)}, u32[]{:S(2)}) %collective-permute-start.4) | collective-permute-done | bytes 49184 | tf_op jit(solution)/shard_map/ppermute | solution.py:389
  80.2 0.6 copy-done.6
  80.8 1.7 %shard_map.40.lr_ref = f32[4,2,4,128]{3,2,1,0:T(4,128)} custom-call(s32[1]{0:T(128)} %bitcast.28.me_ref, f32[4,6,4,128]{3,2,1,0:T(4,128)} %get-tuple-element.29.refs_0_, f32[4,6,4,128]{3,2,1,0:T(4,128)} %copy-done.6, f32[4,6,4,128]{3,2,1,0:T(4,128)} %copy-done.5, f32[4,6,4,128]{3,2,1,0:T(4,128)} %copy-done.4), custom_call_target="tpu_custom_call" | custom-call | tf_op jit(solution)/shard_map/pallas_call | solution.py:391
  82.5 3.0 %shard_map.41 = f32[64,8,128]{2,1,0:T(8,128)} custom-call(f32[128,4,128]{2,1,0:T(4,128)} %get-tuple-element.26.yw_ref, f32[128,4,128]{2,1,0:T(4,128)} %get-tuple-element.27.vw_ref, f32[128,4,128]{2,1,0:T(4,128)} %get-tuple-element.28.ww_ref, f32[4,2,4,128]{3,2,1,0:T(4,128)} %shard_map.40.lr_ref, f32[64,8,128]{2,1,0:T(8,128)} %bitcast.53, ...), custom_call_target="tpu_custom_call" | custom-call | tf_op jit(solution)/shard_map/pallas_call | solution.py:271
  (18 shorter events, 0.1 us)
Async XLA Ops:
  1.1 17.2 %collective-permute-start = (f32[64,128]{1,0:T(8,128)S(1)}, f32[64,128]{1,0:T(8,128)S(1)}, u32[]{:S(2)}, u32[]{:S(2)}) collective-permute-start(f32[64,128]{1,0:T(8,128)S(1)} %bitcast.57), channel_id=1, source_target_pairs={{0,4},{4,8},{8,12},{12,16},{16,20},{20,24},{24,28},{28,32},{32,36}... | collective-permute-start | bytes 98312 | tf_op jit(solution)/shard_map/ppermute | solution.py:358
  5.6 12.7 %collective-permute-start.1 = (f32[64,128]{1,0:T(8,128)S(1)}, f32[64,128]{1,0:T(8,128)S(1)}, u32[]{:S(2)}, u32[]{:S(2)}) collective-permute-start(f32[64,128]{1,0:T(8,128)S(1)} %bitcast.56), channel_id=1, source_target_pairs={{4,0},{8,4},{12,8},{16,12},{20,16},{24,20},{28,24},{32,28},{36,32}... | collective-permute-start | bytes 98312 | tf_op jit(solution)/shard_map/ppermute | solution.py:359
  8.8 8.6 %collective-permute-start.2 = (f32[64,8]{0,1:T(8,128)S(1)}, f32[64,8]{0,1:T(8,128)S(1)}, u32[]{:S(2)}, u32[]{:S(2)}) collective-permute-start(f32[64,8]{0,1:T(8,128)S(1)} %bitcast.59), channel_id=1, source_target_pairs={{0,1},{1,2},{2,3},{4,5},{5,6},{6,7},{8,9},{9,10},{10,11},{12,13},{... | collective-permute-start | bytes 6152 | tf_op jit(solution)/shard_map/ppermute | solution.py:360
  12.2 4.4 %collective-permute-start.3 = (f32[64,8]{0,1:T(8,128)S(1)}, f32[64,8]{0,1:T(8,128)S(1)}, u32[]{:S(2)}, u32[]{:S(2)}) collective-permute-start(f32[64,8]{0,1:T(8,128)S(1)} %bitcast.61), channel_id=1, source_target_pairs={{1,0},{2,1},{3,2},{5,4},{6,5},{7,6},{9,8},{10,9},{11,10},{13,12},{... | collective-permute-start | bytes 6152 | tf_op jit(solution)/shard_map/ppermute | solution.py:361
  18.3 0.6 copy-start.7
  18.3 0.6 copy-start.8
  51.3 7.2 %copy-start.3 = (f32[512,128]{1,0:T(8,128)S(1)}, f32[512,128]{1,0:T(8,128)}, u32[]{:S(2)}) copy-start(f32[512,128]{1,0:T(8,128)} %get-tuple-element.23) | copy-start | bytes 786436
  53.8 14.9 %all-to-all-start.1 = ((f32[64,1,2,128]{3,2,1,0:T(2,128)}), f32[64,1,2,128]{3,2,1,0:T(2,128)S(1)}, u32[]{:S(2)}, u32[]{:S(2)}) async-start(f32[64,1,2,128]{3,2,1,0:T(2,128)} %shard_map.38), calls=%async_computation.1 | async-start | bytes 131072 | tf_op jit(solution)/shard_map/all_to_all | solution.py:378
  58.6 1.0 %copy-start.2 = (f32[512,128]{1,0:T(8,128)S(1)}, f32[512,128]{1,0:T(8,128)}, u32[]{:S(2)}) copy-start(f32[512,128]{1,0:T(8,128)} %get-tuple-element.24) | copy-start | bytes 786436
  59.5 0.9 %copy-start.1 = (f32[512,128]{1,0:T(8,128)S(1)}, f32[512,128]{1,0:T(8,128)}, u32[]{:S(2)}) copy-start(f32[512,128]{1,0:T(8,128)} %get-tuple-element.25) | copy-start | bytes 786436
  68.7 0.6 copy-start
  72.6 3.5 %collective-permute-start.6 = (f32[4,6,4,128]{3,2,1,0:T(4,128)}, f32[4,6,4,128]{3,2,1,0:T(4,128)S(1)}, u32[]{:S(2)}, u32[]{:S(2)}) collective-permute-start(f32[4,6,4,128]{3,2,1,0:T(4,128)} %get-tuple-element.29.refs_0_), channel_id=1, source_target_pairs={{0,3},{1,0},{2,1},{3,2},{4,7},{5,4},{6,5},{7,6},{8,11},{9,8},{10,9... | collective-permute-start | bytes 147464 | tf_op jit(solution)/shard_map/ppermute | solution.py:389
  73.5 4.7 %collective-permute-start.5 = (f32[4,6,4,128]{3,2,1,0:T(4,128)}, f32[4,6,4,128]{3,2,1,0:T(4,128)S(1)}, u32[]{:S(2)}, u32[]{:S(2)}) collective-permute-start(f32[4,6,4,128]{3,2,1,0:T(4,128)} %get-tuple-element.29.refs_0_), channel_id=1, source_target_pairs={{0,2},{1,3},{2,0},{3,1},{4,6},{5,7},{6,4},{7,5},{8,10},{9,11},{10,... | collective-permute-start | bytes 147464 | tf_op jit(solution)/shard_map/ppermute | solution.py:389
  75.7 4.5 %collective-permute-start.4 = (f32[4,6,4,128]{3,2,1,0:T(4,128)}, f32[4,6,4,128]{3,2,1,0:T(4,128)S(1)}, u32[]{:S(2)}, u32[]{:S(2)}) collective-permute-start(f32[4,6,4,128]{3,2,1,0:T(4,128)} %get-tuple-element.29.refs_0_), channel_id=1, source_target_pairs={{0,1},{1,2},{2,3},{3,0},{4,5},{5,6},{6,7},{7,4},{8,9},{9,10},{10,1... | collective-permute-start | bytes 147464 | tf_op jit(solution)/shard_map/ppermute | solution.py:389
  76.1 4.1 %copy-start.4 = (f32[4,6,4,128]{3,2,1,0:T(4,128)}, f32[4,6,4,128]{3,2,1,0:T(4,128)S(1)}, u32[]{:S(2)}) copy-start(f32[4,6,4,128]{3,2,1,0:T(4,128)S(1)} %collective-permute-done.6.refs_3_) | copy-start | bytes 147460
  78.2 2.0 %copy-start.5 = (f32[4,6,4,128]{3,2,1,0:T(4,128)}, f32[4,6,4,128]{3,2,1,0:T(4,128)S(1)}, u32[]{:S(2)}) copy-start(f32[4,6,4,128]{3,2,1,0:T(4,128)S(1)} %collective-permute-done.5.refs_2_) | copy-start | bytes 147460
  80.2 0.6 copy-start.6

commit v7 on v6

--- a/solution.py
+++ b/solution.py
@@ -115,8 +115,10 @@
 
     lane = lax.broadcasted_iota(jnp.int32, (nt, nwl), 1)
     tix = lax.broadcasted_iota(jnp.int32, (nt, nwl), 0)
-    cast_lo = medium_parameters(hcl_ref[...])
-    cast_hi = medium_parameters(hch_ref[...])
+    even = fl_ref[4] > 0.5
+    got_a, got_b = hcl_ref[...], hch_ref[...]
+    cast_lo = medium_parameters(jnp.where(even, got_b, got_a))
+    cast_hi = medium_parameters(jnp.where(even, got_a, got_b))
     g_c = n * n * 4.0 * 0.5
     g_w = nwl * nwl / 4.0 * 0.5
     g_t = nt * nt / 4.0 * 0.5
@@ -142,8 +144,8 @@
             Tq, kq, sq = (row(r, n + c + 1) for r in (tp_ref, kp_ref, sp2_ref))
         Ttm, ktm, stm = (row(r, c) for r in (tp_ref, kp_ref, sp2_ref))
         Ttp, ktp, stp = (row(r, 2 * n + c) for r in (tp_ref, kp_ref, sp2_ref))
-        wlo = medium_parameters(hwl_ref[c])
-        whi = medium_parameters(hwh_ref[c])
+        wlo = medium_parameters(hwl_ref[:, c : c + 1])
+        whi = medium_parameters(hwh_ref[:, c : c + 1])
         Twm, kwm, swm = (jnp.where(lane == 0, b, pltpu.roll(f, 1, 1)) for f, b in zip((T0, k0, s0), wlo))
         Twp, kwp, swp = (
             jnp.where(lane == nwl - 1, b, pltpu.roll(f, nwl - 1, 1)) for f, b in zip((T0, k0, s0), whi)
@@ -355,19 +357,23 @@
     ci, wi = lax.axis_index("cast"), lax.axis_index("width")
     up_c = [(i, i + 1) for i in range(nc - 1)]
     up_w = [(i, i + 1) for i in range(nw - 1)]
-    h_cl = lax.ppermute(h[:, -1, :], "cast", up_c)
-    h_ch = lax.ppermute(h[:, 0, :], "cast", [(b, a) for a, b in up_c])
-    h_wl = lax.ppermute(h[:, :, -1], "width", up_w)[:, :, None]
-    h_wh = lax.ppermute(h[:, :, 0], "width", [(b, a) for a, b in up_w])[:, :, None]
+    even = ci % 2 == 0
+    first, last = h[:, 0, :], h[:, -1, :]
+    in_chip = [(i, i ^ 1) for i in range(nc)]
+    across = [(i, i + 1) for i in range(1, nc - 1, 2)] + [(i + 1, i) for i in range(1, nc - 1, 2)]
+    got_a = lax.ppermute(jnp.where(even, last, first), "cast", in_chip)
+    got_b = lax.ppermute(jnp.where(even, first, last), "cast", across)
+    h_wl = lax.ppermute(h[:, :, -1], "width", up_w)
+    h_wh = lax.ppermute(h[:, :, 0], "width", [(b, a) for a, b in up_w])
 
     cast_low = (ci > 0).astype(F32)
     cast_high = (ci < nc - 1).astype(F32)
     width_low = (wi > 0).astype(F32)
     width_high = (wi < nw - 1).astype(F32)
-    flags = jnp.stack([cast_low, cast_high, width_low, width_high])
+    flags = jnp.stack([cast_low, cast_high, width_low, width_high, even.astype(F32)])
     outs = prep_solve(
-        h.reshape(nt * ncl, nwl), h_cl, h_ch,
-        jnp.transpose(h_wl, (1, 0, 2)), jnp.transpose(h_wh, (1, 0, 2)),
+        h.reshape(nt * ncl, nwl), got_a, got_b,
+        h_wl, h_wh,
         zones.reshape(2 * ncl, nwl), spray_coef, flags, ncl,
     )
     y, v, w, summ = outs[:4]

time: 86.1 us -> 80.9 us (0.940)
  local copies, waits for them, and re-layouts: 8.82 us -> 6.84 us
  starting transfers between devices: 19.2 us -> 17.4 us
  blocking collectives: 27.6 us -> 26.3 us
    ppermute x4, starting transfers between devices: 10.9 us -> 9.1 us  [the longest x1 4.5 us: shards(): got_b = lax.ppermute(jnp.where(even, first, last), 'cast', across)]
    broadcast_in_dim x2 -> x0, local copies, waits for them, and re-layouts: 1.73 us -> none  [the longest x1 0.87 us: shards(): lax.ppermute(h[:, :, 0], 'width', [(b, a) for a, b in up_w])[:, :, None]]
    all_to_all x1, blocking collectives: 27.6 us -> 26.3 us  [shards(): lax.all_to_all(summ.reshape(nc, nt // nc, 8, nwl), 'cast', 0, 0, tiled=True)]
    slice x2, local copies, waits for them, and re-layouts: 2.23 us -> 1.27 us  [the longest x1 1.14 us: shards(): first, last = (h[:, 0, :], h[:, -1, :])]
    unnamed x20 -> x26, local copies, waits for them, and re-layouts: 2.34 us -> 2.95 us
  transfers between devices with their start and end apart: 8 -> 8, of which waited for: 4 -> 4; matrix products, arithmetic and copies ran while one was open for 7% -> 5% of each run, Pallas kernels for 0% -> 0%
where the time goes in v7:
time: 80.9 us; the launch traced here: 80.4 us
  blocking collectives  26.3 us (33%)
  starting transfers between devices  17.4 us (22%)
  Pallas kernels  15.1 us (19%)
  waiting for transfers between devices  14 us (17%)
  local copies, waits for them, and re-layouts  6.84 us (8%)
    all_to_all x1, blocking collectives, shards(): lax.all_to_all(summ.reshape(nc, nt // nc, 8, nwl), 'cast', 0, 0, tiled=True)  26.3 us
    all_to_all x1, waiting for transfers between devices, shards(): back = lax.all_to_all(lr, 'cast', 0, 0, tiled=True).reshape(nt, 2, nwl)  7.32 us
    all_to_all x1, starting transfers between devices, shards(): back = lax.all_to_all(lr, 'cast', 0, 0, tiled=True).reshape(nt, 2, nwl)  4.77 us
    pallas_call x1, Pallas kernels, prep_solve(): pl.pallas_call(functools.partial(_prep_kernel, n), out_shape=[shp] * 3 +...  4.63 us
    ppermute x1, starting transfers between devices, shards(): got_b = lax.ppermute(jnp.where(even, first, last), 'cast', across)  4.5 us
    ppermute x3, waiting for transfers between devices, shards(): lax.ppermute(summ, 'width', [(i, (i + q) % nw) for i in range(nw)])  4.06 us
    ppermute x3, starting transfers between devices, shards(): lax.ppermute(summ, 'width', [(i, (i + q) % nw) for i in range(nw)])  3.48 us
    pallas_call x1, Pallas kernels, width_solve(): pl.pallas_call(functools.partial(_width_kernel, nsub), out_shape=[shp, sh...  3.34 us
  transfers between devices with their start and end apart: 8, of which 4 were waited for; matrix products, arithmetic and copies ran while one was open for 5% of the time, Pallas kernels for 0%

profile of v7, /device:TPU:1, one launch (start us, length us, event | category | flops | bytes accessed | tf_op | source)
XLA Modules:
  0.0 80.4 jit_solution(16597861834845449872)
XLA Ops:
  0.0 1.1 %fusion.1 = (f32[64,1,128]{2,1,0:T(1,128)S(1)}, f32[64,1,128]{2,1,0:T(1,128)S(1)}) fusion(f32[64,8,128]{2,1,0:T(8,128)} %h_ref.1), kind=kLoop, calls=%fused_computation.3 | loop fusion | bytes 131072 | tf_op jit(solution)/shard_map/slice | solution.py:361
  1.2 4.5 %collective-permute-start.1 = (f32[64,128]{1,0:T(8,128)S(1)}, f32[64,128]{1,0:T(8,128)S(1)}, u32[]{:S(2)}, u32[]{:S(2)}) collective-permute-start(f32[64,128]{1,0:T(8,128)S(1)} %get-tuple-element.37), channel_id=1, source_target_pairs={{4,8},{12,16},{20,24},{28,32},{36,40},{44,48},{52,56},{60,64},{68,... | collective-permute-start | bytes 98312 | tf_op jit(solution)/shard_map/ppermute | solution.py:365
  5.7 0.1 collective-permute-start
  5.8 0.1 fusion
  5.9 0.4 copy.29
  6.4 3.2 %collective-permute-start.2 = (f32[64,8]{1,0:T(8,128)S(1)}, f32[64,8]{1,0:T(8,128)S(1)}, u32[]{:S(2)}, u32[]{:S(2)}) collective-permute-start(f32[64,8]{1,0:T(8,128)S(1)} %bitcast.53), channel_id=1, source_target_pairs={{0,1},{1,2},{2,3},{4,5},{5,6},{6,7},{8,9},{9,10},{10,11},{12,13},{... | collective-permute-start | bytes 6152 | tf_op jit(solution)/shard_map/ppermute | solution.py:366
  9.6 0.4 copy.30
  10.0 1.3 %collective-permute-start.3 = (f32[64,8]{1,0:T(8,128)S(1)}, f32[64,8]{1,0:T(8,128)S(1)}, u32[]{:S(2)}, u32[]{:S(2)}) collective-permute-start(f32[64,8]{1,0:T(8,128)S(1)} %bitcast.54), channel_id=1, source_target_pairs={{1,0},{2,1},{3,2},{5,4},{6,5},{7,6},{9,8},{10,9},{11,10},{13,12},{... | collective-permute-start | bytes 6152 | tf_op jit(solution)/shard_map/ppermute | solution.py:367
  11.3 0.1 stack.30
  11.4 0.6 stack.31.fl_ref
  12.0 2.7 %collective-permute-done.3.hwh_ref = f32[64,8]{1,0:T(8,128)S(1)} collective-permute-done((f32[64,8]{1,0:T(8,128)S(1)}, f32[64,8]{1,0:T(8,128)S(1)}, u32[]{:S(2)}, u32[]{:S(2)}) %collective-permute-start.3) | collective-permute-done | bytes 2080 | tf_op jit(solution)/shard_map/ppermute | solution.py:367
  14.7 0.6 copy-done.11
  15.3 4.6 %shard_map.37 = (f32[512,128]{1,0:T(8,128)}, f32[512,128]{1,0:T(8,128)}, f32[512,128]{1,0:T(8,128)}, f32[512,128]{1,0:T(8,128)}, f32[512,128]{1,0:T(8,128)}, /*i...) custom-call(f32[512,128]{1,0:T(8,128)} %bitcast.39, ...), custom_call_target="tpu_custom_call" | custom-call | tf_op jit(solution)/shard_map/pallas_call | solution.py:202
  19.9 26.3 %all_to_all.10.s_ref = f32[64,1,8,128]{3,2,1,0:T(8,128)} all-to-all(f32[64,1,8,128]{3,2,1,0:T(8,128)} %bitcast.47), channel_id=1, replica_groups=mesh['cast'=64,'width'=4] {'cast'}, dimensions={0} | all-to-all | bytes 524288 | tf_op jit(solution)/shard_map/all_to_all | solution.py:381
  46.2 2.4 %shard_map.38 = f32[64,1,2,128]{3,2,1,0:T(2,128)} custom-call(f32[64,1,8,128]{3,2,1,0:T(8,128)} %all_to_all.10.s_ref), custom_call_target="tpu_custom_call" | custom-call | tf_op jit(solution)/shard_map/pallas_call | solution.py:383
  48.7 4.8 %all-to-all-start.1 = ((f32[64,1,2,128]{3,2,1,0:T(2,128)}), f32[64,1,2,128]{3,2,1,0:T(2,128)S(1)}, u32[]{:S(2)}, u32[]{:S(2)}) async-start(f32[64,1,2,128]{3,2,1,0:T(2,128)} %shard_map.38), calls=%async_computation.1 | async-start | bytes 131072 | tf_op jit(solution)/shard_map/all_to_all | solution.py:384
  53.5 0.8 %copy.24.a_ref = f32[128,4,128]{2,1,0:T(4,128)} copy(f32[128,4,128]{0,2,1:T(8,128)S(1)} %bitcast.46) | data formatting | bytes 524288 | tf_op jit(solution)/shard_map/reshape | solution.py:391
  54.3 0.1 copy-done.3
  54.4 0.8 %copy.25.b_ref = f32[128,4,128]{2,1,0:T(4,128)} copy(f32[128,4,128]{0,2,1:T(8,128)S(1)} %bitcast.45) | data formatting | bytes 524288 | tf_op jit(solution)/shard_map/reshape | solution.py:391
  55.3 0.1 copy-done.2
  55.4 0.8 %copy.26.c_ref = f32[128,4,128]{2,1,0:T(4,128)} copy(f32[128,4,128]{0,2,1:T(8,128)S(1)} %bitcast.44) | data formatting | bytes 524288 | tf_op jit(solution)/shard_map/reshape | solution.py:391
  56.2 7.3 %all-to-all-done.1 = f32[64,1,2,128]{3,2,1,0:T(2,128)S(1)} async-done(((f32[64,1,2,128]{3,2,1,0:T(2,128)}), f32[64,1,2,128]{3,2,1,0:T(2,128)S(1)}, u32[]{:S(2)}, u32[]{:S(2)}) %all-to-all-start.1) | async-done | bytes 65568 | tf_op jit(solution)/shard_map/all_to_all | solution.py:384
  63.6 0.6 copy-done.1
  64.2 3.3 %shard_map.39 = (f32[128,4,128]{2,1,0:T(4,128)}, f32[128,4,128]{2,1,0:T(4,128)}, f32[128,4,128]{2,1,0:T(4,128)}, f32[4,6,4,128]{3,2,1,0:T(4,128)}) custom-call(f32[64,8,128]{2,1,0:T(8,128)} %bitcast.40, f32[64,8,128]{2,1,0:T(8,128)} %bitcast.41, f32[64,8,128]{2,1,0:T(8,128)} %bitcast.42, f32[64,2,128]{2,1,0:T(2,128)} %bitcast.43, ...), custom_call_target="tpu_custom_call" | custom-call | tf_op jit(solution)/shard_map/pallas_call | solution.py:265
  67.5 0.9 %collective-permute-start.6 = (f32[4,6,4,128]{3,2,1,0:T(4,128)}, f32[4,6,4,128]{3,2,1,0:T(4,128)S(1)}, u32[]{:S(2)}, u32[]{:S(2)}) collective-permute-start(f32[4,6,4,128]{3,2,1,0:T(4,128)} %get-tuple-element.29.refs_0_), channel_id=1, source_target_pairs={{0,3},{1,0},{2,1},{3,2},{4,7},{5,4},{6,5},{7,6},{8,11},{9,8},{10,9... | collective-permute-start | bytes 147464 | tf_op jit(solution)/shard_map/ppermute | solution.py:395
  68.4 2.2 %collective-permute-start.5 = (f32[4,6,4,128]{3,2,1,0:T(4,128)}, f32[4,6,4,128]{3,2,1,0:T(4,128)S(1)}, u32[]{:S(2)}, u32[]{:S(2)}) collective-permute-start(f32[4,6,4,128]{3,2,1,0:T(4,128)} %get-tuple-element.29.refs_0_), channel_id=1, source_target_pairs={{0,2},{1,3},{2,0},{3,1},{4,6},{5,7},{6,4},{7,5},{8,10},{9,11},{10,... | collective-permute-start | bytes 147464 | tf_op jit(solution)/shard_map/ppermute | solution.py:395
  70.6 0.4 collective-permute-start.4
  71.0 2.0 %collective-permute-done.5.refs_2_ = f32[4,6,4,128]{3,2,1,0:T(4,128)S(1)} collective-permute-done((f32[4,6,4,128]{3,2,1,0:T(4,128)}, f32[4,6,4,128]{3,2,1,0:T(4,128)S(1)}, u32[]{:S(2)}, u32[]{:S(2)}) %collective-permute-start.5) | collective-permute-done | bytes 49184 | tf_op jit(solution)/shard_map/ppermute | solution.py:395
  73.0 2.0 %collective-permute-done.4.refs_1_ = f32[4,6,4,128]{3,2,1,0:T(4,128)S(1)} collective-permute-done((f32[4,6,4,128]{3,2,1,0:T(4,128)}, f32[4,6,4,128]{3,2,1,0:T(4,128)S(1)}, u32[]{:S(2)}, u32[]{:S(2)}) %collective-permute-start.4) | collective-permute-done | bytes 49184 | tf_op jit(solution)/shard_map/ppermute | solution.py:395
  75.1 0.6 copy-done.7
  75.7 1.7 %shard_map.40.lr_ref = f32[4,2,4,128]{3,2,1,0:T(4,128)} custom-call(s32[1]{0:T(128)} %bitcast.25.me_ref, f32[4,6,4,128]{3,2,1,0:T(4,128)} %get-tuple-element.29.refs_0_, f32[4,6,4,128]{3,2,1,0:T(4,128)} %copy-done.7, f32[4,6,4,128]{3,2,1,0:T(4,128)} %copy-done.6, f32[4,6,4,128]{3,2,1,0:T(4,128)} %copy-done.5), custom_call_target="tpu_custom_call" | custom-call | tf_op jit(solution)/shard_map/pallas_call | solution.py:397
  77.4 3.0 %shard_map.41 = f32[64,8,128]{2,1,0:T(8,128)} custom-call(f32[128,4,128]{2,1,0:T(4,128)} %get-tuple-element.26.yw_ref, f32[128,4,128]{2,1,0:T(4,128)} %get-tuple-element.27.vw_ref, f32[128,4,128]{2,1,0:T(4,128)} %get-tuple-element.28.ww_ref, f32[4,2,4,128]{3,2,1,0:T(4,128)} %shard_map.40.lr_ref, f32[64,8,128]{2,1,0:T(8,128)} %bitcast.48, ...), custom_call_target="tpu_custom_call" | custom-call | tf_op jit(solution)/shard_map/pallas_call | solution.py:273
  (24 shorter events, 0.1 us)
Async XLA Ops:
  0.0 5.8 %copy-start = (f32[64,8,128]{2,1,0:T(8,128)S(1)}, f32[64,8,128]{2,1,0:T(8,128)}, u32[]{:S(2)}) copy-start(f32[64,8,128]{2,1,0:T(8,128)} %h_ref.1) | copy-start | bytes 786436
  1.2 13.5 %collective-permute-start.1 = (f32[64,128]{1,0:T(8,128)S(1)}, f32[64,128]{1,0:T(8,128)S(1)}, u32[]{:S(2)}, u32[]{:S(2)}) collective-permute-start(f32[64,128]{1,0:T(8,128)S(1)} %get-tuple-element.37), channel_id=1, source_target_pairs={{4,8},{12,16},{20,24},{28,32},{36,40},{44,48},{52,56},{60,64},{68,... | collective-permute-start | bytes 98312 | tf_op jit(solution)/shard_map/ppermute | solution.py:365
  5.7 9.0 %collective-permute-start = (f32[64,128]{1,0:T(8,128)S(1)}, f32[64,128]{1,0:T(8,128)S(1)}, u32[]{:S(2)}, u32[]{:S(2)}) collective-permute-start(f32[64,128]{1,0:T(8,128)S(1)} %get-tuple-element.38), channel_id=1, source_target_pairs={{0,4},{4,0},{8,12},{12,8},{16,20},{20,16},{24,28},{28,24},{32,36},... | collective-permute-start | bytes 98312 | tf_op jit(solution)/shard_map/ppermute | solution.py:364
  6.4 5.7 %collective-permute-start.2 = (f32[64,8]{1,0:T(8,128)S(1)}, f32[64,8]{1,0:T(8,128)S(1)}, u32[]{:S(2)}, u32[]{:S(2)}) collective-permute-start(f32[64,8]{1,0:T(8,128)S(1)} %bitcast.53), channel_id=1, source_target_pairs={{0,1},{1,2},{2,3},{4,5},{5,6},{6,7},{8,9},{9,10},{10,11},{12,13},{... | collective-permute-start | bytes 6152 | tf_op jit(solution)/shard_map/ppermute | solution.py:366
  10.0 4.7 %collective-permute-start.3 = (f32[64,8]{1,0:T(8,128)S(1)}, f32[64,8]{1,0:T(8,128)S(1)}, u32[]{:S(2)}, u32[]{:S(2)}) collective-permute-start(f32[64,8]{1,0:T(8,128)S(1)} %bitcast.54), channel_id=1, source_target_pairs={{1,0},{2,1},{3,2},{5,4},{6,5},{7,6},{9,8},{10,9},{11,10},{13,12},{... | collective-permute-start | bytes 6152 | tf_op jit(solution)/shard_map/ppermute | solution.py:367
  12.0 2.7 %copy-start.10 = (f32[64,8]{1,0:T(8,128)}, f32[64,8]{1,0:T(8,128)S(1)}, u32[]{:S(2)}) copy-start(f32[64,8]{1,0:T(8,128)S(1)} %collective-permute-done.2.hwl_ref) | copy-start | bytes 6148
  14.7 0.6 copy-start.11
  14.7 0.6 copy-start.8
  14.7 0.6 copy-start.9
  46.2 7.2 %copy-start.4 = (f32[512,128]{1,0:T(8,128)S(1)}, f32[512,128]{1,0:T(8,128)}, u32[]{:S(2)}) copy-start(f32[512,128]{1,0:T(8,128)} %get-tuple-element.23) | copy-start | bytes 786436
  48.7 14.9 %all-to-all-start.1 = ((f32[64,1,2,128]{3,2,1,0:T(2,128)}), f32[64,1,2,128]{3,2,1,0:T(2,128)S(1)}, u32[]{:S(2)}, u32[]{:S(2)}) async-start(f32[64,1,2,128]{3,2,1,0:T(2,128)} %shard_map.38), calls=%async_computation.1 | async-start | bytes 131072 | tf_op jit(solution)/shard_map/all_to_all | solution.py:384
  53.5 1.0 %copy-start.3 = (f32[512,128]{1,0:T(8,128)S(1)}, f32[512,128]{1,0:T(8,128)}, u32[]{:S(2)}) copy-start(f32[512,128]{1,0:T(8,128)} %get-tuple-element.24) | copy-start | bytes 786436
  54.4 0.9 %copy-start.2 = (f32[512,128]{1,0:T(8,128)S(1)}, f32[512,128]{1,0:T(8,128)}, u32[]{:S(2)}) copy-start(f32[512,128]{1,0:T(8,128)} %get-tuple-element.25) | copy-start | bytes 786436
  63.5 0.6 copy-start.1
  67.5 3.5 %collective-permute-start.6 = (f32[4,6,4,128]{3,2,1,0:T(4,128)}, f32[4,6,4,128]{3,2,1,0:T(4,128)S(1)}, u32[]{:S(2)}, u32[]{:S(2)}) collective-permute-start(f32[4,6,4,128]{3,2,1,0:T(4,128)} %get-tuple-element.29.refs_0_), channel_id=1, source_target_pairs={{0,3},{1,0},{2,1},{3,2},{4,7},{5,4},{6,5},{7,6},{8,11},{9,8},{10,9... | collective-permute-start | bytes 147464 | tf_op jit(solution)/shard_map/ppermute | solution.py:395
  68.4 4.7 %collective-permute-start.5 = (f32[4,6,4,128]{3,2,1,0:T(4,128)}, f32[4,6,4,128]{3,2,1,0:T(4,128)S(1)}, u32[]{:S(2)}, u32[]{:S(2)}) collective-permute-start(f32[4,6,4,128]{3,2,1,0:T(4,128)} %get-tuple-element.29.refs_0_), channel_id=1, source_target_pairs={{0,2},{1,3},{2,0},{3,1},{4,6},{5,7},{6,4},{7,5},{8,10},{9,11},{10,... | collective-permute-start | bytes 147464 | tf_op jit(solution)/shard_map/ppermute | solution.py:395
  70.6 4.5 %collective-permute-start.4 = (f32[4,6,4,128]{3,2,1,0:T(4,128)}, f32[4,6,4,128]{3,2,1,0:T(4,128)S(1)}, u32[]{:S(2)}, u32[]{:S(2)}) collective-permute-start(f32[4,6,4,128]{3,2,1,0:T(4,128)} %get-tuple-element.29.refs_0_), channel_id=1, source_target_pairs={{0,1},{1,2},{2,3},{3,0},{4,5},{5,6},{6,7},{7,4},{8,9},{9,10},{10,1... | collective-permute-start | bytes 147464 | tf_op jit(solution)/shard_map/ppermute | solution.py:395
  71.0 4.1 %copy-start.5 = (f32[4,6,4,128]{3,2,1,0:T(4,128)}, f32[4,6,4,128]{3,2,1,0:T(4,128)S(1)}, u32[]{:S(2)}) copy-start(f32[4,6,4,128]{3,2,1,0:T(4,128)S(1)} %collective-permute-done.6.refs_3_) | copy-start | bytes 147460
  73.0 2.0 %copy-start.6 = (f32[4,6,4,128]{3,2,1,0:T(4,128)}, f32[4,6,4,128]{3,2,1,0:T(4,128)S(1)}, u32[]{:S(2)}) copy-start(f32[4,6,4,128]{3,2,1,0:T(4,128)S(1)} %collective-permute-done.5.refs_2_) | copy-start | bytes 147460
  75.1 0.6 copy-start.7

commit v8 on v7

--- a/solution.py
+++ b/solution.py
@@ -223,12 +223,15 @@
             sm_ref[q, k] = val
 
 
-def _thick_kernel(nsub, tsub, yw_ref, vw_ref, ww_ref, lr_ref, a_ref, b_ref, c_ref, h_ref,
-                  o_ref, sw_ref, d_ref, y_ref, v_ref, w_ref, cp_ref):
+def _thick_kernel(nsub, tsub, nw, me_ref, *refs):
+    r_refs = refs[:nw]
+    (yw_ref, vw_ref, ww_ref, a_ref, b_ref, c_ref, h_ref,
+     o_ref, sw_ref, d_ref, y_ref, v_ref, w_ref, cp_ref) = refs[nw:]
+    lrw = _width_reduce(me_ref[0], r_refs)
     m = yw_ref.shape[0] // nsub
     for q in range(nsub):
         sl = slice(q * m, (q + 1) * m)
-        sw_ref[sl] = yw_ref[sl] + vw_ref[sl] * lr_ref[q, 0] + ww_ref[sl] * lr_ref[q, 1]
+        sw_ref[sl] = yw_ref[sl] + vw_ref[sl] * lrw[q][0] + ww_ref[sl] * lrw[q][1]
     nt, ncl, nwl = a_ref.shape
     per_q = 128 // ncl
     for q in range(sw_ref.shape[1]):
@@ -269,12 +272,14 @@
     )(yc, vc, wc, bk, a, b, c)
 
 
-def thick_solve(yw, vw, ww, lr, a, b, c, h, nsub, tsub):
+def thick_solve(me, got, yw, vw, ww, a, b, c, h, nsub, tsub):
+    vm = pl.BlockSpec(memory_space=pltpu.VMEM)
     return pl.pallas_call(
-        functools.partial(_thick_kernel, nsub, tsub),
+        functools.partial(_thick_kernel, nsub, tsub, len(got)),
         out_shape=jax.ShapeDtypeStruct(a.shape, F32),
+        in_specs=[SMEM_SPEC] + [vm] * (len(got) + 7),
         scratch_shapes=[pltpu.VMEM(yw.shape, F32)] + [pltpu.VMEM(a.shape, F32)] * 5,
-    )(yw, vw, ww, lr, a, b, c, h)
+    )(me, *got, yw, vw, ww, a, b, c, h)
 
 
 def _reduce_blocks(nb, blk, emit, zero):
@@ -307,11 +312,10 @@
     _reduce_blocks(nb, blk, emit, jnp.zeros((s_ref.shape[1], s_ref.shape[3]), F32))
 
 
-def _width_reduced_kernel(me_ref, *refs):
-    *r_refs, lr_ref = refs
+def _width_reduce(me, r_refs):
     nw = len(r_refs)
     nsub = r_refs[0].shape[0]
-    me = me_ref[0]
+    out = [[None, None] for _ in range(nsub)]
 
     def blk(b):
         dev, q = divmod(b, nsub)
@@ -326,13 +330,12 @@
 
     def emit(b, left, right):
         dev, q = divmod(b, nsub)
-
-        @pl.when(me == dev)
-        def _():
-            lr_ref[q, 0] = left
-            lr_ref[q, 1] = right
+        mine = me == dev
+        for j, val in enumerate((left, right)):
+            out[q][j] = val if out[q][j] is None else jnp.where(mine, val, out[q][j])
 
     _reduce_blocks(nw * nsub, blk, emit, jnp.zeros(r_refs[0].shape[2:], F32))
+    return out
 
 
 def _surface_kernel(scale, z_ref, sp_ref, o_ref):
@@ -394,12 +397,8 @@
     got = [summ] + [
         lax.ppermute(summ, "width", [(i, (i + q) % nw) for i in range(nw)]) for q in range(1, nw)
     ]
-    lr = pl.pallas_call(
-        _width_reduced_kernel,
-        out_shape=jax.ShapeDtypeStruct((nsub, 2) + summ.shape[2:], F32),
-        in_specs=[SMEM_SPEC] + [pl.BlockSpec(memory_space=pltpu.VMEM)] * nw,
-    )(wi.astype(jnp.int32).reshape(1), *got)
-    return thick_solve(y, v, w, lr, tlo, tmd, thi, h, nsub, 4)
+    me = wi.astype(jnp.int32).reshape(1)
+    return thick_solve(me, got, y, v, w, tlo, tmd, thi, h, nsub, 4)
 
 
 def solution(mesh):

time: 80.9 us -> 79.4 us (0.981)
  Pallas kernels: 15.1 us -> 13.7 us
    pallas_call x2 -> x1, Pallas kernels: 4.7 us -> 3.26 us  [thick_solve(): pl.pallas_call(functools.partial(_thick_kernel, nsub, tsub, len(got)), ou...]
where the time goes in v8:
time: 79.4 us; the launch traced here: 78.9 us
  blocking collectives  26.3 us (33%)
  starting transfers between devices  17.4 us (22%)
  waiting for transfers between devices  14 us (18%)
  Pallas kernels  13.7 us (17%)
  local copies, waits for them, and re-layouts  6.84 us (9%)
    all_to_all x1, blocking collectives, shards(): lax.all_to_all(summ.reshape(nc, nt // nc, 8, nwl), 'cast', 0, 0, tiled=True)  26.3 us
    all_to_all x1, waiting for transfers between devices, shards(): back = lax.all_to_all(lr, 'cast', 0, 0, tiled=True).reshape(nt, 2, nwl)  7.32 us
    all_to_all x1, starting transfers between devices, shards(): back = lax.all_to_all(lr, 'cast', 0, 0, tiled=True).reshape(nt, 2, nwl)  4.77 us
    pallas_call x1, Pallas kernels, prep_solve(): pl.pallas_call(functools.partial(_prep_kernel, n), out_shape=[shp] * 3 +...  4.63 us
    ppermute x1, starting transfers between devices, shards(): got_b = lax.ppermute(jnp.where(even, first, last), 'cast', across)  4.5 us
    ppermute x3, waiting for transfers between devices, shards(): lax.ppermute(summ, 'width', [(i, (i + q) % nw) for i in range(nw)])  4.06 us
    ppermute x3, starting transfers between devices, shards(): lax.ppermute(summ, 'width', [(i, (i + q) % nw) for i in range(nw)])  3.48 us
    pallas_call x1, Pallas kernels, width_solve(): pl.pallas_call(functools.partial(_width_kernel, nsub), out_shape=[shp, sh...  3.34 us
  transfers between devices with their start and end apart: 8, of which 4 were waited for; matrix products, arithmetic and copies ran while one was open for 5% of the time, Pallas kernels for 0%

profile of v8, /device:TPU:1, one launch (start us, length us, event | category | flops | bytes accessed | tf_op | source)
XLA Modules:
  0.0 78.9 jit_solution(2823336809330180165)
XLA Ops:
  0.0 1.1 %fusion.1 = (f32[64,1,128]{2,1,0:T(1,128)S(1)}, f32[64,1,128]{2,1,0:T(1,128)S(1)}) fusion(f32[64,8,128]{2,1,0:T(8,128)} %refs_10_.1), kind=kLoop, calls=%fused_computation.3 | loop fusion | bytes 131072 | tf_op jit(solution)/shard_map/slice | solution.py:364
  1.2 4.5 %collective-permute-start.1 = (f32[64,128]{1,0:T(8,128)S(1)}, f32[64,128]{1,0:T(8,128)S(1)}, u32[]{:S(2)}, u32[]{:S(2)}) collective-permute-start(f32[64,128]{1,0:T(8,128)S(1)} %get-tuple-element.37), channel_id=1, source_target_pairs={{4,8},{12,16},{20,24},{28,32},{36,40},{44,48},{52,56},{60,64},{68,... | collective-permute-start | bytes 98312 | tf_op jit(solution)/shard_map/ppermute | solution.py:368
  5.7 0.1 collective-permute-start
  5.8 0.1 fusion
  5.9 0.4 copy.29
  6.4 3.2 %collective-permute-start.2 = (f32[64,8]{1,0:T(8,128)S(1)}, f32[64,8]{1,0:T(8,128)S(1)}, u32[]{:S(2)}, u32[]{:S(2)}) collective-permute-start(f32[64,8]{1,0:T(8,128)S(1)} %bitcast.53), channel_id=1, source_target_pairs={{0,1},{1,2},{2,3},{4,5},{5,6},{6,7},{8,9},{9,10},{10,11},{12,13},{... | collective-permute-start | bytes 6152 | tf_op jit(solution)/shard_map/ppermute | solution.py:369
  9.6 0.4 copy.30
  10.0 1.3 %collective-permute-start.3 = (f32[64,8]{1,0:T(8,128)S(1)}, f32[64,8]{1,0:T(8,128)S(1)}, u32[]{:S(2)}, u32[]{:S(2)}) collective-permute-start(f32[64,8]{1,0:T(8,128)S(1)} %bitcast.54), channel_id=1, source_target_pairs={{1,0},{2,1},{3,2},{5,4},{6,5},{7,6},{9,8},{10,9},{11,10},{13,12},{... | collective-permute-start | bytes 6152 | tf_op jit(solution)/shard_map/ppermute | solution.py:370
  11.3 0.1 stack.30
  11.4 0.6 stack.31.fl_ref
  12.0 2.7 %collective-permute-done.3.hwh_ref = f32[64,8]{1,0:T(8,128)S(1)} collective-permute-done((f32[64,8]{1,0:T(8,128)S(1)}, f32[64,8]{1,0:T(8,128)S(1)}, u32[]{:S(2)}, u32[]{:S(2)}) %collective-permute-start.3) | collective-permute-done | bytes 2080 | tf_op jit(solution)/shard_map/ppermute | solution.py:370
  14.7 0.6 copy-done.11
  15.3 0.0 copy-done.8
  15.3 4.6 %shard_map.37 = (f32[512,128]{1,0:T(8,128)}, f32[512,128]{1,0:T(8,128)}, f32[512,128]{1,0:T(8,128)}, f32[512,128]{1,0:T(8,128)}, f32[512,128]{1,0:T(8,128)}, /*i...) custom-call(f32[512,128]{1,0:T(8,128)} %bitcast.39, ...), custom_call_target="tpu_custom_call" | custom-call | tf_op jit(solution)/shard_map/pallas_call | solution.py:202
  19.9 26.3 %all_to_all.10.s_ref = f32[64,1,8,128]{3,2,1,0:T(8,128)} all-to-all(f32[64,1,8,128]{3,2,1,0:T(8,128)} %bitcast.50), channel_id=1, replica_groups=mesh['cast'=64,'width'=4] {'cast'}, dimensions={0} | all-to-all | bytes 524288 | tf_op jit(solution)/shard_map/all_to_all | solution.py:384
  46.2 2.4 %shard_map.38 = f32[64,1,2,128]{3,2,1,0:T(2,128)} custom-call(f32[64,1,8,128]{3,2,1,0:T(8,128)} %all_to_all.10.s_ref), custom_call_target="tpu_custom_call" | custom-call | tf_op jit(solution)/shard_map/pallas_call | solution.py:386
  48.7 4.8 %all-to-all-start.1 = ((f32[64,1,2,128]{3,2,1,0:T(2,128)}), f32[64,1,2,128]{3,2,1,0:T(2,128)S(1)}, u32[]{:S(2)}, u32[]{:S(2)}) async-start(f32[64,1,2,128]{3,2,1,0:T(2,128)} %shard_map.38), calls=%async_computation.1 | async-start | bytes 131072 | tf_op jit(solution)/shard_map/all_to_all | solution.py:387
  53.5 0.8 %copy.24.a_ref = f32[128,4,128]{2,1,0:T(4,128)} copy(f32[128,4,128]{0,2,1:T(8,128)S(1)} %bitcast.49) | data formatting | bytes 524288 | tf_op jit(solution)/shard_map/reshape | solution.py:394
  54.3 0.1 copy-done.3
  54.4 0.8 %copy.25.b_ref = f32[128,4,128]{2,1,0:T(4,128)} copy(f32[128,4,128]{0,2,1:T(8,128)S(1)} %bitcast.48) | data formatting | bytes 524288 | tf_op jit(solution)/shard_map/reshape | solution.py:394
  55.3 0.1 copy-done.2
  55.4 0.8 %copy.26.c_ref = f32[128,4,128]{2,1,0:T(4,128)} copy(f32[128,4,128]{0,2,1:T(8,128)S(1)} %bitcast.47) | data formatting | bytes 524288 | tf_op jit(solution)/shard_map/reshape | solution.py:394
  56.2 7.3 %all-to-all-done.1 = f32[64,1,2,128]{3,2,1,0:T(2,128)S(1)} async-done(((f32[64,1,2,128]{3,2,1,0:T(2,128)}), f32[64,1,2,128]{3,2,1,0:T(2,128)S(1)}, u32[]{:S(2)}, u32[]{:S(2)}) %all-to-all-start.1) | async-done | bytes 65568 | tf_op jit(solution)/shard_map/all_to_all | solution.py:387
  63.6 0.6 copy-done.1
  64.2 3.3 %shard_map.39 = (f32[128,4,128]{2,1,0:T(4,128)}, f32[128,4,128]{2,1,0:T(4,128)}, f32[128,4,128]{2,1,0:T(4,128)}, f32[4,6,4,128]{3,2,1,0:T(4,128)}) custom-call(f32[64,8,128]{2,1,0:T(8,128)} %bitcast.43, f32[64,8,128]{2,1,0:T(8,128)} %bitcast.44, f32[64,8,128]{2,1,0:T(8,128)} %bitcast.45, f32[64,2,128]{2,1,0:T(2,128)} %bitcast.46, ...), custom_call_target="tpu_custom_call" | custom-call | tf_op jit(solution)/shard_map/pallas_call | solution.py:268
  67.5 0.9 %collective-permute-start.6 = (f32[4,6,4,128]{3,2,1,0:T(4,128)}, f32[4,6,4,128]{3,2,1,0:T(4,128)S(1)}, u32[]{:S(2)}, u32[]{:S(2)}) collective-permute-start(f32[4,6,4,128]{3,2,1,0:T(4,128)} %get-tuple-element.26.refs_0_), channel_id=1, source_target_pairs={{0,3},{1,0},{2,1},{3,2},{4,7},{5,4},{6,5},{7,6},{8,11},{9,8},{10,9... | collective-permute-start | bytes 147464 | tf_op jit(solution)/shard_map/ppermute | solution.py:398
  68.4 2.2 %collective-permute-start.5 = (f32[4,6,4,128]{3,2,1,0:T(4,128)}, f32[4,6,4,128]{3,2,1,0:T(4,128)S(1)}, u32[]{:S(2)}, u32[]{:S(2)}) collective-permute-start(f32[4,6,4,128]{3,2,1,0:T(4,128)} %get-tuple-element.26.refs_0_), channel_id=1, source_target_pairs={{0,2},{1,3},{2,0},{3,1},{4,6},{5,7},{6,4},{7,5},{8,10},{9,11},{10,... | collective-permute-start | bytes 147464 | tf_op jit(solution)/shard_map/ppermute | solution.py:398
  70.6 0.4 collective-permute-start.4
  71.0 2.0 %collective-permute-done.5.refs_2_ = f32[4,6,4,128]{3,2,1,0:T(4,128)S(1)} collective-permute-done((f32[4,6,4,128]{3,2,1,0:T(4,128)}, f32[4,6,4,128]{3,2,1,0:T(4,128)S(1)}, u32[]{:S(2)}, u32[]{:S(2)}) %collective-permute-start.5) | collective-permute-done | bytes 49184 | tf_op jit(solution)/shard_map/ppermute | solution.py:398
  73.0 2.0 %collective-permute-done.4.refs_1_ = f32[4,6,4,128]{3,2,1,0:T(4,128)S(1)} collective-permute-done((f32[4,6,4,128]{3,2,1,0:T(4,128)}, f32[4,6,4,128]{3,2,1,0:T(4,128)S(1)}, u32[]{:S(2)}, u32[]{:S(2)}) %collective-permute-start.4) | collective-permute-done | bytes 49184 | tf_op jit(solution)/shard_map/ppermute | solution.py:398
  75.1 0.6 copy-done.7
  75.7 3.3 %shard_map.40 = f32[64,8,128]{2,1,0:T(8,128)} custom-call(s32[1]{0:T(128)} %bitcast.me_ref, f32[4,6,4,128]{3,2,1,0:T(4,128)} %get-tuple-element.26.refs_0_, f32[4,6,4,128]{3,2,1,0:T(4,128)} %copy-done.7, f32[4,6,4,128]{3,2,1,0:T(4,128)} %copy-done.6, f32[4,6,4,128]{3,2,1,0:T(4,128)} %copy-done.5, f32[128,4,128]{2,1,0:T(4,128)} %get-tuple-element.27.refs_4_, ...), custom_call_target="tpu_custom_call" | custom-call | tf_op jit(solution)/shard_map/pallas_call | solution.py:277
  (23 shorter events, 0.1 us)
Async XLA Ops:
  0.0 5.8 %copy-start = (f32[64,8,128]{2,1,0:T(8,128)S(1)}, f32[64,8,128]{2,1,0:T(8,128)}, u32[]{:S(2)}) copy-start(f32[64,8,128]{2,1,0:T(8,128)} %refs_10_.1) | copy-start | bytes 786436
  1.2 13.5 %collective-permute-start.1 = (f32[64,128]{1,0:T(8,128)S(1)}, f32[64,128]{1,0:T(8,128)S(1)}, u32[]{:S(2)}, u32[]{:S(2)}) collective-permute-start(f32[64,128]{1,0:T(8,128)S(1)} %get-tuple-element.37), channel_id=1, source_target_pairs={{4,8},{12,16},{20,24},{28,32},{36,40},{44,48},{52,56},{60,64},{68,... | collective-permute-start | bytes 98312 | tf_op jit(solution)/shard_map/ppermute | solution.py:368
  5.7 9.0 %collective-permute-start = (f32[64,128]{1,0:T(8,128)S(1)}, f32[64,128]{1,0:T(8,128)S(1)}, u32[]{:S(2)}, u32[]{:S(2)}) collective-permute-start(f32[64,128]{1,0:T(8,128)S(1)} %get-tuple-element.38), channel_id=1, source_target_pairs={{0,4},{4,0},{8,12},{12,8},{16,20},{20,16},{24,28},{28,24},{32,36},... | collective-permute-start | bytes 98312 | tf_op jit(solution)/shard_map/ppermute | solution.py:367
  6.4 5.7 %collective-permute-start.2 = (f32[64,8]{1,0:T(8,128)S(1)}, f32[64,8]{1,0:T(8,128)S(1)}, u32[]{:S(2)}, u32[]{:S(2)}) collective-permute-start(f32[64,8]{1,0:T(8,128)S(1)} %bitcast.53), channel_id=1, source_target_pairs={{0,1},{1,2},{2,3},{4,5},{5,6},{6,7},{8,9},{9,10},{10,11},{12,13},{... | collective-permute-start | bytes 6152 | tf_op jit(solution)/shard_map/ppermute | solution.py:369
  10.0 4.7 %collective-permute-start.3 = (f32[64,8]{1,0:T(8,128)S(1)}, f32[64,8]{1,0:T(8,128)S(1)}, u32[]{:S(2)}, u32[]{:S(2)}) collective-permute-start(f32[64,8]{1,0:T(8,128)S(1)} %bitcast.54), channel_id=1, source_target_pairs={{1,0},{2,1},{3,2},{5,4},{6,5},{7,6},{9,8},{10,9},{11,10},{13,12},{... | collective-permute-start | bytes 6152 | tf_op jit(solution)/shard_map/ppermute | solution.py:370
  12.0 2.7 %copy-start.10 = (f32[64,8]{1,0:T(8,128)}, f32[64,8]{1,0:T(8,128)S(1)}, u32[]{:S(2)}) copy-start(f32[64,8]{1,0:T(8,128)S(1)} %collective-permute-done.2.hwl_ref) | copy-start | bytes 6148
  14.7 0.6 copy-start.11
  14.7 0.6 copy-start.8
  14.7 0.6 copy-start.9
  46.2 7.2 %copy-start.4 = (f32[512,128]{1,0:T(8,128)S(1)}, f32[512,128]{1,0:T(8,128)}, u32[]{:S(2)}) copy-start(f32[512,128]{1,0:T(8,128)} %get-tuple-element.23) | copy-start | bytes 786436
  48.7 14.9 %all-to-all-start.1 = ((f32[64,1,2,128]{3,2,1,0:T(2,128)}), f32[64,1,2,128]{3,2,1,0:T(2,128)S(1)}, u32[]{:S(2)}, u32[]{:S(2)}) async-start(f32[64,1,2,128]{3,2,1,0:T(2,128)} %shard_map.38), calls=%async_computation.1 | async-start | bytes 131072 | tf_op jit(solution)/shard_map/all_to_all | solution.py:387
  53.5 1.0 %copy-start.3 = (f32[512,128]{1,0:T(8,128)S(1)}, f32[512,128]{1,0:T(8,128)}, u32[]{:S(2)}) copy-start(f32[512,128]{1,0:T(8,128)} %get-tuple-element.24) | copy-start | bytes 786436
  54.4 0.9 %copy-start.2 = (f32[512,128]{1,0:T(8,128)S(1)}, f32[512,128]{1,0:T(8,128)}, u32[]{:S(2)}) copy-start(f32[512,128]{1,0:T(8,128)} %get-tuple-element.25) | copy-start | bytes 786436
  63.5 0.6 copy-start.1
  67.5 3.5 %collective-permute-start.6 = (f32[4,6,4,128]{3,2,1,0:T(4,128)}, f32[4,6,4,128]{3,2,1,0:T(4,128)S(1)}, u32[]{:S(2)}, u32[]{:S(2)}) collective-permute-start(f32[4,6,4,128]{3,2,1,0:T(4,128)} %get-tuple-element.26.refs_0_), channel_id=1, source_target_pairs={{0,3},{1,0},{2,1},{3,2},{4,7},{5,4},{6,5},{7,6},{8,11},{9,8},{10,9... | collective-permute-start | bytes 147464 | tf_op jit(solution)/shard_map/ppermute | solution.py:398
  68.4 4.7 %collective-permute-start.5 = (f32[4,6,4,128]{3,2,1,0:T(4,128)}, f32[4,6,4,128]{3,2,1,0:T(4,128)S(1)}, u32[]{:S(2)}, u32[]{:S(2)}) collective-permute-start(f32[4,6,4,128]{3,2,1,0:T(4,128)} %get-tuple-element.26.refs_0_), channel_id=1, source_target_pairs={{0,2},{1,3},{2,0},{3,1},{4,6},{5,7},{6,4},{7,5},{8,10},{9,11},{10,... | collective-permute-start | bytes 147464 | tf_op jit(solution)/shard_map/ppermute | solution.py:398
  70.6 4.5 %collective-permute-start.4 = (f32[4,6,4,128]{3,2,1,0:T(4,128)}, f32[4,6,4,128]{3,2,1,0:T(4,128)S(1)}, u32[]{:S(2)}, u32[]{:S(2)}) collective-permute-start(f32[4,6,4,128]{3,2,1,0:T(4,128)} %get-tuple-element.26.refs_0_), channel_id=1, source_target_pairs={{0,1},{1,2},{2,3},{3,0},{4,5},{5,6},{6,7},{7,4},{8,9},{9,10},{10,1... | collective-permute-start | bytes 147464 | tf_op jit(solution)/shard_map/ppermute | solution.py:398
  71.0 4.1 %copy-start.5 = (f32[4,6,4,128]{3,2,1,0:T(4,128)}, f32[4,6,4,128]{3,2,1,0:T(4,128)S(1)}, u32[]{:S(2)}) copy-start(f32[4,6,4,128]{3,2,1,0:T(4,128)S(1)} %collective-permute-done.6.refs_3_) | copy-start | bytes 147460
  73.0 2.0 %copy-start.6 = (f32[4,6,4,128]{3,2,1,0:T(4,128)}, f32[4,6,4,128]{3,2,1,0:T(4,128)S(1)}, u32[]{:S(2)}) copy-start(f32[4,6,4,128]{3,2,1,0:T(4,128)S(1)} %collective-permute-done.5.refs_2_) | copy-start | bytes 147460
  75.1 0.6 copy-start.7

commit v9 on v8

--- a/solution.py
+++ b/solution.py
@@ -207,8 +207,84 @@
     )(h2, hcl, hch, hwl, hwh, z2, spray, flags)
 
 
-def _width_kernel(nsub, yc_ref, vc_ref, wc_ref, bk_ref, a_ref, b_ref, c_ref,
-                  y_ref, v_ref, w_ref, sm_ref, cp_ref, d_ref):
+def _factor(n, subs, ld, st, a_ref, b_ref, c_ref, r_ref, cp_ref, v_ref, w_ref, unroll, shape):
+    zero = jnp.zeros(shape, F32)
+    one = jnp.ones(shape, F32)
+
+    def fwd(i, carries):
+        out = []
+        for s0, (cprev, vprev) in zip(subs, carries):
+            j = s0 + i
+            a = ld(a_ref, j)
+            r = 1.0 / (ld(b_ref, j) - a * cprev)
+            cn = ld(c_ref, j) * r
+            vprev = -(a * vprev) * r
+            st(r_ref, j, r)
+            st(cp_ref, j, cn)
+            st(v_ref, j, vprev)
+            out.append((cn, vprev))
+        return tuple(out)
+
+    carries = lax.fori_loop(0, n, fwd, tuple((zero, one) for _ in subs), unroll=unroll)
+    for s0, (cl, _) in zip(subs, carries):
+        st(w_ref, s0 + n - 1, -cl)
+
+    def bwd(jj, carries):
+        i = n - 2 - jj
+        out = []
+        for s0, (vn, wn) in zip(subs, carries):
+            j = s0 + i
+            cp = ld(cp_ref, j)
+            vn = ld(v_ref, j) - cp * vn
+            wn = -cp * wn
+            st(v_ref, j, vn)
+            st(w_ref, j, wn)
+            out.append((vn, wn))
+        return tuple(out)
+
+    lax.fori_loop(0, n - 1, bwd, tuple((vl, -cl) for cl, vl in carries), unroll=unroll)
+
+
+def _solve_rhs(n, subs, ld, st, a_ref, r_ref, cp_ref, d_ref, y_ref, unroll, shape):
+    zero = jnp.zeros(shape, F32)
+
+    def fwd(i, carries):
+        out = []
+        for s0, dprev in zip(subs, carries):
+            j = s0 + i
+            dn = (ld(d_ref, j) - ld(a_ref, j) * dprev) * ld(r_ref, j)
+            st(y_ref, j, dn)
+            out.append(dn)
+        return tuple(out)
+
+    carries = lax.fori_loop(0, n, fwd, tuple(zero for _ in subs), unroll=unroll)
+
+    def bwd(jj, carries):
+        i = n - 2 - jj
+        out = []
+        for s0, yn in zip(subs, carries):
+            j = s0 + i
+            yn = ld(y_ref, j) - ld(cp_ref, j) * yn
+            st(y_ref, j, yn)
+            out.append(yn)
+        return tuple(out)
+
+    lax.fori_loop(0, n - 1, bwd, carries, unroll=unroll)
+
+
+def _factor_kernel(nsub, a_ref, b_ref, c_ref, r_ref, cp_ref, v_ref, w_ref):
+    n = a_ref.shape[0] // nsub
+    subs = [q * n for q in range(nsub)]
+    _factor(n, subs, _lead_ld, _lead_st, a_ref, b_ref, c_ref, r_ref, cp_ref, v_ref, w_ref, 4, a_ref.shape[1:])
+
+
+def factor(a, b, c, nsub):
+    shp = jax.ShapeDtypeStruct(a.shape, F32)
+    return pl.pallas_call(functools.partial(_factor_kernel, nsub), out_shape=[shp] * 4)(a, b, c)
+
+
+def _width_kernel(nsub, yc_ref, vc_ref, wc_ref, bk_ref, a_ref, r_ref, cp_ref, v_ref, w_ref,
+                  y_ref, sm_ref, d_ref):
     sc = yc_ref[...] + vc_ref[...] * bk_ref[:, 0:1, :] + wc_ref[...] * bk_ref[:, 1:2, :]
     nt, ncl, nwl = sc.shape
     sc = sc.reshape(nt * ncl, nwl)
@@ -216,8 +292,7 @@
         d_ref[:, q, :] = sc[q * 128 : (q + 1) * 128, :].T
     n = a_ref.shape[0] // nsub
     subs = [q * n for q in range(nsub)]
-    shape = a_ref.shape[1:]
-    _sweep(n, subs, _lead_ld, _lead_st, a_ref, b_ref, c_ref, d_ref, y_ref, v_ref, w_ref, cp_ref, 4, shape)
+    _solve_rhs(n, subs, _lead_ld, _lead_st, a_ref, r_ref, cp_ref, d_ref, y_ref, 4, a_ref.shape[1:])
     for q, s0 in enumerate(subs):
         for k, val in enumerate(_summary_rows(_lead_ld, s0, n, y_ref, v_ref, w_ref)):
             sm_ref[q, k] = val
@@ -225,8 +300,8 @@
 
 def _thick_kernel(nsub, tsub, nw, me_ref, *refs):
     r_refs = refs[:nw]
-    (yw_ref, vw_ref, ww_ref, a_ref, b_ref, c_ref, h_ref,
-     o_ref, sw_ref, d_ref, y_ref, v_ref, w_ref, cp_ref) = refs[nw:]
+    (yw_ref, vw_ref, ww_ref, a_ref, r_ref, cp_ref, v_ref, w_ref, h_ref,
+     o_ref, sw_ref, d_ref, y_ref) = refs[nw:]
     lrw = _width_reduce(me_ref[0], r_refs)
     m = yw_ref.shape[0] // nsub
     for q in range(nsub):
@@ -239,7 +314,7 @@
     n = nt // tsub
     subs = [q * n for q in range(tsub)]
     shape = a_ref.shape[1:]
-    _sweep(n, subs, _lead_ld, _lead_st, a_ref, b_ref, c_ref, d_ref, y_ref, v_ref, w_ref, cp_ref, 4, shape)
+    _solve_rhs(n, subs, _lead_ld, _lead_st, a_ref, r_ref, cp_ref, d_ref, y_ref, 4, shape)
     sums = [tuple(_summary_rows(_lead_ld, s0, n, y_ref, v_ref, w_ref)) for s0 in subs]
     lrs = [None] * tsub
 
@@ -263,23 +338,23 @@
     )(a, b, c, d)
 
 
-def width_solve(yc, vc, wc, bk, a, b, c, nsub):
+def width_solve(yc, vc, wc, bk, a, fac, nsub):
     shp = jax.ShapeDtypeStruct(a.shape, F32)
     return pl.pallas_call(
         functools.partial(_width_kernel, nsub),
-        out_shape=[shp, shp, shp, jax.ShapeDtypeStruct((nsub, 6) + a.shape[1:], F32)],
-        scratch_shapes=[pltpu.VMEM(a.shape, F32), pltpu.VMEM(a.shape, F32)],
-    )(yc, vc, wc, bk, a, b, c)
-
-
-def thick_solve(me, got, yw, vw, ww, a, b, c, h, nsub, tsub):
+        out_shape=[shp, jax.ShapeDtypeStruct((nsub, 6) + a.shape[1:], F32)],
+        scratch_shapes=[pltpu.VMEM(a.shape, F32)],
+    )(yc, vc, wc, bk, a, *fac)
+
+
+def thick_solve(me, got, yw, vw, ww, a, fac, h, nsub, tsub):
     vm = pl.BlockSpec(memory_space=pltpu.VMEM)
     return pl.pallas_call(
         functools.partial(_thick_kernel, nsub, tsub, len(got)),
         out_shape=jax.ShapeDtypeStruct(a.shape, F32),
-        in_specs=[SMEM_SPEC] + [vm] * (len(got) + 7),
-        scratch_shapes=[pltpu.VMEM(yw.shape, F32)] + [pltpu.VMEM(a.shape, F32)] * 5,
-    )(me, *got, yw, vw, ww, a, b, c, h)
+        in_specs=[SMEM_SPEC] + [vm] * (len(got) + 9),
+        scratch_shapes=[pltpu.VMEM(yw.shape, F32)] + [pltpu.VMEM(a.shape, F32)] * 2,
+    )(me, *got, yw, vw, ww, a, *fac, h)
 
 
 def _reduce_blocks(nb, blk, emit, zero):
@@ -393,12 +468,15 @@
     def wl(x):
         return jnp.transpose(x, (2, 0, 1)).reshape(nwl, lines // 128, 128)
 
-    y, v, w, summ = width_solve(y, v, w, back, wl(wlo), wl(wmd), wl(whi), nsub)
+    wa = wl(wlo)
+    wfac = factor(wa, wl(wmd), wl(whi), nsub)
+    tfac = factor(tlo, tmd, thi, 4)
+    yw, summ = width_solve(y, v, w, back, wa, wfac, nsub)
     got = [summ] + [
         lax.ppermute(summ, "width", [(i, (i + q) % nw) for i in range(nw)]) for q in range(1, nw)
     ]
     me = wi.astype(jnp.int32).reshape(1)
-    return thick_solve(me, got, y, v, w, tlo, tmd, thi, h, nsub, 4)
+    return thick_solve(me, got, yw, wfac[2], wfac[3], tlo, tfac, h, nsub, 4)
 
 
 def solution(mesh):

time: 79.4 us -> 79.1 us (level)
  waiting for transfers between devices: 14 us -> 8.83 us
  Pallas kernels: 13.7 us -> 18.6 us
    pallas_call x1 -> x3, Pallas kernels: 3.34 us -> 8.25 us  [the longest x2 5.28 us: factor(): pl.pallas_call(functools.partial(_factor_kernel, nsub), out_shape=[shp] * 4)]
    all_to_all x1, waiting for transfers between devices: 7.32 us -> 4.53 us  [shards(): back = lax.all_to_all(lr, 'cast', 0, 0, tiled=True).reshape(nt, 2, nwl)]
    ppermute x3, waiting for transfers between devices: 4.06 us -> 1.57 us  [shards(): lax.ppermute(summ, 'width', [(i, (i + q) % nw) for i in range(nw)])]
  transfers between devices with their start and end apart: 8 -> 8, of which waited for: 4 -> 3; matrix products, arithmetic and copies ran while one was open for 5% -> 5% of each run, Pallas kernels for 0% -> 7%
where the time goes in v9:
time: 79.1 us; the launch traced here: 78.6 us
  blocking collectives  26.3 us (33%)
  Pallas kernels  18.6 us (24%)
  starting transfers between devices  17.4 us (22%)
  waiting for transfers between devices  8.83 us (11%)
  local copies, waits for them, and re-layouts  6.84 us (9%)
    all_to_all x1, blocking collectives, shards(): lax.all_to_all(summ.reshape(nc, nt // nc, 8, nwl), 'cast', 0, 0, tiled=True)  26.3 us
    pallas_call x2, Pallas kernels, factor(): pl.pallas_call(functools.partial(_factor_kernel, nsub), out_shape=[shp] * 4)  5.28 us
    all_to_all x1, starting transfers between devices, shards(): back = lax.all_to_all(lr, 'cast', 0, 0, tiled=True).reshape(nt, 2, nwl)  4.77 us
    pallas_call x1, Pallas kernels, prep_solve(): pl.pallas_call(functools.partial(_prep_kernel, n), out_shape=[shp] * 3 +...  4.63 us
    all_to_all x1, waiting for transfers between devices, shards(): back = lax.all_to_all(lr, 'cast', 0, 0, tiled=True).reshape(nt, 2, nwl)  4.53 us
    ppermute x1, starting transfers between devices, shards(): got_b = lax.ppermute(jnp.where(even, first, last), 'cast', across)  4.5 us
    ppermute x3, starting transfers between devices, shards(): lax.ppermute(summ, 'width', [(i, (i + q) % nw) for i in range(nw)])  3.48 us
    pallas_call x1, Pallas kernels, thick_solve(): pl.pallas_call(functools.partial(_thick_kernel, nsub, tsub, len(got)), ou...  3.25 us
  transfers between devices with their start and end apart: 8, of which 3 were waited for; matrix products, arithmetic and copies ran while one was open for 5% of the time, Pallas kernels for 7%

profile of v9, /device:TPU:1, one launch (start us, length us, event | category | flops | bytes accessed | tf_op | source)
XLA Modules:
  0.0 78.6 jit_solution(16005816290866947855)
XLA Ops:
  0.0 1.1 %fusion.1 = (f32[64,1,128]{2,1,0:T(1,128)S(1)}, f32[64,1,128]{2,1,0:T(1,128)S(1)}) fusion(f32[64,8,128]{2,1,0:T(8,128)} %refs_12_.1), kind=kLoop, calls=%fused_computation.3 | loop fusion | bytes 131072 | tf_op jit(solution)/shard_map/slice | solution.py:439
  1.2 4.5 %collective-permute-start.1 = (f32[64,128]{1,0:T(8,128)S(1)}, f32[64,128]{1,0:T(8,128)S(1)}, u32[]{:S(2)}, u32[]{:S(2)}) collective-permute-start(f32[64,128]{1,0:T(8,128)S(1)} %get-tuple-element.49), channel_id=1, source_target_pairs={{4,8},{12,16},{20,24},{28,32},{36,40},{44,48},{52,56},{60,64},{68,... | collective-permute-start | bytes 98312 | tf_op jit(solution)/shard_map/ppermute | solution.py:443
  5.7 0.1 collective-permute-start
  5.8 0.1 fusion
  5.9 0.4 copy.31
  6.4 3.2 %collective-permute-start.2 = (f32[64,8]{1,0:T(8,128)S(1)}, f32[64,8]{1,0:T(8,128)S(1)}, u32[]{:S(2)}, u32[]{:S(2)}) collective-permute-start(f32[64,8]{1,0:T(8,128)S(1)} %bitcast.54), channel_id=1, source_target_pairs={{0,1},{1,2},{2,3},{4,5},{5,6},{6,7},{8,9},{9,10},{10,11},{12,13},{... | collective-permute-start | bytes 6152 | tf_op jit(solution)/shard_map/ppermute | solution.py:444
  9.6 0.4 copy.32
  10.0 1.3 %collective-permute-start.3 = (f32[64,8]{1,0:T(8,128)S(1)}, f32[64,8]{1,0:T(8,128)S(1)}, u32[]{:S(2)}, u32[]{:S(2)}) collective-permute-start(f32[64,8]{1,0:T(8,128)S(1)} %bitcast.55), channel_id=1, source_target_pairs={{1,0},{2,1},{3,2},{5,4},{6,5},{7,6},{9,8},{10,9},{11,10},{13,12},{... | collective-permute-start | bytes 6152 | tf_op jit(solution)/shard_map/ppermute | solution.py:445
  11.3 0.1 stack.30
  11.4 0.5 stack.31.fl_ref
  11.9 2.7 %collective-permute-done.3.hwh_ref = f32[64,8]{1,0:T(8,128)S(1)} collective-permute-done((f32[64,8]{1,0:T(8,128)S(1)}, f32[64,8]{1,0:T(8,128)S(1)}, u32[]{:S(2)}, u32[]{:S(2)}) %collective-permute-start.3) | collective-permute-done | bytes 2080 | tf_op jit(solution)/shard_map/ppermute | solution.py:445
  14.7 0.6 copy-done.11
  15.3 4.6 %shard_map.37 = (f32[512,128]{1,0:T(8,128)}, f32[512,128]{1,0:T(8,128)}, f32[512,128]{1,0:T(8,128)}, f32[512,128]{1,0:T(8,128)}, f32[512,128]{1,0:T(8,128)}, /*i...) custom-call(f32[512,128]{1,0:T(8,128)} %bitcast.39, ...), custom_call_target="tpu_custom_call" | custom-call | tf_op jit(solution)/shard_map/pallas_call | solution.py:202
  19.9 26.3 %all_to_all.10.s_ref = f32[64,1,8,128]{3,2,1,0:T(8,128)} all-to-all(f32[64,1,8,128]{3,2,1,0:T(8,128)} %bitcast.51), channel_id=1, replica_groups=mesh['cast'=64,'width'=4] {'cast'}, dimensions={0} | all-to-all | bytes 524288 | tf_op jit(solution)/shard_map/all_to_all | solution.py:459
  46.2 2.5 %shard_map.38 = f32[64,1,2,128]{3,2,1,0:T(2,128)} custom-call(f32[64,1,8,128]{3,2,1,0:T(8,128)} %all_to_all.10.s_ref), custom_call_target="tpu_custom_call" | custom-call | tf_op jit(solution)/shard_map/pallas_call | solution.py:461
  48.7 4.8 %all-to-all-start.1 = ((f32[64,1,2,128]{3,2,1,0:T(2,128)}), f32[64,1,2,128]{3,2,1,0:T(2,128)S(1)}, u32[]{:S(2)}, u32[]{:S(2)}) async-start(f32[64,1,2,128]{3,2,1,0:T(2,128)} %shard_map.38), calls=%async_computation.1 | async-start | bytes 131072 | tf_op jit(solution)/shard_map/all_to_all | solution.py:462
  53.5 0.8 %copy.28.a_ref = f32[128,4,128]{2,1,0:T(4,128)} copy(f32[128,4,128]{0,2,1:T(8,128)S(1)} %bitcast.50) | data formatting | bytes 524288 | tf_op jit(solution)/shard_map/reshape | solution.py:469
  54.3 0.1 copy-done.3
  54.4 0.8 %copy.26.b_ref = f32[128,4,128]{2,1,0:T(4,128)} copy(f32[128,4,128]{0,2,1:T(8,128)S(1)} %bitcast.49) | data formatting | bytes 524288 | tf_op jit(solution)/shard_map/reshape | solution.py:469
  55.3 0.1 copy-done.2
  55.4 0.8 %copy.27.c_ref = f32[128,4,128]{2,1,0:T(4,128)} copy(f32[128,4,128]{0,2,1:T(8,128)S(1)} %bitcast.48) | data formatting | bytes 524288 | tf_op jit(solution)/shard_map/reshape | solution.py:469
  56.2 2.8 %shard_map.39 = (f32[128,4,128]{2,1,0:T(4,128)}, f32[128,4,128]{2,1,0:T(4,128)}, f32[128,4,128]{2,1,0:T(4,128)}, f32[128,4,128]{2,1,0:T(4,128)}) custom-call(f32[128,4,128]{2,1,0:T(4,128)} %copy.28.a_ref, f32[128,4,128]{2,1,0:T(4,128)} %copy.26.b_ref, f32[128,4,128]{2,1,0:T(4,128)} %copy.27.c_ref), custom_call_target="tpu_custom_call" | custom-call | tf_op jit(solution)/shard_map/pallas_call | solution.py:283
  59.0 4.5 %all-to-all-done.1 = f32[64,1,2,128]{3,2,1,0:T(2,128)S(1)} async-done(((f32[64,1,2,128]{3,2,1,0:T(2,128)}), f32[64,1,2,128]{3,2,1,0:T(2,128)S(1)}, u32[]{:S(2)}, u32[]{:S(2)}) %all-to-all-start.1) | async-done | bytes 65568 | tf_op jit(solution)/shard_map/all_to_all | solution.py:462
  63.6 0.6 copy-done.1
  64.2 3.0 %shard_map.40 = (f32[128,4,128]{2,1,0:T(4,128)}, f32[4,6,4,128]{3,2,1,0:T(4,128)}) custom-call(f32[64,8,128]{2,1,0:T(8,128)} %bitcast.44, f32[64,8,128]{2,1,0:T(8,128)} %bitcast.45, f32[64,8,128]{2,1,0:T(8,128)} %bitcast.46, f32[64,2,128]{2,1,0:T(2,128)} %bitcast.47, f32[128,4,128]{2,1,0:T(4,128)} %copy.28.a_ref, f32[128,4,128]{2,1,0:T(4,128)} %get-tuple-element.32.r_ref, ...), custom_call_target="tpu_custom_call" | custom-call | tf_op jit(solution)/shard_map/pallas_call | solution.py:343
  67.2 0.9 %collective-permute-start.6 = (f32[4,6,4,128]{3,2,1,0:T(4,128)}, f32[4,6,4,128]{3,2,1,0:T(4,128)S(1)}, u32[]{:S(2)}, u32[]{:S(2)}) collective-permute-start(f32[4,6,4,128]{3,2,1,0:T(4,128)} %get-tuple-element.36.refs_0_), channel_id=1, source_target_pairs={{0,3},{1,0},{2,1},{3,2},{4,7},{5,4},{6,5},{7,6},{8,11},{9,8},{10,9... | collective-permute-start | bytes 147464 | tf_op jit(solution)/shard_map/ppermute | solution.py:476
  68.0 2.2 %collective-permute-start.5 = (f32[4,6,4,128]{3,2,1,0:T(4,128)}, f32[4,6,4,128]{3,2,1,0:T(4,128)S(1)}, u32[]{:S(2)}, u32[]{:S(2)}) collective-permute-start(f32[4,6,4,128]{3,2,1,0:T(4,128)} %get-tuple-element.36.refs_0_), channel_id=1, source_target_pairs={{0,2},{1,3},{2,0},{3,1},{4,6},{5,7},{6,4},{7,5},{8,10},{9,11},{10,... | collective-permute-start | bytes 147464 | tf_op jit(solution)/shard_map/ppermute | solution.py:476
  70.2 0.4 collective-permute-start.4
  70.6 2.5 %shard_map.41 = (f32[64,8,128]{2,1,0:T(8,128)}, f32[64,8,128]{2,1,0:T(8,128)}, f32[64,8,128]{2,1,0:T(8,128)}, f32[64,8,128]{2,1,0:T(8,128)}) custom-call(f32[64,8,128]{2,1,0:T(8,128)} %bitcast.40, f32[64,8,128]{2,1,0:T(8,128)} %bitcast.42, f32[64,8,128]{2,1,0:T(8,128)} %bitcast.43), custom_call_target="tpu_custom_call" | custom-call | tf_op jit(solution)/shard_map/pallas_call | solution.py:283
  73.1 1.6 %collective-permute-done.4.refs_1_ = f32[4,6,4,128]{3,2,1,0:T(4,128)S(1)} collective-permute-done((f32[4,6,4,128]{3,2,1,0:T(4,128)}, f32[4,6,4,128]{3,2,1,0:T(4,128)S(1)}, u32[]{:S(2)}, u32[]{:S(2)}) %collective-permute-start.4) | collective-permute-done | bytes 49184 | tf_op jit(solution)/shard_map/ppermute | solution.py:476
  74.7 0.6 copy-done.7
  75.3 3.2 %shard_map.42 = f32[64,8,128]{2,1,0:T(8,128)} custom-call(s32[1]{0:T(128)} %bitcast.me_ref, f32[4,6,4,128]{3,2,1,0:T(4,128)} %get-tuple-element.36.refs_0_, f32[4,6,4,128]{3,2,1,0:T(4,128)} %copy-done.7, f32[4,6,4,128]{3,2,1,0:T(4,128)} %copy-done.6, f32[4,6,4,128]{3,2,1,0:T(4,128)} %copy-done.5, f32[128,4,128]{2,1,0:T(4,128)} %get-tuple-element.37.refs_4_, ...), custom_call_target="tpu_custom_call" | custom-call | tf_op jit(solution)/shard_map/pallas_call | solution.py:352
  (25 shorter events, 0.1 us)
Async XLA Ops:
  0.0 5.8 %copy-start = (f32[64,8,128]{2,1,0:T(8,128)S(1)}, f32[64,8,128]{2,1,0:T(8,128)}, u32[]{:S(2)}) copy-start(f32[64,8,128]{2,1,0:T(8,128)} %refs_12_.1) | copy-start | bytes 786436
  1.2 13.5 %collective-permute-start.1 = (f32[64,128]{1,0:T(8,128)S(1)}, f32[64,128]{1,0:T(8,128)S(1)}, u32[]{:S(2)}, u32[]{:S(2)}) collective-permute-start(f32[64,128]{1,0:T(8,128)S(1)} %get-tuple-element.49), channel_id=1, source_target_pairs={{4,8},{12,16},{20,24},{28,32},{36,40},{44,48},{52,56},{60,64},{68,... | collective-permute-start | bytes 98312 | tf_op jit(solution)/shard_map/ppermute | solution.py:443
  5.7 9.0 %collective-permute-start = (f32[64,128]{1,0:T(8,128)S(1)}, f32[64,128]{1,0:T(8,128)S(1)}, u32[]{:S(2)}, u32[]{:S(2)}) collective-permute-start(f32[64,128]{1,0:T(8,128)S(1)} %get-tuple-element.50), channel_id=1, source_target_pairs={{0,4},{4,0},{8,12},{12,8},{16,20},{20,16},{24,28},{28,24},{32,36},... | collective-permute-start | bytes 98312 | tf_op jit(solution)/shard_map/ppermute | solution.py:442
  6.4 5.6 %collective-permute-start.2 = (f32[64,8]{1,0:T(8,128)S(1)}, f32[64,8]{1,0:T(8,128)S(1)}, u32[]{:S(2)}, u32[]{:S(2)}) collective-permute-start(f32[64,8]{1,0:T(8,128)S(1)} %bitcast.54), channel_id=1, source_target_pairs={{0,1},{1,2},{2,3},{4,5},{5,6},{6,7},{8,9},{9,10},{10,11},{12,13},{... | collective-permute-start | bytes 6152 | tf_op jit(solution)/shard_map/ppermute | solution.py:444
  10.0 4.7 %collective-permute-start.3 = (f32[64,8]{1,0:T(8,128)S(1)}, f32[64,8]{1,0:T(8,128)S(1)}, u32[]{:S(2)}, u32[]{:S(2)}) collective-permute-start(f32[64,8]{1,0:T(8,128)S(1)} %bitcast.55), channel_id=1, source_target_pairs={{1,0},{2,1},{3,2},{5,4},{6,5},{7,6},{9,8},{10,9},{11,10},{13,12},{... | collective-permute-start | bytes 6152 | tf_op jit(solution)/shard_map/ppermute | solution.py:445
  11.9 2.8 %copy-start.10 = (f32[64,8]{1,0:T(8,128)}, f32[64,8]{1,0:T(8,128)S(1)}, u32[]{:S(2)}) copy-start(f32[64,8]{1,0:T(8,128)S(1)} %collective-permute-done.2.hwl_ref) | copy-start | bytes 6148
  14.7 0.6 copy-start.11
  14.7 0.6 copy-start.8
  14.7 0.6 copy-start.9
  46.2 7.2 %copy-start.4 = (f32[512,128]{1,0:T(8,128)S(1)}, f32[512,128]{1,0:T(8,128)}, u32[]{:S(2)}) copy-start(f32[512,128]{1,0:T(8,128)} %get-tuple-element.29) | copy-start | bytes 786436
  48.7 14.9 %all-to-all-start.1 = ((f32[64,1,2,128]{3,2,1,0:T(2,128)}), f32[64,1,2,128]{3,2,1,0:T(2,128)S(1)}, u32[]{:S(2)}, u32[]{:S(2)}) async-start(f32[64,1,2,128]{3,2,1,0:T(2,128)} %shard_map.38), calls=%async_computation.1 | async-start | bytes 131072 | tf_op jit(solution)/shard_map/all_to_all | solution.py:462
  53.5 1.0 %copy-start.3 = (f32[512,128]{1,0:T(8,128)S(1)}, f32[512,128]{1,0:T(8,128)}, u32[]{:S(2)}) copy-start(f32[512,128]{1,0:T(8,128)} %get-tuple-element.30) | copy-start | bytes 786436
  54.4 0.9 %copy-start.2 = (f32[512,128]{1,0:T(8,128)S(1)}, f32[512,128]{1,0:T(8,128)}, u32[]{:S(2)}) copy-start(f32[512,128]{1,0:T(8,128)} %get-tuple-element.31) | copy-start | bytes 786436
  63.6 0.6 copy-start.1
  67.2 6.0 %collective-permute-start.6 = (f32[4,6,4,128]{3,2,1,0:T(4,128)}, f32[4,6,4,128]{3,2,1,0:T(4,128)S(1)}, u32[]{:S(2)}, u32[]{:S(2)}) collective-permute-start(f32[4,6,4,128]{3,2,1,0:T(4,128)} %get-tuple-element.36.refs_0_), channel_id=1, source_target_pairs={{0,3},{1,0},{2,1},{3,2},{4,7},{5,4},{6,5},{7,6},{8,11},{9,8},{10,9... | collective-permute-start | bytes 147464 | tf_op jit(solution)/shard_map/ppermute | solution.py:476
  68.0 5.1 %collective-permute-start.5 = (f32[4,6,4,128]{3,2,1,0:T(4,128)}, f32[4,6,4,128]{3,2,1,0:T(4,128)S(1)}, u32[]{:S(2)}, u32[]{:S(2)}) collective-permute-start(f32[4,6,4,128]{3,2,1,0:T(4,128)} %get-tuple-element.36.refs_0_), channel_id=1, source_target_pairs={{0,2},{1,3},{2,0},{3,1},{4,6},{5,7},{6,4},{7,5},{8,10},{9,11},{10,... | collective-permute-start | bytes 147464 | tf_op jit(solution)/shard_map/ppermute | solution.py:476
  70.2 4.5 %collective-permute-start.4 = (f32[4,6,4,128]{3,2,1,0:T(4,128)}, f32[4,6,4,128]{3,2,1,0:T(4,128)S(1)}, u32[]{:S(2)}, u32[]{:S(2)}) collective-permute-start(f32[4,6,4,128]{3,2,1,0:T(4,128)} %get-tuple-element.36.refs_0_), channel_id=1, source_target_pairs={{0,1},{1,2},{2,3},{3,0},{4,5},{5,6},{6,7},{7,4},{8,9},{9,10},{10,1... | collective-permute-start | bytes 147464 | tf_op jit(solution)/shard_map/ppermute | solution.py:476
  73.1 1.6 %copy-start.5 = (f32[4,6,4,128]{3,2,1,0:T(4,128)}, f32[4,6,4,128]{3,2,1,0:T(4,128)S(1)}, u32[]{:S(2)}) copy-start(f32[4,6,4,128]{3,2,1,0:T(4,128)S(1)} %collective-permute-done.6.refs_3_) | copy-start | bytes 147460
  73.1 1.6 %copy-start.6 = (f32[4,6,4,128]{3,2,1,0:T(4,128)}, f32[4,6,4,128]{3,2,1,0:T(4,128)S(1)}, u32[]{:S(2)}) copy-start(f32[4,6,4,128]{3,2,1,0:T(4,128)S(1)} %collective-permute-done.5.refs_2_) | copy-start | bytes 147460
  74.7 0.6 copy-start.7

commit v10 on v8

--- a/solution.py
+++ b/solution.py
@@ -98,9 +98,111 @@
     ref[i] = val
 
 
-def _prep_kernel(n, h_ref, hcl_ref, hch_ref, hwl_ref, hwh_ref, z_ref, sp_ref, fl_ref,
-                 y_ref, v_ref, w_ref, sm_ref, wa_ref, wb_ref, wc_ref, ta_ref, tb_ref, tc_ref,
-                 tp_ref, kp_ref, sp2_ref, a_ref, b_ref, c_ref, d_ref, cp_ref):
+def _loop(n, body, carry, unroll):
+    if unroll is True:
+        for i in range(n):
+            carry = body(i, carry)
+        return carry
+    return lax.fori_loop(0, n, body, carry, unroll=unroll)
+
+
+def _factor(n, subs, ld, st, a_ref, b_ref, c_ref, r_ref, cp_ref, v_ref, w_ref, unroll, shape):
+    zero = jnp.zeros(shape, F32)
+    one = jnp.ones(shape, F32)
+
+    def fwd(i, carries):
+        out = []
+        for s0, (cprev, vprev) in zip(subs, carries):
+            j = s0 + i
+            a = ld(a_ref, j)
+            r = 1.0 / (ld(b_ref, j) - a * cprev)
+            cn = ld(c_ref, j) * r
+            vprev = -(a * vprev) * r
+            st(r_ref, j, r)
+            st(cp_ref, j, cn)
+            st(v_ref, j, vprev)
+            out.append((cn, vprev))
+        return tuple(out)
+
+    carries = _loop(n, fwd, tuple((zero, one) for _ in subs), unroll)
+    for s0, (cl, _) in zip(subs, carries):
+        st(w_ref, s0 + n - 1, -cl)
+
+    def bwd(jj, carries):
+        i = n - 2 - jj
+        out = []
+        for s0, (vn, wn) in zip(subs, carries):
+            j = s0 + i
+            cp = ld(cp_ref, j)
+            vn = ld(v_ref, j) - cp * vn
+            wn = -cp * wn
+            st(v_ref, j, vn)
+            st(w_ref, j, wn)
+            out.append((vn, wn))
+        return tuple(out)
+
+    _loop(n - 1, bwd, tuple((vl, -cl) for cl, vl in carries), unroll)
+
+
+def _solve_rhs(n, subs, ld, st, a_ref, r_ref, cp_ref, d_ref, y_ref, unroll, shape):
+    zero = jnp.zeros(shape, F32)
+
+    def fwd(i, carries):
+        out = []
+        for s0, dprev in zip(subs, carries):
+            j = s0 + i
+            dn = (ld(d_ref, j) - ld(a_ref, j) * dprev) * ld(r_ref, j)
+            st(y_ref, j, dn)
+            out.append(dn)
+        return tuple(out)
+
+    carries = _loop(n, fwd, tuple(zero for _ in subs), unroll)
+
+    def bwd(jj, carries):
+        i = n - 2 - jj
+        out = []
+        for s0, yn in zip(subs, carries):
+            j = s0 + i
+            yn = ld(y_ref, j) - ld(cp_ref, j) * yn
+            st(y_ref, j, yn)
+            out.append(yn)
+        return tuple(out)
+
+    _loop(n - 1, bwd, carries, unroll)
+
+
+def _factor_kernel(nsub, a_ref, b_ref, c_ref, r_ref, cp_ref, v_ref, w_ref):
+    n = a_ref.shape[0] // nsub
+    subs = [q * n for q in range(nsub)]
+    _factor(n, subs, _lead_ld, _lead_st, a_ref, b_ref, c_ref, r_ref, cp_ref, v_ref, w_ref, 4, a_ref.shape[1:])
+
+
+def factor(a, b, c, nsub):
+    shp = jax.ShapeDtypeStruct(a.shape, F32)
+    return pl.pallas_call(functools.partial(_factor_kernel, nsub), out_shape=[shp] * 4)(a, b, c)
+
+
+def _width_faces(n, c, T0, k0, s0, lane, wlo, whi, fl_ref):
+    nwl = T0.shape[1]
+    g_w = nwl * nwl / 4.0 * 0.5
+    if wlo is None:
+        wlo = (T0, k0, s0)
+        whi = (T0, k0, s0)
+        e_lo, e_hi = 0.0, 0.0
+    else:
+        e_lo, e_hi = fl_ref[2], fl_ref[3]
+    Twm, kwm, swm = (jnp.where(lane == 0, b, pltpu.roll(f, 1, 1)) for f, b in zip((T0, k0, s0), wlo))
+    Twp, kwp, swp = (
+        jnp.where(lane == nwl - 1, b, pltpu.roll(f, nwl - 1, 1)) for f, b in zip((T0, k0, s0), whi)
+    )
+    gwl = g_w * (k0 + kwm) * jnp.where(lane == 0, e_lo, 1.0)
+    gwh = g_w * (kwp + k0) * jnp.where(lane == nwl - 1, e_hi, 1.0)
+    return Twm, swm, Twp, swp, gwl, gwh
+
+
+def _prep_kernel(n, h_ref, hcl_ref, hch_ref, z_ref, sp_ref, fl_ref,
+                 y_ref, v_ref, w_ref, sm_ref, a_ref, r_ref, cp_ref, ta_ref, tb_ref, tc_ref,
+                 tp_ref, kp_ref, sp2_ref, b_ref, c_ref, d_ref):
     rows, nwl = h_ref.shape
     nt = rows // n
     hot, cond, slope = medium_parameters(h_ref[...])
@@ -120,10 +222,7 @@
     cast_lo = medium_parameters(jnp.where(even, got_b, got_a))
     cast_hi = medium_parameters(jnp.where(even, got_a, got_b))
     g_c = n * n * 4.0 * 0.5
-    g_w = nwl * nwl / 4.0 * 0.5
     g_t = nt * nt / 4.0 * 0.5
-    edge_wl = jnp.where(lane == 0, fl_ref[2], 1.0)
-    edge_wh = jnp.where(lane == nwl - 1, fl_ref[3], 1.0)
     nz = sp_ref.shape[0]
 
     def surf_row(zr):
@@ -144,20 +243,13 @@
             Tq, kq, sq = (row(r, n + c + 1) for r in (tp_ref, kp_ref, sp2_ref))
         Ttm, ktm, stm = (row(r, c) for r in (tp_ref, kp_ref, sp2_ref))
         Ttp, ktp, stp = (row(r, 2 * n + c) for r in (tp_ref, kp_ref, sp2_ref))
-        wlo = medium_parameters(hwl_ref[:, c : c + 1])
-        whi = medium_parameters(hwh_ref[:, c : c + 1])
-        Twm, kwm, swm = (jnp.where(lane == 0, b, pltpu.roll(f, 1, 1)) for f, b in zip((T0, k0, s0), wlo))
-        Twp, kwp, swp = (
-            jnp.where(lane == nwl - 1, b, pltpu.roll(f, nwl - 1, 1)) for f, b in zip((T0, k0, s0), whi)
-        )
+        Twm, _, Twp, _, gwl, gwh = _width_faces(n, c, T0, k0, s0, lane, None, None, fl_ref)
         gcl = g_c * (k0 + km)
         if c == 0:
             gcl = gcl * fl_ref[0]
         gch = g_c * (kq + k0)
         if c == n - 1:
             gch = gch * fl_ref[1]
-        gwl = g_w * (k0 + kwm) * edge_wl
-        gwh = g_w * (kwp + k0) * edge_wh
         gtl = jnp.where(tix == 0, 0.0, g_t * (k0 + ktm))
         gth = jnp.where(tix == nt - 1, 0.0, g_t * (ktp + k0))
         s_lo = surf_row(z_ref[c : c + 1, :])
@@ -172,9 +264,6 @@
         c_ref[sel, :] = -gch * sq
         b_ref[sel, :] = 1.0 + s0 * (gcl + gch)
         d_ref[sel, :] = ex
-        wa_ref[sel, :] = -gwl * swm
-        wc_ref[sel, :] = -gwh * swp
-        wb_ref[sel, :] = 1.0 + s0 * (gwl + gwh)
         ta_ref[sel, :] = -gtl * stm
         tc_ref[sel, :] = -gth * stp
         tb_ref[sel, :] = 1.0 + s0 * (gtl + gth + rim)
@@ -186,14 +275,15 @@
         ref[pl.ds(i, nt, stride=n), :] = val
 
     shape = (nt, nwl)
-    _sweep(n, [0], ld, st, a_ref, b_ref, c_ref, d_ref, y_ref, v_ref, w_ref, cp_ref, True, shape)
+    _factor(n, [0], ld, st, a_ref, b_ref, c_ref, r_ref, cp_ref, v_ref, w_ref, True, shape)
+    _solve_rhs(n, [0], ld, st, a_ref, r_ref, cp_ref, d_ref, y_ref, True, shape)
     rws = _summary_rows(ld, 0, n, y_ref, v_ref, w_ref)
     rws += [jnp.zeros(shape, F32)] * (8 - len(rws))
     for k, val in enumerate(rws):
         sm_ref[pl.ds(k, nt, stride=8), :] = val
 
 
-def prep_solve(h2, hcl, hch, hwl, hwh, z2, spray, flags, n):
+def prep_solve(h2, hcl, hch, z2, spray, flags, n):
     rows, nwl = h2.shape
     nt = rows // n
     shp = jax.ShapeDtypeStruct(h2.shape, F32)
@@ -202,13 +292,85 @@
     return pl.pallas_call(
         functools.partial(_prep_kernel, n),
         out_shape=[shp] * 3 + [jax.ShapeDtypeStruct((nt * 8, nwl), F32)] + [shp] * 6,
-        in_specs=[vm] * 6 + [SMEM_SPEC, SMEM_SPEC],
-        scratch_shapes=[pad, pad, pad] + [pltpu.VMEM(h2.shape, F32)] * 5,
-    )(h2, hcl, hch, hwl, hwh, z2, spray, flags)
-
-
-def _width_kernel(nsub, yc_ref, vc_ref, wc_ref, bk_ref, a_ref, b_ref, c_ref,
-                  y_ref, v_ref, w_ref, sm_ref, cp_ref, d_ref):
+        in_specs=[vm] * 4 + [SMEM_SPEC, SMEM_SPEC],
+        scratch_shapes=[pad, pad, pad] + [pltpu.VMEM(h2.shape, F32)] * 3,
+    )(h2, hcl, hch, z2, spray, flags)
+
+
+def _edge_kernel(n, h_ref, hwl_ref, hwh_ref, fl_ref, a_ref, r_ref, cp_ref, y_ref, sm_ref,
+                 yo_ref, smo_ref, d_ref, e_ref):
+    rows, nwl = h_ref.shape
+    nt = rows // n
+    lane = lax.broadcasted_iota(jnp.int32, (nt, nwl), 1)
+    for c in range(n):
+        sel = pl.ds(c, nt, stride=n)
+        T0, k0, s0 = medium_parameters(h_ref[sel, :])
+        wlo = medium_parameters(hwl_ref[:, c : c + 1])
+        whi = medium_parameters(hwh_ref[:, c : c + 1])
+        Twm, _, Twp, _, gwl, gwh = _width_faces(n, c, T0, k0, s0, lane, wlo, whi, fl_ref)
+        edge = jnp.where(lane == 0, -gwl * (T0 - Twm), jnp.where(lane == nwl - 1, gwh * (Twp - T0), 0.0))
+        d_ref[sel, :] = edge
+
+    def ld(ref, i):
+        return ref[pl.ds(i, nt, stride=n), :]
+
+    def st(ref, i, val):
+        ref[pl.ds(i, nt, stride=n), :] = val
+
+    _solve_rhs(n, [0], ld, st, a_ref, r_ref, cp_ref, d_ref, e_ref, True, (nt, nwl))
+    yo_ref[...] = y_ref[...] + e_ref[...]
+    smo_ref[...] = sm_ref[...]
+    smo_ref[pl.ds(0, nt, stride=8), :] = sm_ref[pl.ds(0, nt, stride=8), :] + ld(e_ref, 0)
+    smo_ref[pl.ds(3, nt, stride=8), :] = sm_ref[pl.ds(3, nt, stride=8), :] + ld(e_ref, n - 1)
+
+
+def edge_solve(h2, hwl, hwh, flags, a, r, cp, y, sm, n):
+    vm = pl.BlockSpec(memory_space=pltpu.VMEM)
+    return pl.pallas_call(
+        functools.partial(_edge_kernel, n),
+        out_shape=[jax.ShapeDtypeStruct(y.shape, F32), jax.ShapeDtypeStruct(sm.shape, F32)],
+        in_specs=[vm] * 3 + [SMEM_SPEC] + [vm] * 5,
+        scratch_shapes=[pltpu.VMEM(y.shape, F32)] * 2,
+    )(h2, hwl, hwh, flags, a, r, cp, y, sm)
+
+
+def _wfactor_kernel(n, nsub, h_ref, hwl_ref, hwh_ref, fl_ref, a_ref, r_ref, cp_ref, v_ref, w_ref,
+                    at_ref, bt_ref, ct_ref, b_ref, c_ref):
+    rows, nwl = h_ref.shape
+    nt = rows // n
+    lane = lax.broadcasted_iota(jnp.int32, (nt, nwl), 1)
+    for c in range(n):
+        sel = pl.ds(c, nt, stride=n)
+        T0, k0, s0 = medium_parameters(h_ref[sel, :])
+        wlo = medium_parameters(hwl_ref[:, c : c + 1])
+        whi = medium_parameters(hwh_ref[:, c : c + 1])
+        _, swm, _, swp, gwl, gwh = _width_faces(n, c, T0, k0, s0, lane, wlo, whi, fl_ref)
+        at_ref[sel, :] = -gwl * swm
+        ct_ref[sel, :] = -gwh * swp
+        bt_ref[sel, :] = 1.0 + s0 * (gwl + gwh)
+    for src, dst in ((at_ref, a_ref), (bt_ref, b_ref), (ct_ref, c_ref)):
+        for q in range(dst.shape[1]):
+            dst[:, q, :] = src[q * 128 : (q + 1) * 128, :].T
+    m = a_ref.shape[0] // nsub
+    subs = [q * m for q in range(nsub)]
+    _factor(m, subs, _lead_ld, _lead_st, a_ref, b_ref, c_ref, r_ref, cp_ref, v_ref, w_ref, 4, a_ref.shape[1:])
+
+
+def wfactor(h2, hwl, hwh, flags, n, nsub):
+    rows, nwl = h2.shape
+    wshape = (nwl, rows // 128, 128)
+    shp = jax.ShapeDtypeStruct(wshape, F32)
+    vm = pl.BlockSpec(memory_space=pltpu.VMEM)
+    return pl.pallas_call(
+        functools.partial(_wfactor_kernel, n, nsub),
+        out_shape=[shp] * 5,
+        in_specs=[vm] * 3 + [SMEM_SPEC],
+        scratch_shapes=[pltpu.VMEM(h2.shape, F32)] * 3 + [pltpu.VMEM(wshape, F32)] * 2,
+    )(h2, hwl, hwh, flags)
+
+
+def _width_kernel(nsub, yc_ref, vc_ref, wc_ref, bk_ref, a_ref, r_ref, cp_ref, v_ref, w_ref,
+                  y_ref, sm_ref, d_ref):
     sc = yc_ref[...] + vc_ref[...] * bk_ref[:, 0:1, :] + wc_ref[...] * bk_ref[:, 1:2, :]
     nt, ncl, nwl = sc.shape
     sc = sc.reshape(nt * ncl, nwl)
@@ -216,8 +378,7 @@
         d_ref[:, q, :] = sc[q * 128 : (q + 1) * 128, :].T
     n = a_ref.shape[0] // nsub
     subs = [q * n for q in range(nsub)]
-    shape = a_ref.shape[1:]
-    _sweep(n, subs, _lead_ld, _lead_st, a_ref, b_ref, c_ref, d_ref, y_ref, v_ref, w_ref, cp_ref, 4, shape)
+    _solve_rhs(n, subs, _lead_ld, _lead_st, a_ref, r_ref, cp_ref, d_ref, y_ref, 4, a_ref.shape[1:])
     for q, s0 in enumerate(subs):
         for k, val in enumerate(_summary_rows(_lead_ld, s0, n, y_ref, v_ref, w_ref)):
             sm_ref[q, k] = val
@@ -225,8 +386,8 @@
 
 def _thick_kernel(nsub, tsub, nw, me_ref, *refs):
     r_refs = refs[:nw]
-    (yw_ref, vw_ref, ww_ref, a_ref, b_ref, c_ref, h_ref,
-     o_ref, sw_ref, d_ref, y_ref, v_ref, w_ref, cp_ref) = refs[nw:]
+    (yw_ref, vw_ref, ww_ref, a_ref, r_ref, cp_ref, v_ref, w_ref, h_ref,
+     o_ref, sw_ref, d_ref, y_ref) = refs[nw:]
     lrw = _width_reduce(me_ref[0], r_refs)
     m = yw_ref.shape[0] // nsub
     for q in range(nsub):
@@ -239,7 +400,7 @@
     n = nt // tsub
     subs = [q * n for q in range(tsub)]
     shape = a_ref.shape[1:]
-    _sweep(n, subs, _lead_ld, _lead_st, a_ref, b_ref, c_ref, d_ref, y_ref, v_ref, w_ref, cp_ref, 4, shape)
+    _solve_rhs(n, subs, _lead_ld, _lead_st, a_ref, r_ref, cp_ref, d_ref, y_ref, 4, shape)
     sums = [tuple(_summary_rows(_lead_ld, s0, n, y_ref, v_ref, w_ref)) for s0 in subs]
     lrs = [None] * tsub
 
@@ -263,23 +424,23 @@
     )(a, b, c, d)
 
 
-def width_solve(yc, vc, wc, bk, a, b, c, nsub):
+def width_solve(yc, vc, wc, bk, a, fac, nsub):
     shp = jax.ShapeDtypeStruct(a.shape, F32)
     return pl.pallas_call(
         functools.partial(_width_kernel, nsub),
-        out_shape=[shp, shp, shp, jax.ShapeDtypeStruct((nsub, 6) + a.shape[1:], F32)],
-        scratch_shapes=[pltpu.VMEM(a.shape, F32), pltpu.VMEM(a.shape, F32)],
-    )(yc, vc, wc, bk, a, b, c)
-
-
-def thick_solve(me, got, yw, vw, ww, a, b, c, h, nsub, tsub):
+        out_shape=[shp, jax.ShapeDtypeStruct((nsub, 6) + a.shape[1:], F32)],
+        scratch_shapes=[pltpu.VMEM(a.shape, F32)],
+    )(yc, vc, wc, bk, a, *fac)
+
+
+def thick_solve(me, got, yw, vw, ww, a, fac, h, nsub, tsub):
     vm = pl.BlockSpec(memory_space=pltpu.VMEM)
     return pl.pallas_call(
         functools.partial(_thick_kernel, nsub, tsub, len(got)),
         out_shape=jax.ShapeDtypeStruct(a.shape, F32),
-        in_specs=[SMEM_SPEC] + [vm] * (len(got) + 7),
-        scratch_shapes=[pltpu.VMEM(yw.shape, F32)] + [pltpu.VMEM(a.shape, F32)] * 5,
-    )(me, *got, yw, vw, ww, a, b, c, h)
+        in_specs=[SMEM_SPEC] + [vm] * (len(got) + 9),
+        scratch_shapes=[pltpu.VMEM(yw.shape, F32)] + [pltpu.VMEM(a.shape, F32)] * 2,
+    )(me, *got, yw, vw, ww, a, *fac, h)
 
 
 def _reduce_blocks(nb, blk, emit, zero):
@@ -374,13 +535,11 @@
     width_low = (wi > 0).astype(F32)
     width_high = (wi < nw - 1).astype(F32)
     flags = jnp.stack([cast_low, cast_high, width_low, width_high, even.astype(F32)])
-    outs = prep_solve(
-        h.reshape(nt * ncl, nwl), got_a, got_b,
-        h_wl, h_wh,
-        zones.reshape(2 * ncl, nwl), spray_coef, flags, ncl,
-    )
-    y, v, w, summ = outs[:4]
-    wlo, wmd, whi, tlo, tmd, thi = (x.reshape(nt, ncl, nwl) for x in outs[4:])
+    h2 = h.reshape(nt * ncl, nwl)
+    outs = prep_solve(h2, got_a, got_b, zones.reshape(2 * ncl, nwl), spray_coef, flags, ncl)
+    y, v, w, summ, a_c, r_c, cp_c = outs[:7]
+    tlo, tmd, thi = (x.reshape(nt, ncl, nwl) for x in outs[7:])
+    y, summ = edge_solve(h2, h_wl, h_wh, flags, a_c, r_c, cp_c, y, summ, ncl)
     recv = lax.all_to_all(summ.reshape(nc, nt // nc, 8, nwl), "cast", 0, 0, tiled=True)
     lr_shape = recv.shape[:2] + (2, nwl)
     lr = pl.pallas_call(_cast_reduced_kernel, out_shape=jax.ShapeDtypeStruct(lr_shape, F32))(recv)
@@ -393,12 +552,14 @@
     def wl(x):
         return jnp.transpose(x, (2, 0, 1)).reshape(nwl, lines // 128, 128)
 
-    y, v, w, summ = width_solve(y, v, w, back, wl(wlo), wl(wmd), wl(whi), nsub)
+    wa, *wfac = wfactor(h2, h_wl, h_wh, flags, ncl, nsub)
+    tfac = factor(tlo, tmd, thi, 4)
+    yw, summ = width_solve(y, v, w, back, wa, wfac, nsub)
     got = [summ] + [
         lax.ppermute(summ, "width", [(i, (i + q) % nw) for i in range(nw)]) for q in range(1, nw)
     ]
     me = wi.astype(jnp.int32).reshape(1)
-    return thick_solve(me, got, y, v, w, tlo, tmd, thi, h, nsub, 4)
+    return thick_solve(me, got, yw, wfac[2], wfac[3], tlo, tfac, h, nsub, 4)
 
 
 def solution(mesh):

time: 79.4 us -> 78.9 us (level)
  Pallas kernels: 13.7 us -> 22.3 us
  waiting for transfers between devices: 14 us -> 6.23 us
  starting transfers between devices: 17.4 us -> 19.9 us
  local copies, waits for them, and re-layouts: 6.84 us -> 4.69 us
  blocking collectives: 26.3 us -> 24.5 us
    pallas_call x1 -> x4, Pallas kernels: 3.34 us -> 12.4 us  [the longest x1 3.88 us: wfactor(): pl.pallas_call(functools.partial(_wfactor_kernel, n, nsub), out_shape=[sh...]
    ppermute x3, waiting for transfers between devices: 4.06 us -> 0.01 us  [shards(): lax.ppermute(summ, 'width', [(i, (i + q) % nw) for i in range(nw)])]
    ppermute x1, starting transfers between devices: 0.09 us -> 3.29 us  [shards(): got_a = lax.ppermute(jnp.where(even, last, first), 'cast', in_chip)]
    ppermute x1, waiting for transfers between devices: 2.66 us -> 0.01 us  [shards(): h_wh = lax.ppermute(h[:, :, 0], 'width', [(b, a) for a, b in up_w])]
    ppermute x1, starting transfers between devices: 4.5 us -> 1.91 us  [shards(): got_b = lax.ppermute(jnp.where(even, first, last), 'cast', across)]
    ppermute x3, starting transfers between devices: 3.48 us -> 6.05 us  [shards(): lax.ppermute(summ, 'width', [(i, (i + q) % nw) for i in range(nw)])]
    reshape x3 -> x0, local copies, waits for them, and re-layouts: 2.52 us -> none  [wl(): return jnp.transpose(x, (2, 0, 1)).reshape(nwl, lines // 128, 128)]
    all_to_all x1, blocking collectives: 26.3 us -> 24.5 us  [shards(): lax.all_to_all(summ.reshape(nc, nt // nc, 8, nwl), 'cast', 0, 0, tiled=True)]
  transfers between devices with their start and end apart: 8 -> 8, of which waited for: 4 -> 1; matrix products, arithmetic and copies ran while one was open for 5% -> 2% of each run, Pallas kernels for 0% -> 14%
where the time goes in v10:
time: 78.9 us; the launch traced here: 78.4 us
  blocking collectives  24.5 us (31%)
  Pallas kernels  22.3 us (28%)
  starting transfers between devices  19.9 us (25%)
  waiting for transfers between devices  6.23 us (8%)
  local copies, waits for them, and re-layouts  4.69 us (6%)
    all_to_all x1, blocking collectives, shards(): lax.all_to_all(summ.reshape(nc, nt // nc, 8, nwl), 'cast', 0, 0, tiled=True)  24.5 us
    all_to_all x1, waiting for transfers between devices, shards(): back = lax.all_to_all(lr, 'cast', 0, 0, tiled=True).reshape(nt, 2, nwl)  6.21 us
    ppermute x3, starting transfers between devices, shards(): lax.ppermute(summ, 'width', [(i, (i + q) % nw) for i in range(nw)])  6.05 us
    all_to_all x1, starting transfers between devices, shards(): back = lax.all_to_all(lr, 'cast', 0, 0, tiled=True).reshape(nt, 2, nwl)  4.77 us
    pallas_call x1, Pallas kernels, prep_solve(): pl.pallas_call(functools.partial(_prep_kernel, n), out_shape=[shp] * 3 +...  4.27 us
    pallas_call x1, Pallas kernels, wfactor(): pl.pallas_call(functools.partial(_wfactor_kernel, n, nsub), out_shape=[sh...  3.88 us
    unnamed x20, local copies, waits for them, and re-layouts  3.31 us
    ppermute x1, starting transfers between devices, shards(): got_a = lax.ppermute(jnp.where(even, last, first), 'cast', in_chip)  3.29 us
  transfers between devices with their start and end apart: 8, of which 1 were waited for; matrix products, arithmetic and copies ran while one was open for 2% of the time, Pallas kernels for 14%

profile of v10, /device:TPU:1, one launch (start us, length us, event | category | flops | bytes accessed | tf_op | source)
XLA Modules:
  0.0 78.4 jit_solution(18269634520345597888)
XLA Ops:
  0.0 1.1 %fusion = (f32[64,1,128]{2,1,0:T(1,128)S(1)}, f32[64,1,128]{2,1,0:T(1,128)S(1)}) fusion(f32[64,8,128]{2,1,0:T(8,128)} %refs_12_.1), kind=kLoop, calls=%fused_computation.2 | loop fusion | bytes 131072 | tf_op jit(solution)/shard_map/slice | solution.py:525
  1.2 3.3 %collective-permute-start.2 = (f32[64,128]{1,0:T(8,128)S(1)}, f32[64,128]{1,0:T(8,128)S(1)}, u32[]{:S(2)}, u32[]{:S(2)}) collective-permute-start(f32[64,128]{1,0:T(8,128)S(1)} %get-tuple-element.56), channel_id=1, source_target_pairs={{0,4},{4,0},{8,12},{12,8},{16,20},{20,16},{24,28},{28,24},{32,36},... | collective-permute-start | bytes 98312 | tf_op jit(solution)/shard_map/ppermute | solution.py:528
  4.5 1.9 %collective-permute-start.3 = (f32[64,128]{1,0:T(8,128)S(1)}, f32[64,128]{1,0:T(8,128)S(1)}, u32[]{:S(2)}, u32[]{:S(2)}) collective-permute-start(f32[64,128]{1,0:T(8,128)S(1)} %get-tuple-element.55), channel_id=1, source_target_pairs={{4,8},{12,16},{20,24},{28,32},{36,40},{44,48},{52,56},{60,64},{68,... | collective-permute-start | bytes 98312 | tf_op jit(solution)/shard_map/ppermute | solution.py:529
  6.4 0.1 fusion.1
  6.5 0.4 copy.13
  7.0 2.6 %collective-permute-start = (f32[64,8]{1,0:T(8,128)S(1)}, f32[64,8]{1,0:T(8,128)S(1)}, u32[]{:S(2)}, u32[]{:S(2)}) collective-permute-start(f32[64,8]{1,0:T(8,128)S(1)} %bitcast.38), channel_id=1, source_target_pairs={{0,1},{1,2},{2,3},{4,5},{5,6},{6,7},{8,9},{9,10},{10,11},{12,13},{... | collective-permute-start | bytes 6152 | tf_op jit(solution)/shard_map/ppermute | solution.py:530
  9.6 0.4 copy.14
  10.0 1.3 %collective-permute-start.1 = (f32[64,8]{1,0:T(8,128)S(1)}, f32[64,8]{1,0:T(8,128)S(1)}, u32[]{:S(2)}, u32[]{:S(2)}) collective-permute-start(f32[64,8]{1,0:T(8,128)S(1)} %bitcast.39), channel_id=1, source_target_pairs={{1,0},{2,1},{3,2},{5,4},{6,5},{7,6},{9,8},{10,9},{11,10},{13,12},{... | collective-permute-start | bytes 6152 | tf_op jit(solution)/shard_map/ppermute | solution.py:531
  11.3 0.1 stack.30
  11.4 0.5 stack.31.fl_ref
  12.0 0.0 collective-permute-done.2.hcl_ref
  12.0 0.6 copy-done.7
  12.6 0.0 copy-done.8
  12.6 4.3 %shard_map.37 = (f32[512,128]{1,0:T(8,128)}, f32[512,128]{1,0:T(8,128)}, f32[512,128]{1,0:T(8,128)}, f32[512,128]{1,0:T(8,128)}, f32[512,128]{1,0:T(8,128)}, /*i...) custom-call(f32[512,128]{1,0:T(8,128)} %bitcast.24, ...), custom_call_target="tpu_custom_call" | custom-call | tf_op jit(solution)/shard_map/pallas_call | solution.py:292
  16.9 0.6 copy-done.2
  17.5 0.0 copy-done.3
  17.5 3.1 %shard_map.38 = (f32[512,128]{1,0:T(8,128)}, f32[512,128]{1,0:T(8,128)}) custom-call(f32[512,128]{1,0:T(8,128)} %bitcast.25, f32[64,8]{1,0:T(8,128)} %copy-done.2, f32[64,8]{1,0:T(8,128)} %copy-done.3, f32[5]{0:T(128)} %stack.31.fl_ref, f32[512,128]{1,0:T(8,128)} %get-tuple-element.28.a_ref, f32[512,128]{1,0:T(8,128)} %get-tuple-element.29.r_ref, ...), custom_call_target="tpu_custom_call" | custom-call | tf_op jit(solution)/shard_map/pallas_call | solution.py:329
  20.6 24.5 %all_to_all.10.s_ref = f32[64,1,8,128]{3,2,1,0:T(8,128)} all-to-all(f32[64,1,8,128]{3,2,1,0:T(8,128)} %bitcast.35), channel_id=1, replica_groups=mesh['cast'=64,'width'=4] {'cast'}, dimensions={0} | all-to-all | bytes 524288 | tf_op jit(solution)/shard_map/all_to_all | solution.py:543
  45.1 2.4 %shard_map.39 = f32[64,1,2,128]{3,2,1,0:T(2,128)} custom-call(f32[64,1,8,128]{3,2,1,0:T(8,128)} %all_to_all.10.s_ref), custom_call_target="tpu_custom_call" | custom-call | tf_op jit(solution)/shard_map/pallas_call | solution.py:545
  47.5 4.8 %all-to-all-start.1 = ((f32[64,1,2,128]{3,2,1,0:T(2,128)}), f32[64,1,2,128]{3,2,1,0:T(2,128)S(1)}, u32[]{:S(2)}, u32[]{:S(2)}) async-start(f32[64,1,2,128]{3,2,1,0:T(2,128)} %shard_map.39), calls=%async_computation.1 | async-start | bytes 131072 | tf_op jit(solution)/shard_map/all_to_all | solution.py:546
  52.3 3.9 %shard_map.40 = (f32[128,4,128]{2,1,0:T(4,128)}, f32[128,4,128]{2,1,0:T(4,128)}, f32[128,4,128]{2,1,0:T(4,128)}, f32[128,4,128]{2,1,0:T(4,128)}, f32[128,4,128]{2,1,0:T(4,128)}) custom-call(f32[512,128]{1,0:T(8,128)} %bitcast.26, f32[64,8]{1,0:T(8,128)} %copy-done.2, f32[64,8]{1,0:T(8,128)} %copy-done.3, f32[5]{0:T(128)} %stack.31.fl_ref), custom_call_target="tpu_custom_call" | custom-call | tf_op jit(solution)/shard_map/pallas_call | solution.py:364
  56.2 6.2 %all-to-all-done.1 = f32[64,1,2,128]{3,2,1,0:T(2,128)S(1)} async-done(((f32[64,1,2,128]{3,2,1,0:T(2,128)}), f32[64,1,2,128]{3,2,1,0:T(2,128)S(1)}, u32[]{:S(2)}, u32[]{:S(2)}) %all-to-all-start.1) | async-done | bytes 65568 | tf_op jit(solution)/shard_map/all_to_all | solution.py:546
  62.4 0.6 copy-done.1
  63.0 3.0 %shard_map.41 = (f32[128,4,128]{2,1,0:T(4,128)}, f32[4,6,4,128]{3,2,1,0:T(4,128)}) custom-call(f32[64,8,128]{2,1,0:T(8,128)} %bitcast.33, f32[64,8,128]{2,1,0:T(8,128)} %bitcast.31, f32[64,8,128]{2,1,0:T(8,128)} %bitcast.32, f32[64,2,128]{2,1,0:T(2,128)} %bitcast.34, f32[128,4,128]{2,1,0:T(4,128)} %get-tuple-element.37.a_ref, ...), custom_call_target="tpu_custom_call" | custom-call | tf_op jit(solution)/shard_map/pallas_call | solution.py:429
  66.0 2.4 %collective-permute-start.4 = (f32[4,6,4,128]{3,2,1,0:T(4,128)}, f32[4,6,4,128]{3,2,1,0:T(4,128)S(1)}, u32[]{:S(2)}, u32[]{:S(2)}) collective-permute-start(f32[4,6,4,128]{3,2,1,0:T(4,128)} %get-tuple-element.42.refs_0_), channel_id=1, source_target_pairs={{0,1},{1,2},{2,3},{3,0},{4,5},{5,6},{6,7},{7,4},{8,9},{9,10},{10,1... | collective-permute-start | bytes 147464 | tf_op jit(solution)/shard_map/ppermute | solution.py:559
  68.3 2.6 %collective-permute-start.5 = (f32[4,6,4,128]{3,2,1,0:T(4,128)}, f32[4,6,4,128]{3,2,1,0:T(4,128)S(1)}, u32[]{:S(2)}, u32[]{:S(2)}) collective-permute-start(f32[4,6,4,128]{3,2,1,0:T(4,128)} %get-tuple-element.42.refs_0_), channel_id=1, source_target_pairs={{0,2},{1,3},{2,0},{3,1},{4,6},{5,7},{6,4},{7,5},{8,10},{9,11},{10,... | collective-permute-start | bytes 147464 | tf_op jit(solution)/shard_map/ppermute | solution.py:559
  71.0 1.1 %collective-permute-start.6 = (f32[4,6,4,128]{3,2,1,0:T(4,128)}, f32[4,6,4,128]{3,2,1,0:T(4,128)S(1)}, u32[]{:S(2)}, u32[]{:S(2)}) collective-permute-start(f32[4,6,4,128]{3,2,1,0:T(4,128)} %get-tuple-element.42.refs_0_), channel_id=1, source_target_pairs={{0,3},{1,0},{2,1},{3,2},{4,7},{5,4},{6,5},{7,6},{8,11},{9,8},{10,9... | collective-permute-start | bytes 147464 | tf_op jit(solution)/shard_map/ppermute | solution.py:559
  72.0 2.4 %shard_map.42 = (f32[64,8,128]{2,1,0:T(8,128)}, f32[64,8,128]{2,1,0:T(8,128)}, f32[64,8,128]{2,1,0:T(8,128)}, f32[64,8,128]{2,1,0:T(8,128)}) custom-call(f32[64,8,128]{2,1,0:T(8,128)} %bitcast.27, f32[64,8,128]{2,1,0:T(8,128)} %bitcast.29, f32[64,8,128]{2,1,0:T(8,128)} %bitcast.30), custom_call_target="tpu_custom_call" | custom-call | tf_op jit(solution)/shard_map/pallas_call | solution.py:182
  74.5 0.6 copy-done.4
  75.1 0.0 copy-done.5
  75.1 0.0 copy-done.6
  75.1 3.2 %shard_map.43 = f32[64,8,128]{2,1,0:T(8,128)} custom-call(s32[1]{0:T(128)} %bitcast.me_ref, f32[4,6,4,128]{3,2,1,0:T(4,128)} %get-tuple-element.42.refs_0_, f32[4,6,4,128]{3,2,1,0:T(4,128)} %copy-done.4, f32[4,6,4,128]{3,2,1,0:T(4,128)} %copy-done.5, f32[4,6,4,128]{3,2,1,0:T(4,128)} %copy-done.6, f32[128,4,128]{2,1,0:T(4,128)} %get-tuple-element.43.refs_4_, ...), custom_call_target="tpu_custom_call" | custom-call | tf_op jit(solution)/shard_map/pallas_call | solution.py:438
  (17 shorter events, 0.0 us)
Async XLA Ops:
  0.0 6.4 %copy-start = (f32[64,8,128]{2,1,0:T(8,128)S(1)}, f32[64,8,128]{2,1,0:T(8,128)}, u32[]{:S(2)}) copy-start(f32[64,8,128]{2,1,0:T(8,128)} %refs_12_.1) | copy-start | bytes 786436
  1.2 10.8 %collective-permute-start.2 = (f32[64,128]{1,0:T(8,128)S(1)}, f32[64,128]{1,0:T(8,128)S(1)}, u32[]{:S(2)}, u32[]{:S(2)}) collective-permute-start(f32[64,128]{1,0:T(8,128)S(1)} %get-tuple-element.56), channel_id=1, source_target_pairs={{0,4},{4,0},{8,12},{12,8},{16,20},{20,16},{24,28},{28,24},{32,36},... | collective-permute-start | bytes 98312 | tf_op jit(solution)/shard_map/ppermute | solution.py:528
  4.5 7.5 %collective-permute-start.3 = (f32[64,128]{1,0:T(8,128)S(1)}, f32[64,128]{1,0:T(8,128)S(1)}, u32[]{:S(2)}, u32[]{:S(2)}) collective-permute-start(f32[64,128]{1,0:T(8,128)S(1)} %get-tuple-element.55), channel_id=1, source_target_pairs={{4,8},{12,16},{20,24},{28,32},{36,40},{44,48},{52,56},{60,64},{68,... | collective-permute-start | bytes 98312 | tf_op jit(solution)/shard_map/ppermute | solution.py:529
  7.0 9.9 %collective-permute-start = (f32[64,8]{1,0:T(8,128)S(1)}, f32[64,8]{1,0:T(8,128)S(1)}, u32[]{:S(2)}, u32[]{:S(2)}) collective-permute-start(f32[64,8]{1,0:T(8,128)S(1)} %bitcast.38), channel_id=1, source_target_pairs={{0,1},{1,2},{2,3},{4,5},{5,6},{6,7},{8,9},{9,10},{10,11},{12,13},{... | collective-permute-start | bytes 6152 | tf_op jit(solution)/shard_map/ppermute | solution.py:530
  10.0 6.9 %collective-permute-start.1 = (f32[64,8]{1,0:T(8,128)S(1)}, f32[64,8]{1,0:T(8,128)S(1)}, u32[]{:S(2)}, u32[]{:S(2)}) collective-permute-start(f32[64,8]{1,0:T(8,128)S(1)} %bitcast.39), channel_id=1, source_target_pairs={{1,0},{2,1},{3,2},{5,4},{6,5},{7,6},{9,8},{10,9},{11,10},{13,12},{... | collective-permute-start | bytes 6152 | tf_op jit(solution)/shard_map/ppermute | solution.py:531
  12.0 0.6 copy-start.7
  12.0 0.6 copy-start.8
  16.9 0.6 copy-start.2
  16.9 0.6 copy-start.3
  47.5 14.9 %all-to-all-start.1 = ((f32[64,1,2,128]{3,2,1,0:T(2,128)}), f32[64,1,2,128]{3,2,1,0:T(2,128)S(1)}, u32[]{:S(2)}, u32[]{:S(2)}) async-start(f32[64,1,2,128]{3,2,1,0:T(2,128)} %shard_map.39), calls=%async_computation.1 | async-start | bytes 131072 | tf_op jit(solution)/shard_map/all_to_all | solution.py:546
  62.4 0.6 copy-start.1
  66.0 8.5 %collective-permute-start.4 = (f32[4,6,4,128]{3,2,1,0:T(4,128)}, f32[4,6,4,128]{3,2,1,0:T(4,128)S(1)}, u32[]{:S(2)}, u32[]{:S(2)}) collective-permute-start(f32[4,6,4,128]{3,2,1,0:T(4,128)} %get-tuple-element.42.refs_0_), channel_id=1, source_target_pairs={{0,1},{1,2},{2,3},{3,0},{4,5},{5,6},{6,7},{7,4},{8,9},{9,10},{10,1... | collective-permute-start | bytes 147464 | tf_op jit(solution)/shard_map/ppermute | solution.py:559
  68.3 6.2 %collective-permute-start.5 = (f32[4,6,4,128]{3,2,1,0:T(4,128)}, f32[4,6,4,128]{3,2,1,0:T(4,128)S(1)}, u32[]{:S(2)}, u32[]{:S(2)}) collective-permute-start(f32[4,6,4,128]{3,2,1,0:T(4,128)} %get-tuple-element.42.refs_0_), channel_id=1, source_target_pairs={{0,2},{1,3},{2,0},{3,1},{4,6},{5,7},{6,4},{7,5},{8,10},{9,11},{10,... | collective-permute-start | bytes 147464 | tf_op jit(solution)/shard_map/ppermute | solution.py:559
  71.0 3.6 %collective-permute-start.6 = (f32[4,6,4,128]{3,2,1,0:T(4,128)}, f32[4,6,4,128]{3,2,1,0:T(4,128)S(1)}, u32[]{:S(2)}, u32[]{:S(2)}) collective-permute-start(f32[4,6,4,128]{3,2,1,0:T(4,128)} %get-tuple-element.42.refs_0_), channel_id=1, source_target_pairs={{0,3},{1,0},{2,1},{3,2},{4,7},{5,4},{6,5},{7,6},{8,11},{9,8},{10,9... | collective-permute-start | bytes 147464 | tf_op jit(solution)/shard_map/ppermute | solution.py:559
  74.5 0.6 copy-start.4
  74.5 0.6 copy-start.5
  74.5 0.6 copy-start.6

commit v11 on v10

--- a/solution.py
+++ b/solution.py
@@ -7,87 +7,16 @@
 from jax.experimental.pallas import tpu as pltpu
 from jax.sharding import PartitionSpec as P
 
+
 F32 = jnp.float32
 solidification_release = 0.4
 quench_medium_hotness = -2.0
 SMEM_SPEC = pl.BlockSpec(memory_space=pltpu.SMEM)
 
 
-def _sweep(n, subs, ld, st, a_ref, b_ref, c_ref, d_ref, y_ref, v_ref, w_ref, cp_ref, unroll, shape):
-    with_vw = v_ref is not None
-    zero = jnp.zeros(shape, F32)
-    one = jnp.ones(shape, F32)
-
-    def fwd(i, carries):
-        out = []
-        for s0, (cprev, dprev, vprev) in zip(subs, carries):
-            j = s0 + i
-            a = ld(a_ref, j)
-            r = 1.0 / (ld(b_ref, j) - a * cprev)
-            cn = ld(c_ref, j) * r
-            dn = (ld(d_ref, j) - a * dprev) * r
-            st(cp_ref, j, cn)
-            st(y_ref, j, dn)
-            if with_vw:
-                vprev = -(a * vprev) * r
-                st(v_ref, j, vprev)
-            out.append((cn, dn, vprev))
-        return tuple(out)
-
-    carries = tuple((zero, zero, one) for _ in subs)
-    if unroll is True:
-        for i in range(n):
-            carries = fwd(i, carries)
-    else:
-        carries = lax.fori_loop(0, n, fwd, carries, unroll=unroll)
-    if with_vw:
-        for s0, (cl, _, _) in zip(subs, carries):
-            st(w_ref, s0 + n - 1, -cl)
-
-    def bwd(jj, carries):
-        i = n - 2 - jj
-        out = []
-        for s0, (yn, vn, wn) in zip(subs, carries):
-            j = s0 + i
-            cp = ld(cp_ref, j)
-            yn = ld(y_ref, j) - cp * yn
-            st(y_ref, j, yn)
-            if with_vw:
-                vn = ld(v_ref, j) - cp * vn
-                wn = -cp * wn
-                st(v_ref, j, vn)
-                st(w_ref, j, wn)
-            out.append((yn, vn, wn))
-        return tuple(out)
-
-    carries = tuple((dl, vl, -cl) for cl, dl, vl in carries)
-    if unroll is True:
-        for jj in range(n - 1):
-            carries = bwd(jj, carries)
-    else:
-        lax.fori_loop(0, n - 1, bwd, carries, unroll=unroll)
-
-
 def _summary_rows(ld, s0, n, y_ref, v_ref, w_ref):
     return [ld(y_ref, s0), ld(v_ref, s0), ld(w_ref, s0),
             ld(y_ref, s0 + n - 1), ld(v_ref, s0 + n - 1), ld(w_ref, s0 + n - 1)]
-
-
-def _cast_kernel(n, a_ref, b_ref, c_ref, d_ref, y_ref, v_ref, w_ref, sm_ref, cp_ref):
-    m = a_ref.shape[0] // n
-
-    def ld(ref, i):
-        return ref[pl.ds(i, m, stride=n), :]
-
-    def st(ref, i, val):
-        ref[pl.ds(i, m, stride=n), :] = val
-
-    shape = (m, a_ref.shape[1])
-    _sweep(n, [0], ld, st, a_ref, b_ref, c_ref, d_ref, y_ref, v_ref, w_ref, cp_ref, True, shape)
-    rows = _summary_rows(ld, 0, n, y_ref, v_ref, w_ref)
-    rows += [jnp.zeros(shape, F32)] * (8 - len(rows))
-    for k, val in enumerate(rows):
-        sm_ref[pl.ds(k, m, stride=8), :] = val
 
 
 def _lead_ld(ref, i):
@@ -182,7 +111,7 @@
     return pl.pallas_call(functools.partial(_factor_kernel, nsub), out_shape=[shp] * 4)(a, b, c)
 
 
-def _width_faces(n, c, T0, k0, s0, lane, wlo, whi, fl_ref):
+def _width_faces(T0, k0, s0, lane, wlo, whi, fl_ref):
     nwl = T0.shape[1]
     g_w = nwl * nwl / 4.0 * 0.5
     if wlo is None:
@@ -243,7 +172,7 @@
             Tq, kq, sq = (row(r, n + c + 1) for r in (tp_ref, kp_ref, sp2_ref))
         Ttm, ktm, stm = (row(r, c) for r in (tp_ref, kp_ref, sp2_ref))
         Ttp, ktp, stp = (row(r, 2 * n + c) for r in (tp_ref, kp_ref, sp2_ref))
-        Twm, _, Twp, _, gwl, gwh = _width_faces(n, c, T0, k0, s0, lane, None, None, fl_ref)
+        Twm, _, Twp, _, gwl, gwh = _width_faces(T0, k0, s0, lane, None, None, fl_ref)
         gcl = g_c * (k0 + km)
         if c == 0:
             gcl = gcl * fl_ref[0]
@@ -307,7 +236,7 @@
         T0, k0, s0 = medium_parameters(h_ref[sel, :])
         wlo = medium_parameters(hwl_ref[:, c : c + 1])
         whi = medium_parameters(hwh_ref[:, c : c + 1])
-        Twm, _, Twp, _, gwl, gwh = _width_faces(n, c, T0, k0, s0, lane, wlo, whi, fl_ref)
+        Twm, _, Twp, _, gwl, gwh = _width_faces(T0, k0, s0, lane, wlo, whi, fl_ref)
         edge = jnp.where(lane == 0, -gwl * (T0 - Twm), jnp.where(lane == nwl - 1, gwh * (Twp - T0), 0.0))
         d_ref[sel, :] = edge
 
@@ -344,7 +273,7 @@
         T0, k0, s0 = medium_parameters(h_ref[sel, :])
         wlo = medium_parameters(hwl_ref[:, c : c + 1])
         whi = medium_parameters(hwh_ref[:, c : c + 1])
-        _, swm, _, swp, gwl, gwh = _width_faces(n, c, T0, k0, s0, lane, wlo, whi, fl_ref)
+        _, swm, _, swp, gwl, gwh = _width_faces(T0, k0, s0, lane, wlo, whi, fl_ref)
         at_ref[sel, :] = -gwl * swm
         ct_ref[sel, :] = -gwh * swp
         bt_ref[sel, :] = 1.0 + s0 * (gwl + gwh)
@@ -414,16 +343,6 @@
         o_ref[sl] = h_ref[sl] + (y_ref[sl] + v_ref[sl] * left + w_ref[sl] * right)
 
 
-def cast_solve(a, b, c, d, n):
-    shp = jax.ShapeDtypeStruct(a.shape, F32)
-    m = a.shape[0] // n
-    return pl.pallas_call(
-        functools.partial(_cast_kernel, n),
-        out_shape=[shp, shp, shp, jax.ShapeDtypeStruct((m * 8, a.shape[1]), F32)],
-        scratch_shapes=[pltpu.VMEM(a.shape, F32)],
-    )(a, b, c, d)
-
-
 def width_solve(yc, vc, wc, bk, a, fac, nsub):
     shp = jax.ShapeDtypeStruct(a.shape, F32)
     return pl.pallas_call(
@@ -463,6 +382,7 @@
 
 def _cast_reduced_kernel(s_ref, lr_ref):
     nb = s_ref.shape[0]
+
     def blk(p):
         return tuple(s_ref[p, :, k, :] for k in range(6))
 
@@ -499,14 +419,6 @@
     return out
 
 
-def _surface_kernel(scale, z_ref, sp_ref, o_ref):
-    z = z_ref[...]
-    acc = jnp.zeros(z.shape, F32)
-    for q in range(sp_ref.shape[0]):
-        acc = jnp.where(z == q, sp_ref[q], acc)
-    o_ref[...] = acc * scale
-
-
 def medium_parameters(x):
     t = jnp.tanh(x)
     hot = x - solidification_release * t
@@ -515,11 +427,10 @@
     return hot, cond, slope
 
 
-def shards(h, zones, spray_coef):
+def _shards(h, zones, spray_coef):
     nt, ncl, nwl = h.shape
     nc, nw = lax.axis_size("cast"), lax.axis_size("width")
     ci, wi = lax.axis_index("cast"), lax.axis_index("width")
-    up_c = [(i, i + 1) for i in range(nc - 1)]
     up_w = [(i, i + 1) for i in range(nw - 1)]
     even = ci % 2 == 0
     first, last = h[:, 0, :], h[:, -1, :]
@@ -546,11 +457,7 @@
     back = lax.all_to_all(lr, "cast", 0, 0, tiled=True).reshape(nt, 2, nwl)
     y, v, w = (x.reshape(nt, ncl, nwl) for x in (y, v, w))
 
-    lines = nt * ncl
     nsub = 4
-
-    def wl(x):
-        return jnp.transpose(x, (2, 0, 1)).reshape(nwl, lines // 128, 128)
 
     wa, *wfac = wfactor(h2, h_wl, h_wh, flags, ncl, nsub)
     tfac = factor(tlo, tmd, thi, 4)
@@ -565,5 +472,5 @@
 def solution(mesh):
     spec = P(None, "cast", "width")
     return jax.shard_map(
-        shards, mesh=mesh, in_specs=(spec, spec, P()), out_specs=spec, check_vma=False
+        _shards, mesh=mesh, in_specs=(spec, spec, P()), out_specs=spec, check_vma=False
     )

time: 78.9 us -> 78.9 us (level)
  no operation moved by 1% of the time
where the time goes in v11:
time: 78.9 us; the launch traced here: 78.4 us
  blocking collectives  24.5 us (31%)
  Pallas kernels  22.3 us (28%)
  starting transfers between devices  19.9 us (25%)
  waiting for transfers between devices  6.23 us (8%)
  local copies, waits for them, and re-layouts  4.69 us (6%)
    all_to_all x1, blocking collectives, _shards(): lax.all_to_all(summ.reshape(nc, nt // nc, 8, nwl), 'cast', 0, 0, tiled=True)  24.5 us
    all_to_all x1, waiting for transfers between devices, _shards(): back = lax.all_to_all(lr, 'cast', 0, 0, tiled=True).reshape(nt, 2, nwl)  6.21 us
    ppermute x3, starting transfers between devices, _shards(): lax.ppermute(summ, 'width', [(i, (i + q) % nw) for i in range(nw)])  6.05 us
    all_to_all x1, starting transfers between devices, _shards(): back = lax.all_to_all(lr, 'cast', 0, 0, tiled=True).reshape(nt, 2, nwl)  4.77 us
    pallas_call x1, Pallas kernels, prep_solve(): pl.pallas_call(functools.partial(_prep_kernel, n), out_shape=[shp] * 3 +...  4.27 us
    pallas_call x1, Pallas kernels, wfactor(): pl.pallas_call(functools.partial(_wfactor_kernel, n, nsub), out_shape=[sh...  3.88 us
    unnamed x20, local copies, waits for them, and re-layouts  3.31 us
    ppermute x1, starting transfers between devices, _shards(): got_a = lax.ppermute(jnp.where(even, last, first), 'cast', in_chip)  3.29 us
  transfers between devices with their start and end apart: 8, of which 1 were waited for; matrix products, arithmetic and copies ran while one was open for 2% of the time, Pallas kernels for 14%

profile of v11, /device:TPU:1, one launch (start us, length us, event | category | flops | bytes accessed | tf_op | source)
XLA Modules:
  0.0 78.4 jit_solution(18269634520345597888)
XLA Ops:
  0.0 1.1 %fusion = (f32[64,1,128]{2,1,0:T(1,128)S(1)}, f32[64,1,128]{2,1,0:T(1,128)S(1)}) fusion(f32[64,8,128]{2,1,0:T(8,128)} %refs_12_.1), kind=kLoop, calls=%fused_computation.2 | loop fusion | bytes 131072 | tf_op jit(solution)/shard_map/slice | solution.py:436
  1.2 3.3 %collective-permute-start.2 = (f32[64,128]{1,0:T(8,128)S(1)}, f32[64,128]{1,0:T(8,128)S(1)}, u32[]{:S(2)}, u32[]{:S(2)}) collective-permute-start(f32[64,128]{1,0:T(8,128)S(1)} %get-tuple-element.56), channel_id=1, source_target_pairs={{0,4},{4,0},{8,12},{12,8},{16,20},{20,16},{24,28},{28,24},{32,36},... | collective-permute-start | bytes 98312 | tf_op jit(solution)/shard_map/ppermute | solution.py:439
  4.5 1.9 %collective-permute-start.3 = (f32[64,128]{1,0:T(8,128)S(1)}, f32[64,128]{1,0:T(8,128)S(1)}, u32[]{:S(2)}, u32[]{:S(2)}) collective-permute-start(f32[64,128]{1,0:T(8,128)S(1)} %get-tuple-element.55), channel_id=1, source_target_pairs={{4,8},{12,16},{20,24},{28,32},{36,40},{44,48},{52,56},{60,64},{68,... | collective-permute-start | bytes 98312 | tf_op jit(solution)/shard_map/ppermute | solution.py:440
  6.4 0.1 fusion.1
  6.5 0.4 copy.13
  7.0 2.6 %collective-permute-start = (f32[64,8]{1,0:T(8,128)S(1)}, f32[64,8]{1,0:T(8,128)S(1)}, u32[]{:S(2)}, u32[]{:S(2)}) collective-permute-start(f32[64,8]{1,0:T(8,128)S(1)} %bitcast.38), channel_id=1, source_target_pairs={{0,1},{1,2},{2,3},{4,5},{5,6},{6,7},{8,9},{9,10},{10,11},{12,13},{... | collective-permute-start | bytes 6152 | tf_op jit(solution)/shard_map/ppermute | solution.py:441
  9.6 0.4 copy.14
  10.0 1.3 %collective-permute-start.1 = (f32[64,8]{1,0:T(8,128)S(1)}, f32[64,8]{1,0:T(8,128)S(1)}, u32[]{:S(2)}, u32[]{:S(2)}) collective-permute-start(f32[64,8]{1,0:T(8,128)S(1)} %bitcast.39), channel_id=1, source_target_pairs={{1,0},{2,1},{3,2},{5,4},{6,5},{7,6},{9,8},{10,9},{11,10},{13,12},{... | collective-permute-start | bytes 6152 | tf_op jit(solution)/shard_map/ppermute | solution.py:442
  11.3 0.1 stack.30
  11.4 0.5 stack.31.fl_ref
  12.0 0.6 copy-done.7
  12.6 0.0 copy-done.8
  12.6 4.3 %shard_map.37 = (f32[512,128]{1,0:T(8,128)}, f32[512,128]{1,0:T(8,128)}, f32[512,128]{1,0:T(8,128)}, f32[512,128]{1,0:T(8,128)}, f32[512,128]{1,0:T(8,128)}, /*i...) custom-call(f32[512,128]{1,0:T(8,128)} %bitcast.24, ...), custom_call_target="tpu_custom_call" | custom-call | tf_op jit(solution)/shard_map/pallas_call | solution.py:221
  16.9 0.0 collective-permute-done.1.hwh_ref
  16.9 0.6 copy-done.2
  17.5 0.0 copy-done.3
  17.5 3.1 %shard_map.38 = (f32[512,128]{1,0:T(8,128)}, f32[512,128]{1,0:T(8,128)}) custom-call(f32[512,128]{1,0:T(8,128)} %bitcast.25, f32[64,8]{1,0:T(8,128)} %copy-done.2, f32[64,8]{1,0:T(8,128)} %copy-done.3, f32[5]{0:T(128)} %stack.31.fl_ref, f32[512,128]{1,0:T(8,128)} %get-tuple-element.28.a_ref, f32[512,128]{1,0:T(8,128)} %get-tuple-element.29.r_ref, ...), custom_call_target="tpu_custom_call" | custom-call | tf_op jit(solution)/shard_map/pallas_call | solution.py:258
  20.6 24.5 %all_to_all.10.s_ref = f32[64,1,8,128]{3,2,1,0:T(8,128)} all-to-all(f32[64,1,8,128]{3,2,1,0:T(8,128)} %bitcast.35), channel_id=1, replica_groups=mesh['cast'=64,'width'=4] {'cast'}, dimensions={0} | all-to-all | bytes 524288 | tf_op jit(solution)/shard_map/all_to_all | solution.py:454
  45.1 2.4 %shard_map.39 = f32[64,1,2,128]{3,2,1,0:T(2,128)} custom-call(f32[64,1,8,128]{3,2,1,0:T(8,128)} %all_to_all.10.s_ref), custom_call_target="tpu_custom_call" | custom-call | tf_op jit(solution)/shard_map/pallas_call | solution.py:456
  47.5 4.8 %all-to-all-start.1 = ((f32[64,1,2,128]{3,2,1,0:T(2,128)}), f32[64,1,2,128]{3,2,1,0:T(2,128)S(1)}, u32[]{:S(2)}, u32[]{:S(2)}) async-start(f32[64,1,2,128]{3,2,1,0:T(2,128)} %shard_map.39), calls=%async_computation.1 | async-start | bytes 131072 | tf_op jit(solution)/shard_map/all_to_all | solution.py:457
  52.3 3.9 %shard_map.40 = (f32[128,4,128]{2,1,0:T(4,128)}, f32[128,4,128]{2,1,0:T(4,128)}, f32[128,4,128]{2,1,0:T(4,128)}, f32[128,4,128]{2,1,0:T(4,128)}, f32[128,4,128]{2,1,0:T(4,128)}) custom-call(f32[512,128]{1,0:T(8,128)} %bitcast.26, f32[64,8]{1,0:T(8,128)} %copy-done.2, f32[64,8]{1,0:T(8,128)} %copy-done.3, f32[5]{0:T(128)} %stack.31.fl_ref), custom_call_target="tpu_custom_call" | custom-call | tf_op jit(solution)/shard_map/pallas_call | solution.py:293
  56.2 6.2 %all-to-all-done.1 = f32[64,1,2,128]{3,2,1,0:T(2,128)S(1)} async-done(((f32[64,1,2,128]{3,2,1,0:T(2,128)}), f32[64,1,2,128]{3,2,1,0:T(2,128)S(1)}, u32[]{:S(2)}, u32[]{:S(2)}) %all-to-all-start.1) | async-done | bytes 65568 | tf_op jit(solution)/shard_map/all_to_all | solution.py:457
  62.4 0.6 copy-done.1
  63.0 3.0 %shard_map.41 = (f32[128,4,128]{2,1,0:T(4,128)}, f32[4,6,4,128]{3,2,1,0:T(4,128)}) custom-call(f32[64,8,128]{2,1,0:T(8,128)} %bitcast.33, f32[64,8,128]{2,1,0:T(8,128)} %bitcast.31, f32[64,8,128]{2,1,0:T(8,128)} %bitcast.32, f32[64,2,128]{2,1,0:T(2,128)} %bitcast.34, f32[128,4,128]{2,1,0:T(4,128)} %get-tuple-element.37.a_ref, ...), custom_call_target="tpu_custom_call" | custom-call | tf_op jit(solution)/shard_map/pallas_call | solution.py:348
  66.0 2.4 %collective-permute-start.4 = (f32[4,6,4,128]{3,2,1,0:T(4,128)}, f32[4,6,4,128]{3,2,1,0:T(4,128)S(1)}, u32[]{:S(2)}, u32[]{:S(2)}) collective-permute-start(f32[4,6,4,128]{3,2,1,0:T(4,128)} %get-tuple-element.42.refs_0_), channel_id=1, source_target_pairs={{0,1},{1,2},{2,3},{3,0},{4,5},{5,6},{6,7},{7,4},{8,9},{9,10},{10,1... | collective-permute-start | bytes 147464 | tf_op jit(solution)/shard_map/ppermute | solution.py:466
  68.3 2.6 %collective-permute-start.5 = (f32[4,6,4,128]{3,2,1,0:T(4,128)}, f32[4,6,4,128]{3,2,1,0:T(4,128)S(1)}, u32[]{:S(2)}, u32[]{:S(2)}) collective-permute-start(f32[4,6,4,128]{3,2,1,0:T(4,128)} %get-tuple-element.42.refs_0_), channel_id=1, source_target_pairs={{0,2},{1,3},{2,0},{3,1},{4,6},{5,7},{6,4},{7,5},{8,10},{9,11},{10,... | collective-permute-start | bytes 147464 | tf_op jit(solution)/shard_map/ppermute | solution.py:466
  71.0 1.1 %collective-permute-start.6 = (f32[4,6,4,128]{3,2,1,0:T(4,128)}, f32[4,6,4,128]{3,2,1,0:T(4,128)S(1)}, u32[]{:S(2)}, u32[]{:S(2)}) collective-permute-start(f32[4,6,4,128]{3,2,1,0:T(4,128)} %get-tuple-element.42.refs_0_), channel_id=1, source_target_pairs={{0,3},{1,0},{2,1},{3,2},{4,7},{5,4},{6,5},{7,6},{8,11},{9,8},{10,9... | collective-permute-start | bytes 147464 | tf_op jit(solution)/shard_map/ppermute | solution.py:466
  72.0 2.4 %shard_map.42 = (f32[64,8,128]{2,1,0:T(8,128)}, f32[64,8,128]{2,1,0:T(8,128)}, f32[64,8,128]{2,1,0:T(8,128)}, f32[64,8,128]{2,1,0:T(8,128)}) custom-call(f32[64,8,128]{2,1,0:T(8,128)} %bitcast.27, f32[64,8,128]{2,1,0:T(8,128)} %bitcast.29, f32[64,8,128]{2,1,0:T(8,128)} %bitcast.30), custom_call_target="tpu_custom_call" | custom-call | tf_op jit(solution)/shard_map/pallas_call | solution.py:111
  74.5 0.6 copy-done.4
  75.1 0.0 copy-done.5
  75.1 0.0 copy-done.6
  75.1 3.2 %shard_map.43 = f32[64,8,128]{2,1,0:T(8,128)} custom-call(s32[1]{0:T(128)} %bitcast.me_ref, f32[4,6,4,128]{3,2,1,0:T(4,128)} %get-tuple-element.42.refs_0_, f32[4,6,4,128]{3,2,1,0:T(4,128)} %copy-done.4, f32[4,6,4,128]{3,2,1,0:T(4,128)} %copy-done.5, f32[4,6,4,128]{3,2,1,0:T(4,128)} %copy-done.6, f32[128,4,128]{2,1,0:T(4,128)} %get-tuple-element.43.refs_4_, ...), custom_call_target="tpu_custom_call" | custom-call | tf_op jit(solution)/shard_map/pallas_call | solution.py:357
  (17 shorter events, 0.0 us)
Async XLA Ops:
  0.0 6.4 %copy-start = (f32[64,8,128]{2,1,0:T(8,128)S(1)}, f32[64,8,128]{2,1,0:T(8,128)}, u32[]{:S(2)}) copy-start(f32[64,8,128]{2,1,0:T(8,128)} %refs_12_.1) | copy-start | bytes 786436
  1.2 10.8 %collective-permute-start.2 = (f32[64,128]{1,0:T(8,128)S(1)}, f32[64,128]{1,0:T(8,128)S(1)}, u32[]{:S(2)}, u32[]{:S(2)}) collective-permute-start(f32[64,128]{1,0:T(8,128)S(1)} %get-tuple-element.56), channel_id=1, source_target_pairs={{0,4},{4,0},{8,12},{12,8},{16,20},{20,16},{24,28},{28,24},{32,36},... | collective-permute-start | bytes 98312 | tf_op jit(solution)/shard_map/ppermute | solution.py:439
  4.5 7.5 %collective-permute-start.3 = (f32[64,128]{1,0:T(8,128)S(1)}, f32[64,128]{1,0:T(8,128)S(1)}, u32[]{:S(2)}, u32[]{:S(2)}) collective-permute-start(f32[64,128]{1,0:T(8,128)S(1)} %get-tuple-element.55), channel_id=1, source_target_pairs={{4,8},{12,16},{20,24},{28,32},{36,40},{44,48},{52,56},{60,64},{68,... | collective-permute-start | bytes 98312 | tf_op jit(solution)/shard_map/ppermute | solution.py:440
  7.0 9.9 %collective-permute-start = (f32[64,8]{1,0:T(8,128)S(1)}, f32[64,8]{1,0:T(8,128)S(1)}, u32[]{:S(2)}, u32[]{:S(2)}) collective-permute-start(f32[64,8]{1,0:T(8,128)S(1)} %bitcast.38), channel_id=1, source_target_pairs={{0,1},{1,2},{2,3},{4,5},{5,6},{6,7},{8,9},{9,10},{10,11},{12,13},{... | collective-permute-start | bytes 6152 | tf_op jit(solution)/shard_map/ppermute | solution.py:441
  10.0 6.9 %collective-permute-start.1 = (f32[64,8]{1,0:T(8,128)S(1)}, f32[64,8]{1,0:T(8,128)S(1)}, u32[]{:S(2)}, u32[]{:S(2)}) collective-permute-start(f32[64,8]{1,0:T(8,128)S(1)} %bitcast.39), channel_id=1, source_target_pairs={{1,0},{2,1},{3,2},{5,4},{6,5},{7,6},{9,8},{10,9},{11,10},{13,12},{... | collective-permute-start | bytes 6152 | tf_op jit(solution)/shard_map/ppermute | solution.py:442
  12.0 0.6 copy-start.7
  12.0 0.6 copy-start.8
  16.9 0.6 copy-start.2
  16.9 0.6 copy-start.3
  47.5 14.9 %all-to-all-start.1 = ((f32[64,1,2,128]{3,2,1,0:T(2,128)}), f32[64,1,2,128]{3,2,1,0:T(2,128)S(1)}, u32[]{:S(2)}, u32[]{:S(2)}) async-start(f32[64,1,2,128]{3,2,1,0:T(2,128)} %shard_map.39), calls=%async_computation.1 | async-start | bytes 131072 | tf_op jit(solution)/shard_map/all_to_all | solution.py:457
  62.4 0.6 copy-start.1
  66.0 8.5 %collective-permute-start.4 = (f32[4,6,4,128]{3,2,1,0:T(4,128)}, f32[4,6,4,128]{3,2,1,0:T(4,128)S(1)}, u32[]{:S(2)}, u32[]{:S(2)}) collective-permute-start(f32[4,6,4,128]{3,2,1,0:T(4,128)} %get-tuple-element.42.refs_0_), channel_id=1, source_target_pairs={{0,1},{1,2},{2,3},{3,0},{4,5},{5,6},{6,7},{7,4},{8,9},{9,10},{10,1... | collective-permute-start | bytes 147464 | tf_op jit(solution)/shard_map/ppermute | solution.py:466
  68.3 6.2 %collective-permute-start.5 = (f32[4,6,4,128]{3,2,1,0:T(4,128)}, f32[4,6,4,128]{3,2,1,0:T(4,128)S(1)}, u32[]{:S(2)}, u32[]{:S(2)}) collective-permute-start(f32[4,6,4,128]{3,2,1,0:T(4,128)} %get-tuple-element.42.refs_0_), channel_id=1, source_target_pairs={{0,2},{1,3},{2,0},{3,1},{4,6},{5,7},{6,4},{7,5},{8,10},{9,11},{10,... | collective-permute-start | bytes 147464 | tf_op jit(solution)/shard_map/ppermute | solution.py:466
  71.0 3.6 %collective-permute-start.6 = (f32[4,6,4,128]{3,2,1,0:T(4,128)}, f32[4,6,4,128]{3,2,1,0:T(4,128)S(1)}, u32[]{:S(2)}, u32[]{:S(2)}) collective-permute-start(f32[4,6,4,128]{3,2,1,0:T(4,128)} %get-tuple-element.42.refs_0_), channel_id=1, source_target_pairs={{0,3},{1,0},{2,1},{3,2},{4,7},{5,4},{6,5},{7,6},{8,11},{9,8},{10,9... | collective-permute-start | bytes 147464 | tf_op jit(solution)/shard_map/ppermute | solution.py:466
  74.5 0.6 copy-start.4
  74.5 0.6 copy-start.5
  74.5 0.6 copy-start.6

commit v12 on v10

--- a/solution.py
+++ b/solution.py
@@ -461,16 +461,78 @@
         f_next = f
 
 
+def _merge(A, B):
+    yA0, vA0, wA0, yAn, vAn, wAn = A
+    yB0, vB0, wB0, yBn, vBn, wBn = B
+    rd = 1.0 / (1.0 - wAn * vB0)
+    ey = (yAn + wAn * yB0) * rd
+    ev = vAn * rd
+    ew = wAn * wB0 * rd
+    fy = yB0 + vB0 * ey
+    fv = vB0 * ev
+    fw = wB0 + vB0 * ew
+    return (yA0 + wA0 * fy, vA0 + wA0 * fv, wA0 * fw, yBn + vBn * ey, vBn * ev, wBn + vBn * ew)
+
+
+def _chain(nb, blk, emit, left, right):
+    pp, qq = left, jnp.zeros_like(left)
+    saved = []
+    for p in range(nb):
+        y0, v0, w0, yn, vn, wn = blk(p)
+        rd = 1.0 / (1.0 - v0 * qq)
+        fa = (y0 + v0 * pp) * rd
+        fb = w0 * rd
+        saved.append((fa, fb, pp, qq))
+        pp, qq = yn + vn * (pp + qq * fa), wn + vn * qq * fb
+    f_next = right
+    for p in range(nb - 1, -1, -1):
+        fa, fb, pp, qq = saved[p]
+        f = fa + fb * f_next
+        emit(p, pp + qq * f, f_next)
+        f_next = f
+
+
 def _cast_reduced_kernel(s_ref, lr_ref):
-    nb = s_ref.shape[0]
-    def blk(p):
-        return tuple(s_ref[p, :, k, :] for k in range(6))
-
-    def emit(p, left, right):
-        lr_ref[p, :, 0:1, :] = left[:, None]
-        lr_ref[p, :, 1:2, :] = right[:, None]
-
-    _reduce_blocks(nb, blk, emit, jnp.zeros((s_ref.shape[1], s_ref.shape[3]), F32))
+    nb, g, _, nl = s_ref.shape
+    ng = 8
+    if g != 1 or nb % ng:
+        def blk(p):
+            return tuple(s_ref[p, :, k, :] for k in range(6))
+
+        def emit(p, left, right):
+            lr_ref[p, :, 0:1, :] = left[:, None]
+            lr_ref[p, :, 1:2, :] = right[:, None]
+
+        _reduce_blocks(nb, blk, emit, jnp.zeros((g, nl), F32))
+        return
+    m = nb // ng
+
+    def member(j):
+        return tuple(
+            jnp.concatenate([s_ref[G * m + j, 0, k : k + 1, :] for G in range(ng)], 0)
+            for k in range(6)
+        )
+
+    members = [member(j) for j in range(m)]
+    acc = members[0]
+    for j in range(1, m):
+        acc = _merge(acc, members[j])
+    outer = [None] * ng
+
+    def emit_g(G, left, right):
+        outer[G] = (left, right)
+
+    zero1 = jnp.zeros((1, nl), F32)
+    _chain(ng, lambda G: tuple(x[G : G + 1] for x in acc), emit_g, zero1, zero1)
+    left_g = jnp.concatenate([outer[G][0] for G in range(ng)], 0)
+    right_g = jnp.concatenate([outer[G][1] for G in range(ng)], 0)
+
+    def emit(j, left, right):
+        for G in range(ng):
+            lr_ref[G * m + j, 0, 0:1, :] = left[G : G + 1]
+            lr_ref[G * m + j, 0, 1:2, :] = right[G : G + 1]
+
+    _chain(m, lambda j: members[j], emit, left_g, right_g)
 
 
 def _width_reduce(me, r_refs):

time: 78.9 us -> 78.3 us (level)
  no operation moved by 1% of the time
where the time goes in v12:
time: 78.3 us; the launch traced here: 77.9 us
  blocking collectives  24.5 us (31%)
  Pallas kernels  21.8 us (28%)
  starting transfers between devices  19.9 us (25%)
  waiting for transfers between devices  6.23 us (8%)
  local copies, waits for them, and re-layouts  4.69 us (6%)
    all_to_all x1, blocking collectives, shards(): lax.all_to_all(summ.reshape(nc, nt // nc, 8, nwl), 'cast', 0, 0, tiled=True)  24.5 us
    all_to_all x1, waiting for transfers between devices, shards(): back = lax.all_to_all(lr, 'cast', 0, 0, tiled=True).reshape(nt, 2, nwl)  6.21 us
    ppermute x3, starting transfers between devices, shards(): lax.ppermute(summ, 'width', [(i, (i + q) % nw) for i in range(nw)])  6.05 us
    all_to_all x1, starting transfers between devices, shards(): back = lax.all_to_all(lr, 'cast', 0, 0, tiled=True).reshape(nt, 2, nwl)  4.77 us
    pallas_call x1, Pallas kernels, prep_solve(): pl.pallas_call(functools.partial(_prep_kernel, n), out_shape=[shp] * 3 +...  4.27 us
    pallas_call x1, Pallas kernels, wfactor(): pl.pallas_call(functools.partial(_wfactor_kernel, n, nsub), out_shape=[sh...  3.88 us
    unnamed x20, local copies, waits for them, and re-layouts  3.31 us
    ppermute x1, starting transfers between devices, shards(): got_a = lax.ppermute(jnp.where(even, last, first), 'cast', in_chip)  3.29 us
  transfers between devices with their start and end apart: 8, of which 1 were waited for; matrix products, arithmetic and copies ran while one was open for 2% of the time, Pallas kernels for 14%

profile of v12, /device:TPU:1, one launch (start us, length us, event | category | flops | bytes accessed | tf_op | source)
XLA Modules:
  0.0 77.9 jit_solution(9993611285175524360)
XLA Ops:
  0.0 1.1 %fusion = (f32[64,1,128]{2,1,0:T(1,128)S(1)}, f32[64,1,128]{2,1,0:T(1,128)S(1)}) fusion(f32[64,8,128]{2,1,0:T(8,128)} %refs_12_.1), kind=kLoop, calls=%fused_computation.2 | loop fusion | bytes 131072 | tf_op jit(solution)/shard_map/slice | solution.py:587
  1.2 3.3 %collective-permute-start.2 = (f32[64,128]{1,0:T(8,128)S(1)}, f32[64,128]{1,0:T(8,128)S(1)}, u32[]{:S(2)}, u32[]{:S(2)}) collective-permute-start(f32[64,128]{1,0:T(8,128)S(1)} %get-tuple-element.56), channel_id=1, source_target_pairs={{0,4},{4,0},{8,12},{12,8},{16,20},{20,16},{24,28},{28,24},{32,36},... | collective-permute-start | bytes 98312 | tf_op jit(solution)/shard_map/ppermute | solution.py:590
  4.5 1.9 %collective-permute-start.3 = (f32[64,128]{1,0:T(8,128)S(1)}, f32[64,128]{1,0:T(8,128)S(1)}, u32[]{:S(2)}, u32[]{:S(2)}) collective-permute-start(f32[64,128]{1,0:T(8,128)S(1)} %get-tuple-element.55), channel_id=1, source_target_pairs={{4,8},{12,16},{20,24},{28,32},{36,40},{44,48},{52,56},{60,64},{68,... | collective-permute-start | bytes 98312 | tf_op jit(solution)/shard_map/ppermute | solution.py:591
  6.4 0.1 fusion.1
  6.5 0.4 copy.13
  7.0 2.6 %collective-permute-start = (f32[64,8]{1,0:T(8,128)S(1)}, f32[64,8]{1,0:T(8,128)S(1)}, u32[]{:S(2)}, u32[]{:S(2)}) collective-permute-start(f32[64,8]{1,0:T(8,128)S(1)} %bitcast.38), channel_id=1, source_target_pairs={{0,1},{1,2},{2,3},{4,5},{5,6},{6,7},{8,9},{9,10},{10,11},{12,13},{... | collective-permute-start | bytes 6152 | tf_op jit(solution)/shard_map/ppermute | solution.py:592
  9.6 0.4 copy.14
  10.0 1.3 %collective-permute-start.1 = (f32[64,8]{1,0:T(8,128)S(1)}, f32[64,8]{1,0:T(8,128)S(1)}, u32[]{:S(2)}, u32[]{:S(2)}) collective-permute-start(f32[64,8]{1,0:T(8,128)S(1)} %bitcast.39), channel_id=1, source_target_pairs={{1,0},{2,1},{3,2},{5,4},{6,5},{7,6},{9,8},{10,9},{11,10},{13,12},{... | collective-permute-start | bytes 6152 | tf_op jit(solution)/shard_map/ppermute | solution.py:593
  11.3 0.1 stack.30
  11.4 0.5 stack.31.fl_ref
  12.0 0.0 collective-permute-done.2.hcl_ref
  12.0 0.6 copy-done.7
  12.6 0.0 copy-done.8
  12.6 4.3 %shard_map.37 = (f32[512,128]{1,0:T(8,128)}, f32[512,128]{1,0:T(8,128)}, f32[512,128]{1,0:T(8,128)}, f32[512,128]{1,0:T(8,128)}, f32[512,128]{1,0:T(8,128)}, /*i...) custom-call(f32[512,128]{1,0:T(8,128)} %bitcast.24, ...), custom_call_target="tpu_custom_call" | custom-call | tf_op jit(solution)/shard_map/pallas_call | solution.py:292
  16.9 0.6 copy-done.2
  17.5 0.0 copy-done.3
  17.5 3.1 %shard_map.38 = (f32[512,128]{1,0:T(8,128)}, f32[512,128]{1,0:T(8,128)}) custom-call(f32[512,128]{1,0:T(8,128)} %bitcast.25, f32[64,8]{1,0:T(8,128)} %copy-done.2, f32[64,8]{1,0:T(8,128)} %copy-done.3, f32[5]{0:T(128)} %stack.31.fl_ref, f32[512,128]{1,0:T(8,128)} %get-tuple-element.28.a_ref, f32[512,128]{1,0:T(8,128)} %get-tuple-element.29.r_ref, ...), custom_call_target="tpu_custom_call" | custom-call | tf_op jit(solution)/shard_map/pallas_call | solution.py:329
  20.6 24.5 %all_to_all.10.s_ref = f32[64,1,8,128]{3,2,1,0:T(8,128)} all-to-all(f32[64,1,8,128]{3,2,1,0:T(8,128)} %bitcast.35), channel_id=1, replica_groups=mesh['cast'=64,'width'=4] {'cast'}, dimensions={0} | all-to-all | bytes 524288 | tf_op jit(solution)/shard_map/all_to_all | solution.py:605
  45.1 1.9 %shard_map.39 = f32[64,1,2,128]{3,2,1,0:T(2,128)} custom-call(f32[64,1,8,128]{3,2,1,0:T(8,128)} %all_to_all.10.s_ref), custom_call_target="tpu_custom_call" | custom-call | tf_op jit(solution)/shard_map/pallas_call | solution.py:607
  47.0 4.8 %all-to-all-start.1 = ((f32[64,1,2,128]{3,2,1,0:T(2,128)}), f32[64,1,2,128]{3,2,1,0:T(2,128)S(1)}, u32[]{:S(2)}, u32[]{:S(2)}) async-start(f32[64,1,2,128]{3,2,1,0:T(2,128)} %shard_map.39), calls=%async_computation.1 | async-start | bytes 131072 | tf_op jit(solution)/shard_map/all_to_all | solution.py:608
  51.8 3.9 %shard_map.40 = (f32[128,4,128]{2,1,0:T(4,128)}, f32[128,4,128]{2,1,0:T(4,128)}, f32[128,4,128]{2,1,0:T(4,128)}, f32[128,4,128]{2,1,0:T(4,128)}, f32[128,4,128]{2,1,0:T(4,128)}) custom-call(f32[512,128]{1,0:T(8,128)} %bitcast.26, f32[64,8]{1,0:T(8,128)} %copy-done.2, f32[64,8]{1,0:T(8,128)} %copy-done.3, f32[5]{0:T(128)} %stack.31.fl_ref), custom_call_target="tpu_custom_call" | custom-call | tf_op jit(solution)/shard_map/pallas_call | solution.py:364
  55.7 6.2 %all-to-all-done.1 = f32[64,1,2,128]{3,2,1,0:T(2,128)S(1)} async-done(((f32[64,1,2,128]{3,2,1,0:T(2,128)}), f32[64,1,2,128]{3,2,1,0:T(2,128)S(1)}, u32[]{:S(2)}, u32[]{:S(2)}) %all-to-all-start.1) | async-done | bytes 65568 | tf_op jit(solution)/shard_map/all_to_all | solution.py:608
  61.9 0.6 copy-done.1
  62.5 3.0 %shard_map.41 = (f32[128,4,128]{2,1,0:T(4,128)}, f32[4,6,4,128]{3,2,1,0:T(4,128)}) custom-call(f32[64,8,128]{2,1,0:T(8,128)} %bitcast.33, f32[64,8,128]{2,1,0:T(8,128)} %bitcast.31, f32[64,8,128]{2,1,0:T(8,128)} %bitcast.32, f32[64,2,128]{2,1,0:T(2,128)} %bitcast.34, f32[128,4,128]{2,1,0:T(4,128)} %get-tuple-element.37.a_ref, ...), custom_call_target="tpu_custom_call" | custom-call | tf_op jit(solution)/shard_map/pallas_call | solution.py:429
  65.5 2.4 %collective-permute-start.4 = (f32[4,6,4,128]{3,2,1,0:T(4,128)}, f32[4,6,4,128]{3,2,1,0:T(4,128)S(1)}, u32[]{:S(2)}, u32[]{:S(2)}) collective-permute-start(f32[4,6,4,128]{3,2,1,0:T(4,128)} %get-tuple-element.42.refs_0_), channel_id=1, source_target_pairs={{0,1},{1,2},{2,3},{3,0},{4,5},{5,6},{6,7},{7,4},{8,9},{9,10},{10,1... | collective-permute-start | bytes 147464 | tf_op jit(solution)/shard_map/ppermute | solution.py:621
  67.8 2.6 %collective-permute-start.5 = (f32[4,6,4,128]{3,2,1,0:T(4,128)}, f32[4,6,4,128]{3,2,1,0:T(4,128)S(1)}, u32[]{:S(2)}, u32[]{:S(2)}) collective-permute-start(f32[4,6,4,128]{3,2,1,0:T(4,128)} %get-tuple-element.42.refs_0_), channel_id=1, source_target_pairs={{0,2},{1,3},{2,0},{3,1},{4,6},{5,7},{6,4},{7,5},{8,10},{9,11},{10,... | collective-permute-start | bytes 147464 | tf_op jit(solution)/shard_map/ppermute | solution.py:621
  70.4 1.1 %collective-permute-start.6 = (f32[4,6,4,128]{3,2,1,0:T(4,128)}, f32[4,6,4,128]{3,2,1,0:T(4,128)S(1)}, u32[]{:S(2)}, u32[]{:S(2)}) collective-permute-start(f32[4,6,4,128]{3,2,1,0:T(4,128)} %get-tuple-element.42.refs_0_), channel_id=1, source_target_pairs={{0,3},{1,0},{2,1},{3,2},{4,7},{5,4},{6,5},{7,6},{8,11},{9,8},{10,9... | collective-permute-start | bytes 147464 | tf_op jit(solution)/shard_map/ppermute | solution.py:621
  71.5 2.4 %shard_map.42 = (f32[64,8,128]{2,1,0:T(8,128)}, f32[64,8,128]{2,1,0:T(8,128)}, f32[64,8,128]{2,1,0:T(8,128)}, f32[64,8,128]{2,1,0:T(8,128)}) custom-call(f32[64,8,128]{2,1,0:T(8,128)} %bitcast.27, f32[64,8,128]{2,1,0:T(8,128)} %bitcast.29, f32[64,8,128]{2,1,0:T(8,128)} %bitcast.30), custom_call_target="tpu_custom_call" | custom-call | tf_op jit(solution)/shard_map/pallas_call | solution.py:182
  74.0 0.6 copy-done.4
  74.6 0.0 copy-done.5
  74.6 0.0 copy-done.6
  74.6 3.2 %shard_map.43 = f32[64,8,128]{2,1,0:T(8,128)} custom-call(s32[1]{0:T(128)} %bitcast.me_ref, f32[4,6,4,128]{3,2,1,0:T(4,128)} %get-tuple-element.42.refs_0_, f32[4,6,4,128]{3,2,1,0:T(4,128)} %copy-done.4, f32[4,6,4,128]{3,2,1,0:T(4,128)} %copy-done.5, f32[4,6,4,128]{3,2,1,0:T(4,128)} %copy-done.6, f32[128,4,128]{2,1,0:T(4,128)} %get-tuple-element.43.refs_4_, ...), custom_call_target="tpu_custom_call" | custom-call | tf_op jit(solution)/shard_map/pallas_call | solution.py:438
  (17 shorter events, 0.0 us)
Async XLA Ops:
  0.0 6.4 %copy-start = (f32[64,8,128]{2,1,0:T(8,128)S(1)}, f32[64,8,128]{2,1,0:T(8,128)}, u32[]{:S(2)}) copy-start(f32[64,8,128]{2,1,0:T(8,128)} %refs_12_.1) | copy-start | bytes 786436
  1.2 10.8 %collective-permute-start.2 = (f32[64,128]{1,0:T(8,128)S(1)}, f32[64,128]{1,0:T(8,128)S(1)}, u32[]{:S(2)}, u32[]{:S(2)}) collective-permute-start(f32[64,128]{1,0:T(8,128)S(1)} %get-tuple-element.56), channel_id=1, source_target_pairs={{0,4},{4,0},{8,12},{12,8},{16,20},{20,16},{24,28},{28,24},{32,36},... | collective-permute-start | bytes 98312 | tf_op jit(solution)/shard_map/ppermute | solution.py:590
  4.5 7.5 %collective-permute-start.3 = (f32[64,128]{1,0:T(8,128)S(1)}, f32[64,128]{1,0:T(8,128)S(1)}, u32[]{:S(2)}, u32[]{:S(2)}) collective-permute-start(f32[64,128]{1,0:T(8,128)S(1)} %get-tuple-element.55), channel_id=1, source_target_pairs={{4,8},{12,16},{20,24},{28,32},{36,40},{44,48},{52,56},{60,64},{68,... | collective-permute-start | bytes 98312 | tf_op jit(solution)/shard_map/ppermute | solution.py:591
  7.0 9.9 %collective-permute-start = (f32[64,8]{1,0:T(8,128)S(1)}, f32[64,8]{1,0:T(8,128)S(1)}, u32[]{:S(2)}, u32[]{:S(2)}) collective-permute-start(f32[64,8]{1,0:T(8,128)S(1)} %bitcast.38), channel_id=1, source_target_pairs={{0,1},{1,2},{2,3},{4,5},{5,6},{6,7},{8,9},{9,10},{10,11},{12,13},{... | collective-permute-start | bytes 6152 | tf_op jit(solution)/shard_map/ppermute | solution.py:592
  10.0 6.9 %collective-permute-start.1 = (f32[64,8]{1,0:T(8,128)S(1)}, f32[64,8]{1,0:T(8,128)S(1)}, u32[]{:S(2)}, u32[]{:S(2)}) collective-permute-start(f32[64,8]{1,0:T(8,128)S(1)} %bitcast.39), channel_id=1, source_target_pairs={{1,0},{2,1},{3,2},{5,4},{6,5},{7,6},{9,8},{10,9},{11,10},{13,12},{... | collective-permute-start | bytes 6152 | tf_op jit(solution)/shard_map/ppermute | solution.py:593
  12.0 0.6 copy-start.7
  12.0 0.6 copy-start.8
  16.9 0.6 copy-start.2
  16.9 0.6 copy-start.3
  47.0 14.9 %all-to-all-start.1 = ((f32[64,1,2,128]{3,2,1,0:T(2,128)}), f32[64,1,2,128]{3,2,1,0:T(2,128)S(1)}, u32[]{:S(2)}, u32[]{:S(2)}) async-start(f32[64,1,2,128]{3,2,1,0:T(2,128)} %shard_map.39), calls=%async_computation.1 | async-start | bytes 131072 | tf_op jit(solution)/shard_map/all_to_all | solution.py:608
  61.9 0.6 copy-start.1
  65.5 8.5 %collective-permute-start.4 = (f32[4,6,4,128]{3,2,1,0:T(4,128)}, f32[4,6,4,128]{3,2,1,0:T(4,128)S(1)}, u32[]{:S(2)}, u32[]{:S(2)}) collective-permute-start(f32[4,6,4,128]{3,2,1,0:T(4,128)} %get-tuple-element.42.refs_0_), channel_id=1, source_target_pairs={{0,1},{1,2},{2,3},{3,0},{4,5},{5,6},{6,7},{7,4},{8,9},{9,10},{10,1... | collective-permute-start | bytes 147464 | tf_op jit(solution)/shard_map/ppermute | solution.py:621
  67.8 6.2 %collective-permute-start.5 = (f32[4,6,4,128]{3,2,1,0:T(4,128)}, f32[4,6,4,128]{3,2,1,0:T(4,128)S(1)}, u32[]{:S(2)}, u32[]{:S(2)}) collective-permute-start(f32[4,6,4,128]{3,2,1,0:T(4,128)} %get-tuple-element.42.refs_0_), channel_id=1, source_target_pairs={{0,2},{1,3},{2,0},{3,1},{4,6},{5,7},{6,4},{7,5},{8,10},{9,11},{10,... | collective-permute-start | bytes 147464 | tf_op jit(solution)/shard_map/ppermute | solution.py:621
  70.4 3.6 %collective-permute-start.6 = (f32[4,6,4,128]{3,2,1,0:T(4,128)}, f32[4,6,4,128]{3,2,1,0:T(4,128)S(1)}, u32[]{:S(2)}, u32[]{:S(2)}) collective-permute-start(f32[4,6,4,128]{3,2,1,0:T(4,128)} %get-tuple-element.42.refs_0_), channel_id=1, source_target_pairs={{0,3},{1,0},{2,1},{3,2},{4,7},{5,4},{6,5},{7,6},{8,11},{9,8},{10,9... | collective-permute-start | bytes 147464 | tf_op jit(solution)/shard_map/ppermute | solution.py:621
  74.0 0.6 copy-start.4
  74.0 0.6 copy-start.5
  74.0 0.6 copy-start.6

commit v13 on v12

--- a/solution.py
+++ b/solution.py
@@ -615,13 +615,13 @@
         return jnp.transpose(x, (2, 0, 1)).reshape(nwl, lines // 128, 128)
 
     wa, *wfac = wfactor(h2, h_wl, h_wh, flags, ncl, nsub)
-    tfac = factor(tlo, tmd, thi, 4)
+    tfac = factor(tlo, tmd, thi, 8)
     yw, summ = width_solve(y, v, w, back, wa, wfac, nsub)
     got = [summ] + [
         lax.ppermute(summ, "width", [(i, (i + q) % nw) for i in range(nw)]) for q in range(1, nw)
     ]
     me = wi.astype(jnp.int32).reshape(1)
-    return thick_solve(me, got, yw, wfac[2], wfac[3], tlo, tfac, h, nsub, 4)
+    return thick_solve(me, got, yw, wfac[2], wfac[3], tlo, tfac, h, nsub, 8)
 
 
 def solution(mesh):

time: 78.3 us -> 78.2 us (level)
  transfers between devices with their start and end apart: 8 -> 8, of which waited for: 1 -> 1; matrix products, arithmetic and copies ran while one was open for 2% -> 2% of each run, Pallas kernels for 14% -> 13%
where the time goes in v13:
time: 78.2 us; the launch traced here: 77.7 us
  blocking collectives  24.5 us (31%)
  Pallas kernels  21.6 us (28%)
  starting transfers between devices  19.9 us (25%)
  waiting for transfers between devices  6.26 us (8%)
  local copies, waits for them, and re-layouts  4.68 us (6%)
    all_to_all x1, blocking collectives, shards(): lax.all_to_all(summ.reshape(nc, nt // nc, 8, nwl), 'cast', 0, 0, tiled=True)  24.5 us
    all_to_all x1, waiting for transfers between devices, shards(): back = lax.all_to_all(lr, 'cast', 0, 0, tiled=True).reshape(nt, 2, nwl)  6.21 us
    ppermute x3, starting transfers between devices, shards(): lax.ppermute(summ, 'width', [(i, (i + q) % nw) for i in range(nw)])  6.05 us
    all_to_all x1, starting transfers between devices, shards(): back = lax.all_to_all(lr, 'cast', 0, 0, tiled=True).reshape(nt, 2, nwl)  4.77 us
    pallas_call x1, Pallas kernels, prep_solve(): pl.pallas_call(functools.partial(_prep_kernel, n), out_shape=[shp] * 3 +...  4.27 us
    pallas_call x1, Pallas kernels, wfactor(): pl.pallas_call(functools.partial(_wfactor_kernel, n, nsub), out_shape=[sh...  3.88 us
    unnamed x20, local copies, waits for them, and re-layouts  3.31 us
    ppermute x1, starting transfers between devices, shards(): got_a = lax.ppermute(jnp.where(even, last, first), 'cast', in_chip)  3.29 us
  transfers between devices with their start and end apart: 8, of which 1 were waited for; matrix products, arithmetic and copies ran while one was open for 2% of the time, Pallas kernels for 13%

profile of v13, /device:TPU:1, one launch (start us, length us, event | category | flops | bytes accessed | tf_op | source)
XLA Modules:
  0.0 77.7 jit_solution(7321342270578551305)
XLA Ops:
  0.0 1.1 %fusion = (f32[64,1,128]{2,1,0:T(1,128)S(1)}, f32[64,1,128]{2,1,0:T(1,128)S(1)}) fusion(f32[64,8,128]{2,1,0:T(8,128)} %refs_12_.1), kind=kLoop, calls=%fused_computation.2 | loop fusion | bytes 131072 | tf_op jit(solution)/shard_map/slice | solution.py:587
  1.2 3.3 %collective-permute-start.2 = (f32[64,128]{1,0:T(8,128)S(1)}, f32[64,128]{1,0:T(8,128)S(1)}, u32[]{:S(2)}, u32[]{:S(2)}) collective-permute-start(f32[64,128]{1,0:T(8,128)S(1)} %get-tuple-element.56), channel_id=1, source_target_pairs={{0,4},{4,0},{8,12},{12,8},{16,20},{20,16},{24,28},{28,24},{32,36},... | collective-permute-start | bytes 98312 | tf_op jit(solution)/shard_map/ppermute | solution.py:590
  4.5 1.9 %collective-permute-start.3 = (f32[64,128]{1,0:T(8,128)S(1)}, f32[64,128]{1,0:T(8,128)S(1)}, u32[]{:S(2)}, u32[]{:S(2)}) collective-permute-start(f32[64,128]{1,0:T(8,128)S(1)} %get-tuple-element.55), channel_id=1, source_target_pairs={{4,8},{12,16},{20,24},{28,32},{36,40},{44,48},{52,56},{60,64},{68,... | collective-permute-start | bytes 98312 | tf_op jit(solution)/shard_map/ppermute | solution.py:591
  6.4 0.1 fusion.1
  6.5 0.4 copy.13
  7.0 2.6 %collective-permute-start = (f32[64,8]{1,0:T(8,128)S(1)}, f32[64,8]{1,0:T(8,128)S(1)}, u32[]{:S(2)}, u32[]{:S(2)}) collective-permute-start(f32[64,8]{1,0:T(8,128)S(1)} %bitcast.38), channel_id=1, source_target_pairs={{0,1},{1,2},{2,3},{4,5},{5,6},{6,7},{8,9},{9,10},{10,11},{12,13},{... | collective-permute-start | bytes 6152 | tf_op jit(solution)/shard_map/ppermute | solution.py:592
  9.6 0.4 copy.14
  10.0 1.3 %collective-permute-start.1 = (f32[64,8]{1,0:T(8,128)S(1)}, f32[64,8]{1,0:T(8,128)S(1)}, u32[]{:S(2)}, u32[]{:S(2)}) collective-permute-start(f32[64,8]{1,0:T(8,128)S(1)} %bitcast.39), channel_id=1, source_target_pairs={{1,0},{2,1},{3,2},{5,4},{6,5},{7,6},{9,8},{10,9},{11,10},{13,12},{... | collective-permute-start | bytes 6152 | tf_op jit(solution)/shard_map/ppermute | solution.py:593
  11.3 0.1 stack.30
  11.4 0.5 stack.31.fl_ref
  12.0 0.6 copy-done.7
  12.6 0.0 copy-done.8
  12.6 4.3 %shard_map.37 = (f32[512,128]{1,0:T(8,128)}, f32[512,128]{1,0:T(8,128)}, f32[512,128]{1,0:T(8,128)}, f32[512,128]{1,0:T(8,128)}, f32[512,128]{1,0:T(8,128)}, /*i...) custom-call(f32[512,128]{1,0:T(8,128)} %bitcast.24, ...), custom_call_target="tpu_custom_call" | custom-call | tf_op jit(solution)/shard_map/pallas_call | solution.py:292
  16.9 0.6 copy-done.2
  17.5 0.0 copy-done.3
  17.5 3.1 %shard_map.38 = (f32[512,128]{1,0:T(8,128)}, f32[512,128]{1,0:T(8,128)}) custom-call(f32[512,128]{1,0:T(8,128)} %bitcast.25, f32[64,8]{1,0:T(8,128)} %copy-done.2, f32[64,8]{1,0:T(8,128)} %copy-done.3, f32[5]{0:T(128)} %stack.31.fl_ref, f32[512,128]{1,0:T(8,128)} %get-tuple-element.28.a_ref, f32[512,128]{1,0:T(8,128)} %get-tuple-element.29.r_ref, ...), custom_call_target="tpu_custom_call" | custom-call | tf_op jit(solution)/shard_map/pallas_call | solution.py:329
  20.6 24.5 %all_to_all.10.s_ref = f32[64,1,8,128]{3,2,1,0:T(8,128)} all-to-all(f32[64,1,8,128]{3,2,1,0:T(8,128)} %bitcast.35), channel_id=1, replica_groups=mesh['cast'=64,'width'=4] {'cast'}, dimensions={0} | all-to-all | bytes 524288 | tf_op jit(solution)/shard_map/all_to_all | solution.py:605
  45.1 1.9 %shard_map.39 = f32[64,1,2,128]{3,2,1,0:T(2,128)} custom-call(f32[64,1,8,128]{3,2,1,0:T(8,128)} %all_to_all.10.s_ref), custom_call_target="tpu_custom_call" | custom-call | tf_op jit(solution)/shard_map/pallas_call | solution.py:607
  47.0 4.8 %all-to-all-start.1 = ((f32[64,1,2,128]{3,2,1,0:T(2,128)}), f32[64,1,2,128]{3,2,1,0:T(2,128)S(1)}, u32[]{:S(2)}, u32[]{:S(2)}) async-start(f32[64,1,2,128]{3,2,1,0:T(2,128)} %shard_map.39), calls=%async_computation.1 | async-start | bytes 131072 | tf_op jit(solution)/shard_map/all_to_all | solution.py:608
  51.8 3.9 %shard_map.40 = (f32[128,4,128]{2,1,0:T(4,128)}, f32[128,4,128]{2,1,0:T(4,128)}, f32[128,4,128]{2,1,0:T(4,128)}, f32[128,4,128]{2,1,0:T(4,128)}, f32[128,4,128]{2,1,0:T(4,128)}) custom-call(f32[512,128]{1,0:T(8,128)} %bitcast.26, f32[64,8]{1,0:T(8,128)} %copy-done.2, f32[64,8]{1,0:T(8,128)} %copy-done.3, f32[5]{0:T(128)} %stack.31.fl_ref), custom_call_target="tpu_custom_call" | custom-call | tf_op jit(solution)/shard_map/pallas_call | solution.py:364
  55.7 6.2 %all-to-all-done.1 = f32[64,1,2,128]{3,2,1,0:T(2,128)S(1)} async-done(((f32[64,1,2,128]{3,2,1,0:T(2,128)}), f32[64,1,2,128]{3,2,1,0:T(2,128)S(1)}, u32[]{:S(2)}, u32[]{:S(2)}) %all-to-all-start.1) | async-done | bytes 65568 | tf_op jit(solution)/shard_map/all_to_all | solution.py:608
  61.9 0.6 copy-done.1
  62.5 3.0 %shard_map.41 = (f32[128,4,128]{2,1,0:T(4,128)}, f32[4,6,4,128]{3,2,1,0:T(4,128)}) custom-call(f32[64,8,128]{2,1,0:T(8,128)} %bitcast.33, f32[64,8,128]{2,1,0:T(8,128)} %bitcast.31, f32[64,8,128]{2,1,0:T(8,128)} %bitcast.32, f32[64,2,128]{2,1,0:T(2,128)} %bitcast.34, f32[128,4,128]{2,1,0:T(4,128)} %get-tuple-element.37.a_ref, ...), custom_call_target="tpu_custom_call" | custom-call | tf_op jit(solution)/shard_map/pallas_call | solution.py:429
  65.5 2.4 %collective-permute-start.4 = (f32[4,6,4,128]{3,2,1,0:T(4,128)}, f32[4,6,4,128]{3,2,1,0:T(4,128)S(1)}, u32[]{:S(2)}, u32[]{:S(2)}) collective-permute-start(f32[4,6,4,128]{3,2,1,0:T(4,128)} %get-tuple-element.42.refs_0_), channel_id=1, source_target_pairs={{0,1},{1,2},{2,3},{3,0},{4,5},{5,6},{6,7},{7,4},{8,9},{9,10},{10,1... | collective-permute-start | bytes 147464 | tf_op jit(solution)/shard_map/ppermute | solution.py:621
  67.8 2.6 %collective-permute-start.5 = (f32[4,6,4,128]{3,2,1,0:T(4,128)}, f32[4,6,4,128]{3,2,1,0:T(4,128)S(1)}, u32[]{:S(2)}, u32[]{:S(2)}) collective-permute-start(f32[4,6,4,128]{3,2,1,0:T(4,128)} %get-tuple-element.42.refs_0_), channel_id=1, source_target_pairs={{0,2},{1,3},{2,0},{3,1},{4,6},{5,7},{6,4},{7,5},{8,10},{9,11},{10,... | collective-permute-start | bytes 147464 | tf_op jit(solution)/shard_map/ppermute | solution.py:621
  70.4 1.1 %collective-permute-start.6 = (f32[4,6,4,128]{3,2,1,0:T(4,128)}, f32[4,6,4,128]{3,2,1,0:T(4,128)S(1)}, u32[]{:S(2)}, u32[]{:S(2)}) collective-permute-start(f32[4,6,4,128]{3,2,1,0:T(4,128)} %get-tuple-element.42.refs_0_), channel_id=1, source_target_pairs={{0,3},{1,0},{2,1},{3,2},{4,7},{5,4},{6,5},{7,6},{8,11},{9,8},{10,9... | collective-permute-start | bytes 147464 | tf_op jit(solution)/shard_map/ppermute | solution.py:621
  71.5 2.3 %shard_map.42 = (f32[64,8,128]{2,1,0:T(8,128)}, f32[64,8,128]{2,1,0:T(8,128)}, f32[64,8,128]{2,1,0:T(8,128)}, f32[64,8,128]{2,1,0:T(8,128)}) custom-call(f32[64,8,128]{2,1,0:T(8,128)} %bitcast.27, f32[64,8,128]{2,1,0:T(8,128)} %bitcast.29, f32[64,8,128]{2,1,0:T(8,128)} %bitcast.30), custom_call_target="tpu_custom_call" | custom-call | tf_op jit(solution)/shard_map/pallas_call | solution.py:182
  73.9 0.0 collective-permute-done.6.refs_3_
  73.9 0.6 copy-done.4
  74.4 0.0 copy-done.5
  74.5 0.0 copy-done.6
  74.5 3.2 %shard_map.43 = f32[64,8,128]{2,1,0:T(8,128)} custom-call(s32[1]{0:T(128)} %bitcast.me_ref, f32[4,6,4,128]{3,2,1,0:T(4,128)} %get-tuple-element.42.refs_0_, f32[4,6,4,128]{3,2,1,0:T(4,128)} %copy-done.4, f32[4,6,4,128]{3,2,1,0:T(4,128)} %copy-done.5, f32[4,6,4,128]{3,2,1,0:T(4,128)} %copy-done.6, f32[128,4,128]{2,1,0:T(4,128)} %get-tuple-element.43.refs_4_, ...), custom_call_target="tpu_custom_call" | custom-call | tf_op jit(solution)/shard_map/pallas_call | solution.py:438
  (17 shorter events, 0.0 us)
Async XLA Ops:
  0.0 6.4 %copy-start = (f32[64,8,128]{2,1,0:T(8,128)S(1)}, f32[64,8,128]{2,1,0:T(8,128)}, u32[]{:S(2)}) copy-start(f32[64,8,128]{2,1,0:T(8,128)} %refs_12_.1) | copy-start | bytes 786436
  1.2 10.8 %collective-permute-start.2 = (f32[64,128]{1,0:T(8,128)S(1)}, f32[64,128]{1,0:T(8,128)S(1)}, u32[]{:S(2)}, u32[]{:S(2)}) collective-permute-start(f32[64,128]{1,0:T(8,128)S(1)} %get-tuple-element.56), channel_id=1, source_target_pairs={{0,4},{4,0},{8,12},{12,8},{16,20},{20,16},{24,28},{28,24},{32,36},... | collective-permute-start | bytes 98312 | tf_op jit(solution)/shard_map/ppermute | solution.py:590
  4.5 7.5 %collective-permute-start.3 = (f32[64,128]{1,0:T(8,128)S(1)}, f32[64,128]{1,0:T(8,128)S(1)}, u32[]{:S(2)}, u32[]{:S(2)}) collective-permute-start(f32[64,128]{1,0:T(8,128)S(1)} %get-tuple-element.55), channel_id=1, source_target_pairs={{4,8},{12,16},{20,24},{28,32},{36,40},{44,48},{52,56},{60,64},{68,... | collective-permute-start | bytes 98312 | tf_op jit(solution)/shard_map/ppermute | solution.py:591
  7.0 9.9 %collective-permute-start = (f32[64,8]{1,0:T(8,128)S(1)}, f32[64,8]{1,0:T(8,128)S(1)}, u32[]{:S(2)}, u32[]{:S(2)}) collective-permute-start(f32[64,8]{1,0:T(8,128)S(1)} %bitcast.38), channel_id=1, source_target_pairs={{0,1},{1,2},{2,3},{4,5},{5,6},{6,7},{8,9},{9,10},{10,11},{12,13},{... | collective-permute-start | bytes 6152 | tf_op jit(solution)/shard_map/ppermute | solution.py:592
  10.0 6.9 %collective-permute-start.1 = (f32[64,8]{1,0:T(8,128)S(1)}, f32[64,8]{1,0:T(8,128)S(1)}, u32[]{:S(2)}, u32[]{:S(2)}) collective-permute-start(f32[64,8]{1,0:T(8,128)S(1)} %bitcast.39), channel_id=1, source_target_pairs={{1,0},{2,1},{3,2},{5,4},{6,5},{7,6},{9,8},{10,9},{11,10},{13,12},{... | collective-permute-start | bytes 6152 | tf_op jit(solution)/shard_map/ppermute | solution.py:593
  12.0 0.6 copy-start.7
  12.0 0.6 copy-start.8
  16.9 0.6 copy-start.2
  16.9 0.6 copy-start.3
  47.0 14.9 %all-to-all-start.1 = ((f32[64,1,2,128]{3,2,1,0:T(2,128)}), f32[64,1,2,128]{3,2,1,0:T(2,128)S(1)}, u32[]{:S(2)}, u32[]{:S(2)}) async-start(f32[64,1,2,128]{3,2,1,0:T(2,128)} %shard_map.39), calls=%async_computation.1 | async-start | bytes 131072 | tf_op jit(solution)/shard_map/all_to_all | solution.py:608
  61.9 0.6 copy-start.1
  65.5 8.4 %collective-permute-start.4 = (f32[4,6,4,128]{3,2,1,0:T(4,128)}, f32[4,6,4,128]{3,2,1,0:T(4,128)S(1)}, u32[]{:S(2)}, u32[]{:S(2)}) collective-permute-start(f32[4,6,4,128]{3,2,1,0:T(4,128)} %get-tuple-element.42.refs_0_), channel_id=1, source_target_pairs={{0,1},{1,2},{2,3},{3,0},{4,5},{5,6},{6,7},{7,4},{8,9},{9,10},{10,1... | collective-permute-start | bytes 147464 | tf_op jit(solution)/shard_map/ppermute | solution.py:621
  67.8 6.0 %collective-permute-start.5 = (f32[4,6,4,128]{3,2,1,0:T(4,128)}, f32[4,6,4,128]{3,2,1,0:T(4,128)S(1)}, u32[]{:S(2)}, u32[]{:S(2)}) collective-permute-start(f32[4,6,4,128]{3,2,1,0:T(4,128)} %get-tuple-element.42.refs_0_), channel_id=1, source_target_pairs={{0,2},{1,3},{2,0},{3,1},{4,6},{5,7},{6,4},{7,5},{8,10},{9,11},{10,... | collective-permute-start | bytes 147464 | tf_op jit(solution)/shard_map/ppermute | solution.py:621
  70.4 3.4 %collective-permute-start.6 = (f32[4,6,4,128]{3,2,1,0:T(4,128)}, f32[4,6,4,128]{3,2,1,0:T(4,128)S(1)}, u32[]{:S(2)}, u32[]{:S(2)}) collective-permute-start(f32[4,6,4,128]{3,2,1,0:T(4,128)} %get-tuple-element.42.refs_0_), channel_id=1, source_target_pairs={{0,3},{1,0},{2,1},{3,2},{4,7},{5,4},{6,5},{7,6},{8,11},{9,8},{10,9... | collective-permute-start | bytes 147464 | tf_op jit(solution)/shard_map/ppermute | solution.py:621
  73.8 0.6 copy-start.4
  73.8 0.6 copy-start.5
  73.9 0.6 copy-start.6

commit v14 on v13

--- a/solution.py
+++ b/solution.py
@@ -609,7 +609,7 @@
     y, v, w = (x.reshape(nt, ncl, nwl) for x in (y, v, w))
 
     lines = nt * ncl
-    nsub = 4
+    nsub = 8
 
     def wl(x):
         return jnp.transpose(x, (2, 0, 1)).reshape(nwl, lines // 128, 128)

time: 78.2 us -> 79.9 us (1.022)
  waiting for transfers between devices: 6.26 us -> 7.73 us
    ppermute x3, waiting for transfers between devices: 0.04 us -> 1.42 us  [shards(): lax.ppermute(summ, 'width', [(i, (i + q) % nw) for i in range(nw)])]
  transfers between devices with their start and end apart: 8 -> 8, of which waited for: 1 -> 2; matrix products, arithmetic and copies ran while one was open for 2% -> 2% of each run, Pallas kernels for 13% -> 13%
where the time goes in v14:
time: 79.9 us; the launch traced here: 79.4 us
  blocking collectives  24.5 us (31%)
  Pallas kernels  21.8 us (27%)
  starting transfers between devices  19.9 us (25%)
  waiting for transfers between devices  7.73 us (10%)
  local copies, waits for them, and re-layouts  4.72 us (6%)
    all_to_all x1, blocking collectives, shards(): lax.all_to_all(summ.reshape(nc, nt // nc, 8, nwl), 'cast', 0, 0, tiled=True)  24.5 us
    all_to_all x1, waiting for transfers between devices, shards(): back = lax.all_to_all(lr, 'cast', 0, 0, tiled=True).reshape(nt, 2, nwl)  6.29 us
    ppermute x3, starting transfers between devices, shards(): lax.ppermute(summ, 'width', [(i, (i + q) % nw) for i in range(nw)])  6.05 us
    all_to_all x1, starting transfers between devices, shards(): back = lax.all_to_all(lr, 'cast', 0, 0, tiled=True).reshape(nt, 2, nwl)  4.77 us
    pallas_call x1, Pallas kernels, prep_solve(): pl.pallas_call(functools.partial(_prep_kernel, n), out_shape=[shp] * 3 +...  4.27 us
    pallas_call x1, Pallas kernels, wfactor(): pl.pallas_call(functools.partial(_wfactor_kernel, n, nsub), out_shape=[sh...  3.79 us
    pallas_call x1, Pallas kernels, thick_solve(): pl.pallas_call(functools.partial(_thick_kernel, nsub, tsub, len(got)), ou...  3.5 us
    unnamed x20, local copies, waits for them, and re-layouts  3.35 us
  transfers between devices with their start and end apart: 8, of which 2 were waited for; matrix products, arithmetic and copies ran while one was open for 2% of the time, Pallas kernels for 13%

profile of v14, /device:TPU:1, one launch (start us, length us, event | category | flops | bytes accessed | tf_op | source)
XLA Modules:
  0.0 79.4 jit_solution(10346098138807676100)
XLA Ops:
  0.0 1.1 %fusion = (f32[64,1,128]{2,1,0:T(1,128)S(1)}, f32[64,1,128]{2,1,0:T(1,128)S(1)}) fusion(f32[64,8,128]{2,1,0:T(8,128)} %refs_12_.1), kind=kLoop, calls=%fused_computation.2 | loop fusion | bytes 131072 | tf_op jit(solution)/shard_map/slice | solution.py:587
  1.2 3.3 %collective-permute-start.2 = (f32[64,128]{1,0:T(8,128)S(1)}, f32[64,128]{1,0:T(8,128)S(1)}, u32[]{:S(2)}, u32[]{:S(2)}) collective-permute-start(f32[64,128]{1,0:T(8,128)S(1)} %get-tuple-element.56), channel_id=1, source_target_pairs={{0,4},{4,0},{8,12},{12,8},{16,20},{20,16},{24,28},{28,24},{32,36},... | collective-permute-start | bytes 98312 | tf_op jit(solution)/shard_map/ppermute | solution.py:590
  4.5 1.9 %collective-permute-start.3 = (f32[64,128]{1,0:T(8,128)S(1)}, f32[64,128]{1,0:T(8,128)S(1)}, u32[]{:S(2)}, u32[]{:S(2)}) collective-permute-start(f32[64,128]{1,0:T(8,128)S(1)} %get-tuple-element.55), channel_id=1, source_target_pairs={{4,8},{12,16},{20,24},{28,32},{36,40},{44,48},{52,56},{60,64},{68,... | collective-permute-start | bytes 98312 | tf_op jit(solution)/shard_map/ppermute | solution.py:591
  6.4 0.1 fusion.1
  6.5 0.4 copy.13
  7.0 2.6 %collective-permute-start = (f32[64,8]{1,0:T(8,128)S(1)}, f32[64,8]{1,0:T(8,128)S(1)}, u32[]{:S(2)}, u32[]{:S(2)}) collective-permute-start(f32[64,8]{1,0:T(8,128)S(1)} %bitcast.38), channel_id=1, source_target_pairs={{0,1},{1,2},{2,3},{4,5},{5,6},{6,7},{8,9},{9,10},{10,11},{12,13},{... | collective-permute-start | bytes 6152 | tf_op jit(solution)/shard_map/ppermute | solution.py:592
  9.6 0.4 copy.14
  10.0 1.3 %collective-permute-start.1 = (f32[64,8]{1,0:T(8,128)S(1)}, f32[64,8]{1,0:T(8,128)S(1)}, u32[]{:S(2)}, u32[]{:S(2)}) collective-permute-start(f32[64,8]{1,0:T(8,128)S(1)} %bitcast.39), channel_id=1, source_target_pairs={{1,0},{2,1},{3,2},{5,4},{6,5},{7,6},{9,8},{10,9},{11,10},{13,12},{... | collective-permute-start | bytes 6152 | tf_op jit(solution)/shard_map/ppermute | solution.py:593
  11.3 0.1 stack.30
  11.4 0.5 stack.31.fl_ref
  12.0 0.0 collective-permute-done.2.hcl_ref
  12.0 0.6 copy-done.7
  12.6 0.0 copy-done.8
  12.6 4.3 %shard_map.37 = (f32[512,128]{1,0:T(8,128)}, f32[512,128]{1,0:T(8,128)}, f32[512,128]{1,0:T(8,128)}, f32[512,128]{1,0:T(8,128)}, f32[512,128]{1,0:T(8,128)}, /*i...) custom-call(f32[512,128]{1,0:T(8,128)} %bitcast.24, ...), custom_call_target="tpu_custom_call" | custom-call | tf_op jit(solution)/shard_map/pallas_call | solution.py:292
  16.9 0.6 copy-done.2
  17.5 0.0 copy-done.3
  17.5 3.1 %shard_map.38 = (f32[512,128]{1,0:T(8,128)}, f32[512,128]{1,0:T(8,128)}) custom-call(f32[512,128]{1,0:T(8,128)} %bitcast.25, f32[64,8]{1,0:T(8,128)} %copy-done.2, f32[64,8]{1,0:T(8,128)} %copy-done.3, f32[5]{0:T(128)} %stack.31.fl_ref, f32[512,128]{1,0:T(8,128)} %get-tuple-element.28.a_ref, f32[512,128]{1,0:T(8,128)} %get-tuple-element.29.r_ref, ...), custom_call_target="tpu_custom_call" | custom-call | tf_op jit(solution)/shard_map/pallas_call | solution.py:329
  20.6 24.5 %all_to_all.10.s_ref = f32[64,1,8,128]{3,2,1,0:T(8,128)} all-to-all(f32[64,1,8,128]{3,2,1,0:T(8,128)} %bitcast.35), channel_id=1, replica_groups=mesh['cast'=64,'width'=4] {'cast'}, dimensions={0} | all-to-all | bytes 524288 | tf_op jit(solution)/shard_map/all_to_all | solution.py:605
  45.1 1.9 %shard_map.39 = f32[64,1,2,128]{3,2,1,0:T(2,128)} custom-call(f32[64,1,8,128]{3,2,1,0:T(8,128)} %all_to_all.10.s_ref), custom_call_target="tpu_custom_call" | custom-call | tf_op jit(solution)/shard_map/pallas_call | solution.py:607
  47.0 4.8 %all-to-all-start.1 = ((f32[64,1,2,128]{3,2,1,0:T(2,128)}), f32[64,1,2,128]{3,2,1,0:T(2,128)S(1)}, u32[]{:S(2)}, u32[]{:S(2)}) async-start(f32[64,1,2,128]{3,2,1,0:T(2,128)} %shard_map.39), calls=%async_computation.1 | async-start | bytes 131072 | tf_op jit(solution)/shard_map/all_to_all | solution.py:608
  51.8 3.8 %shard_map.40 = (f32[128,4,128]{2,1,0:T(4,128)}, f32[128,4,128]{2,1,0:T(4,128)}, f32[128,4,128]{2,1,0:T(4,128)}, f32[128,4,128]{2,1,0:T(4,128)}, f32[128,4,128]{2,1,0:T(4,128)}) custom-call(f32[512,128]{1,0:T(8,128)} %bitcast.26, f32[64,8]{1,0:T(8,128)} %copy-done.2, f32[64,8]{1,0:T(8,128)} %copy-done.3, f32[5]{0:T(128)} %stack.31.fl_ref), custom_call_target="tpu_custom_call" | custom-call | tf_op jit(solution)/shard_map/pallas_call | solution.py:364
  55.6 6.3 %all-to-all-done.1 = f32[64,1,2,128]{3,2,1,0:T(2,128)S(1)} async-done(((f32[64,1,2,128]{3,2,1,0:T(2,128)}), f32[64,1,2,128]{3,2,1,0:T(2,128)S(1)}, u32[]{:S(2)}, u32[]{:S(2)}) %all-to-all-start.1) | async-done | bytes 65568 | tf_op jit(solution)/shard_map/all_to_all | solution.py:608
  61.9 0.6 copy-done.1
  62.5 3.0 %shard_map.41 = (f32[128,4,128]{2,1,0:T(4,128)}, f32[8,6,4,128]{3,2,1,0:T(4,128)}) custom-call(f32[64,8,128]{2,1,0:T(8,128)} %bitcast.33, f32[64,8,128]{2,1,0:T(8,128)} %bitcast.31, f32[64,8,128]{2,1,0:T(8,128)} %bitcast.32, f32[64,2,128]{2,1,0:T(2,128)} %bitcast.34, f32[128,4,128]{2,1,0:T(4,128)} %get-tuple-element.37.a_ref, ...), custom_call_target="tpu_custom_call" | custom-call | tf_op jit(solution)/shard_map/pallas_call | solution.py:429
  65.5 2.4 %collective-permute-start.4 = (f32[8,6,4,128]{3,2,1,0:T(4,128)}, f32[8,6,4,128]{3,2,1,0:T(4,128)S(1)}, u32[]{:S(2)}, u32[]{:S(2)}) collective-permute-start(f32[8,6,4,128]{3,2,1,0:T(4,128)} %get-tuple-element.42.refs_0_), channel_id=1, source_target_pairs={{0,1},{1,2},{2,3},{3,0},{4,5},{5,6},{6,7},{7,4},{8,9},{9,10},{10,1... | collective-permute-start | bytes 294920 | tf_op jit(solution)/shard_map/ppermute | solution.py:621
  67.8 2.6 %collective-permute-start.5 = (f32[8,6,4,128]{3,2,1,0:T(4,128)}, f32[8,6,4,128]{3,2,1,0:T(4,128)S(1)}, u32[]{:S(2)}, u32[]{:S(2)}) collective-permute-start(f32[8,6,4,128]{3,2,1,0:T(4,128)} %get-tuple-element.42.refs_0_), channel_id=1, source_target_pairs={{0,2},{1,3},{2,0},{3,1},{4,6},{5,7},{6,4},{7,5},{8,10},{9,11},{10,... | collective-permute-start | bytes 294920 | tf_op jit(solution)/shard_map/ppermute | solution.py:621
  70.4 1.1 %collective-permute-start.6 = (f32[8,6,4,128]{3,2,1,0:T(4,128)}, f32[8,6,4,128]{3,2,1,0:T(4,128)S(1)}, u32[]{:S(2)}, u32[]{:S(2)}) collective-permute-start(f32[8,6,4,128]{3,2,1,0:T(4,128)} %get-tuple-element.42.refs_0_), channel_id=1, source_target_pairs={{0,3},{1,0},{2,1},{3,2},{4,7},{5,4},{6,5},{7,6},{8,11},{9,8},{10,9... | collective-permute-start | bytes 294920 | tf_op jit(solution)/shard_map/ppermute | solution.py:621
  71.5 2.3 %shard_map.42 = (f32[64,8,128]{2,1,0:T(8,128)}, f32[64,8,128]{2,1,0:T(8,128)}, f32[64,8,128]{2,1,0:T(8,128)}, f32[64,8,128]{2,1,0:T(8,128)}) custom-call(f32[64,8,128]{2,1,0:T(8,128)} %bitcast.27, f32[64,8,128]{2,1,0:T(8,128)} %bitcast.29, f32[64,8,128]{2,1,0:T(8,128)} %bitcast.30), custom_call_target="tpu_custom_call" | custom-call | tf_op jit(solution)/shard_map/pallas_call | solution.py:182
  73.8 1.4 %collective-permute-done.5.refs_2_ = f32[8,6,4,128]{3,2,1,0:T(4,128)S(1)} collective-permute-done((f32[8,6,4,128]{3,2,1,0:T(4,128)}, f32[8,6,4,128]{3,2,1,0:T(4,128)S(1)}, u32[]{:S(2)}, u32[]{:S(2)}) %collective-permute-start.5) | collective-permute-done | bytes 98336 | tf_op jit(solution)/shard_map/ppermute | solution.py:621
  75.3 0.6 copy-done.5
  75.9 0.0 copy-done.6
  75.9 3.5 %shard_map.43 = f32[64,8,128]{2,1,0:T(8,128)} custom-call(s32[1]{0:T(128)} %bitcast.me_ref, f32[8,6,4,128]{3,2,1,0:T(4,128)} %get-tuple-element.42.refs_0_, f32[8,6,4,128]{3,2,1,0:T(4,128)} %copy-done.4, f32[8,6,4,128]{3,2,1,0:T(4,128)} %copy-done.5, f32[8,6,4,128]{3,2,1,0:T(4,128)} %copy-done.6, f32[128,4,128]{2,1,0:T(4,128)} %get-tuple-element.43.refs_4_, ...), custom_call_target="tpu_custom_call" | custom-call | tf_op jit(solution)/shard_map/pallas_call | solution.py:438
  (17 shorter events, 0.0 us)
Async XLA Ops:
  0.0 6.4 %copy-start = (f32[64,8,128]{2,1,0:T(8,128)S(1)}, f32[64,8,128]{2,1,0:T(8,128)}, u32[]{:S(2)}) copy-start(f32[64,8,128]{2,1,0:T(8,128)} %refs_12_.1) | copy-start | bytes 786436
  1.2 10.8 %collective-permute-start.2 = (f32[64,128]{1,0:T(8,128)S(1)}, f32[64,128]{1,0:T(8,128)S(1)}, u32[]{:S(2)}, u32[]{:S(2)}) collective-permute-start(f32[64,128]{1,0:T(8,128)S(1)} %get-tuple-element.56), channel_id=1, source_target_pairs={{0,4},{4,0},{8,12},{12,8},{16,20},{20,16},{24,28},{28,24},{32,36},... | collective-permute-start | bytes 98312 | tf_op jit(solution)/shard_map/ppermute | solution.py:590
  4.5 7.5 %collective-permute-start.3 = (f32[64,128]{1,0:T(8,128)S(1)}, f32[64,128]{1,0:T(8,128)S(1)}, u32[]{:S(2)}, u32[]{:S(2)}) collective-permute-start(f32[64,128]{1,0:T(8,128)S(1)} %get-tuple-element.55), channel_id=1, source_target_pairs={{4,8},{12,16},{20,24},{28,32},{36,40},{44,48},{52,56},{60,64},{68,... | collective-permute-start | bytes 98312 | tf_op jit(solution)/shard_map/ppermute | solution.py:591
  7.0 9.9 %collective-permute-start = (f32[64,8]{1,0:T(8,128)S(1)}, f32[64,8]{1,0:T(8,128)S(1)}, u32[]{:S(2)}, u32[]{:S(2)}) collective-permute-start(f32[64,8]{1,0:T(8,128)S(1)} %bitcast.38), channel_id=1, source_target_pairs={{0,1},{1,2},{2,3},{4,5},{5,6},{6,7},{8,9},{9,10},{10,11},{12,13},{... | collective-permute-start | bytes 6152 | tf_op jit(solution)/shard_map/ppermute | solution.py:592
  10.0 6.9 %collective-permute-start.1 = (f32[64,8]{1,0:T(8,128)S(1)}, f32[64,8]{1,0:T(8,128)S(1)}, u32[]{:S(2)}, u32[]{:S(2)}) collective-permute-start(f32[64,8]{1,0:T(8,128)S(1)} %bitcast.39), channel_id=1, source_target_pairs={{1,0},{2,1},{3,2},{5,4},{6,5},{7,6},{9,8},{10,9},{11,10},{13,12},{... | collective-permute-start | bytes 6152 | tf_op jit(solution)/shard_map/ppermute | solution.py:593
  12.0 0.6 copy-start.7
  12.0 0.6 copy-start.8
  16.9 0.6 copy-start.2
  16.9 0.6 copy-start.3
  47.0 14.9 %all-to-all-start.1 = ((f32[64,1,2,128]{3,2,1,0:T(2,128)}), f32[64,1,2,128]{3,2,1,0:T(2,128)S(1)}, u32[]{:S(2)}, u32[]{:S(2)}) async-start(f32[64,1,2,128]{3,2,1,0:T(2,128)} %shard_map.39), calls=%async_computation.1 | async-start | bytes 131072 | tf_op jit(solution)/shard_map/all_to_all | solution.py:608
  61.9 0.6 copy-start.1
  65.5 8.4 %collective-permute-start.4 = (f32[8,6,4,128]{3,2,1,0:T(4,128)}, f32[8,6,4,128]{3,2,1,0:T(4,128)S(1)}, u32[]{:S(2)}, u32[]{:S(2)}) collective-permute-start(f32[8,6,4,128]{3,2,1,0:T(4,128)} %get-tuple-element.42.refs_0_), channel_id=1, source_target_pairs={{0,1},{1,2},{2,3},{3,0},{4,5},{5,6},{6,7},{7,4},{8,9},{9,10},{10,1... | collective-permute-start | bytes 294920 | tf_op jit(solution)/shard_map/ppermute | solution.py:621
  67.8 7.4 %collective-permute-start.5 = (f32[8,6,4,128]{3,2,1,0:T(4,128)}, f32[8,6,4,128]{3,2,1,0:T(4,128)S(1)}, u32[]{:S(2)}, u32[]{:S(2)}) collective-permute-start(f32[8,6,4,128]{3,2,1,0:T(4,128)} %get-tuple-element.42.refs_0_), channel_id=1, source_target_pairs={{0,2},{1,3},{2,0},{3,1},{4,6},{5,7},{6,4},{7,5},{8,10},{9,11},{10,... | collective-permute-start | bytes 294920 | tf_op jit(solution)/shard_map/ppermute | solution.py:621
  70.4 4.8 %collective-permute-start.6 = (f32[8,6,4,128]{3,2,1,0:T(4,128)}, f32[8,6,4,128]{3,2,1,0:T(4,128)S(1)}, u32[]{:S(2)}, u32[]{:S(2)}) collective-permute-start(f32[8,6,4,128]{3,2,1,0:T(4,128)} %get-tuple-element.42.refs_0_), channel_id=1, source_target_pairs={{0,3},{1,0},{2,1},{3,2},{4,7},{5,4},{6,5},{7,6},{8,11},{9,8},{10,9... | collective-permute-start | bytes 294920 | tf_op jit(solution)/shard_map/ppermute | solution.py:621
  73.8 1.4 %copy-start.4 = (f32[8,6,4,128]{3,2,1,0:T(4,128)}, f32[8,6,4,128]{3,2,1,0:T(4,128)S(1)}, u32[]{:S(2)}) copy-start(f32[8,6,4,128]{3,2,1,0:T(4,128)S(1)} %collective-permute-done.4.refs_1_) | copy-start | bytes 294916
  75.2 0.6 copy-start.5
  75.3 0.7 copy-start.6

commit v15 on v13

--- a/solution.py
+++ b/solution.py
@@ -335,7 +335,7 @@
 
 
 def _wfactor_kernel(n, nsub, h_ref, hwl_ref, hwh_ref, fl_ref, a_ref, r_ref, cp_ref, v_ref, w_ref,
-                    at_ref, bt_ref, ct_ref, b_ref, c_ref):
+                    vws_ref, at_ref, bt_ref, ct_ref, b_ref, c_ref):
     rows, nwl = h_ref.shape
     nt = rows // n
     lane = lax.broadcasted_iota(jnp.int32, (nt, nwl), 1)
@@ -354,6 +354,9 @@
     m = a_ref.shape[0] // nsub
     subs = [q * m for q in range(nsub)]
     _factor(m, subs, _lead_ld, _lead_st, a_ref, b_ref, c_ref, r_ref, cp_ref, v_ref, w_ref, 4, a_ref.shape[1:])
+    for q, s0 in enumerate(subs):
+        for k, val in enumerate((v_ref[s0], w_ref[s0], v_ref[s0 + m - 1], w_ref[s0 + m - 1])):
+            vws_ref[q, k] = val
 
 
 def wfactor(h2, hwl, hwh, flags, n, nsub):
@@ -363,13 +366,13 @@
     vm = pl.BlockSpec(memory_space=pltpu.VMEM)
     return pl.pallas_call(
         functools.partial(_wfactor_kernel, n, nsub),
-        out_shape=[shp] * 5,
+        out_shape=[shp] * 5 + [jax.ShapeDtypeStruct((nsub, 4) + wshape[1:], F32)],
         in_specs=[vm] * 3 + [SMEM_SPEC],
         scratch_shapes=[pltpu.VMEM(h2.shape, F32)] * 3 + [pltpu.VMEM(wshape, F32)] * 2,
     )(h2, hwl, hwh, flags)
 
 
-def _width_kernel(nsub, yc_ref, vc_ref, wc_ref, bk_ref, a_ref, r_ref, cp_ref, v_ref, w_ref,
+def _width_kernel(nsub, yc_ref, vc_ref, wc_ref, bk_ref, a_ref, r_ref, cp_ref, vws_ref,
                   y_ref, sm_ref, d_ref):
     sc = yc_ref[...] + vc_ref[...] * bk_ref[:, 0:1, :] + wc_ref[...] * bk_ref[:, 1:2, :]
     nt, ncl, nwl = sc.shape
@@ -380,7 +383,8 @@
     subs = [q * n for q in range(nsub)]
     _solve_rhs(n, subs, _lead_ld, _lead_st, a_ref, r_ref, cp_ref, d_ref, y_ref, 4, a_ref.shape[1:])
     for q, s0 in enumerate(subs):
-        for k, val in enumerate(_summary_rows(_lead_ld, s0, n, y_ref, v_ref, w_ref)):
+        rows = (y_ref[s0], vws_ref[q, 0], vws_ref[q, 1], y_ref[s0 + n - 1], vws_ref[q, 2], vws_ref[q, 3])
+        for k, val in enumerate(rows):
             sm_ref[q, k] = val
 
 
@@ -614,9 +618,10 @@
     def wl(x):
         return jnp.transpose(x, (2, 0, 1)).reshape(nwl, lines // 128, 128)
 
-    wa, *wfac = wfactor(h2, h_wl, h_wh, flags, ncl, nsub)
+    wa, r_w, cp_w, v_w, w_w, vws = wfactor(h2, h_wl, h_wh, flags, ncl, nsub)
+    wfac = (r_w, cp_w, v_w, w_w)
     tfac = factor(tlo, tmd, thi, 8)
-    yw, summ = width_solve(y, v, w, back, wa, wfac, nsub)
+    yw, summ = width_solve(y, v, w, back, wa, (r_w, cp_w, vws), nsub)
     got = [summ] + [
         lax.ppermute(summ, "width", [(i, (i + q) % nw) for i in range(nw)]) for q in range(1, nw)
     ]

time: 78.2 us -> 78 us (level)
  transfers between devices with their start and end apart: 8 -> 8, of which waited for: 1 -> 1; matrix products, arithmetic and copies ran while one was open for 2% -> 2% of each run, Pallas kernels for 13% -> 14%
where the time goes in v15:
time: 78 us; the launch traced here: 77.5 us
  blocking collectives  24.5 us (31%)
  Pallas kernels  21.5 us (28%)
  starting transfers between devices  19.9 us (26%)
  waiting for transfers between devices  6.25 us (8%)
  local copies, waits for them, and re-layouts  4.68 us (6%)
    all_to_all x1, blocking collectives, shards(): lax.all_to_all(summ.reshape(nc, nt // nc, 8, nwl), 'cast', 0, 0, tiled=True)  24.5 us
    all_to_all x1, waiting for transfers between devices, shards(): back = lax.all_to_all(lr, 'cast', 0, 0, tiled=True).reshape(nt, 2, nwl)  6.2 us
    ppermute x3, starting transfers between devices, shards(): lax.ppermute(summ, 'width', [(i, (i + q) % nw) for i in range(nw)])  6.05 us
    all_to_all x1, starting transfers between devices, shards(): back = lax.all_to_all(lr, 'cast', 0, 0, tiled=True).reshape(nt, 2, nwl)  4.77 us
    pallas_call x1, Pallas kernels, prep_solve(): pl.pallas_call(functools.partial(_prep_kernel, n), out_shape=[shp] * 3 +...  4.27 us
    pallas_call x1, Pallas kernels, wfactor(): pl.pallas_call(functools.partial(_wfactor_kernel, n, nsub), out_shape=[sh...  3.89 us
    unnamed x20, local copies, waits for them, and re-layouts  3.31 us
    ppermute x1, starting transfers between devices, shards(): got_a = lax.ppermute(jnp.where(even, last, first), 'cast', in_chip)  3.29 us
  transfers between devices with their start and end apart: 8, of which 1 were waited for; matrix products, arithmetic and copies ran while one was open for 2% of the time, Pallas kernels for 14%

profile of v15, /device:TPU:1, one launch (start us, length us, event | category | flops | bytes accessed | tf_op | source)
XLA Modules:
  0.0 77.5 jit_solution(15905246348546368925)
XLA Ops:
  0.0 1.1 %fusion = (f32[64,1,128]{2,1,0:T(1,128)S(1)}, f32[64,1,128]{2,1,0:T(1,128)S(1)}) fusion(f32[64,8,128]{2,1,0:T(8,128)} %refs_12_.1), kind=kLoop, calls=%fused_computation.2 | loop fusion | bytes 131072 | tf_op jit(solution)/shard_map/slice | solution.py:591
  1.2 3.3 %collective-permute-start.2 = (f32[64,128]{1,0:T(8,128)S(1)}, f32[64,128]{1,0:T(8,128)S(1)}, u32[]{:S(2)}, u32[]{:S(2)}) collective-permute-start(f32[64,128]{1,0:T(8,128)S(1)} %get-tuple-element.58), channel_id=1, source_target_pairs={{0,4},{4,0},{8,12},{12,8},{16,20},{20,16},{24,28},{28,24},{32,36},... | collective-permute-start | bytes 98312 | tf_op jit(solution)/shard_map/ppermute | solution.py:594
  4.5 1.9 %collective-permute-start.3 = (f32[64,128]{1,0:T(8,128)S(1)}, f32[64,128]{1,0:T(8,128)S(1)}, u32[]{:S(2)}, u32[]{:S(2)}) collective-permute-start(f32[64,128]{1,0:T(8,128)S(1)} %get-tuple-element.57), channel_id=1, source_target_pairs={{4,8},{12,16},{20,24},{28,32},{36,40},{44,48},{52,56},{60,64},{68,... | collective-permute-start | bytes 98312 | tf_op jit(solution)/shard_map/ppermute | solution.py:595
  6.4 0.1 fusion.1
  6.5 0.4 copy.13
  7.0 2.6 %collective-permute-start = (f32[64,8]{1,0:T(8,128)S(1)}, f32[64,8]{1,0:T(8,128)S(1)}, u32[]{:S(2)}, u32[]{:S(2)}) collective-permute-start(f32[64,8]{1,0:T(8,128)S(1)} %bitcast.38), channel_id=1, source_target_pairs={{0,1},{1,2},{2,3},{4,5},{5,6},{6,7},{8,9},{9,10},{10,11},{12,13},{... | collective-permute-start | bytes 6152 | tf_op jit(solution)/shard_map/ppermute | solution.py:596
  9.6 0.4 copy.14
  10.0 1.3 %collective-permute-start.1 = (f32[64,8]{1,0:T(8,128)S(1)}, f32[64,8]{1,0:T(8,128)S(1)}, u32[]{:S(2)}, u32[]{:S(2)}) collective-permute-start(f32[64,8]{1,0:T(8,128)S(1)} %bitcast.39), channel_id=1, source_target_pairs={{1,0},{2,1},{3,2},{5,4},{6,5},{7,6},{9,8},{10,9},{11,10},{13,12},{... | collective-permute-start | bytes 6152 | tf_op jit(solution)/shard_map/ppermute | solution.py:597
  11.3 0.1 stack.30
  11.4 0.5 stack.31.fl_ref
  12.0 0.6 copy-done.7
  12.6 0.0 copy-done.8
  12.6 4.3 %shard_map.37 = (f32[512,128]{1,0:T(8,128)}, f32[512,128]{1,0:T(8,128)}, f32[512,128]{1,0:T(8,128)}, f32[512,128]{1,0:T(8,128)}, f32[512,128]{1,0:T(8,128)}, /*i...) custom-call(f32[512,128]{1,0:T(8,128)} %bitcast.24, ...), custom_call_target="tpu_custom_call" | custom-call | tf_op jit(solution)/shard_map/pallas_call | solution.py:292
  16.9 0.6 copy-done.2
  17.5 0.0 copy-done.3
  17.5 3.1 %shard_map.38 = (f32[512,128]{1,0:T(8,128)}, f32[512,128]{1,0:T(8,128)}) custom-call(f32[512,128]{1,0:T(8,128)} %bitcast.25, f32[64,8]{1,0:T(8,128)} %copy-done.2, f32[64,8]{1,0:T(8,128)} %copy-done.3, f32[5]{0:T(128)} %stack.31.fl_ref, f32[512,128]{1,0:T(8,128)} %get-tuple-element.29.a_ref, f32[512,128]{1,0:T(8,128)} %get-tuple-element.30.r_ref, ...), custom_call_target="tpu_custom_call" | custom-call | tf_op jit(solution)/shard_map/pallas_call | solution.py:329
  20.6 24.5 %all_to_all.10.s_ref = f32[64,1,8,128]{3,2,1,0:T(8,128)} all-to-all(f32[64,1,8,128]{3,2,1,0:T(8,128)} %bitcast.35), channel_id=1, replica_groups=mesh['cast'=64,'width'=4] {'cast'}, dimensions={0} | all-to-all | bytes 524288 | tf_op jit(solution)/shard_map/all_to_all | solution.py:609
  45.1 1.9 %shard_map.39 = f32[64,1,2,128]{3,2,1,0:T(2,128)} custom-call(f32[64,1,8,128]{3,2,1,0:T(8,128)} %all_to_all.10.s_ref), custom_call_target="tpu_custom_call" | custom-call | tf_op jit(solution)/shard_map/pallas_call | solution.py:611
  47.0 4.8 %all-to-all-start.1 = ((f32[64,1,2,128]{3,2,1,0:T(2,128)}), f32[64,1,2,128]{3,2,1,0:T(2,128)S(1)}, u32[]{:S(2)}, u32[]{:S(2)}) async-start(f32[64,1,2,128]{3,2,1,0:T(2,128)} %shard_map.39), calls=%async_computation.1 | async-start | bytes 131072 | tf_op jit(solution)/shard_map/all_to_all | solution.py:612
  51.8 3.9 %shard_map.40 = (f32[128,4,128]{2,1,0:T(4,128)}, f32[128,4,128]{2,1,0:T(4,128)}, f32[128,4,128]{2,1,0:T(4,128)}, f32[128,4,128]{2,1,0:T(4,128)}, f32[128,4,128]{2,1,0:T(4,128)}, /*index=5*/f32[4,4,4,128]{3,2,1,0:T(4,128)}) custom-call(f32[512,128]{1,0:T(8,128)} %bitcast.26, f32[64,8]{1,0:T(8,128)} %copy-done.2, f32[64,8]{1,0:T(8,128)} %copy-done.3, ...), custom_call_target="tpu_custom_call" | custom-call | tf_op jit(solution)/shard_map/pallas_call | solution.py:367
  55.7 6.2 %all-to-all-done.1 = f32[64,1,2,128]{3,2,1,0:T(2,128)S(1)} async-done(((f32[64,1,2,128]{3,2,1,0:T(2,128)}), f32[64,1,2,128]{3,2,1,0:T(2,128)S(1)}, u32[]{:S(2)}, u32[]{:S(2)}) %all-to-all-start.1) | async-done | bytes 65568 | tf_op jit(solution)/shard_map/all_to_all | solution.py:612
  61.9 0.6 copy-done.1
  62.5 2.8 %shard_map.41 = (f32[128,4,128]{2,1,0:T(4,128)}, f32[4,6,4,128]{3,2,1,0:T(4,128)}) custom-call(f32[64,8,128]{2,1,0:T(8,128)} %bitcast.33, f32[64,8,128]{2,1,0:T(8,128)} %bitcast.31, f32[64,8,128]{2,1,0:T(8,128)} %bitcast.32, f32[64,2,128]{2,1,0:T(2,128)} %bitcast.34, f32[128,4,128]{2,1,0:T(4,128)} %get-tuple-element.38.a_ref, ...), custom_call_target="tpu_custom_call" | custom-call | tf_op jit(solution)/shard_map/pallas_call | solution.py:433
  65.3 2.4 %collective-permute-start.4 = (f32[4,6,4,128]{3,2,1,0:T(4,128)}, f32[4,6,4,128]{3,2,1,0:T(4,128)S(1)}, u32[]{:S(2)}, u32[]{:S(2)}) collective-permute-start(f32[4,6,4,128]{3,2,1,0:T(4,128)} %get-tuple-element.42.refs_0_), channel_id=1, source_target_pairs={{0,1},{1,2},{2,3},{3,0},{4,5},{5,6},{6,7},{7,4},{8,9},{9,10},{10,1... | collective-permute-start | bytes 147464 | tf_op jit(solution)/shard_map/ppermute | solution.py:626
  67.7 2.6 %collective-permute-start.5 = (f32[4,6,4,128]{3,2,1,0:T(4,128)}, f32[4,6,4,128]{3,2,1,0:T(4,128)S(1)}, u32[]{:S(2)}, u32[]{:S(2)}) collective-permute-start(f32[4,6,4,128]{3,2,1,0:T(4,128)} %get-tuple-element.42.refs_0_), channel_id=1, source_target_pairs={{0,2},{1,3},{2,0},{3,1},{4,6},{5,7},{6,4},{7,5},{8,10},{9,11},{10,... | collective-permute-start | bytes 147464 | tf_op jit(solution)/shard_map/ppermute | solution.py:626
  70.3 1.1 %collective-permute-start.6 = (f32[4,6,4,128]{3,2,1,0:T(4,128)}, f32[4,6,4,128]{3,2,1,0:T(4,128)S(1)}, u32[]{:S(2)}, u32[]{:S(2)}) collective-permute-start(f32[4,6,4,128]{3,2,1,0:T(4,128)} %get-tuple-element.42.refs_0_), channel_id=1, source_target_pairs={{0,3},{1,0},{2,1},{3,2},{4,7},{5,4},{6,5},{7,6},{8,11},{9,8},{10,9... | collective-permute-start | bytes 147464 | tf_op jit(solution)/shard_map/ppermute | solution.py:626
  71.3 2.3 %shard_map.42 = (f32[64,8,128]{2,1,0:T(8,128)}, f32[64,8,128]{2,1,0:T(8,128)}, f32[64,8,128]{2,1,0:T(8,128)}, f32[64,8,128]{2,1,0:T(8,128)}) custom-call(f32[64,8,128]{2,1,0:T(8,128)} %bitcast.27, f32[64,8,128]{2,1,0:T(8,128)} %bitcast.29, f32[64,8,128]{2,1,0:T(8,128)} %bitcast.30), custom_call_target="tpu_custom_call" | custom-call | tf_op jit(solution)/shard_map/pallas_call | solution.py:182
  73.7 0.0 collective-permute-done.6.refs_3_
  73.7 0.6 copy-done.4
  74.3 0.0 copy-done.5
  74.3 0.0 copy-done.6
  74.3 3.2 %shard_map.43 = f32[64,8,128]{2,1,0:T(8,128)} custom-call(s32[1]{0:T(128)} %bitcast.me_ref, f32[4,6,4,128]{3,2,1,0:T(4,128)} %get-tuple-element.42.refs_0_, f32[4,6,4,128]{3,2,1,0:T(4,128)} %copy-done.4, f32[4,6,4,128]{3,2,1,0:T(4,128)} %copy-done.5, f32[4,6,4,128]{3,2,1,0:T(4,128)} %copy-done.6, f32[128,4,128]{2,1,0:T(4,128)} %get-tuple-element.43.refs_4_, ...), custom_call_target="tpu_custom_call" | custom-call | tf_op jit(solution)/shard_map/pallas_call | solution.py:442
  (17 shorter events, 0.0 us)
Async XLA Ops:
  0.0 6.4 %copy-start = (f32[64,8,128]{2,1,0:T(8,128)S(1)}, f32[64,8,128]{2,1,0:T(8,128)}, u32[]{:S(2)}) copy-start(f32[64,8,128]{2,1,0:T(8,128)} %refs_12_.1) | copy-start | bytes 786436
  1.2 10.8 %collective-permute-start.2 = (f32[64,128]{1,0:T(8,128)S(1)}, f32[64,128]{1,0:T(8,128)S(1)}, u32[]{:S(2)}, u32[]{:S(2)}) collective-permute-start(f32[64,128]{1,0:T(8,128)S(1)} %get-tuple-element.58), channel_id=1, source_target_pairs={{0,4},{4,0},{8,12},{12,8},{16,20},{20,16},{24,28},{28,24},{32,36},... | collective-permute-start | bytes 98312 | tf_op jit(solution)/shard_map/ppermute | solution.py:594
  4.5 7.5 %collective-permute-start.3 = (f32[64,128]{1,0:T(8,128)S(1)}, f32[64,128]{1,0:T(8,128)S(1)}, u32[]{:S(2)}, u32[]{:S(2)}) collective-permute-start(f32[64,128]{1,0:T(8,128)S(1)} %get-tuple-element.57), channel_id=1, source_target_pairs={{4,8},{12,16},{20,24},{28,32},{36,40},{44,48},{52,56},{60,64},{68,... | collective-permute-start | bytes 98312 | tf_op jit(solution)/shard_map/ppermute | solution.py:595
  7.0 9.9 %collective-permute-start = (f32[64,8]{1,0:T(8,128)S(1)}, f32[64,8]{1,0:T(8,128)S(1)}, u32[]{:S(2)}, u32[]{:S(2)}) collective-permute-start(f32[64,8]{1,0:T(8,128)S(1)} %bitcast.38), channel_id=1, source_target_pairs={{0,1},{1,2},{2,3},{4,5},{5,6},{6,7},{8,9},{9,10},{10,11},{12,13},{... | collective-permute-start | bytes 6152 | tf_op jit(solution)/shard_map/ppermute | solution.py:596
  10.0 6.9 %collective-permute-start.1 = (f32[64,8]{1,0:T(8,128)S(1)}, f32[64,8]{1,0:T(8,128)S(1)}, u32[]{:S(2)}, u32[]{:S(2)}) collective-permute-start(f32[64,8]{1,0:T(8,128)S(1)} %bitcast.39), channel_id=1, source_target_pairs={{1,0},{2,1},{3,2},{5,4},{6,5},{7,6},{9,8},{10,9},{11,10},{13,12},{... | collective-permute-start | bytes 6152 | tf_op jit(solution)/shard_map/ppermute | solution.py:597
  12.0 0.6 copy-start.7
  12.0 0.6 copy-start.8
  16.9 0.6 copy-start.2
  16.9 0.6 copy-start.3
  47.0 14.9 %all-to-all-start.1 = ((f32[64,1,2,128]{3,2,1,0:T(2,128)}), f32[64,1,2,128]{3,2,1,0:T(2,128)S(1)}, u32[]{:S(2)}, u32[]{:S(2)}) async-start(f32[64,1,2,128]{3,2,1,0:T(2,128)} %shard_map.39), calls=%async_computation.1 | async-start | bytes 131072 | tf_op jit(solution)/shard_map/all_to_all | solution.py:612
  61.9 0.6 copy-start.1
  65.3 8.4 %collective-permute-start.4 = (f32[4,6,4,128]{3,2,1,0:T(4,128)}, f32[4,6,4,128]{3,2,1,0:T(4,128)S(1)}, u32[]{:S(2)}, u32[]{:S(2)}) collective-permute-start(f32[4,6,4,128]{3,2,1,0:T(4,128)} %get-tuple-element.42.refs_0_), channel_id=1, source_target_pairs={{0,1},{1,2},{2,3},{3,0},{4,5},{5,6},{6,7},{7,4},{8,9},{9,10},{10,1... | collective-permute-start | bytes 147464 | tf_op jit(solution)/shard_map/ppermute | solution.py:626
  67.7 6.0 %collective-permute-start.5 = (f32[4,6,4,128]{3,2,1,0:T(4,128)}, f32[4,6,4,128]{3,2,1,0:T(4,128)S(1)}, u32[]{:S(2)}, u32[]{:S(2)}) collective-permute-start(f32[4,6,4,128]{3,2,1,0:T(4,128)} %get-tuple-element.42.refs_0_), channel_id=1, source_target_pairs={{0,2},{1,3},{2,0},{3,1},{4,6},{5,7},{6,4},{7,5},{8,10},{9,11},{10,... | collective-permute-start | bytes 147464 | tf_op jit(solution)/shard_map/ppermute | solution.py:626
  70.3 3.4 %collective-permute-start.6 = (f32[4,6,4,128]{3,2,1,0:T(4,128)}, f32[4,6,4,128]{3,2,1,0:T(4,128)S(1)}, u32[]{:S(2)}, u32[]{:S(2)}) collective-permute-start(f32[4,6,4,128]{3,2,1,0:T(4,128)} %get-tuple-element.42.refs_0_), channel_id=1, source_target_pairs={{0,3},{1,0},{2,1},{3,2},{4,7},{5,4},{6,5},{7,6},{8,11},{9,8},{10,9... | collective-permute-start | bytes 147464 | tf_op jit(solution)/shard_map/ppermute | solution.py:626
  73.7 0.6 copy-start.4
  73.7 0.6 copy-start.5
  73.7 0.6 copy-start.6

commit v16 on v15

--- a/solution.py
+++ b/solution.py
@@ -620,13 +620,13 @@
 
     wa, r_w, cp_w, v_w, w_w, vws = wfactor(h2, h_wl, h_wh, flags, ncl, nsub)
     wfac = (r_w, cp_w, v_w, w_w)
-    tfac = factor(tlo, tmd, thi, 8)
+    tfac = factor(tlo, tmd, thi, 16)
     yw, summ = width_solve(y, v, w, back, wa, (r_w, cp_w, vws), nsub)
     got = [summ] + [
         lax.ppermute(summ, "width", [(i, (i + q) % nw) for i in range(nw)]) for q in range(1, nw)
     ]
     me = wi.astype(jnp.int32).reshape(1)
-    return thick_solve(me, got, yw, wfac[2], wfac[3], tlo, tfac, h, nsub, 8)
+    return thick_solve(me, got, yw, wfac[2], wfac[3], tlo, tfac, h, nsub, 16)
 
 
 def solution(mesh):

time: 78 us -> 78.1 us (level)
  transfers between devices with their start and end apart: 8 -> 8, of which waited for: 1 -> 1; matrix products, arithmetic and copies ran while one was open for 2% -> 2% of each run, Pallas kernels for 14% -> 13%
where the time goes in v16:
time: 78.1 us; the launch traced here: 77.6 us
  blocking collectives  24.5 us (31%)
  Pallas kernels  21.6 us (28%)
  starting transfers between devices  19.9 us (25%)
  waiting for transfers between devices  6.25 us (8%)
  local copies, waits for them, and re-layouts  4.68 us (6%)
    all_to_all x1, blocking collectives, shards(): lax.all_to_all(summ.reshape(nc, nt // nc, 8, nwl), 'cast', 0, 0, tiled=True)  24.5 us
    all_to_all x1, waiting for transfers between devices, shards(): back = lax.all_to_all(lr, 'cast', 0, 0, tiled=True).reshape(nt, 2, nwl)  6.2 us
    ppermute x3, starting transfers between devices, shards(): lax.ppermute(summ, 'width', [(i, (i + q) % nw) for i in range(nw)])  6.05 us
    all_to_all x1, starting transfers between devices, shards(): back = lax.all_to_all(lr, 'cast', 0, 0, tiled=True).reshape(nt, 2, nwl)  4.77 us
    pallas_call x1, Pallas kernels, prep_solve(): pl.pallas_call(functools.partial(_prep_kernel, n), out_shape=[shp] * 3 +...  4.27 us
    pallas_call x1, Pallas kernels, wfactor(): pl.pallas_call(functools.partial(_wfactor_kernel, n, nsub), out_shape=[sh...  3.89 us
    unnamed x20, local copies, waits for them, and re-layouts  3.31 us
    ppermute x1, starting transfers between devices, shards(): got_a = lax.ppermute(jnp.where(even, last, first), 'cast', in_chip)  3.29 us
  transfers between devices with their start and end apart: 8, of which 1 were waited for; matrix products, arithmetic and copies ran while one was open for 2% of the time, Pallas kernels for 13%

profile of v16, /device:TPU:1, one launch (start us, length us, event | category | flops | bytes accessed | tf_op | source)
XLA Modules:
  0.0 77.6 jit_solution(3263765805635659916)
XLA Ops:
  0.0 1.1 %fusion = (f32[64,1,128]{2,1,0:T(1,128)S(1)}, f32[64,1,128]{2,1,0:T(1,128)S(1)}) fusion(f32[64,8,128]{2,1,0:T(8,128)} %refs_12_.1), kind=kLoop, calls=%fused_computation.2 | loop fusion | bytes 131072 | tf_op jit(solution)/shard_map/slice | solution.py:591
  1.2 3.3 %collective-permute-start.2 = (f32[64,128]{1,0:T(8,128)S(1)}, f32[64,128]{1,0:T(8,128)S(1)}, u32[]{:S(2)}, u32[]{:S(2)}) collective-permute-start(f32[64,128]{1,0:T(8,128)S(1)} %get-tuple-element.58), channel_id=1, source_target_pairs={{0,4},{4,0},{8,12},{12,8},{16,20},{20,16},{24,28},{28,24},{32,36},... | collective-permute-start | bytes 98312 | tf_op jit(solution)/shard_map/ppermute | solution.py:594
  4.5 1.9 %collective-permute-start.3 = (f32[64,128]{1,0:T(8,128)S(1)}, f32[64,128]{1,0:T(8,128)S(1)}, u32[]{:S(2)}, u32[]{:S(2)}) collective-permute-start(f32[64,128]{1,0:T(8,128)S(1)} %get-tuple-element.57), channel_id=1, source_target_pairs={{4,8},{12,16},{20,24},{28,32},{36,40},{44,48},{52,56},{60,64},{68,... | collective-permute-start | bytes 98312 | tf_op jit(solution)/shard_map/ppermute | solution.py:595
  6.4 0.1 fusion.1
  6.5 0.4 copy.13
  7.0 2.6 %collective-permute-start = (f32[64,8]{1,0:T(8,128)S(1)}, f32[64,8]{1,0:T(8,128)S(1)}, u32[]{:S(2)}, u32[]{:S(2)}) collective-permute-start(f32[64,8]{1,0:T(8,128)S(1)} %bitcast.38), channel_id=1, source_target_pairs={{0,1},{1,2},{2,3},{4,5},{5,6},{6,7},{8,9},{9,10},{10,11},{12,13},{... | collective-permute-start | bytes 6152 | tf_op jit(solution)/shard_map/ppermute | solution.py:596
  9.6 0.4 copy.14
  10.0 1.3 %collective-permute-start.1 = (f32[64,8]{1,0:T(8,128)S(1)}, f32[64,8]{1,0:T(8,128)S(1)}, u32[]{:S(2)}, u32[]{:S(2)}) collective-permute-start(f32[64,8]{1,0:T(8,128)S(1)} %bitcast.39), channel_id=1, source_target_pairs={{1,0},{2,1},{3,2},{5,4},{6,5},{7,6},{9,8},{10,9},{11,10},{13,12},{... | collective-permute-start | bytes 6152 | tf_op jit(solution)/shard_map/ppermute | solution.py:597
  11.3 0.1 stack.30
  11.4 0.5 stack.31.fl_ref
  12.0 0.6 copy-done.7
  12.6 0.0 copy-done.8
  12.6 4.3 %shard_map.37 = (f32[512,128]{1,0:T(8,128)}, f32[512,128]{1,0:T(8,128)}, f32[512,128]{1,0:T(8,128)}, f32[512,128]{1,0:T(8,128)}, f32[512,128]{1,0:T(8,128)}, /*i...) custom-call(f32[512,128]{1,0:T(8,128)} %bitcast.24, ...), custom_call_target="tpu_custom_call" | custom-call | tf_op jit(solution)/shard_map/pallas_call | solution.py:292
  16.9 0.6 copy-done.2
  17.5 0.0 copy-done.3
  17.5 3.1 %shard_map.38 = (f32[512,128]{1,0:T(8,128)}, f32[512,128]{1,0:T(8,128)}) custom-call(f32[512,128]{1,0:T(8,128)} %bitcast.25, f32[64,8]{1,0:T(8,128)} %copy-done.2, f32[64,8]{1,0:T(8,128)} %copy-done.3, f32[5]{0:T(128)} %stack.31.fl_ref, f32[512,128]{1,0:T(8,128)} %get-tuple-element.29.a_ref, f32[512,128]{1,0:T(8,128)} %get-tuple-element.30.r_ref, ...), custom_call_target="tpu_custom_call" | custom-call | tf_op jit(solution)/shard_map/pallas_call | solution.py:329
  20.6 24.5 %all_to_all.10.s_ref = f32[64,1,8,128]{3,2,1,0:T(8,128)} all-to-all(f32[64,1,8,128]{3,2,1,0:T(8,128)} %bitcast.35), channel_id=1, replica_groups=mesh['cast'=64,'width'=4] {'cast'}, dimensions={0} | all-to-all | bytes 524288 | tf_op jit(solution)/shard_map/all_to_all | solution.py:609
  45.1 1.9 %shard_map.39 = f32[64,1,2,128]{3,2,1,0:T(2,128)} custom-call(f32[64,1,8,128]{3,2,1,0:T(8,128)} %all_to_all.10.s_ref), custom_call_target="tpu_custom_call" | custom-call | tf_op jit(solution)/shard_map/pallas_call | solution.py:611
  47.0 4.8 %all-to-all-start.1 = ((f32[64,1,2,128]{3,2,1,0:T(2,128)}), f32[64,1,2,128]{3,2,1,0:T(2,128)S(1)}, u32[]{:S(2)}, u32[]{:S(2)}) async-start(f32[64,1,2,128]{3,2,1,0:T(2,128)} %shard_map.39), calls=%async_computation.1 | async-start | bytes 131072 | tf_op jit(solution)/shard_map/all_to_all | solution.py:612
  51.8 3.9 %shard_map.40 = (f32[128,4,128]{2,1,0:T(4,128)}, f32[128,4,128]{2,1,0:T(4,128)}, f32[128,4,128]{2,1,0:T(4,128)}, f32[128,4,128]{2,1,0:T(4,128)}, f32[128,4,128]{2,1,0:T(4,128)}, /*index=5*/f32[4,4,4,128]{3,2,1,0:T(4,128)}) custom-call(f32[512,128]{1,0:T(8,128)} %bitcast.26, f32[64,8]{1,0:T(8,128)} %copy-done.2, f32[64,8]{1,0:T(8,128)} %copy-done.3, ...), custom_call_target="tpu_custom_call" | custom-call | tf_op jit(solution)/shard_map/pallas_call | solution.py:367
  55.7 6.2 %all-to-all-done.1 = f32[64,1,2,128]{3,2,1,0:T(2,128)S(1)} async-done(((f32[64,1,2,128]{3,2,1,0:T(2,128)}), f32[64,1,2,128]{3,2,1,0:T(2,128)S(1)}, u32[]{:S(2)}, u32[]{:S(2)}) %all-to-all-start.1) | async-done | bytes 65568 | tf_op jit(solution)/shard_map/all_to_all | solution.py:612
  61.9 0.6 copy-done.1
  62.5 2.8 %shard_map.41 = (f32[128,4,128]{2,1,0:T(4,128)}, f32[4,6,4,128]{3,2,1,0:T(4,128)}) custom-call(f32[64,8,128]{2,1,0:T(8,128)} %bitcast.33, f32[64,8,128]{2,1,0:T(8,128)} %bitcast.31, f32[64,8,128]{2,1,0:T(8,128)} %bitcast.32, f32[64,2,128]{2,1,0:T(2,128)} %bitcast.34, f32[128,4,128]{2,1,0:T(4,128)} %get-tuple-element.38.a_ref, ...), custom_call_target="tpu_custom_call" | custom-call | tf_op jit(solution)/shard_map/pallas_call | solution.py:433
  65.3 2.4 %collective-permute-start.4 = (f32[4,6,4,128]{3,2,1,0:T(4,128)}, f32[4,6,4,128]{3,2,1,0:T(4,128)S(1)}, u32[]{:S(2)}, u32[]{:S(2)}) collective-permute-start(f32[4,6,4,128]{3,2,1,0:T(4,128)} %get-tuple-element.42.refs_0_), channel_id=1, source_target_pairs={{0,1},{1,2},{2,3},{3,0},{4,5},{5,6},{6,7},{7,4},{8,9},{9,10},{10,1... | collective-permute-start | bytes 147464 | tf_op jit(solution)/shard_map/ppermute | solution.py:626
  67.7 2.6 %collective-permute-start.5 = (f32[4,6,4,128]{3,2,1,0:T(4,128)}, f32[4,6,4,128]{3,2,1,0:T(4,128)S(1)}, u32[]{:S(2)}, u32[]{:S(2)}) collective-permute-start(f32[4,6,4,128]{3,2,1,0:T(4,128)} %get-tuple-element.42.refs_0_), channel_id=1, source_target_pairs={{0,2},{1,3},{2,0},{3,1},{4,6},{5,7},{6,4},{7,5},{8,10},{9,11},{10,... | collective-permute-start | bytes 147464 | tf_op jit(solution)/shard_map/ppermute | solution.py:626
  70.3 1.1 %collective-permute-start.6 = (f32[4,6,4,128]{3,2,1,0:T(4,128)}, f32[4,6,4,128]{3,2,1,0:T(4,128)S(1)}, u32[]{:S(2)}, u32[]{:S(2)}) collective-permute-start(f32[4,6,4,128]{3,2,1,0:T(4,128)} %get-tuple-element.42.refs_0_), channel_id=1, source_target_pairs={{0,3},{1,0},{2,1},{3,2},{4,7},{5,4},{6,5},{7,6},{8,11},{9,8},{10,9... | collective-permute-start | bytes 147464 | tf_op jit(solution)/shard_map/ppermute | solution.py:626
  71.3 2.3 %shard_map.42 = (f32[64,8,128]{2,1,0:T(8,128)}, f32[64,8,128]{2,1,0:T(8,128)}, f32[64,8,128]{2,1,0:T(8,128)}, f32[64,8,128]{2,1,0:T(8,128)}) custom-call(f32[64,8,128]{2,1,0:T(8,128)} %bitcast.27, f32[64,8,128]{2,1,0:T(8,128)} %bitcast.29, f32[64,8,128]{2,1,0:T(8,128)} %bitcast.30), custom_call_target="tpu_custom_call" | custom-call | tf_op jit(solution)/shard_map/pallas_call | solution.py:182
  73.7 0.0 collective-permute-done.6.refs_3_
  73.7 0.6 copy-done.4
  74.3 0.0 copy-done.5
  74.3 0.0 copy-done.6
  74.3 3.3 %shard_map.43 = f32[64,8,128]{2,1,0:T(8,128)} custom-call(s32[1]{0:T(128)} %bitcast.me_ref, f32[4,6,4,128]{3,2,1,0:T(4,128)} %get-tuple-element.42.refs_0_, f32[4,6,4,128]{3,2,1,0:T(4,128)} %copy-done.4, f32[4,6,4,128]{3,2,1,0:T(4,128)} %copy-done.5, f32[4,6,4,128]{3,2,1,0:T(4,128)} %copy-done.6, f32[128,4,128]{2,1,0:T(4,128)} %get-tuple-element.43.refs_4_, ...), custom_call_target="tpu_custom_call" | custom-call | tf_op jit(solution)/shard_map/pallas_call | solution.py:442
  (17 shorter events, 0.0 us)
Async XLA Ops:
  0.0 6.4 %copy-start = (f32[64,8,128]{2,1,0:T(8,128)S(1)}, f32[64,8,128]{2,1,0:T(8,128)}, u32[]{:S(2)}) copy-start(f32[64,8,128]{2,1,0:T(8,128)} %refs_12_.1) | copy-start | bytes 786436
  1.2 10.8 %collective-permute-start.2 = (f32[64,128]{1,0:T(8,128)S(1)}, f32[64,128]{1,0:T(8,128)S(1)}, u32[]{:S(2)}, u32[]{:S(2)}) collective-permute-start(f32[64,128]{1,0:T(8,128)S(1)} %get-tuple-element.58), channel_id=1, source_target_pairs={{0,4},{4,0},{8,12},{12,8},{16,20},{20,16},{24,28},{28,24},{32,36},... | collective-permute-start | bytes 98312 | tf_op jit(solution)/shard_map/ppermute | solution.py:594
  4.5 7.5 %collective-permute-start.3 = (f32[64,128]{1,0:T(8,128)S(1)}, f32[64,128]{1,0:T(8,128)S(1)}, u32[]{:S(2)}, u32[]{:S(2)}) collective-permute-start(f32[64,128]{1,0:T(8,128)S(1)} %get-tuple-element.57), channel_id=1, source_target_pairs={{4,8},{12,16},{20,24},{28,32},{36,40},{44,48},{52,56},{60,64},{68,... | collective-permute-start | bytes 98312 | tf_op jit(solution)/shard_map/ppermute | solution.py:595
  7.0 9.9 %collective-permute-start = (f32[64,8]{1,0:T(8,128)S(1)}, f32[64,8]{1,0:T(8,128)S(1)}, u32[]{:S(2)}, u32[]{:S(2)}) collective-permute-start(f32[64,8]{1,0:T(8,128)S(1)} %bitcast.38), channel_id=1, source_target_pairs={{0,1},{1,2},{2,3},{4,5},{5,6},{6,7},{8,9},{9,10},{10,11},{12,13},{... | collective-permute-start | bytes 6152 | tf_op jit(solution)/shard_map/ppermute | solution.py:596
  10.0 6.9 %collective-permute-start.1 = (f32[64,8]{1,0:T(8,128)S(1)}, f32[64,8]{1,0:T(8,128)S(1)}, u32[]{:S(2)}, u32[]{:S(2)}) collective-permute-start(f32[64,8]{1,0:T(8,128)S(1)} %bitcast.39), channel_id=1, source_target_pairs={{1,0},{2,1},{3,2},{5,4},{6,5},{7,6},{9,8},{10,9},{11,10},{13,12},{... | collective-permute-start | bytes 6152 | tf_op jit(solution)/shard_map/ppermute | solution.py:597
  12.0 0.6 copy-start.7
  12.0 0.6 copy-start.8
  16.9 0.6 copy-start.2
  16.9 0.6 copy-start.3
  47.0 14.9 %all-to-all-start.1 = ((f32[64,1,2,128]{3,2,1,0:T(2,128)}), f32[64,1,2,128]{3,2,1,0:T(2,128)S(1)}, u32[]{:S(2)}, u32[]{:S(2)}) async-start(f32[64,1,2,128]{3,2,1,0:T(2,128)} %shard_map.39), calls=%async_computation.1 | async-start | bytes 131072 | tf_op jit(solution)/shard_map/all_to_all | solution.py:612
  61.9 0.6 copy-start.1
  65.3 8.4 %collective-permute-start.4 = (f32[4,6,4,128]{3,2,1,0:T(4,128)}, f32[4,6,4,128]{3,2,1,0:T(4,128)S(1)}, u32[]{:S(2)}, u32[]{:S(2)}) collective-permute-start(f32[4,6,4,128]{3,2,1,0:T(4,128)} %get-tuple-element.42.refs_0_), channel_id=1, source_target_pairs={{0,1},{1,2},{2,3},{3,0},{4,5},{5,6},{6,7},{7,4},{8,9},{9,10},{10,1... | collective-permute-start | bytes 147464 | tf_op jit(solution)/shard_map/ppermute | solution.py:626
  67.7 6.0 %collective-permute-start.5 = (f32[4,6,4,128]{3,2,1,0:T(4,128)}, f32[4,6,4,128]{3,2,1,0:T(4,128)S(1)}, u32[]{:S(2)}, u32[]{:S(2)}) collective-permute-start(f32[4,6,4,128]{3,2,1,0:T(4,128)} %get-tuple-element.42.refs_0_), channel_id=1, source_target_pairs={{0,2},{1,3},{2,0},{3,1},{4,6},{5,7},{6,4},{7,5},{8,10},{9,11},{10,... | collective-permute-start | bytes 147464 | tf_op jit(solution)/shard_map/ppermute | solution.py:626
  70.3 3.4 %collective-permute-start.6 = (f32[4,6,4,128]{3,2,1,0:T(4,128)}, f32[4,6,4,128]{3,2,1,0:T(4,128)S(1)}, u32[]{:S(2)}, u32[]{:S(2)}) collective-permute-start(f32[4,6,4,128]{3,2,1,0:T(4,128)} %get-tuple-element.42.refs_0_), channel_id=1, source_target_pairs={{0,3},{1,0},{2,1},{3,2},{4,7},{5,4},{6,5},{7,6},{8,11},{9,8},{10,9... | collective-permute-start | bytes 147464 | tf_op jit(solution)/shard_map/ppermute | solution.py:626
  73.7 0.6 copy-start.4
  73.7 0.6 copy-start.5
  73.7 0.6 copy-start.6

commit v17 on v15

--- a/solution.py
+++ b/solution.py
@@ -613,7 +613,7 @@
     y, v, w = (x.reshape(nt, ncl, nwl) for x in (y, v, w))
 
     lines = nt * ncl
-    nsub = 4
+    nsub = 2
 
     def wl(x):
         return jnp.transpose(x, (2, 0, 1)).reshape(nwl, lines // 128, 128)

time: 78 us -> 78 us (level)
  no operation moved by 1% of the time
where the time goes in v17:
time: 78 us; the launch traced here: 77.5 us
  blocking collectives  24.5 us (31%)
  Pallas kernels  21.8 us (28%)
  starting transfers between devices  19.9 us (26%)
  waiting for transfers between devices  5.93 us (8%)
  local copies, waits for them, and re-layouts  4.66 us (6%)
    all_to_all x1, blocking collectives, shards(): lax.all_to_all(summ.reshape(nc, nt // nc, 8, nwl), 'cast', 0, 0, tiled=True)  24.5 us
    ppermute x3, starting transfers between devices, shards(): lax.ppermute(summ, 'width', [(i, (i + q) % nw) for i in range(nw)])  6.05 us
    all_to_all x1, waiting for transfers between devices, shards(): back = lax.all_to_all(lr, 'cast', 0, 0, tiled=True).reshape(nt, 2, nwl)  5.91 us
    all_to_all x1, starting transfers between devices, shards(): back = lax.all_to_all(lr, 'cast', 0, 0, tiled=True).reshape(nt, 2, nwl)  4.77 us
    pallas_call x1, Pallas kernels, prep_solve(): pl.pallas_call(functools.partial(_prep_kernel, n), out_shape=[shp] * 3 +...  4.27 us
    pallas_call x1, Pallas kernels, wfactor(): pl.pallas_call(functools.partial(_wfactor_kernel, n, nsub), out_shape=[sh...  4.17 us
    ppermute x1, starting transfers between devices, shards(): got_a = lax.ppermute(jnp.where(even, last, first), 'cast', in_chip)  3.29 us
    unnamed x20, local copies, waits for them, and re-layouts  3.29 us
  transfers between devices with their start and end apart: 8, of which 1 were waited for; matrix products, arithmetic and copies ran while one was open for 2% of the time, Pallas kernels for 14%

profile of v17, /device:TPU:1, one launch (start us, length us, event | category | flops | bytes accessed | tf_op | source)
XLA Modules:
  0.0 77.5 jit_solution(7400320861310390272)
XLA Ops:
  0.0 1.1 %fusion = (f32[64,1,128]{2,1,0:T(1,128)S(1)}, f32[64,1,128]{2,1,0:T(1,128)S(1)}) fusion(f32[64,8,128]{2,1,0:T(8,128)} %refs_12_.1), kind=kLoop, calls=%fused_computation.2 | loop fusion | bytes 131072 | tf_op jit(solution)/shard_map/slice | solution.py:591
  1.2 3.3 %collective-permute-start.2 = (f32[64,128]{1,0:T(8,128)S(1)}, f32[64,128]{1,0:T(8,128)S(1)}, u32[]{:S(2)}, u32[]{:S(2)}) collective-permute-start(f32[64,128]{1,0:T(8,128)S(1)} %get-tuple-element.58), channel_id=1, source_target_pairs={{0,4},{4,0},{8,12},{12,8},{16,20},{20,16},{24,28},{28,24},{32,36},... | collective-permute-start | bytes 98312 | tf_op jit(solution)/shard_map/ppermute | solution.py:594
  4.5 1.9 %collective-permute-start.3 = (f32[64,128]{1,0:T(8,128)S(1)}, f32[64,128]{1,0:T(8,128)S(1)}, u32[]{:S(2)}, u32[]{:S(2)}) collective-permute-start(f32[64,128]{1,0:T(8,128)S(1)} %get-tuple-element.57), channel_id=1, source_target_pairs={{4,8},{12,16},{20,24},{28,32},{36,40},{44,48},{52,56},{60,64},{68,... | collective-permute-start | bytes 98312 | tf_op jit(solution)/shard_map/ppermute | solution.py:595
  6.4 0.1 fusion.1
  6.5 0.4 copy.13
  7.0 2.6 %collective-permute-start = (f32[64,8]{1,0:T(8,128)S(1)}, f32[64,8]{1,0:T(8,128)S(1)}, u32[]{:S(2)}, u32[]{:S(2)}) collective-permute-start(f32[64,8]{1,0:T(8,128)S(1)} %bitcast.38), channel_id=1, source_target_pairs={{0,1},{1,2},{2,3},{4,5},{5,6},{6,7},{8,9},{9,10},{10,11},{12,13},{... | collective-permute-start | bytes 6152 | tf_op jit(solution)/shard_map/ppermute | solution.py:596
  9.6 0.4 copy.14
  10.0 1.3 %collective-permute-start.1 = (f32[64,8]{1,0:T(8,128)S(1)}, f32[64,8]{1,0:T(8,128)S(1)}, u32[]{:S(2)}, u32[]{:S(2)}) collective-permute-start(f32[64,8]{1,0:T(8,128)S(1)} %bitcast.39), channel_id=1, source_target_pairs={{1,0},{2,1},{3,2},{5,4},{6,5},{7,6},{9,8},{10,9},{11,10},{13,12},{... | collective-permute-start | bytes 6152 | tf_op jit(solution)/shard_map/ppermute | solution.py:597
  11.3 0.1 stack.30
  11.4 0.5 stack.31.fl_ref
  12.0 0.6 copy-done.4
  12.6 0.0 copy-done.5
  12.6 4.3 %shard_map.37 = (f32[512,128]{1,0:T(8,128)}, f32[512,128]{1,0:T(8,128)}, f32[512,128]{1,0:T(8,128)}, f32[512,128]{1,0:T(8,128)}, f32[512,128]{1,0:T(8,128)}, /*i...) custom-call(f32[512,128]{1,0:T(8,128)} %bitcast.24, ...), custom_call_target="tpu_custom_call" | custom-call | tf_op jit(solution)/shard_map/pallas_call | solution.py:292
  16.9 0.0 collective-permute-done.1.hwh_ref
  16.9 0.6 copy-done.2
  17.5 0.0 copy-done.3
  17.5 3.1 %shard_map.38 = (f32[512,128]{1,0:T(8,128)}, f32[512,128]{1,0:T(8,128)}) custom-call(f32[512,128]{1,0:T(8,128)} %bitcast.25, f32[64,8]{1,0:T(8,128)} %copy-done.2, f32[64,8]{1,0:T(8,128)} %copy-done.3, f32[5]{0:T(128)} %stack.31.fl_ref, f32[512,128]{1,0:T(8,128)} %get-tuple-element.29.a_ref, f32[512,128]{1,0:T(8,128)} %get-tuple-element.30.r_ref, ...), custom_call_target="tpu_custom_call" | custom-call | tf_op jit(solution)/shard_map/pallas_call | solution.py:329
  20.6 24.5 %all_to_all.10.s_ref = f32[64,1,8,128]{3,2,1,0:T(8,128)} all-to-all(f32[64,1,8,128]{3,2,1,0:T(8,128)} %bitcast.35), channel_id=1, replica_groups=mesh['cast'=64,'width'=4] {'cast'}, dimensions={0} | all-to-all | bytes 524288 | tf_op jit(solution)/shard_map/all_to_all | solution.py:609
  45.1 1.9 %shard_map.39 = f32[64,1,2,128]{3,2,1,0:T(2,128)} custom-call(f32[64,1,8,128]{3,2,1,0:T(8,128)} %all_to_all.10.s_ref), custom_call_target="tpu_custom_call" | custom-call | tf_op jit(solution)/shard_map/pallas_call | solution.py:611
  47.0 4.8 %all-to-all-start.1 = ((f32[64,1,2,128]{3,2,1,0:T(2,128)}), f32[64,1,2,128]{3,2,1,0:T(2,128)S(1)}, u32[]{:S(2)}, u32[]{:S(2)}) async-start(f32[64,1,2,128]{3,2,1,0:T(2,128)} %shard_map.39), calls=%async_computation.1 | async-start | bytes 131072 | tf_op jit(solution)/shard_map/all_to_all | solution.py:612
  51.8 4.2 %shard_map.40 = (f32[128,4,128]{2,1,0:T(4,128)}, f32[128,4,128]{2,1,0:T(4,128)}, f32[128,4,128]{2,1,0:T(4,128)}, f32[128,4,128]{2,1,0:T(4,128)}, f32[128,4,128]{2,1,0:T(4,128)}, /*index=5*/f32[2,4,4,128]{3,2,1,0:T(4,128)}) custom-call(f32[512,128]{1,0:T(8,128)} %bitcast.26, f32[64,8]{1,0:T(8,128)} %copy-done.2, f32[64,8]{1,0:T(8,128)} %copy-done.3, ...), custom_call_target="tpu_custom_call" | custom-call | tf_op jit(solution)/shard_map/pallas_call | solution.py:367
  55.9 5.9 %all-to-all-done.1 = f32[64,1,2,128]{3,2,1,0:T(2,128)S(1)} async-done(((f32[64,1,2,128]{3,2,1,0:T(2,128)}), f32[64,1,2,128]{3,2,1,0:T(2,128)S(1)}, u32[]{:S(2)}, u32[]{:S(2)}) %all-to-all-start.1) | async-done | bytes 65568 | tf_op jit(solution)/shard_map/all_to_all | solution.py:612
  61.9 0.6 copy-done.1
  62.5 2.9 %shard_map.41 = (f32[128,4,128]{2,1,0:T(4,128)}, f32[2,6,4,128]{3,2,1,0:T(4,128)}) custom-call(f32[64,8,128]{2,1,0:T(8,128)} %bitcast.33, f32[64,8,128]{2,1,0:T(8,128)} %bitcast.31, f32[64,8,128]{2,1,0:T(8,128)} %bitcast.32, f32[64,2,128]{2,1,0:T(2,128)} %bitcast.34, f32[128,4,128]{2,1,0:T(4,128)} %get-tuple-element.38.a_ref, ...), custom_call_target="tpu_custom_call" | custom-call | tf_op jit(solution)/shard_map/pallas_call | solution.py:433
  65.4 2.4 %collective-permute-start.4 = (f32[2,6,4,128]{3,2,1,0:T(4,128)}, f32[2,6,4,128]{3,2,1,0:T(4,128)S(1)}, u32[]{:S(2)}, u32[]{:S(2)}) collective-permute-start(f32[2,6,4,128]{3,2,1,0:T(4,128)} %get-tuple-element.42.refs_0_), channel_id=1, source_target_pairs={{0,1},{1,2},{2,3},{3,0},{4,5},{5,6},{6,7},{7,4},{8,9},{9,10},{10,1... | collective-permute-start | bytes 73736 | tf_op jit(solution)/shard_map/ppermute | solution.py:626
  67.8 2.6 %collective-permute-start.5 = (f32[2,6,4,128]{3,2,1,0:T(4,128)}, f32[2,6,4,128]{3,2,1,0:T(4,128)S(1)}, u32[]{:S(2)}, u32[]{:S(2)}) collective-permute-start(f32[2,6,4,128]{3,2,1,0:T(4,128)} %get-tuple-element.42.refs_0_), channel_id=1, source_target_pairs={{0,2},{1,3},{2,0},{3,1},{4,6},{5,7},{6,4},{7,5},{8,10},{9,11},{10,... | collective-permute-start | bytes 73736 | tf_op jit(solution)/shard_map/ppermute | solution.py:626
  70.4 1.1 %collective-permute-start.6 = (f32[2,6,4,128]{3,2,1,0:T(4,128)}, f32[2,6,4,128]{3,2,1,0:T(4,128)S(1)}, u32[]{:S(2)}, u32[]{:S(2)}) collective-permute-start(f32[2,6,4,128]{3,2,1,0:T(4,128)} %get-tuple-element.42.refs_0_), channel_id=1, source_target_pairs={{0,3},{1,0},{2,1},{3,2},{4,7},{5,4},{6,5},{7,6},{8,11},{9,8},{10,9... | collective-permute-start | bytes 73736 | tf_op jit(solution)/shard_map/ppermute | solution.py:626
  71.5 2.3 %shard_map.42 = (f32[64,8,128]{2,1,0:T(8,128)}, f32[64,8,128]{2,1,0:T(8,128)}, f32[64,8,128]{2,1,0:T(8,128)}, f32[64,8,128]{2,1,0:T(8,128)}) custom-call(f32[64,8,128]{2,1,0:T(8,128)} %bitcast.27, f32[64,8,128]{2,1,0:T(8,128)} %bitcast.29, f32[64,8,128]{2,1,0:T(8,128)} %bitcast.30), custom_call_target="tpu_custom_call" | custom-call | tf_op jit(solution)/shard_map/pallas_call | solution.py:182
  73.8 0.6 copy-done.6
  74.4 0.0 copy-done.7
  74.4 0.0 copy-done.8
  74.4 3.1 %shard_map.43 = f32[64,8,128]{2,1,0:T(8,128)} custom-call(s32[1]{0:T(128)} %bitcast.me_ref, f32[2,6,4,128]{3,2,1,0:T(4,128)} %get-tuple-element.42.refs_0_, f32[2,6,4,128]{3,2,1,0:T(4,128)} %copy-done.6, f32[2,6,4,128]{3,2,1,0:T(4,128)} %copy-done.7, f32[2,6,4,128]{3,2,1,0:T(4,128)} %copy-done.8, f32[128,4,128]{2,1,0:T(4,128)} %get-tuple-element.43.refs_4_, ...), custom_call_target="tpu_custom_call" | custom-call | tf_op jit(solution)/shard_map/pallas_call | solution.py:442
  (17 shorter events, 0.0 us)
Async XLA Ops:
  0.0 6.4 %copy-start = (f32[64,8,128]{2,1,0:T(8,128)S(1)}, f32[64,8,128]{2,1,0:T(8,128)}, u32[]{:S(2)}) copy-start(f32[64,8,128]{2,1,0:T(8,128)} %refs_12_.1) | copy-start | bytes 786436
  1.2 10.8 %collective-permute-start.2 = (f32[64,128]{1,0:T(8,128)S(1)}, f32[64,128]{1,0:T(8,128)S(1)}, u32[]{:S(2)}, u32[]{:S(2)}) collective-permute-start(f32[64,128]{1,0:T(8,128)S(1)} %get-tuple-element.58), channel_id=1, source_target_pairs={{0,4},{4,0},{8,12},{12,8},{16,20},{20,16},{24,28},{28,24},{32,36},... | collective-permute-start | bytes 98312 | tf_op jit(solution)/shard_map/ppermute | solution.py:594
  4.5 7.5 %collective-permute-start.3 = (f32[64,128]{1,0:T(8,128)S(1)}, f32[64,128]{1,0:T(8,128)S(1)}, u32[]{:S(2)}, u32[]{:S(2)}) collective-permute-start(f32[64,128]{1,0:T(8,128)S(1)} %get-tuple-element.57), channel_id=1, source_target_pairs={{4,8},{12,16},{20,24},{28,32},{36,40},{44,48},{52,56},{60,64},{68,... | collective-permute-start | bytes 98312 | tf_op jit(solution)/shard_map/ppermute | solution.py:595
  7.0 9.9 %collective-permute-start = (f32[64,8]{1,0:T(8,128)S(1)}, f32[64,8]{1,0:T(8,128)S(1)}, u32[]{:S(2)}, u32[]{:S(2)}) collective-permute-start(f32[64,8]{1,0:T(8,128)S(1)} %bitcast.38), channel_id=1, source_target_pairs={{0,1},{1,2},{2,3},{4,5},{5,6},{6,7},{8,9},{9,10},{10,11},{12,13},{... | collective-permute-start | bytes 6152 | tf_op jit(solution)/shard_map/ppermute | solution.py:596
  10.0 6.9 %collective-permute-start.1 = (f32[64,8]{1,0:T(8,128)S(1)}, f32[64,8]{1,0:T(8,128)S(1)}, u32[]{:S(2)}, u32[]{:S(2)}) collective-permute-start(f32[64,8]{1,0:T(8,128)S(1)} %bitcast.39), channel_id=1, source_target_pairs={{1,0},{2,1},{3,2},{5,4},{6,5},{7,6},{9,8},{10,9},{11,10},{13,12},{... | collective-permute-start | bytes 6152 | tf_op jit(solution)/shard_map/ppermute | solution.py:597
  12.0 0.6 copy-start.4
  12.0 0.6 copy-start.5
  16.9 0.6 copy-start.2
  16.9 0.6 copy-start.3
  47.0 14.9 %all-to-all-start.1 = ((f32[64,1,2,128]{3,2,1,0:T(2,128)}), f32[64,1,2,128]{3,2,1,0:T(2,128)S(1)}, u32[]{:S(2)}, u32[]{:S(2)}) async-start(f32[64,1,2,128]{3,2,1,0:T(2,128)} %shard_map.39), calls=%async_computation.1 | async-start | bytes 131072 | tf_op jit(solution)/shard_map/all_to_all | solution.py:612
  61.9 0.6 copy-start.1
  65.4 8.4 %collective-permute-start.4 = (f32[2,6,4,128]{3,2,1,0:T(4,128)}, f32[2,6,4,128]{3,2,1,0:T(4,128)S(1)}, u32[]{:S(2)}, u32[]{:S(2)}) collective-permute-start(f32[2,6,4,128]{3,2,1,0:T(4,128)} %get-tuple-element.42.refs_0_), channel_id=1, source_target_pairs={{0,1},{1,2},{2,3},{3,0},{4,5},{5,6},{6,7},{7,4},{8,9},{9,10},{10,1... | collective-permute-start | bytes 73736 | tf_op jit(solution)/shard_map/ppermute | solution.py:626
  67.8 6.0 %collective-permute-start.5 = (f32[2,6,4,128]{3,2,1,0:T(4,128)}, f32[2,6,4,128]{3,2,1,0:T(4,128)S(1)}, u32[]{:S(2)}, u32[]{:S(2)}) collective-permute-start(f32[2,6,4,128]{3,2,1,0:T(4,128)} %get-tuple-element.42.refs_0_), channel_id=1, source_target_pairs={{0,2},{1,3},{2,0},{3,1},{4,6},{5,7},{6,4},{7,5},{8,10},{9,11},{10,... | collective-permute-start | bytes 73736 | tf_op jit(solution)/shard_map/ppermute | solution.py:626
  70.4 3.4 %collective-permute-start.6 = (f32[2,6,4,128]{3,2,1,0:T(4,128)}, f32[2,6,4,128]{3,2,1,0:T(4,128)S(1)}, u32[]{:S(2)}, u32[]{:S(2)}) collective-permute-start(f32[2,6,4,128]{3,2,1,0:T(4,128)} %get-tuple-element.42.refs_0_), channel_id=1, source_target_pairs={{0,3},{1,0},{2,1},{3,2},{4,7},{5,4},{6,5},{7,6},{8,11},{9,8},{10,9... | collective-permute-start | bytes 73736 | tf_op jit(solution)/shard_map/ppermute | solution.py:626
  73.8 0.6 copy-start.6
  73.8 0.6 copy-start.7
  73.8 0.6 copy-start.8

commit v18 on v15

--- a/solution.py
+++ b/solution.py
@@ -174,7 +174,7 @@
 def _factor_kernel(nsub, a_ref, b_ref, c_ref, r_ref, cp_ref, v_ref, w_ref):
     n = a_ref.shape[0] // nsub
     subs = [q * n for q in range(nsub)]
-    _factor(n, subs, _lead_ld, _lead_st, a_ref, b_ref, c_ref, r_ref, cp_ref, v_ref, w_ref, 4, a_ref.shape[1:])
+    _factor(n, subs, _lead_ld, _lead_st, a_ref, b_ref, c_ref, r_ref, cp_ref, v_ref, w_ref, True, a_ref.shape[1:])
 
 
 def factor(a, b, c, nsub):
@@ -353,7 +353,7 @@
             dst[:, q, :] = src[q * 128 : (q + 1) * 128, :].T
     m = a_ref.shape[0] // nsub
     subs = [q * m for q in range(nsub)]
-    _factor(m, subs, _lead_ld, _lead_st, a_ref, b_ref, c_ref, r_ref, cp_ref, v_ref, w_ref, 4, a_ref.shape[1:])
+    _factor(m, subs, _lead_ld, _lead_st, a_ref, b_ref, c_ref, r_ref, cp_ref, v_ref, w_ref, True, a_ref.shape[1:])
     for q, s0 in enumerate(subs):
         for k, val in enumerate((v_ref[s0], w_ref[s0], v_ref[s0 + m - 1], w_ref[s0 + m - 1])):
             vws_ref[q, k] = val
@@ -381,7 +381,7 @@
         d_ref[:, q, :] = sc[q * 128 : (q + 1) * 128, :].T
     n = a_ref.shape[0] // nsub
     subs = [q * n for q in range(nsub)]
-    _solve_rhs(n, subs, _lead_ld, _lead_st, a_ref, r_ref, cp_ref, d_ref, y_ref, 4, a_ref.shape[1:])
+    _solve_rhs(n, subs, _lead_ld, _lead_st, a_ref, r_ref, cp_ref, d_ref, y_ref, True, a_ref.shape[1:])
     for q, s0 in enumerate(subs):
         rows = (y_ref[s0], vws_ref[q, 0], vws_ref[q, 1], y_ref[s0 + n - 1], vws_ref[q, 2], vws_ref[q, 3])
         for k, val in enumerate(rows):
@@ -404,7 +404,7 @@
     n = nt // tsub
     subs = [q * n for q in range(tsub)]
     shape = a_ref.shape[1:]
-    _solve_rhs(n, subs, _lead_ld, _lead_st, a_ref, r_ref, cp_ref, d_ref, y_ref, 4, shape)
+    _solve_rhs(n, subs, _lead_ld, _lead_st, a_ref, r_ref, cp_ref, d_ref, y_ref, True, shape)
     sums = [tuple(_summary_rows(_lead_ld, s0, n, y_ref, v_ref, w_ref)) for s0 in subs]
     lrs = [None] * tsub
 

time: 78 us -> 77.5 us (level)
  Pallas kernels: 21.5 us -> 20.6 us
  transfers between devices with their start and end apart: 8 -> 8, of which waited for: 1 -> 2; matrix products, arithmetic and copies ran while one was open for 2% -> 2% of each run, Pallas kernels for 14% -> 13%
where the time goes in v18:
time: 77.5 us; the launch traced here: 77.1 us
  blocking collectives  24.5 us (32%)
  Pallas kernels  20.6 us (27%)
  starting transfers between devices  19.9 us (26%)
  waiting for transfers between devices  6.69 us (9%)
  local copies, waits for them, and re-layouts  4.68 us (6%)
    all_to_all x1, blocking collectives, shards(): lax.all_to_all(summ.reshape(nc, nt // nc, 8, nwl), 'cast', 0, 0, tiled=True)  24.5 us
    all_to_all x1, waiting for transfers between devices, shards(): back = lax.all_to_all(lr, 'cast', 0, 0, tiled=True).reshape(nt, 2, nwl)  6.58 us
    ppermute x3, starting transfers between devices, shards(): lax.ppermute(summ, 'width', [(i, (i + q) % nw) for i in range(nw)])  6.05 us
    all_to_all x1, starting transfers between devices, shards(): back = lax.all_to_all(lr, 'cast', 0, 0, tiled=True).reshape(nt, 2, nwl)  4.77 us
    pallas_call x1, Pallas kernels, prep_solve(): pl.pallas_call(functools.partial(_prep_kernel, n), out_shape=[shp] * 3 +...  4.27 us
    pallas_call x1, Pallas kernels, wfactor(): pl.pallas_call(functools.partial(_wfactor_kernel, n, nsub), out_shape=[sh...  3.51 us
    unnamed x20, local copies, waits for them, and re-layouts  3.31 us
    ppermute x1, starting transfers between devices, shards(): got_a = lax.ppermute(jnp.where(even, last, first), 'cast', in_chip)  3.29 us
  transfers between devices with their start and end apart: 8, of which 2 were waited for; matrix products, arithmetic and copies ran while one was open for 2% of the time, Pallas kernels for 13%

profile of v18, /device:TPU:1, one launch (start us, length us, event | category | flops | bytes accessed | tf_op | source)
XLA Modules:
  0.0 77.1 jit_solution(15597120750628106580)
XLA Ops:
  0.0 1.1 %fusion = (f32[64,1,128]{2,1,0:T(1,128)S(1)}, f32[64,1,128]{2,1,0:T(1,128)S(1)}) fusion(f32[64,8,128]{2,1,0:T(8,128)} %refs_12_.1), kind=kLoop, calls=%fused_computation.2 | loop fusion | bytes 131072 | tf_op jit(solution)/shard_map/slice | solution.py:591
  1.2 3.3 %collective-permute-start.2 = (f32[64,128]{1,0:T(8,128)S(1)}, f32[64,128]{1,0:T(8,128)S(1)}, u32[]{:S(2)}, u32[]{:S(2)}) collective-permute-start(f32[64,128]{1,0:T(8,128)S(1)} %get-tuple-element.58), channel_id=1, source_target_pairs={{0,4},{4,0},{8,12},{12,8},{16,20},{20,16},{24,28},{28,24},{32,36},... | collective-permute-start | bytes 98312 | tf_op jit(solution)/shard_map/ppermute | solution.py:594
  4.5 1.9 %collective-permute-start.3 = (f32[64,128]{1,0:T(8,128)S(1)}, f32[64,128]{1,0:T(8,128)S(1)}, u32[]{:S(2)}, u32[]{:S(2)}) collective-permute-start(f32[64,128]{1,0:T(8,128)S(1)} %get-tuple-element.57), channel_id=1, source_target_pairs={{4,8},{12,16},{20,24},{28,32},{36,40},{44,48},{52,56},{60,64},{68,... | collective-permute-start | bytes 98312 | tf_op jit(solution)/shard_map/ppermute | solution.py:595
  6.4 0.1 fusion.1
  6.5 0.4 copy.13
  7.0 2.6 %collective-permute-start = (f32[64,8]{1,0:T(8,128)S(1)}, f32[64,8]{1,0:T(8,128)S(1)}, u32[]{:S(2)}, u32[]{:S(2)}) collective-permute-start(f32[64,8]{1,0:T(8,128)S(1)} %bitcast.38), channel_id=1, source_target_pairs={{0,1},{1,2},{2,3},{4,5},{5,6},{6,7},{8,9},{9,10},{10,11},{12,13},{... | collective-permute-start | bytes 6152 | tf_op jit(solution)/shard_map/ppermute | solution.py:596
  9.6 0.4 copy.14
  10.0 1.3 %collective-permute-start.1 = (f32[64,8]{1,0:T(8,128)S(1)}, f32[64,8]{1,0:T(8,128)S(1)}, u32[]{:S(2)}, u32[]{:S(2)}) collective-permute-start(f32[64,8]{1,0:T(8,128)S(1)} %bitcast.39), channel_id=1, source_target_pairs={{1,0},{2,1},{3,2},{5,4},{6,5},{7,6},{9,8},{10,9},{11,10},{13,12},{... | collective-permute-start | bytes 6152 | tf_op jit(solution)/shard_map/ppermute | solution.py:597
  11.3 0.1 stack.30
  11.4 0.5 stack.31.fl_ref
  12.0 0.6 copy-done.7
  12.6 0.0 copy-done.8
  12.6 4.3 %shard_map.37 = (f32[512,128]{1,0:T(8,128)}, f32[512,128]{1,0:T(8,128)}, f32[512,128]{1,0:T(8,128)}, f32[512,128]{1,0:T(8,128)}, f32[512,128]{1,0:T(8,128)}, /*i...) custom-call(f32[512,128]{1,0:T(8,128)} %bitcast.24, ...), custom_call_target="tpu_custom_call" | custom-call | tf_op jit(solution)/shard_map/pallas_call | solution.py:292
  16.9 0.6 copy-done.2
  17.5 0.0 copy-done.3
  17.5 3.1 %shard_map.38 = (f32[512,128]{1,0:T(8,128)}, f32[512,128]{1,0:T(8,128)}) custom-call(f32[512,128]{1,0:T(8,128)} %bitcast.25, f32[64,8]{1,0:T(8,128)} %copy-done.2, f32[64,8]{1,0:T(8,128)} %copy-done.3, f32[5]{0:T(128)} %stack.31.fl_ref, f32[512,128]{1,0:T(8,128)} %get-tuple-element.29.a_ref, f32[512,128]{1,0:T(8,128)} %get-tuple-element.30.r_ref, ...), custom_call_target="tpu_custom_call" | custom-call | tf_op jit(solution)/shard_map/pallas_call | solution.py:329
  20.6 24.5 %all_to_all.10.s_ref = f32[64,1,8,128]{3,2,1,0:T(8,128)} all-to-all(f32[64,1,8,128]{3,2,1,0:T(8,128)} %bitcast.35), channel_id=1, replica_groups=mesh['cast'=64,'width'=4] {'cast'}, dimensions={0} | all-to-all | bytes 524288 | tf_op jit(solution)/shard_map/all_to_all | solution.py:609
  45.1 1.9 %shard_map.39 = f32[64,1,2,128]{3,2,1,0:T(2,128)} custom-call(f32[64,1,8,128]{3,2,1,0:T(8,128)} %all_to_all.10.s_ref), custom_call_target="tpu_custom_call" | custom-call | tf_op jit(solution)/shard_map/pallas_call | solution.py:611
  47.0 4.8 %all-to-all-start.1 = ((f32[64,1,2,128]{3,2,1,0:T(2,128)}), f32[64,1,2,128]{3,2,1,0:T(2,128)S(1)}, u32[]{:S(2)}, u32[]{:S(2)}) async-start(f32[64,1,2,128]{3,2,1,0:T(2,128)} %shard_map.39), calls=%async_computation.1 | async-start | bytes 131072 | tf_op jit(solution)/shard_map/all_to_all | solution.py:612
  51.8 3.5 %shard_map.40 = (f32[128,4,128]{2,1,0:T(4,128)}, f32[128,4,128]{2,1,0:T(4,128)}, f32[128,4,128]{2,1,0:T(4,128)}, f32[128,4,128]{2,1,0:T(4,128)}, f32[128,4,128]{2,1,0:T(4,128)}, /*index=5*/f32[4,4,4,128]{3,2,1,0:T(4,128)}) custom-call(f32[512,128]{1,0:T(8,128)} %bitcast.26, f32[64,8]{1,0:T(8,128)} %copy-done.2, f32[64,8]{1,0:T(8,128)} %copy-done.3, ...), custom_call_target="tpu_custom_call" | custom-call | tf_op jit(solution)/shard_map/pallas_call | solution.py:367
  55.3 6.6 %all-to-all-done.1 = f32[64,1,2,128]{3,2,1,0:T(2,128)S(1)} async-done(((f32[64,1,2,128]{3,2,1,0:T(2,128)}), f32[64,1,2,128]{3,2,1,0:T(2,128)S(1)}, u32[]{:S(2)}, u32[]{:S(2)}) %all-to-all-start.1) | async-done | bytes 65568 | tf_op jit(solution)/shard_map/all_to_all | solution.py:612
  61.9 0.6 copy-done.1
  62.5 2.5 %shard_map.41 = (f32[128,4,128]{2,1,0:T(4,128)}, f32[4,6,4,128]{3,2,1,0:T(4,128)}) custom-call(f32[64,8,128]{2,1,0:T(8,128)} %bitcast.33, f32[64,8,128]{2,1,0:T(8,128)} %bitcast.31, f32[64,8,128]{2,1,0:T(8,128)} %bitcast.32, f32[64,2,128]{2,1,0:T(2,128)} %bitcast.34, f32[128,4,128]{2,1,0:T(4,128)} %get-tuple-element.38.a_ref, ...), custom_call_target="tpu_custom_call" | custom-call | tf_op jit(solution)/shard_map/pallas_call | solution.py:433
  65.0 2.4 %collective-permute-start.4 = (f32[4,6,4,128]{3,2,1,0:T(4,128)}, f32[4,6,4,128]{3,2,1,0:T(4,128)S(1)}, u32[]{:S(2)}, u32[]{:S(2)}) collective-permute-start(f32[4,6,4,128]{3,2,1,0:T(4,128)} %get-tuple-element.42.refs_0_), channel_id=1, source_target_pairs={{0,1},{1,2},{2,3},{3,0},{4,5},{5,6},{6,7},{7,4},{8,9},{9,10},{10,1... | collective-permute-start | bytes 147464 | tf_op jit(solution)/shard_map/ppermute | solution.py:626
  67.4 2.6 %collective-permute-start.5 = (f32[4,6,4,128]{3,2,1,0:T(4,128)}, f32[4,6,4,128]{3,2,1,0:T(4,128)S(1)}, u32[]{:S(2)}, u32[]{:S(2)}) collective-permute-start(f32[4,6,4,128]{3,2,1,0:T(4,128)} %get-tuple-element.42.refs_0_), channel_id=1, source_target_pairs={{0,2},{1,3},{2,0},{3,1},{4,6},{5,7},{6,4},{7,5},{8,10},{9,11},{10,... | collective-permute-start | bytes 147464 | tf_op jit(solution)/shard_map/ppermute | solution.py:626
  70.0 1.1 %collective-permute-start.6 = (f32[4,6,4,128]{3,2,1,0:T(4,128)}, f32[4,6,4,128]{3,2,1,0:T(4,128)S(1)}, u32[]{:S(2)}, u32[]{:S(2)}) collective-permute-start(f32[4,6,4,128]{3,2,1,0:T(4,128)} %get-tuple-element.42.refs_0_), channel_id=1, source_target_pairs={{0,3},{1,0},{2,1},{3,2},{4,7},{5,4},{6,5},{7,6},{8,11},{9,8},{10,9... | collective-permute-start | bytes 147464 | tf_op jit(solution)/shard_map/ppermute | solution.py:626
  71.1 2.2 %shard_map.42 = (f32[64,8,128]{2,1,0:T(8,128)}, f32[64,8,128]{2,1,0:T(8,128)}, f32[64,8,128]{2,1,0:T(8,128)}, f32[64,8,128]{2,1,0:T(8,128)}) custom-call(f32[64,8,128]{2,1,0:T(8,128)} %bitcast.27, f32[64,8,128]{2,1,0:T(8,128)} %bitcast.29, f32[64,8,128]{2,1,0:T(8,128)} %bitcast.30), custom_call_target="tpu_custom_call" | custom-call | tf_op jit(solution)/shard_map/pallas_call | solution.py:182
  73.3 0.1 collective-permute-done.6.refs_3_
  73.4 0.5 copy-done.4
  73.9 0.0 copy-done.5
  73.9 0.1 copy-done.6
  74.0 3.0 %shard_map.43 = f32[64,8,128]{2,1,0:T(8,128)} custom-call(s32[1]{0:T(128)} %bitcast.me_ref, f32[4,6,4,128]{3,2,1,0:T(4,128)} %get-tuple-element.42.refs_0_, f32[4,6,4,128]{3,2,1,0:T(4,128)} %copy-done.4, f32[4,6,4,128]{3,2,1,0:T(4,128)} %copy-done.5, f32[4,6,4,128]{3,2,1,0:T(4,128)} %copy-done.6, f32[128,4,128]{2,1,0:T(4,128)} %get-tuple-element.43.refs_4_, ...), custom_call_target="tpu_custom_call" | custom-call | tf_op jit(solution)/shard_map/pallas_call | solution.py:442
  (17 shorter events, 0.0 us)
Async XLA Ops:
  0.0 6.4 %copy-start = (f32[64,8,128]{2,1,0:T(8,128)S(1)}, f32[64,8,128]{2,1,0:T(8,128)}, u32[]{:S(2)}) copy-start(f32[64,8,128]{2,1,0:T(8,128)} %refs_12_.1) | copy-start | bytes 786436
  1.2 10.8 %collective-permute-start.2 = (f32[64,128]{1,0:T(8,128)S(1)}, f32[64,128]{1,0:T(8,128)S(1)}, u32[]{:S(2)}, u32[]{:S(2)}) collective-permute-start(f32[64,128]{1,0:T(8,128)S(1)} %get-tuple-element.58), channel_id=1, source_target_pairs={{0,4},{4,0},{8,12},{12,8},{16,20},{20,16},{24,28},{28,24},{32,36},... | collective-permute-start | bytes 98312 | tf_op jit(solution)/shard_map/ppermute | solution.py:594
  4.5 7.5 %collective-permute-start.3 = (f32[64,128]{1,0:T(8,128)S(1)}, f32[64,128]{1,0:T(8,128)S(1)}, u32[]{:S(2)}, u32[]{:S(2)}) collective-permute-start(f32[64,128]{1,0:T(8,128)S(1)} %get-tuple-element.57), channel_id=1, source_target_pairs={{4,8},{12,16},{20,24},{28,32},{36,40},{44,48},{52,56},{60,64},{68,... | collective-permute-start | bytes 98312 | tf_op jit(solution)/shard_map/ppermute | solution.py:595
  7.0 9.9 %collective-permute-start = (f32[64,8]{1,0:T(8,128)S(1)}, f32[64,8]{1,0:T(8,128)S(1)}, u32[]{:S(2)}, u32[]{:S(2)}) collective-permute-start(f32[64,8]{1,0:T(8,128)S(1)} %bitcast.38), channel_id=1, source_target_pairs={{0,1},{1,2},{2,3},{4,5},{5,6},{6,7},{8,9},{9,10},{10,11},{12,13},{... | collective-permute-start | bytes 6152 | tf_op jit(solution)/shard_map/ppermute | solution.py:596
  10.0 6.9 %collective-permute-start.1 = (f32[64,8]{1,0:T(8,128)S(1)}, f32[64,8]{1,0:T(8,128)S(1)}, u32[]{:S(2)}, u32[]{:S(2)}) collective-permute-start(f32[64,8]{1,0:T(8,128)S(1)} %bitcast.39), channel_id=1, source_target_pairs={{1,0},{2,1},{3,2},{5,4},{6,5},{7,6},{9,8},{10,9},{11,10},{13,12},{... | collective-permute-start | bytes 6152 | tf_op jit(solution)/shard_map/ppermute | solution.py:597
  12.0 0.6 copy-start.7
  12.0 0.6 copy-start.8
  16.9 0.6 copy-start.2
  16.9 0.6 copy-start.3
  47.0 14.9 %all-to-all-start.1 = ((f32[64,1,2,128]{3,2,1,0:T(2,128)}), f32[64,1,2,128]{3,2,1,0:T(2,128)S(1)}, u32[]{:S(2)}, u32[]{:S(2)}) async-start(f32[64,1,2,128]{3,2,1,0:T(2,128)} %shard_map.39), calls=%async_computation.1 | async-start | bytes 131072 | tf_op jit(solution)/shard_map/all_to_all | solution.py:612
  61.9 0.6 copy-start.1
  65.0 8.3 %collective-permute-start.4 = (f32[4,6,4,128]{3,2,1,0:T(4,128)}, f32[4,6,4,128]{3,2,1,0:T(4,128)S(1)}, u32[]{:S(2)}, u32[]{:S(2)}) collective-permute-start(f32[4,6,4,128]{3,2,1,0:T(4,128)} %get-tuple-element.42.refs_0_), channel_id=1, source_target_pairs={{0,1},{1,2},{2,3},{3,0},{4,5},{5,6},{6,7},{7,4},{8,9},{9,10},{10,1... | collective-permute-start | bytes 147464 | tf_op jit(solution)/shard_map/ppermute | solution.py:626
  67.4 5.9 %collective-permute-start.5 = (f32[4,6,4,128]{3,2,1,0:T(4,128)}, f32[4,6,4,128]{3,2,1,0:T(4,128)S(1)}, u32[]{:S(2)}, u32[]{:S(2)}) collective-permute-start(f32[4,6,4,128]{3,2,1,0:T(4,128)} %get-tuple-element.42.refs_0_), channel_id=1, source_target_pairs={{0,2},{1,3},{2,0},{3,1},{4,6},{5,7},{6,4},{7,5},{8,10},{9,11},{10,... | collective-permute-start | bytes 147464 | tf_op jit(solution)/shard_map/ppermute | solution.py:626
  70.0 3.4 %collective-permute-start.6 = (f32[4,6,4,128]{3,2,1,0:T(4,128)}, f32[4,6,4,128]{3,2,1,0:T(4,128)S(1)}, u32[]{:S(2)}, u32[]{:S(2)}) collective-permute-start(f32[4,6,4,128]{3,2,1,0:T(4,128)} %get-tuple-element.42.refs_0_), channel_id=1, source_target_pairs={{0,3},{1,0},{2,1},{3,2},{4,7},{5,4},{6,5},{7,6},{8,11},{9,8},{10,9... | collective-permute-start | bytes 147464 | tf_op jit(solution)/shard_map/ppermute | solution.py:626
  73.3 0.6 copy-start.4
  73.3 0.6 copy-start.5
  73.4 0.6 copy-start.6

commit v19 on v18

--- a/solution.py
+++ b/solution.py
@@ -620,13 +620,13 @@
 
     wa, r_w, cp_w, v_w, w_w, vws = wfactor(h2, h_wl, h_wh, flags, ncl, nsub)
     wfac = (r_w, cp_w, v_w, w_w)
-    tfac = factor(tlo, tmd, thi, 8)
+    tfac = factor(tlo, tmd, thi, 16)
     yw, summ = width_solve(y, v, w, back, wa, (r_w, cp_w, vws), nsub)
     got = [summ] + [
         lax.ppermute(summ, "width", [(i, (i + q) % nw) for i in range(nw)]) for q in range(1, nw)
     ]
     me = wi.astype(jnp.int32).reshape(1)
-    return thick_solve(me, got, yw, wfac[2], wfac[3], tlo, tfac, h, nsub, 8)
+    return thick_solve(me, got, yw, wfac[2], wfac[3], tlo, tfac, h, nsub, 16)
 
 
 def solution(mesh):

time: 77.5 us -> 77.6 us (level)
  no operation moved by 1% of the time
where the time goes in v19:
time: 77.6 us; the launch traced here: 77.1 us
  blocking collectives  24.5 us (32%)
  Pallas kernels  20.6 us (27%)
  starting transfers between devices  19.9 us (26%)
  waiting for transfers between devices  6.73 us (9%)
  local copies, waits for them, and re-layouts  4.68 us (6%)
    all_to_all x1, blocking collectives, shards(): lax.all_to_all(summ.reshape(nc, nt // nc, 8, nwl), 'cast', 0, 0, tiled=True)  24.5 us
    all_to_all x1, waiting for transfers between devices, shards(): back = lax.all_to_all(lr, 'cast', 0, 0, tiled=True).reshape(nt, 2, nwl)  6.58 us
    ppermute x3, starting transfers between devices, shards(): lax.ppermute(summ, 'width', [(i, (i + q) % nw) for i in range(nw)])  6.05 us
    all_to_all x1, starting transfers between devices, shards(): back = lax.all_to_all(lr, 'cast', 0, 0, tiled=True).reshape(nt, 2, nwl)  4.77 us
    pallas_call x1, Pallas kernels, prep_solve(): pl.pallas_call(functools.partial(_prep_kernel, n), out_shape=[shp] * 3 +...  4.27 us
    pallas_call x1, Pallas kernels, wfactor(): pl.pallas_call(functools.partial(_wfactor_kernel, n, nsub), out_shape=[sh...  3.51 us
    unnamed x20, local copies, waits for them, and re-layouts  3.31 us
    ppermute x1, starting transfers between devices, shards(): got_a = lax.ppermute(jnp.where(even, last, first), 'cast', in_chip)  3.29 us
  transfers between devices with their start and end apart: 8, of which 2 were waited for; matrix products, arithmetic and copies ran while one was open for 2% of the time, Pallas kernels for 13%

profile of v19, /device:TPU:1, one launch (start us, length us, event | category | flops | bytes accessed | tf_op | source)
XLA Modules:
  0.0 77.1 jit_solution(2090135264341889888)
XLA Ops:
  0.0 1.1 %fusion = (f32[64,1,128]{2,1,0:T(1,128)S(1)}, f32[64,1,128]{2,1,0:T(1,128)S(1)}) fusion(f32[64,8,128]{2,1,0:T(8,128)} %refs_12_.1), kind=kLoop, calls=%fused_computation.2 | loop fusion | bytes 131072 | tf_op jit(solution)/shard_map/slice | solution.py:591
  1.2 3.3 %collective-permute-start.2 = (f32[64,128]{1,0:T(8,128)S(1)}, f32[64,128]{1,0:T(8,128)S(1)}, u32[]{:S(2)}, u32[]{:S(2)}) collective-permute-start(f32[64,128]{1,0:T(8,128)S(1)} %get-tuple-element.58), channel_id=1, source_target_pairs={{0,4},{4,0},{8,12},{12,8},{16,20},{20,16},{24,28},{28,24},{32,36},... | collective-permute-start | bytes 98312 | tf_op jit(solution)/shard_map/ppermute | solution.py:594
  4.5 1.9 %collective-permute-start.3 = (f32[64,128]{1,0:T(8,128)S(1)}, f32[64,128]{1,0:T(8,128)S(1)}, u32[]{:S(2)}, u32[]{:S(2)}) collective-permute-start(f32[64,128]{1,0:T(8,128)S(1)} %get-tuple-element.57), channel_id=1, source_target_pairs={{4,8},{12,16},{20,24},{28,32},{36,40},{44,48},{52,56},{60,64},{68,... | collective-permute-start | bytes 98312 | tf_op jit(solution)/shard_map/ppermute | solution.py:595
  6.4 0.1 fusion.1
  6.5 0.4 copy.13
  7.0 2.6 %collective-permute-start = (f32[64,8]{1,0:T(8,128)S(1)}, f32[64,8]{1,0:T(8,128)S(1)}, u32[]{:S(2)}, u32[]{:S(2)}) collective-permute-start(f32[64,8]{1,0:T(8,128)S(1)} %bitcast.38), channel_id=1, source_target_pairs={{0,1},{1,2},{2,3},{4,5},{5,6},{6,7},{8,9},{9,10},{10,11},{12,13},{... | collective-permute-start | bytes 6152 | tf_op jit(solution)/shard_map/ppermute | solution.py:596
  9.6 0.4 copy.14
  10.0 1.3 %collective-permute-start.1 = (f32[64,8]{1,0:T(8,128)S(1)}, f32[64,8]{1,0:T(8,128)S(1)}, u32[]{:S(2)}, u32[]{:S(2)}) collective-permute-start(f32[64,8]{1,0:T(8,128)S(1)} %bitcast.39), channel_id=1, source_target_pairs={{1,0},{2,1},{3,2},{5,4},{6,5},{7,6},{9,8},{10,9},{11,10},{13,12},{... | collective-permute-start | bytes 6152 | tf_op jit(solution)/shard_map/ppermute | solution.py:597
  11.3 0.1 stack.30
  11.4 0.5 stack.31.fl_ref
  12.0 0.6 copy-done.7
  12.6 0.0 copy-done.8
  12.6 4.3 %shard_map.37 = (f32[512,128]{1,0:T(8,128)}, f32[512,128]{1,0:T(8,128)}, f32[512,128]{1,0:T(8,128)}, f32[512,128]{1,0:T(8,128)}, f32[512,128]{1,0:T(8,128)}, /*i...) custom-call(f32[512,128]{1,0:T(8,128)} %bitcast.24, ...), custom_call_target="tpu_custom_call" | custom-call | tf_op jit(solution)/shard_map/pallas_call | solution.py:292
  16.9 0.6 copy-done.2
  17.5 0.0 copy-done.3
  17.5 3.1 %shard_map.38 = (f32[512,128]{1,0:T(8,128)}, f32[512,128]{1,0:T(8,128)}) custom-call(f32[512,128]{1,0:T(8,128)} %bitcast.25, f32[64,8]{1,0:T(8,128)} %copy-done.2, f32[64,8]{1,0:T(8,128)} %copy-done.3, f32[5]{0:T(128)} %stack.31.fl_ref, f32[512,128]{1,0:T(8,128)} %get-tuple-element.29.a_ref, f32[512,128]{1,0:T(8,128)} %get-tuple-element.30.r_ref, ...), custom_call_target="tpu_custom_call" | custom-call | tf_op jit(solution)/shard_map/pallas_call | solution.py:329
  20.6 24.5 %all_to_all.10.s_ref = f32[64,1,8,128]{3,2,1,0:T(8,128)} all-to-all(f32[64,1,8,128]{3,2,1,0:T(8,128)} %bitcast.35), channel_id=1, replica_groups=mesh['cast'=64,'width'=4] {'cast'}, dimensions={0} | all-to-all | bytes 524288 | tf_op jit(solution)/shard_map/all_to_all | solution.py:609
  45.1 1.9 %shard_map.39 = f32[64,1,2,128]{3,2,1,0:T(2,128)} custom-call(f32[64,1,8,128]{3,2,1,0:T(8,128)} %all_to_all.10.s_ref), custom_call_target="tpu_custom_call" | custom-call | tf_op jit(solution)/shard_map/pallas_call | solution.py:611
  47.0 4.8 %all-to-all-start.1 = ((f32[64,1,2,128]{3,2,1,0:T(2,128)}), f32[64,1,2,128]{3,2,1,0:T(2,128)S(1)}, u32[]{:S(2)}, u32[]{:S(2)}) async-start(f32[64,1,2,128]{3,2,1,0:T(2,128)} %shard_map.39), calls=%async_computation.1 | async-start | bytes 131072 | tf_op jit(solution)/shard_map/all_to_all | solution.py:612
  51.8 3.5 %shard_map.40 = (f32[128,4,128]{2,1,0:T(4,128)}, f32[128,4,128]{2,1,0:T(4,128)}, f32[128,4,128]{2,1,0:T(4,128)}, f32[128,4,128]{2,1,0:T(4,128)}, f32[128,4,128]{2,1,0:T(4,128)}, /*index=5*/f32[4,4,4,128]{3,2,1,0:T(4,128)}) custom-call(f32[512,128]{1,0:T(8,128)} %bitcast.26, f32[64,8]{1,0:T(8,128)} %copy-done.2, f32[64,8]{1,0:T(8,128)} %copy-done.3, ...), custom_call_target="tpu_custom_call" | custom-call | tf_op jit(solution)/shard_map/pallas_call | solution.py:367
  55.3 6.6 %all-to-all-done.1 = f32[64,1,2,128]{3,2,1,0:T(2,128)S(1)} async-done(((f32[64,1,2,128]{3,2,1,0:T(2,128)}), f32[64,1,2,128]{3,2,1,0:T(2,128)S(1)}, u32[]{:S(2)}, u32[]{:S(2)}) %all-to-all-start.1) | async-done | bytes 65568 | tf_op jit(solution)/shard_map/all_to_all | solution.py:612
  61.9 0.6 copy-done.1
  62.5 2.5 %shard_map.41 = (f32[128,4,128]{2,1,0:T(4,128)}, f32[4,6,4,128]{3,2,1,0:T(4,128)}) custom-call(f32[64,8,128]{2,1,0:T(8,128)} %bitcast.33, f32[64,8,128]{2,1,0:T(8,128)} %bitcast.31, f32[64,8,128]{2,1,0:T(8,128)} %bitcast.32, f32[64,2,128]{2,1,0:T(2,128)} %bitcast.34, f32[128,4,128]{2,1,0:T(4,128)} %get-tuple-element.38.a_ref, ...), custom_call_target="tpu_custom_call" | custom-call | tf_op jit(solution)/shard_map/pallas_call | solution.py:433
  65.0 2.4 %collective-permute-start.4 = (f32[4,6,4,128]{3,2,1,0:T(4,128)}, f32[4,6,4,128]{3,2,1,0:T(4,128)S(1)}, u32[]{:S(2)}, u32[]{:S(2)}) collective-permute-start(f32[4,6,4,128]{3,2,1,0:T(4,128)} %get-tuple-element.42.refs_0_), channel_id=1, source_target_pairs={{0,1},{1,2},{2,3},{3,0},{4,5},{5,6},{6,7},{7,4},{8,9},{9,10},{10,1... | collective-permute-start | bytes 147464 | tf_op jit(solution)/shard_map/ppermute | solution.py:626
  67.4 2.6 %collective-permute-start.5 = (f32[4,6,4,128]{3,2,1,0:T(4,128)}, f32[4,6,4,128]{3,2,1,0:T(4,128)S(1)}, u32[]{:S(2)}, u32[]{:S(2)}) collective-permute-start(f32[4,6,4,128]{3,2,1,0:T(4,128)} %get-tuple-element.42.refs_0_), channel_id=1, source_target_pairs={{0,2},{1,3},{2,0},{3,1},{4,6},{5,7},{6,4},{7,5},{8,10},{9,11},{10,... | collective-permute-start | bytes 147464 | tf_op jit(solution)/shard_map/ppermute | solution.py:626
  70.0 1.1 %collective-permute-start.6 = (f32[4,6,4,128]{3,2,1,0:T(4,128)}, f32[4,6,4,128]{3,2,1,0:T(4,128)S(1)}, u32[]{:S(2)}, u32[]{:S(2)}) collective-permute-start(f32[4,6,4,128]{3,2,1,0:T(4,128)} %get-tuple-element.42.refs_0_), channel_id=1, source_target_pairs={{0,3},{1,0},{2,1},{3,2},{4,7},{5,4},{6,5},{7,6},{8,11},{9,8},{10,9... | collective-permute-start | bytes 147464 | tf_op jit(solution)/shard_map/ppermute | solution.py:626
  71.1 2.2 %shard_map.42 = (f32[64,8,128]{2,1,0:T(8,128)}, f32[64,8,128]{2,1,0:T(8,128)}, f32[64,8,128]{2,1,0:T(8,128)}, f32[64,8,128]{2,1,0:T(8,128)}) custom-call(f32[64,8,128]{2,1,0:T(8,128)} %bitcast.27, f32[64,8,128]{2,1,0:T(8,128)} %bitcast.29, f32[64,8,128]{2,1,0:T(8,128)} %bitcast.30), custom_call_target="tpu_custom_call" | custom-call | tf_op jit(solution)/shard_map/pallas_call | solution.py:182
  73.3 0.1 collective-permute-done.6.refs_3_
  73.4 0.5 copy-done.4
  73.9 0.0 copy-done.5
  73.9 0.1 copy-done.6
  74.0 3.1 %shard_map.43 = f32[64,8,128]{2,1,0:T(8,128)} custom-call(s32[1]{0:T(128)} %bitcast.me_ref, f32[4,6,4,128]{3,2,1,0:T(4,128)} %get-tuple-element.42.refs_0_, f32[4,6,4,128]{3,2,1,0:T(4,128)} %copy-done.4, f32[4,6,4,128]{3,2,1,0:T(4,128)} %copy-done.5, f32[4,6,4,128]{3,2,1,0:T(4,128)} %copy-done.6, f32[128,4,128]{2,1,0:T(4,128)} %get-tuple-element.43.refs_4_, ...), custom_call_target="tpu_custom_call" | custom-call | tf_op jit(solution)/shard_map/pallas_call | solution.py:442
  (17 shorter events, 0.0 us)
Async XLA Ops:
  0.0 6.4 %copy-start = (f32[64,8,128]{2,1,0:T(8,128)S(1)}, f32[64,8,128]{2,1,0:T(8,128)}, u32[]{:S(2)}) copy-start(f32[64,8,128]{2,1,0:T(8,128)} %refs_12_.1) | copy-start | bytes 786436
  1.2 10.8 %collective-permute-start.2 = (f32[64,128]{1,0:T(8,128)S(1)}, f32[64,128]{1,0:T(8,128)S(1)}, u32[]{:S(2)}, u32[]{:S(2)}) collective-permute-start(f32[64,128]{1,0:T(8,128)S(1)} %get-tuple-element.58), channel_id=1, source_target_pairs={{0,4},{4,0},{8,12},{12,8},{16,20},{20,16},{24,28},{28,24},{32,36},... | collective-permute-start | bytes 98312 | tf_op jit(solution)/shard_map/ppermute | solution.py:594
  4.5 7.5 %collective-permute-start.3 = (f32[64,128]{1,0:T(8,128)S(1)}, f32[64,128]{1,0:T(8,128)S(1)}, u32[]{:S(2)}, u32[]{:S(2)}) collective-permute-start(f32[64,128]{1,0:T(8,128)S(1)} %get-tuple-element.57), channel_id=1, source_target_pairs={{4,8},{12,16},{20,24},{28,32},{36,40},{44,48},{52,56},{60,64},{68,... | collective-permute-start | bytes 98312 | tf_op jit(solution)/shard_map/ppermute | solution.py:595
  7.0 9.9 %collective-permute-start = (f32[64,8]{1,0:T(8,128)S(1)}, f32[64,8]{1,0:T(8,128)S(1)}, u32[]{:S(2)}, u32[]{:S(2)}) collective-permute-start(f32[64,8]{1,0:T(8,128)S(1)} %bitcast.38), channel_id=1, source_target_pairs={{0,1},{1,2},{2,3},{4,5},{5,6},{6,7},{8,9},{9,10},{10,11},{12,13},{... | collective-permute-start | bytes 6152 | tf_op jit(solution)/shard_map/ppermute | solution.py:596
  10.0 6.9 %collective-permute-start.1 = (f32[64,8]{1,0:T(8,128)S(1)}, f32[64,8]{1,0:T(8,128)S(1)}, u32[]{:S(2)}, u32[]{:S(2)}) collective-permute-start(f32[64,8]{1,0:T(8,128)S(1)} %bitcast.39), channel_id=1, source_target_pairs={{1,0},{2,1},{3,2},{5,4},{6,5},{7,6},{9,8},{10,9},{11,10},{13,12},{... | collective-permute-start | bytes 6152 | tf_op jit(solution)/shard_map/ppermute | solution.py:597
  12.0 0.6 copy-start.7
  12.0 0.6 copy-start.8
  16.9 0.6 copy-start.2
  16.9 0.6 copy-start.3
  47.0 14.9 %all-to-all-start.1 = ((f32[64,1,2,128]{3,2,1,0:T(2,128)}), f32[64,1,2,128]{3,2,1,0:T(2,128)S(1)}, u32[]{:S(2)}, u32[]{:S(2)}) async-start(f32[64,1,2,128]{3,2,1,0:T(2,128)} %shard_map.39), calls=%async_computation.1 | async-start | bytes 131072 | tf_op jit(solution)/shard_map/all_to_all | solution.py:612
  61.9 0.6 copy-start.1
  65.0 8.3 %collective-permute-start.4 = (f32[4,6,4,128]{3,2,1,0:T(4,128)}, f32[4,6,4,128]{3,2,1,0:T(4,128)S(1)}, u32[]{:S(2)}, u32[]{:S(2)}) collective-permute-start(f32[4,6,4,128]{3,2,1,0:T(4,128)} %get-tuple-element.42.refs_0_), channel_id=1, source_target_pairs={{0,1},{1,2},{2,3},{3,0},{4,5},{5,6},{6,7},{7,4},{8,9},{9,10},{10,1... | collective-permute-start | bytes 147464 | tf_op jit(solution)/shard_map/ppermute | solution.py:626
  67.4 5.9 %collective-permute-start.5 = (f32[4,6,4,128]{3,2,1,0:T(4,128)}, f32[4,6,4,128]{3,2,1,0:T(4,128)S(1)}, u32[]{:S(2)}, u32[]{:S(2)}) collective-permute-start(f32[4,6,4,128]{3,2,1,0:T(4,128)} %get-tuple-element.42.refs_0_), channel_id=1, source_target_pairs={{0,2},{1,3},{2,0},{3,1},{4,6},{5,7},{6,4},{7,5},{8,10},{9,11},{10,... | collective-permute-start | bytes 147464 | tf_op jit(solution)/shard_map/ppermute | solution.py:626
  70.0 3.4 %collective-permute-start.6 = (f32[4,6,4,128]{3,2,1,0:T(4,128)}, f32[4,6,4,128]{3,2,1,0:T(4,128)S(1)}, u32[]{:S(2)}, u32[]{:S(2)}) collective-permute-start(f32[4,6,4,128]{3,2,1,0:T(4,128)} %get-tuple-element.42.refs_0_), channel_id=1, source_target_pairs={{0,3},{1,0},{2,1},{3,2},{4,7},{5,4},{6,5},{7,6},{8,11},{9,8},{10,9... | collective-permute-start | bytes 147464 | tf_op jit(solution)/shard_map/ppermute | solution.py:626
  73.3 0.6 copy-start.4
  73.3 0.6 copy-start.5
  73.4 0.6 copy-start.6

commit v20 on v18

--- a/solution.py
+++ b/solution.py
@@ -613,7 +613,7 @@
     y, v, w = (x.reshape(nt, ncl, nwl) for x in (y, v, w))
 
     lines = nt * ncl
-    nsub = 4
+    nsub = 2
 
     def wl(x):
         return jnp.transpose(x, (2, 0, 1)).reshape(nwl, lines // 128, 128)

time: 77.5 us -> 77.4 us (level)
  transfers between devices with their start and end apart: 8 -> 8, of which waited for: 2 -> 1; matrix products, arithmetic and copies ran while one was open for 2% -> 2% of each run, Pallas kernels for 13% -> 13%
where the time goes in v20:
time: 77.4 us; the launch traced here: 76.9 us
  blocking collectives  24.5 us (32%)
  Pallas kernels  20.8 us (27%)
  starting transfers between devices  19.9 us (26%)
  waiting for transfers between devices  6.37 us (8%)
  local copies, waits for them, and re-layouts  4.66 us (6%)
    all_to_all x1, blocking collectives, shards(): lax.all_to_all(summ.reshape(nc, nt // nc, 8, nwl), 'cast', 0, 0, tiled=True)  24.5 us
    all_to_all x1, waiting for transfers between devices, shards(): back = lax.all_to_all(lr, 'cast', 0, 0, tiled=True).reshape(nt, 2, nwl)  6.35 us
    ppermute x3, starting transfers between devices, shards(): lax.ppermute(summ, 'width', [(i, (i + q) % nw) for i in range(nw)])  6.05 us
    all_to_all x1, starting transfers between devices, shards(): back = lax.all_to_all(lr, 'cast', 0, 0, tiled=True).reshape(nt, 2, nwl)  4.77 us
    pallas_call x1, Pallas kernels, prep_solve(): pl.pallas_call(functools.partial(_prep_kernel, n), out_shape=[shp] * 3 +...  4.27 us
    pallas_call x1, Pallas kernels, wfactor(): pl.pallas_call(functools.partial(_wfactor_kernel, n, nsub), out_shape=[sh...  3.74 us
    ppermute x1, starting transfers between devices, shards(): got_a = lax.ppermute(jnp.where(even, last, first), 'cast', in_chip)  3.29 us
    unnamed x20, local copies, waits for them, and re-layouts  3.29 us
  transfers between devices with their start and end apart: 8, of which 1 were waited for; matrix products, arithmetic and copies ran while one was open for 2% of the time, Pallas kernels for 13%

profile of v20, /device:TPU:1, one launch (start us, length us, event | category | flops | bytes accessed | tf_op | source)
XLA Modules:
  0.0 76.9 jit_solution(8389488298590457040)
XLA Ops:
  0.0 1.1 %fusion = (f32[64,1,128]{2,1,0:T(1,128)S(1)}, f32[64,1,128]{2,1,0:T(1,128)S(1)}) fusion(f32[64,8,128]{2,1,0:T(8,128)} %refs_12_.1), kind=kLoop, calls=%fused_computation.2 | loop fusion | bytes 131072 | tf_op jit(solution)/shard_map/slice | solution.py:591
  1.2 3.3 %collective-permute-start.2 = (f32[64,128]{1,0:T(8,128)S(1)}, f32[64,128]{1,0:T(8,128)S(1)}, u32[]{:S(2)}, u32[]{:S(2)}) collective-permute-start(f32[64,128]{1,0:T(8,128)S(1)} %get-tuple-element.58), channel_id=1, source_target_pairs={{0,4},{4,0},{8,12},{12,8},{16,20},{20,16},{24,28},{28,24},{32,36},... | collective-permute-start | bytes 98312 | tf_op jit(solution)/shard_map/ppermute | solution.py:594
  4.5 1.9 %collective-permute-start.3 = (f32[64,128]{1,0:T(8,128)S(1)}, f32[64,128]{1,0:T(8,128)S(1)}, u32[]{:S(2)}, u32[]{:S(2)}) collective-permute-start(f32[64,128]{1,0:T(8,128)S(1)} %get-tuple-element.57), channel_id=1, source_target_pairs={{4,8},{12,16},{20,24},{28,32},{36,40},{44,48},{52,56},{60,64},{68,... | collective-permute-start | bytes 98312 | tf_op jit(solution)/shard_map/ppermute | solution.py:595
  6.4 0.1 fusion.1
  6.5 0.4 copy.13
  7.0 2.6 %collective-permute-start = (f32[64,8]{1,0:T(8,128)S(1)}, f32[64,8]{1,0:T(8,128)S(1)}, u32[]{:S(2)}, u32[]{:S(2)}) collective-permute-start(f32[64,8]{1,0:T(8,128)S(1)} %bitcast.38), channel_id=1, source_target_pairs={{0,1},{1,2},{2,3},{4,5},{5,6},{6,7},{8,9},{9,10},{10,11},{12,13},{... | collective-permute-start | bytes 6152 | tf_op jit(solution)/shard_map/ppermute | solution.py:596
  9.6 0.4 copy.14
  10.0 1.3 %collective-permute-start.1 = (f32[64,8]{1,0:T(8,128)S(1)}, f32[64,8]{1,0:T(8,128)S(1)}, u32[]{:S(2)}, u32[]{:S(2)}) collective-permute-start(f32[64,8]{1,0:T(8,128)S(1)} %bitcast.39), channel_id=1, source_target_pairs={{1,0},{2,1},{3,2},{5,4},{6,5},{7,6},{9,8},{10,9},{11,10},{13,12},{... | collective-permute-start | bytes 6152 | tf_op jit(solution)/shard_map/ppermute | solution.py:597
  11.3 0.1 stack.30
  11.4 0.5 stack.31.fl_ref
  12.0 0.0 collective-permute-done.2.hcl_ref
  12.0 0.6 copy-done.4
  12.6 0.0 copy-done.5
  12.6 4.3 %shard_map.37 = (f32[512,128]{1,0:T(8,128)}, f32[512,128]{1,0:T(8,128)}, f32[512,128]{1,0:T(8,128)}, f32[512,128]{1,0:T(8,128)}, f32[512,128]{1,0:T(8,128)}, /*i...) custom-call(f32[512,128]{1,0:T(8,128)} %bitcast.24, ...), custom_call_target="tpu_custom_call" | custom-call | tf_op jit(solution)/shard_map/pallas_call | solution.py:292
  16.9 0.6 copy-done.2
  17.5 0.0 copy-done.3
  17.5 3.1 %shard_map.38 = (f32[512,128]{1,0:T(8,128)}, f32[512,128]{1,0:T(8,128)}) custom-call(f32[512,128]{1,0:T(8,128)} %bitcast.25, f32[64,8]{1,0:T(8,128)} %copy-done.2, f32[64,8]{1,0:T(8,128)} %copy-done.3, f32[5]{0:T(128)} %stack.31.fl_ref, f32[512,128]{1,0:T(8,128)} %get-tuple-element.29.a_ref, f32[512,128]{1,0:T(8,128)} %get-tuple-element.30.r_ref, ...), custom_call_target="tpu_custom_call" | custom-call | tf_op jit(solution)/shard_map/pallas_call | solution.py:329
  20.6 24.5 %all_to_all.10.s_ref = f32[64,1,8,128]{3,2,1,0:T(8,128)} all-to-all(f32[64,1,8,128]{3,2,1,0:T(8,128)} %bitcast.35), channel_id=1, replica_groups=mesh['cast'=64,'width'=4] {'cast'}, dimensions={0} | all-to-all | bytes 524288 | tf_op jit(solution)/shard_map/all_to_all | solution.py:609
  45.1 1.9 %shard_map.39 = f32[64,1,2,128]{3,2,1,0:T(2,128)} custom-call(f32[64,1,8,128]{3,2,1,0:T(8,128)} %all_to_all.10.s_ref), custom_call_target="tpu_custom_call" | custom-call | tf_op jit(solution)/shard_map/pallas_call | solution.py:611
  47.0 4.8 %all-to-all-start.1 = ((f32[64,1,2,128]{3,2,1,0:T(2,128)}), f32[64,1,2,128]{3,2,1,0:T(2,128)S(1)}, u32[]{:S(2)}, u32[]{:S(2)}) async-start(f32[64,1,2,128]{3,2,1,0:T(2,128)} %shard_map.39), calls=%async_computation.1 | async-start | bytes 131072 | tf_op jit(solution)/shard_map/all_to_all | solution.py:612
  51.8 3.7 %shard_map.40 = (f32[128,4,128]{2,1,0:T(4,128)}, f32[128,4,128]{2,1,0:T(4,128)}, f32[128,4,128]{2,1,0:T(4,128)}, f32[128,4,128]{2,1,0:T(4,128)}, f32[128,4,128]{2,1,0:T(4,128)}, /*index=5*/f32[2,4,4,128]{3,2,1,0:T(4,128)}) custom-call(f32[512,128]{1,0:T(8,128)} %bitcast.26, f32[64,8]{1,0:T(8,128)} %copy-done.2, f32[64,8]{1,0:T(8,128)} %copy-done.3, ...), custom_call_target="tpu_custom_call" | custom-call | tf_op jit(solution)/shard_map/pallas_call | solution.py:367
  55.5 6.4 %all-to-all-done.1 = f32[64,1,2,128]{3,2,1,0:T(2,128)S(1)} async-done(((f32[64,1,2,128]{3,2,1,0:T(2,128)}), f32[64,1,2,128]{3,2,1,0:T(2,128)S(1)}, u32[]{:S(2)}, u32[]{:S(2)}) %all-to-all-start.1) | async-done | bytes 65568 | tf_op jit(solution)/shard_map/all_to_all | solution.py:612
  61.9 0.6 copy-done.1
  62.5 2.6 %shard_map.41 = (f32[128,4,128]{2,1,0:T(4,128)}, f32[2,6,4,128]{3,2,1,0:T(4,128)}) custom-call(f32[64,8,128]{2,1,0:T(8,128)} %bitcast.33, f32[64,8,128]{2,1,0:T(8,128)} %bitcast.31, f32[64,8,128]{2,1,0:T(8,128)} %bitcast.32, f32[64,2,128]{2,1,0:T(2,128)} %bitcast.34, f32[128,4,128]{2,1,0:T(4,128)} %get-tuple-element.38.a_ref, ...), custom_call_target="tpu_custom_call" | custom-call | tf_op jit(solution)/shard_map/pallas_call | solution.py:433
  65.1 2.4 %collective-permute-start.4 = (f32[2,6,4,128]{3,2,1,0:T(4,128)}, f32[2,6,4,128]{3,2,1,0:T(4,128)S(1)}, u32[]{:S(2)}, u32[]{:S(2)}) collective-permute-start(f32[2,6,4,128]{3,2,1,0:T(4,128)} %get-tuple-element.42.refs_0_), channel_id=1, source_target_pairs={{0,1},{1,2},{2,3},{3,0},{4,5},{5,6},{6,7},{7,4},{8,9},{9,10},{10,1... | collective-permute-start | bytes 73736 | tf_op jit(solution)/shard_map/ppermute | solution.py:626
  67.5 2.6 %collective-permute-start.5 = (f32[2,6,4,128]{3,2,1,0:T(4,128)}, f32[2,6,4,128]{3,2,1,0:T(4,128)S(1)}, u32[]{:S(2)}, u32[]{:S(2)}) collective-permute-start(f32[2,6,4,128]{3,2,1,0:T(4,128)} %get-tuple-element.42.refs_0_), channel_id=1, source_target_pairs={{0,2},{1,3},{2,0},{3,1},{4,6},{5,7},{6,4},{7,5},{8,10},{9,11},{10,... | collective-permute-start | bytes 73736 | tf_op jit(solution)/shard_map/ppermute | solution.py:626
  70.1 1.1 %collective-permute-start.6 = (f32[2,6,4,128]{3,2,1,0:T(4,128)}, f32[2,6,4,128]{3,2,1,0:T(4,128)S(1)}, u32[]{:S(2)}, u32[]{:S(2)}) collective-permute-start(f32[2,6,4,128]{3,2,1,0:T(4,128)} %get-tuple-element.42.refs_0_), channel_id=1, source_target_pairs={{0,3},{1,0},{2,1},{3,2},{4,7},{5,4},{6,5},{7,6},{8,11},{9,8},{10,9... | collective-permute-start | bytes 73736 | tf_op jit(solution)/shard_map/ppermute | solution.py:626
  71.2 2.2 %shard_map.42 = (f32[64,8,128]{2,1,0:T(8,128)}, f32[64,8,128]{2,1,0:T(8,128)}, f32[64,8,128]{2,1,0:T(8,128)}, f32[64,8,128]{2,1,0:T(8,128)}) custom-call(f32[64,8,128]{2,1,0:T(8,128)} %bitcast.27, f32[64,8,128]{2,1,0:T(8,128)} %bitcast.29, f32[64,8,128]{2,1,0:T(8,128)} %bitcast.30), custom_call_target="tpu_custom_call" | custom-call | tf_op jit(solution)/shard_map/pallas_call | solution.py:182
  73.5 0.6 copy-done.6
  74.0 0.0 copy-done.7
  74.0 0.0 copy-done.8
  74.0 2.9 %shard_map.43 = f32[64,8,128]{2,1,0:T(8,128)} custom-call(s32[1]{0:T(128)} %bitcast.me_ref, f32[2,6,4,128]{3,2,1,0:T(4,128)} %get-tuple-element.42.refs_0_, f32[2,6,4,128]{3,2,1,0:T(4,128)} %copy-done.6, f32[2,6,4,128]{3,2,1,0:T(4,128)} %copy-done.7, f32[2,6,4,128]{3,2,1,0:T(4,128)} %copy-done.8, f32[128,4,128]{2,1,0:T(4,128)} %get-tuple-element.43.refs_4_, ...), custom_call_target="tpu_custom_call" | custom-call | tf_op jit(solution)/shard_map/pallas_call | solution.py:442
  (17 shorter events, 0.0 us)
Async XLA Ops:
  0.0 6.4 %copy-start = (f32[64,8,128]{2,1,0:T(8,128)S(1)}, f32[64,8,128]{2,1,0:T(8,128)}, u32[]{:S(2)}) copy-start(f32[64,8,128]{2,1,0:T(8,128)} %refs_12_.1) | copy-start | bytes 786436
  1.2 10.8 %collective-permute-start.2 = (f32[64,128]{1,0:T(8,128)S(1)}, f32[64,128]{1,0:T(8,128)S(1)}, u32[]{:S(2)}, u32[]{:S(2)}) collective-permute-start(f32[64,128]{1,0:T(8,128)S(1)} %get-tuple-element.58), channel_id=1, source_target_pairs={{0,4},{4,0},{8,12},{12,8},{16,20},{20,16},{24,28},{28,24},{32,36},... | collective-permute-start | bytes 98312 | tf_op jit(solution)/shard_map/ppermute | solution.py:594
  4.5 7.5 %collective-permute-start.3 = (f32[64,128]{1,0:T(8,128)S(1)}, f32[64,128]{1,0:T(8,128)S(1)}, u32[]{:S(2)}, u32[]{:S(2)}) collective-permute-start(f32[64,128]{1,0:T(8,128)S(1)} %get-tuple-element.57), channel_id=1, source_target_pairs={{4,8},{12,16},{20,24},{28,32},{36,40},{44,48},{52,56},{60,64},{68,... | collective-permute-start | bytes 98312 | tf_op jit(solution)/shard_map/ppermute | solution.py:595
  7.0 9.9 %collective-permute-start = (f32[64,8]{1,0:T(8,128)S(1)}, f32[64,8]{1,0:T(8,128)S(1)}, u32[]{:S(2)}, u32[]{:S(2)}) collective-permute-start(f32[64,8]{1,0:T(8,128)S(1)} %bitcast.38), channel_id=1, source_target_pairs={{0,1},{1,2},{2,3},{4,5},{5,6},{6,7},{8,9},{9,10},{10,11},{12,13},{... | collective-permute-start | bytes 6152 | tf_op jit(solution)/shard_map/ppermute | solution.py:596
  10.0 6.9 %collective-permute-start.1 = (f32[64,8]{1,0:T(8,128)S(1)}, f32[64,8]{1,0:T(8,128)S(1)}, u32[]{:S(2)}, u32[]{:S(2)}) collective-permute-start(f32[64,8]{1,0:T(8,128)S(1)} %bitcast.39), channel_id=1, source_target_pairs={{1,0},{2,1},{3,2},{5,4},{6,5},{7,6},{9,8},{10,9},{11,10},{13,12},{... | collective-permute-start | bytes 6152 | tf_op jit(solution)/shard_map/ppermute | solution.py:597
  12.0 0.6 copy-start.4
  12.0 0.6 copy-start.5
  16.9 0.6 copy-start.2
  16.9 0.6 copy-start.3
  47.0 14.9 %all-to-all-start.1 = ((f32[64,1,2,128]{3,2,1,0:T(2,128)}), f32[64,1,2,128]{3,2,1,0:T(2,128)S(1)}, u32[]{:S(2)}, u32[]{:S(2)}) async-start(f32[64,1,2,128]{3,2,1,0:T(2,128)} %shard_map.39), calls=%async_computation.1 | async-start | bytes 131072 | tf_op jit(solution)/shard_map/all_to_all | solution.py:612
  61.9 0.6 copy-start.1
  65.1 8.3 %collective-permute-start.4 = (f32[2,6,4,128]{3,2,1,0:T(4,128)}, f32[2,6,4,128]{3,2,1,0:T(4,128)S(1)}, u32[]{:S(2)}, u32[]{:S(2)}) collective-permute-start(f32[2,6,4,128]{3,2,1,0:T(4,128)} %get-tuple-element.42.refs_0_), channel_id=1, source_target_pairs={{0,1},{1,2},{2,3},{3,0},{4,5},{5,6},{6,7},{7,4},{8,9},{9,10},{10,1... | collective-permute-start | bytes 73736 | tf_op jit(solution)/shard_map/ppermute | solution.py:626
  67.5 5.9 %collective-permute-start.5 = (f32[2,6,4,128]{3,2,1,0:T(4,128)}, f32[2,6,4,128]{3,2,1,0:T(4,128)S(1)}, u32[]{:S(2)}, u32[]{:S(2)}) collective-permute-start(f32[2,6,4,128]{3,2,1,0:T(4,128)} %get-tuple-element.42.refs_0_), channel_id=1, source_target_pairs={{0,2},{1,3},{2,0},{3,1},{4,6},{5,7},{6,4},{7,5},{8,10},{9,11},{10,... | collective-permute-start | bytes 73736 | tf_op jit(solution)/shard_map/ppermute | solution.py:626
  70.1 3.3 %collective-permute-start.6 = (f32[2,6,4,128]{3,2,1,0:T(4,128)}, f32[2,6,4,128]{3,2,1,0:T(4,128)S(1)}, u32[]{:S(2)}, u32[]{:S(2)}) collective-permute-start(f32[2,6,4,128]{3,2,1,0:T(4,128)} %get-tuple-element.42.refs_0_), channel_id=1, source_target_pairs={{0,3},{1,0},{2,1},{3,2},{4,7},{5,4},{6,5},{7,6},{8,11},{9,8},{10,9... | collective-permute-start | bytes 73736 | tf_op jit(solution)/shard_map/ppermute | solution.py:626
  73.4 0.6 copy-start.6
  73.4 0.6 copy-start.7
  73.4 0.6 copy-start.8
